TPU v7x, 512 devices: a whole 4x4x16 slice. The times are simulated.
512 devices in a mesh: outer: 16 (over y, z_hi, core), inner: 32 (over x, z_lo).
Axes of the slice: x: 4, y: 4, z: 16 (z_hi: 2, z_lo: 8; z = z_hi * 8 + z_lo), core: 2. Of those that a mesh axis runs over, the one named last changes fastest.
Arguments:
- signal: bfloat16 [524288, 256], P(('outer', 'inner')), may hold values from -6 to 6
- conv_past: bfloat16 [2, 256, 512], replicated, may hold values from -0.25 to 0.25
- conv_now: bfloat16 [2, 256, 512], replicated, may hold values from -0.25 to 0.25
- out_proj: bfloat16 [2, 256, 256], replicated, may hold values from -0.375 to 0.375
- cotangent: bfloat16 [524288, 256], P(('outer', 'inner')), may hold values from -6 to 6
Outputs:
- result: bfloat16 [524288, 256], P(('outer', 'inner'))
- grad_signal: bfloat16 [524288, 256], P(('outer', 'inner'))
- grad_past: float32 [2, 256, 512], P(None, 'inner')
- grad_now: float32 [2, 256, 512], P(None, 'inner')
- grad_out: float32 [2, 256, 256], P(None, 'inner')
All inputs are finite; a program needn't handle non-finite values.
Results may differ from a plain program's by a relative error of at most 0.0056.
Values may be sent and summed in bfloat16 or wider, within the bound.
No kernel may reach another device: no remote copies, remote signals or barrier semaphores. Data moves between devices by JAX's collectives and lax.ppermute only.
A program may use at most 64 MiB of HBM per device.

v0:
```python
import math

import jax
import jax.numpy as jnp
from jax import lax
from jax.sharding import Mesh
from jax.sharding import PartitionSpec as P

OUTER_INNER = ("outer", "inner_0", "inner_1")
INNER = ("inner_0", "inner_1")


def from_behind(array, axis, by):
    size = lax.axis_size(axis)
    pairs = [(i, i + by) for i in range(size) if 0 <= i + by < size]
    return lax.ppermute(array, axis, pairs)


def sum_by_axis(total, axes):
    for axis in axes:
        total = lax.psum_scatter(total, axis, scatter_dimension=0, tiled=True)
    return total


def copy_for_each(array, axis):
    size = lax.axis_size(axis)
    return lax.all_to_all(
        jnp.broadcast_to(array[None], (size, *array.shape)), axis, 0, 0, tiled=True
    )


def of_everyone(array, axis):
    return copy_for_each(array, axis).sum(axis=0)


def gating(current, earlier, w_past, w_now):
    preact = jnp.dot(earlier, w_past, preferred_element_type=jnp.float32) + jnp.dot(
        current, w_now, preferred_element_type=jnp.float32
    )
    half_width = preact.shape[1] // 2
    return (jnp.tanh(preact[:, :half_width]), jax.nn.sigmoid(preact[:, half_width:]))


def fetch_past(series, layer_at):
    if layer_at == 0:
        return from_behind(series, OUTER_INNER, 1)
    return from_behind(series, "outer", 2)


def fetch_again(series, layer_at):
    if layer_at == 0:
        return from_behind(series, OUTER_INNER, 1)
    return from_behind(series, "outer", 2)


def return_past(series, layer_at):
    if layer_at == 0:
        return from_behind(series, OUTER_INNER, -1)
    return from_behind(series, "outer", -2)


def layer_term(operands, grad_scale):
    earlier, current, gated_out, grad_preact, upstream = operands

    def contract(left_op, right_op):
        return lax.dot_general(
            left_op, right_op, (((0,), (0,)), ((), ())), preferred_element_type=jnp.float32
        )

    return (
        jnp.concatenate(
            [
                contract(earlier, grad_preact),
                contract(current, grad_preact),
                contract(gated_out, upstream),
            ],
            1,
        )
        * grad_scale
    )


def joint_share(operand_list, grad_scale):
    portion = sum_by_axis(
        jnp.concatenate([layer_term(operands, grad_scale) for operands in operand_list], 1), INNER
    )
    return of_everyone(portion, "outer")


def local(signal, conv_past, conv_now, out_proj, cotangent):
    channels = signal.shape[1]
    gate_width = conv_past.shape[2]
    term_width = 2 * gate_width + channels
    tick_count = signal.shape[0] * lax.axis_size("outer") * lax.axis_size(INNER)
    grad_scale = 1.0 / math.sqrt(tick_count)
    layer_count = conv_past.shape[0]
    inputs, earliers, saved = ([], [], [])
    current = signal
    for layer_at in range(layer_count):
        earlier = fetch_past(current, layer_at)
        tanh_part, sig_part = gating(current, earlier, conv_past[layer_at], conv_now[layer_at])
        gated_out = (tanh_part * sig_part).astype(jnp.bfloat16)
        inputs.append(current)
        earliers.append(earlier)
        saved.append((tanh_part, sig_part, gated_out))
        current = (
            current.astype(jnp.float32)
            + jnp.dot(gated_out, out_proj[layer_at], preferred_element_type=jnp.float32)
        ).astype(jnp.bfloat16)
    result = current
    upstream = cotangent
    summed_list = [None] * layer_count
    operand_list = [None] * layer_count
    for layer_at in reversed(range(layer_count)):
        current = inputs[layer_at]
        earlier = fetch_again(current, layer_at)
        tanh_part, sig_part, gated_out = saved[layer_at]
        grad_gated = jnp.dot(upstream, out_proj[layer_at].T, preferred_element_type=jnp.float32)
        grad_filter = grad_gated * sig_part * (1.0 - tanh_part * tanh_part)
        grad_gate = grad_gated * tanh_part * sig_part * (1.0 - sig_part)
        grad_preact = jnp.concatenate([grad_filter, grad_gate], 1).astype(jnp.bfloat16)
        sent_back = jnp.dot(
            grad_preact, conv_past[layer_at].T, preferred_element_type=jnp.float32
        ).astype(jnp.bfloat16)
        arrived = return_past(sent_back, layer_at)
        operands = (earlier, current, gated_out, grad_preact, upstream)
        operand_list[layer_at] = operands
        local_grad = upstream.astype(jnp.float32) + jnp.dot(
            grad_preact, conv_now[layer_at].T, preferred_element_type=jnp.float32
        )
        upstream = (local_grad + arrived.astype(jnp.float32)).astype(jnp.bfloat16)
    whole = joint_share(operand_list, grad_scale)
    summed_list = [
        whole[:, layer_at * term_width : (layer_at + 1) * term_width]
        for layer_at in range(layer_count)
    ]
    past_list = [summed[:, :gate_width] for summed in summed_list]
    now_list = [summed[:, gate_width : 2 * gate_width] for summed in summed_list]
    out_list = [summed[:, 2 * gate_width :] for summed in summed_list]
    return (result, upstream, jnp.stack(past_list), jnp.stack(now_list), jnp.stack(out_list))


def solution(mesh):
    split = Mesh(mesh.devices.reshape(mesh.shape["outer"], 4, 8), ("outer", "inner_0", "inner_1"))
    placed = (P(OUTER_INNER, None), P(), P(), P(), P(OUTER_INNER, None))
    return jax.shard_map(
        local,
        mesh=split,
        in_specs=placed,
        out_specs=(
            P(OUTER_INNER, None),
            P(OUTER_INNER, None),
            P(None, INNER, None),
            P(None, INNER, None),
            P(None, INNER, None),
        ),
        check_vma=False,
    )
```

profile of v0, /device:TPU:1, one launch (start us, length us, event | category | flops | bytes accessed | tf_op | source)
XLA Modules:
  0.0 335.7 jit_solution(14422664342839155761)
XLA Ops:
  7.2 0.0 copy-start.3
  7.2 0.0 reduce-scatter.7.cloned.1.call-start
  7.2 4.5 %collective-permute-start = (bf16[1024,256]{1,0:T(8,128)(2,1)}, bf16[1024,256]{1,0:T(8,128)(2,1)S(1)}, u32[]{:S(2)}, u32[]{:S(2)}) collective-permute-start(bf16[1024,256]{1,0:T(8,128)(2,1)} %param.5), channel_id=1, source_target_pairs={{0,1},{1,2},{2,3},{3,4},{4,5},{5,6},{6,7},{7,8},{8,9},{9,10},{10,1... | collective-permute-start | bytes 1572872 | tf_op jit(solution)/shard_map/ppermute | solution.py:16
  11.7 1.6 fusion.15
  13.3 20.6 %collective-permute-done = bf16[1024,256]{1,0:T(8,128)(2,1)S(1)} collective-permute-done((bf16[1024,256]{1,0:T(8,128)(2,1)}, bf16[1024,256]{1,0:T(8,128)(2,1)S(1)}, u32[]{:S(2)}, u32[]{:S(2)}) %collective-permute-start) | collective-permute-done | bytes 524320 | tf_op jit(solution)/shard_map/ppermute | solution.py:16
  33.9 0.0 copy-done.3
  33.9 0.5 convolution_add_fusion.1
  34.4 0.0 copy-start.2
  34.4 0.0 copy-start.10
  34.4 0.0 copy-start.8
  34.4 0.4 multiply_convert_fusion.5
  34.9 0.6 copy-done.2
  35.4 0.1 copy-done.10
  35.5 0.4 fusion
  35.9 9.4 %collective-permute-start.1 = (bf16[1024,256]{1,0:T(8,128)(2,1)S(1)}, bf16[1024,256]{1,0:T(8,128)(2,1)S(1)}, u32[]{:S(2)}, u32[]{:S(2)}) collective-permute-start(bf16[1024,256]{1,0:T(8,128)(2,1)S(1)} %fusion), channel_id=1, source_target_pairs={{0,64},{32,96},{64,128},{96,160},{128,192},{160,224},{192,256},{22... | collective-permute-start | bytes 1572872 | tf_op jit(solution)/shard_map/ppermute | solution.py:16
  45.3 0.0 copy-done.8
  45.3 0.5 fusion.9
  45.8 0.0 copy-start.5
  45.8 39.3 %collective-permute-done.1 = bf16[1024,256]{1,0:T(8,128)(2,1)S(1)} collective-permute-done((bf16[1024,256]{1,0:T(8,128)(2,1)S(1)}, bf16[1024,256]{1,0:T(8,128)(2,1)S(1)}, u32[]{:S(2)}, u32[]{:S(2)}) %collective-permute-start.1) | collective-permute-done | bytes 524320 | tf_op jit(solution)/shard_map/ppermute | solution.py:16
  85.0 0.5 convolution_add_fusion
  85.5 0.0 copy-done.5
  85.6 0.8 multiply_convert_fusion.3
  86.3 0.0 copy-start
  86.3 0.4 fusion.40
  86.8 0.5 convolution_convert_fusion.1
  87.3 0.0 copy-done
  87.3 0.3 fusion.42
  87.7 1.3 collective-permute-start.2
  89.0 0.4 fusion.39
  89.4 0.1 maximum_multiply_fusion.1
  89.5 22.7 %collective-permute-done.2 = bf16[1024,256]{1,0:T(8,128)(2,1)S(1)} collective-permute-done((bf16[1024,256]{1,0:T(8,128)(2,1)S(1)}, bf16[1024,256]{1,0:T(8,128)(2,1)S(1)}, u32[]{:S(2)}, u32[]{:S(2)}) %collective-permute-start.2) | collective-permute-done | bytes 524320 | tf_op jit(solution)/shard_map/ppermute | solution.py:16
  112.2 0.5 add_convert_fusion.1
  112.7 0.0 copy-start.6
  112.7 0.7 multiply_convert_fusion.1
  113.4 0.1 copy-done.6
  113.5 0.4 fusion.41
  113.9 0.4 convolution_bitcast_fusion
  114.3 0.0 copy-done.11
  114.4 0.1 copy-done.13
  114.5 0.4 convolution_bitcast_fusion.1
  115.0 0.1 maximum_multiply_fusion
  115.1 0.2 pad_maximum_fusion
  115.3 2.1 copy.21
  117.3 0.0 reduce-scatter.7.cloned.1.call-update
  117.4 0.0 reduce-scatter.9.cloned.1.call-start
  117.4 67.1 %reduce-scatter.7.cloned.1.call-done = f32[64,2560]{1,0:T(8,128)} async-done(((f32[256,2560]{1,0:T(8,128)}), f32[64,2560]{1,0:T(8,128)}) %reduce-scatter.7.cloned.1.call-update) | async-done | bytes 655376
  184.5 0.0 reduce-scatter.9.cloned.1.call-update
  184.5 0.0 copy-start.4
  184.5 62.5 %reduce-scatter.9.cloned.1.call-done = f32[8,2560]{1,0:T(8,128)} async-done(((f32[64,2560]{1,0:T(8,128)}), f32[8,2560]{1,0:T(8,128)}) %reduce-scatter.9.cloned.1.call-update) | async-done | bytes 81936 | tf_op jit(solution)/shard_map/reduce_scatter | solution.py:21
  247.0 2.1 broadcast_in_dim.2
  249.1 13.2 %all-to-all-start = ((f32[16,8,2560]{2,1,0:T(8,128)}), f32[16,8,2560]{2,1,0:T(8,128)S(1)}, u32[]{:S(2)}, u32[]{:S(2)}) async-start(f32[16,8,2560]{2,1,0:T(8,128)} %broadcast_in_dim.2), calls=%async_computation | async-start | bytes 2621440 | tf_op jit(solution)/shard_map/all_to_all | solution.py:27
  262.3 0.0 copy-done.4
  262.3 0.0 copy-start.9
  262.3 1.8 convolution_convert_fusion
  264.2 11.3 %collective-permute-start.3 = (bf16[1024,256]{1,0:T(8,128)(2,1)S(1)}, bf16[1024,256]{1,0:T(8,128)(2,1)S(1)}, u32[]{:S(2)}, u32[]{:S(2)}) collective-permute-start(bf16[1024,256]{1,0:T(8,128)(2,1)S(1)} %convolution_convert_fusion), channel_id=1, source_target_pairs={{1,0},{2,1},{3,2},{4,3},{5,4},{6,5},{7,6},{8,7},{9,8},{10,9},{11,1... | collective-permute-start | bytes 1572872 | tf_op jit(solution)/shard_map/ppermute | solution.py:16
  275.5 0.0 copy-done.1
  275.5 1.2 fusion.1
  276.7 49.5 %collective-permute-done.3 = bf16[1024,256]{1,0:T(8,128)(2,1)S(1)} collective-permute-done((bf16[1024,256]{1,0:T(8,128)(2,1)S(1)}, bf16[1024,256]{1,0:T(8,128)(2,1)S(1)}, u32[]{:S(2)}, u32[]{:S(2)}) %collective-permute-start.3) | collective-permute-done | bytes 524320 | tf_op jit(solution)/shard_map/ppermute | solution.py:16
  326.2 0.0 copy-done.14
  326.2 1.3 add_convert_fusion
  327.5 0.0 all-to-all-done
  327.5 0.1 reduce_sum.9
  327.6 0.6 pad_maximum_fusion.5
  328.2 0.6 pad_maximum_fusion.3
  (11 shorter events, 0.0 us)
Async XLA Ops:
  7.2 26.7 %copy-start.3 = (bf16[2,256,512]{2,1,0:T(8,128)(2,1)S(1)}, bf16[2,256,512]{2,1,0:T(8,128)(2,1)}, u32[]{:S(2)}) copy-start(bf16[2,256,512]{2,1,0:T(8,128)(2,1)} %param.6) | copy-start | bytes 1572868
  7.2 177.3 %reduce-scatter.7.cloned.1.call-start = ((), (), s32[]{:S(2)}) async-start(), calls=%async_computation.3 | async-start | bytes 3276800
  7.2 26.7 %collective-permute-start = (bf16[1024,256]{1,0:T(8,128)(2,1)}, bf16[1024,256]{1,0:T(8,128)(2,1)S(1)}, u32[]{:S(2)}, u32[]{:S(2)}) collective-permute-start(bf16[1024,256]{1,0:T(8,128)(2,1)} %param.5), channel_id=1, source_target_pairs={{0,1},{1,2},{2,3},{3,4},{4,5},{5,6},{6,7},{7,8},{8,9},{9,10},{10,1... | collective-permute-start | bytes 1572872 | tf_op jit(solution)/shard_map/ppermute | solution.py:16
  34.4 1.0 copy-start.2
  34.4 1.1 copy-start.10
  34.4 10.9 %copy-start.8 = (bf16[2,256,512]{2,1,0:T(8,128)(2,1)S(1)}, bf16[2,256,512]{2,1,0:T(8,128)(2,1)}, u32[]{:S(2)}) copy-start(bf16[2,256,512]{2,1,0:T(8,128)(2,1)} %param.7) | copy-start | bytes 1572868
  35.9 49.2 %collective-permute-start.1 = (bf16[1024,256]{1,0:T(8,128)(2,1)S(1)}, bf16[1024,256]{1,0:T(8,128)(2,1)S(1)}, u32[]{:S(2)}, u32[]{:S(2)}) collective-permute-start(bf16[1024,256]{1,0:T(8,128)(2,1)S(1)} %fusion), channel_id=1, source_target_pairs={{0,64},{32,96},{64,128},{96,160},{128,192},{160,224},{192,256},{22... | collective-permute-start | bytes 1572872 | tf_op jit(solution)/shard_map/ppermute | solution.py:16
  45.8 39.8 %copy-start.5 = (bf16[1024,256]{1,0:T(8,128)(2,1)S(1)}, bf16[1024,256]{1,0:T(8,128)(2,1)}, u32[]{:S(2)}) copy-start(bf16[1024,256]{1,0:T(8,128)(2,1)} %param.9) | copy-start | bytes 1572868
  86.3 1.0 copy-start
  87.7 24.5 %collective-permute-start.2 = (bf16[1024,256]{1,0:T(8,128)(2,1)S(1)}, bf16[1024,256]{1,0:T(8,128)(2,1)S(1)}, u32[]{:S(2)}, u32[]{:S(2)}) collective-permute-start(bf16[1024,256]{1,0:T(8,128)(2,1)S(1)} %convolution_convert_fusion.1), channel_id=1, source_target_pairs={{64,0},{96,32},{128,64},{160,96},{192,128},{224,160},{256,192},{28... | collective-permute-start | bytes 1572872 | tf_op jit(solution)/shard_map/ppermute | solution.py:16
  112.7 0.8 copy-start.6
  113.5 0.8 copy-start.11
  113.5 1.0 copy-start.13
  117.4 129.6 %reduce-scatter.9.cloned.1.call-start = ((), (), s32[]{:S(2)}) async-start(), calls=%async_computation.4 | async-start | bytes 737280 | tf_op jit(solution)/shard_map/reduce_scatter | solution.py:21
  184.5 77.8 %copy-start.4 = (bf16[2,256,512]{2,1,0:T(8,128)(2,1)S(1)}, bf16[2,256,512]{2,1,0:T(8,128)(2,1)}, u32[]{:S(2)}) copy-start(bf16[2,256,512]{2,1,0:T(8,128)(2,1)} %param.6) | copy-start | bytes 1572868
  249.1 26.4 %copy-start.1 = (bf16[1024,256]{0,1:T(8,128)(2,1)S(1)}, bf16[1024,256]{0,1:T(8,128)(2,1)}, u32[]{:S(2)}) copy-start(bf16[1024,256]{0,1:T(8,128)(2,1)} %copy-done) | copy-start | bytes 1572868
  249.1 78.4 %all-to-all-start = ((f32[16,8,2560]{2,1,0:T(8,128)}), f32[16,8,2560]{2,1,0:T(8,128)S(1)}, u32[]{:S(2)}, u32[]{:S(2)}) async-start(f32[16,8,2560]{2,1,0:T(8,128)} %broadcast_in_dim.2), calls=%async_computation | async-start | bytes 2621440 | tf_op jit(solution)/shard_map/all_to_all | solution.py:27
  262.3 63.9 %copy-start.7 = (bf16[1024,256]{1,0:T(8,128)(2,1)S(1)}, bf16[1024,256]{1,0:T(8,128)(2,1)}, u32[]{:S(2)}) copy-start(bf16[1024,256]{1,0:T(8,128)(2,1)} %copy-done.6) | copy-start | bytes 1572868
  262.3 63.9 %copy-start.9 = (bf16[2,256,512]{2,1,0:T(8,128)(2,1)S(1)}, bf16[2,256,512]{2,1,0:T(8,128)(2,1)}, u32[]{:S(2)}) copy-start(bf16[2,256,512]{2,1,0:T(8,128)(2,1)} %param.7) | copy-start | bytes 1572868
  262.3 63.9 %copy-start.12 = (bf16[1024,256]{0,1:T(8,128)(2,1)S(1)}, bf16[1024,256]{0,1:T(8,128)(2,1)}, u32[]{:S(2)}) copy-start(bf16[1024,256]{0,1:T(8,128)(2,1)} %copy-done.11) | copy-start | bytes 1572868
  262.3 63.9 %copy-start.14 = (bf16[1024,256]{0,1:T(8,128)(2,1)S(1)}, bf16[1024,256]{0,1:T(8,128)(2,1)}, u32[]{:S(2)}) copy-start(bf16[1024,256]{0,1:T(8,128)(2,1)} %copy-done.13) | copy-start | bytes 1572868
  264.2 62.0 %collective-permute-start.3 = (bf16[1024,256]{1,0:T(8,128)(2,1)S(1)}, bf16[1024,256]{1,0:T(8,128)(2,1)S(1)}, u32[]{:S(2)}, u32[]{:S(2)}) collective-permute-start(bf16[1024,256]{1,0:T(8,128)(2,1)S(1)} %convolution_convert_fusion), channel_id=1, source_target_pairs={{1,0},{2,1},{3,2},{4,3},{5,4},{6,5},{7,6},{8,7},{9,8},{10,9},{11,1... | collective-permute-start | bytes 1572872 | tf_op jit(solution)/shard_map/ppermute | solution.py:16
Sparse Core Ops, SparseCore 0:
  117.5 66.9 reduce-scatter.6
  187.3 59.6 reduce-scatter.8
where the time goes:
time: 337 us; the launch traced here: 336 us
  waiting for transfers between devices  262 us (78%)
  starting transfers between devices  39.8 us (12%)
  between operations  14.4 us (4%)
  matrix products  12.6 us (4%)
  local copies, waits for them, and re-layouts  5.16 us (2%)
    ppermute x4, waiting for transfers between devices, from_behind(): return lax.ppermute(array, axis, pairs)  132 us
    unnamed x3, waiting for transfers between devices  67.1 us
    reduce_scatter x1, waiting for transfers between devices, sum_by_axis(): total = lax.psum_scatter(total, axis, scatter_dimension=0, tiled=True)  62.5 us
    ppermute x4, starting transfers between devices, from_behind(): return lax.ppermute(array, axis, pairs)  26.5 us
    all_to_all x1, starting transfers between devices, copy_for_each(): lax.all_to_all(jnp.broadcast_to(array[None], (size, *array.shape)), axis,...  13.2 us
  transfers between devices with their start and end apart: 7, of which 6 were waited for; matrix products, arithmetic and copies ran while one was open for 2% of the time, Pallas kernels for 0%

commit v1 on v0

v1 whole, which is shorter than its diff:
```python
import math

import jax
import jax.numpy as jnp
from jax import lax
from jax.sharding import Mesh
from jax.sharding import PartitionSpec as P

OUTER = ("y", "z_hi", "core")
INNER = ("x", "z_lo")
EVERY = OUTER + INNER


def group_size(axes):
    size = 1
    for axis in axes:
        size *= lax.axis_size(axis)
    return size


def group_index(axes):
    index = 0
    for axis in axes:
        index = index * lax.axis_size(axis) + lax.axis_index(axis)
    return index


def from_behind(array, axes, by):
    size = group_size(axes)
    pairs = [(i, i + by) for i in range(size) if 0 <= i + by < size]
    return lax.ppermute(array, axes, pairs)


def scatter_sum(total, axes):
    size = group_size(axes)
    own = group_index(axes)
    pieces = total.reshape(size, total.shape[0] // size, *total.shape[1:])
    summed = lax.dynamic_index_in_dim(pieces, own, 0, keepdims=False)
    for shift in range(1, size):
        piece = lax.dynamic_index_in_dim(pieces, (own + shift) % size, 0, keepdims=False)
        summed = summed + lax.ppermute(piece, axes, [(i, (i + shift) % size) for i in range(size)])
    return summed


def everyone_sum(total, axes):
    size = group_size(axes)
    step = 1
    while step < size:
        total = total + lax.ppermute(total, axes, [(i, i ^ step) for i in range(size)])
        step *= 2
    return total


def weight_sum(term):
    for axis in INNER:
        term = scatter_sum(term, (axis,))
    return everyone_sum(term, OUTER)


def gating(current, earlier, w_past, w_now):
    preact = jnp.dot(earlier, w_past, preferred_element_type=jnp.float32) + jnp.dot(
        current, w_now, preferred_element_type=jnp.float32
    )
    half_width = preact.shape[1] // 2
    return (jnp.tanh(preact[:, :half_width]), jax.nn.sigmoid(preact[:, half_width:]))


def fetch_past(series, layer_at):
    if layer_at == 0:
        return from_behind(series, EVERY, 1)
    return from_behind(series, OUTER, 2)


def return_past(series, layer_at):
    if layer_at == 0:
        return from_behind(series, EVERY, -1)
    return from_behind(series, OUTER, -2)


def layer_term(operands, grad_scale):
    earlier, current, gated_out, grad_preact, upstream = operands

    def contract(left_op, right_op):
        return lax.dot_general(
            left_op, right_op, (((0,), (0,)), ((), ())), preferred_element_type=jnp.float32
        )

    return (
        jnp.concatenate(
            [
                contract(earlier, grad_preact),
                contract(current, grad_preact),
                contract(gated_out, upstream),
            ],
            1,
        )
        * grad_scale
    )


def local(signal, conv_past, conv_now, out_proj, cotangent):
    gate_width = conv_past.shape[2]
    tick_count = signal.shape[0] * group_size(EVERY)
    grad_scale = 1.0 / math.sqrt(tick_count)
    layer_count = conv_past.shape[0]
    inputs, earliers, saved = ([], [], [])
    current = signal
    for layer_at in range(layer_count):
        earlier = fetch_past(current, layer_at)
        tanh_part, sig_part = gating(current, earlier, conv_past[layer_at], conv_now[layer_at])
        gated_out = (tanh_part * sig_part).astype(jnp.bfloat16)
        inputs.append(current)
        earliers.append(earlier)
        saved.append((tanh_part, sig_part, gated_out))
        current = (
            current.astype(jnp.float32)
            + jnp.dot(gated_out, out_proj[layer_at], preferred_element_type=jnp.float32)
        ).astype(jnp.bfloat16)
    result = current
    upstream = cotangent
    summed_list = [None] * layer_count
    for layer_at in reversed(range(layer_count)):
        current = inputs[layer_at]
        earlier = earliers[layer_at]
        tanh_part, sig_part, gated_out = saved[layer_at]
        grad_gated = jnp.dot(upstream, out_proj[layer_at].T, preferred_element_type=jnp.float32)
        grad_filter = grad_gated * sig_part * (1.0 - tanh_part * tanh_part)
        grad_gate = grad_gated * tanh_part * sig_part * (1.0 - sig_part)
        grad_preact = jnp.concatenate([grad_filter, grad_gate], 1).astype(jnp.bfloat16)
        sent_back = jnp.dot(
            grad_preact, conv_past[layer_at].T, preferred_element_type=jnp.float32
        ).astype(jnp.bfloat16)
        arrived = return_past(sent_back, layer_at)
        operands = (earlier, current, gated_out, grad_preact, upstream)
        summed_list[layer_at] = weight_sum(layer_term(operands, grad_scale))
        local_grad = upstream.astype(jnp.float32) + jnp.dot(
            grad_preact, conv_now[layer_at].T, preferred_element_type=jnp.float32
        )
        upstream = (local_grad + arrived.astype(jnp.float32)).astype(jnp.bfloat16)
    past_list = [summed[:, :gate_width] for summed in summed_list]
    now_list = [summed[:, gate_width : 2 * gate_width] for summed in summed_list]
    out_list = [summed[:, 2 * gate_width :] for summed in summed_list]
    return (result, upstream, jnp.stack(past_list), jnp.stack(now_list), jnp.stack(out_list))


def solution(mesh):
    outer_size = mesh.shape["outer"]
    inner_size = mesh.shape["inner"]
    split = Mesh(
        mesh.devices.reshape(outer_size // 4, 2, 2, inner_size // 8, 8),
        ("y", "z_hi", "core", "x", "z_lo"),
    )
    placed = (P(EVERY, None), P(), P(), P(), P(EVERY, None))
    return jax.shard_map(
        local,
        mesh=split,
        in_specs=placed,
        out_specs=(
            P(EVERY, None),
            P(EVERY, None),
            P(None, INNER, None),
            P(None, INNER, None),
            P(None, INNER, None),
        ),
        check_vma=False,
    )
```

time: 337 us -> 278 us (0.82)
  the two profiles are of different devices: /device:TPU:1 before, /device:TPU:82 now
where the time goes in v1:
time: 278 us; the launch traced here: 277 us
  starting transfers between devices  192 us (69%)
  waiting for transfers between devices  60.7 us (22%)
  matrix products  15.8 us (6%)
  other arithmetic  3.32 us (1%)
  local copies, waits for them, and re-layouts  2.99 us (1%)
    ppermute x20, starting transfers between devices, scatter_sum(): lax.ppermute(piece, axes, [(i, (i + shift) % size) for i in range(size)])  91.2 us
    ppermute x4, starting transfers between devices, from_behind(): return lax.ppermute(array, axes, pairs)  62.5 us
    ppermute x8, starting transfers between devices, everyone_sum(): lax.ppermute(total, axes, [(i, i ^ step) for i in range(size)])  38.4 us
    ppermute x4, waiting for transfers between devices, from_behind(): return lax.ppermute(array, axes, pairs)  37.1 us
    ppermute x8, waiting for transfers between devices, everyone_sum(): lax.ppermute(total, axes, [(i, i ^ step) for i in range(size)])  23.6 us
  transfers between devices with their start and end apart: 32, of which 8 were waited for; matrix products, arithmetic and copies ran while one was open for 4% of the time, Pallas kernels for 0%

profile of v1, /device:TPU:82, one launch (start us, length us, event | category | flops | bytes accessed | tf_op | source)
XLA Modules:
  0.0 276.6 jit_solution(1987234147580823229)
XLA Ops:
  0.6 4.0 %collective-permute-start = (bf16[1024,256]{1,0:T(8,128)(2,1)}, bf16[1024,256]{1,0:T(8,128)(2,1)S(1)}, u32[]{:S(2)}, u32[]{:S(2)}) collective-permute-start(bf16[1024,256]{1,0:T(8,128)(2,1)} %param.5), channel_id=1, source_target_pairs={{0,1},{1,2},{2,3},{3,4},{4,5},{5,6},{6,7},{7,8},{8,9},{9,10},{10,1... | collective-permute-start | bytes 1572872 | tf_op jit(solution)/shard_map/ppermute | solution.py:31
  4.6 1.6 fusion.21
  6.2 10.3 %collective-permute-done = bf16[1024,256]{1,0:T(8,128)(2,1)S(1)} collective-permute-done((bf16[1024,256]{1,0:T(8,128)(2,1)}, bf16[1024,256]{1,0:T(8,128)(2,1)S(1)}, u32[]{:S(2)}, u32[]{:S(2)}) %collective-permute-start) | collective-permute-done | bytes 524320 | tf_op jit(solution)/shard_map/ppermute | solution.py:31
  16.5 0.5 convolution_add_fusion.1
  17.0 0.3 copy-done.10
  17.4 0.4 multiply_convert_fusion.5
  17.8 0.8 copy-done
  18.6 0.4 fusion
  19.0 13.9 %collective-permute-start.1 = (bf16[1024,256]{1,0:T(8,128)(2,1)S(1)}, bf16[1024,256]{1,0:T(8,128)(2,1)}, u32[]{:S(2)}, u32[]{:S(2)}) collective-permute-start(bf16[1024,256]{1,0:T(8,128)(2,1)S(1)} %fusion), channel_id=1, source_target_pairs={{0,64},{32,96},{64,128},{96,160},{128,192},{160,224},{192,256},{22... | collective-permute-start | bytes 1572872 | tf_op jit(solution)/shard_map/ppermute | solution.py:31
  32.9 1.4 fusion.15
  34.4 13.1 %collective-permute-done.1 = bf16[1024,256]{1,0:T(8,128)(2,1)} collective-permute-done((bf16[1024,256]{1,0:T(8,128)(2,1)S(1)}, bf16[1024,256]{1,0:T(8,128)(2,1)}, u32[]{:S(2)}, u32[]{:S(2)}) %collective-permute-start.1) | collective-permute-done | bytes 524320 | tf_op jit(solution)/shard_map/ppermute | solution.py:31
  47.5 1.5 convolution_add_fusion
  49.1 0.8 multiply_convert_fusion.3
  50.2 0.5 fusion.59
  50.7 1.5 fusion.60
  52.4 1.0 dynamic-slice_bitcast_fusion.2
  53.4 3.4 %collective-permute-start.18 = (f32[64,1280]{1,0:T(8,128)}, f32[64,1280]{1,0:T(8,128)}, u32[]{:S(2)}, u32[]{:S(2)}) collective-permute-start(f32[64,1280]{1,0:T(8,128)} %get-tuple-element.13), channel_id=1, source_target_pairs={{0,8},{8,16},{16,24},{24,0},{1,9},{9,17},{17,25},{25,1},{2,10},{10... | collective-permute-start | bytes 983048 | tf_op jit(solution)/shard_map/ppermute | solution.py:41
  56.8 3.3 %collective-permute-start.19 = (f32[64,1280]{1,0:T(8,128)}, f32[64,1280]{1,0:T(8,128)}, u32[]{:S(2)}, u32[]{:S(2)}) collective-permute-start(f32[64,1280]{1,0:T(8,128)} %get-tuple-element.15), channel_id=1, source_target_pairs={{0,16},{8,24},{16,0},{24,8},{1,17},{9,25},{17,1},{25,9},{2,18},{10... | collective-permute-start | bytes 983048 | tf_op jit(solution)/shard_map/ppermute | solution.py:41
  60.1 3.7 %collective-permute-start.20 = (f32[64,1280]{1,0:T(8,128)}, f32[64,1280]{1,0:T(8,128)}, u32[]{:S(2)}, u32[]{:S(2)}) collective-permute-start(f32[64,1280]{1,0:T(8,128)} %get-tuple-element.14), channel_id=1, source_target_pairs={{0,24},{8,0},{16,8},{24,16},{1,25},{9,1},{17,9},{25,17},{2,26},{10... | collective-permute-start | bytes 983048 | tf_op jit(solution)/shard_map/ppermute | solution.py:41
  64.0 1.9 convolution_convert_fusion.1
  65.9 42.7 %collective-permute-start.2 = (bf16[1024,256]{1,0:T(8,128)(2,1)S(1)}, bf16[1024,256]{1,0:T(8,128)(2,1)S(1)}, u32[]{:S(2)}, u32[]{:S(2)}) collective-permute-start(bf16[1024,256]{1,0:T(8,128)(2,1)S(1)} %convolution_convert_fusion.1), channel_id=1, source_target_pairs={{64,0},{96,32},{128,64},{160,96},{192,128},{224,160},{256,192},{28... | collective-permute-start | bytes 1572872 | tf_op jit(solution)/shard_map/ppermute | solution.py:31
  108.6 1.2 fusion.10
  109.9 2.1 collective-permute-start.21
  111.9 1.9 collective-permute-start.22
  113.9 14.5 %collective-permute-start.23 = (f32[8,1280]{1,0:T(8,128)S(1)}, f32[8,1280]{1,0:T(8,128)S(1)}, u32[]{:S(2)}, u32[]{:S(2)}) collective-permute-start(f32[8,1280]{1,0:T(8,128)S(1)} %get-tuple-element.28), channel_id=1, source_target_pairs={{0,3},{1,4},{2,5},{3,6},{4,7},{5,0},{6,1},{7,2},{8,11},{9,12},{10,... | collective-permute-start | bytes 122888 | tf_op jit(solution)/shard_map/ppermute | solution.py:41
  128.3 1.9 collective-permute-start.24
  130.3 13.7 %collective-permute-done.2 = bf16[1024,256]{1,0:T(8,128)(2,1)S(1)} collective-permute-done((bf16[1024,256]{1,0:T(8,128)(2,1)S(1)}, bf16[1024,256]{1,0:T(8,128)(2,1)S(1)}, u32[]{:S(2)}, u32[]{:S(2)}) %collective-permute-start.2) | collective-permute-done | bytes 524320 | tf_op jit(solution)/shard_map/ppermute | solution.py:31
  143.9 9.3 %collective-permute-start.25 = (f32[8,1280]{1,0:T(8,128)S(1)}, f32[8,1280]{1,0:T(8,128)S(1)}, u32[]{:S(2)}, u32[]{:S(2)}) collective-permute-start(f32[8,1280]{1,0:T(8,128)S(1)} %get-tuple-element.26), channel_id=1, source_target_pairs={{0,5},{1,6},{2,7},{3,0},{4,1},{5,2},{6,3},{7,4},{8,13},{9,14},{10,... | collective-permute-start | bytes 122888 | tf_op jit(solution)/shard_map/ppermute | solution.py:41
  153.3 0.5 add_convert_fusion.1
  153.8 0.7 multiply_convert_fusion.1
  154.5 0.3 copy-done.1
  155.2 0.5 fusion.57
  155.9 0.5 fusion.58
  156.5 1.9 collective-permute-start.26
  158.5 3.5 %collective-permute-start.27 = (f32[8,1280]{1,0:T(8,128)S(1)}, f32[8,1280]{1,0:T(8,128)S(1)}, u32[]{:S(2)}, u32[]{:S(2)}) collective-permute-start(f32[8,1280]{1,0:T(8,128)S(1)} %get-tuple-element.24), channel_id=1, source_target_pairs={{0,7},{1,0},{2,1},{3,2},{4,3},{5,4},{6,5},{7,6},{8,15},{9,8},{10,9... | collective-permute-start | bytes 122888 | tf_op jit(solution)/shard_map/ppermute | solution.py:41
  162.1 1.9 collective-permute-start.4
  164.0 4.0 %collective-permute-start.5 = (f32[64,1280]{1,0:T(8,128)S(1)}, f32[64,1280]{1,0:T(8,128)S(1)}, u32[]{:S(2)}, u32[]{:S(2)}) collective-permute-start(f32[64,1280]{1,0:T(8,128)S(1)} %get-tuple-element.12), channel_id=1, source_target_pairs={{0,16},{8,24},{16,0},{24,8},{1,17},{9,25},{17,1},{25,9},{2,18},{10... | collective-permute-start | bytes 983048 | tf_op jit(solution)/shard_map/ppermute | solution.py:41
  168.0 2.0 collective-permute-start.6
  170.0 1.9 collective-permute-start.28
  172.0 1.2 collective-permute-done.28
  173.2 9.9 %collective-permute-start.29 = (f32[8,1280]{1,0:T(8,128)S(1)}, f32[8,1280]{1,0:T(8,128)S(1)}, u32[]{:S(2)}, u32[]{:S(2)}) collective-permute-start(f32[8,1280]{1,0:T(8,128)S(1)} %add.311), channel_id=1, source_target_pairs={{0,64},{32,96},{64,0},{96,32},{128,192},{160,224},{192,128},{224,1... | collective-permute-start | bytes 122888 | tf_op jit(solution)/shard_map/ppermute | solution.py:49
  183.1 4.8 %collective-permute-done.29 = f32[8,1280]{1,0:T(8,128)S(1)} collective-permute-done((f32[8,1280]{1,0:T(8,128)S(1)}, f32[8,1280]{1,0:T(8,128)S(1)}, u32[]{:S(2)}, u32[]{:S(2)}) %collective-permute-start.29) | collective-permute-done | bytes 40992 | tf_op jit(solution)/shard_map/ppermute | solution.py:49
  187.9 1.9 collective-permute-start.30
  190.0 8.3 %collective-permute-start.10 = (f32[8,1280]{1,0:T(8,128)S(1)}, f32[8,1280]{1,0:T(8,128)S(1)}, u32[]{:S(2)}, u32[]{:S(2)}) collective-permute-start(f32[8,1280]{1,0:T(8,128)S(1)} %get-tuple-element.20), channel_id=1, source_target_pairs={{0,4},{1,5},{2,6},{3,7},{4,0},{5,1},{6,2},{7,3},{8,12},{9,13},{10,... | collective-permute-start | bytes 122888 | tf_op jit(solution)/shard_map/ppermute | solution.py:41
  198.3 3.9 %collective-permute-start.11 = (f32[8,1280]{1,0:T(8,128)S(1)}, f32[8,1280]{1,0:T(8,128)S(1)}, u32[]{:S(2)}, u32[]{:S(2)}) collective-permute-start(f32[8,1280]{1,0:T(8,128)S(1)} %get-tuple-element.19), channel_id=1, source_target_pairs={{0,5},{1,6},{2,7},{3,0},{4,1},{5,2},{6,3},{7,4},{8,13},{9,14},{10,... | collective-permute-start | bytes 122888 | tf_op jit(solution)/shard_map/ppermute | solution.py:41
  202.2 8.5 %collective-permute-start.12 = (f32[8,1280]{1,0:T(8,128)S(1)}, f32[8,1280]{1,0:T(8,128)S(1)}, u32[]{:S(2)}, u32[]{:S(2)}) collective-permute-start(f32[8,1280]{1,0:T(8,128)S(1)} %get-tuple-element.18), channel_id=1, source_target_pairs={{0,6},{1,7},{2,0},{3,1},{4,2},{5,3},{6,4},{7,5},{8,14},{9,15},{10,... | collective-permute-start | bytes 122888 | tf_op jit(solution)/shard_map/ppermute | solution.py:41
  210.7 3.8 %collective-permute-start.13 = (f32[8,1280]{1,0:T(8,128)S(1)}, f32[8,1280]{1,0:T(8,128)S(1)}, u32[]{:S(2)}, u32[]{:S(2)}) collective-permute-start(f32[8,1280]{1,0:T(8,128)S(1)} %get-tuple-element.17), channel_id=1, source_target_pairs={{0,7},{1,0},{2,1},{3,2},{4,3},{5,4},{6,5},{7,6},{8,15},{9,8},{10,9... | collective-permute-start | bytes 122888 | tf_op jit(solution)/shard_map/ppermute | solution.py:41
  214.5 2.1 collective-permute-start.7
  216.6 1.9 collective-permute-start.8
  218.5 9.5 %collective-permute-start.9 = (f32[8,1280]{1,0:T(8,128)S(1)}, f32[8,1280]{1,0:T(8,128)S(1)}, u32[]{:S(2)}, u32[]{:S(2)}) collective-permute-start(f32[8,1280]{1,0:T(8,128)S(1)} %get-tuple-element.21), channel_id=1, source_target_pairs={{0,3},{1,4},{2,5},{3,6},{4,7},{5,0},{6,1},{7,2},{8,11},{9,12},{10,... | collective-permute-start | bytes 122888 | tf_op jit(solution)/shard_map/ppermute | solution.py:41
  228.0 0.5 convolution_convert_fusion
  228.5 5.7 %collective-permute-start.31 = (f32[8,1280]{1,0:T(8,128)S(1)}, f32[8,1280]{1,0:T(8,128)S(1)}, u32[]{:S(2)}, u32[]{:S(2)}) collective-permute-start(f32[8,1280]{1,0:T(8,128)S(1)} %add.313), channel_id=1, source_target_pairs={{0,256},{32,288},{64,320},{96,352},{128,384},{160,416},{192,448},{... | collective-permute-start | bytes 122888 | tf_op jit(solution)/shard_map/ppermute | solution.py:49
  234.2 1.9 collective-permute-start.3
  236.2 1.9 collective-permute-start.14
  238.2 1.1 fusion.1
  239.4 12.0 %collective-permute-start.15 = (f32[8,1280]{1,0:T(8,128)S(1)}, f32[8,1280]{1,0:T(8,128)S(1)}, u32[]{:S(2)}, u32[]{:S(2)}) collective-permute-start(f32[8,1280]{1,0:T(8,128)S(1)} %add.297), channel_id=1, source_target_pairs={{0,64},{32,96},{64,0},{96,32},{128,192},{160,224},{192,128},{224,1... | collective-permute-start | bytes 122888 | tf_op jit(solution)/shard_map/ppermute | solution.py:49
  251.4 10.6 %collective-permute-done.15 = f32[8,1280]{1,0:T(8,128)S(1)} collective-permute-done((f32[8,1280]{1,0:T(8,128)S(1)}, f32[8,1280]{1,0:T(8,128)S(1)}, u32[]{:S(2)}, u32[]{:S(2)}) %collective-permute-start.15) | collective-permute-done | bytes 40992 | tf_op jit(solution)/shard_map/ppermute | solution.py:49
  262.0 2.8 %collective-permute-start.16 = (f32[8,1280]{1,0:T(8,128)S(1)}, f32[8,1280]{1,0:T(8,128)S(1)}, u32[]{:S(2)}, u32[]{:S(2)}) collective-permute-start(f32[8,1280]{1,0:T(8,128)S(1)} %add.298), channel_id=1, source_target_pairs={{0,128},{32,160},{64,192},{96,224},{128,0},{160,32},{192,64},{224,... | collective-permute-start | bytes 122888 | tf_op jit(solution)/shard_map/ppermute | solution.py:49
  264.9 3.1 %collective-permute-done.16 = f32[8,1280]{1,0:T(8,128)S(1)} collective-permute-done((f32[8,1280]{1,0:T(8,128)S(1)}, f32[8,1280]{1,0:T(8,128)S(1)}, u32[]{:S(2)}, u32[]{:S(2)}) %collective-permute-start.16) | collective-permute-done | bytes 40992 | tf_op jit(solution)/shard_map/ppermute | solution.py:49
  267.9 2.2 collective-permute-start.17
  270.1 1.3 add_convert_fusion
  271.4 3.9 %collective-permute-done.17 = f32[8,1280]{1,0:T(8,128)S(1)} collective-permute-done((f32[8,1280]{1,0:T(8,128)S(1)}, f32[8,1280]{1,0:T(8,128)S(1)}, u32[]{:S(2)}, u32[]{:S(2)}) %collective-permute-start.17) | collective-permute-done | bytes 40992 | tf_op jit(solution)/shard_map/ppermute | solution.py:49
  275.4 0.6 pad_maximum_fusion.4
  276.0 0.6 pad_maximum_fusion.2
  (85 shorter events, 1.6 us)
Async XLA Ops:
  0.6 15.9 %copy-start.8 = (bf16[2,256,512]{2,1,0:T(8,128)(2,1)S(1)}, bf16[2,256,512]{2,1,0:T(8,128)(2,1)}, u32[]{:S(2)}) copy-start(bf16[2,256,512]{2,1,0:T(8,128)(2,1)} %param.6) | copy-start | bytes 1572868
  0.6 15.9 %collective-permute-start = (bf16[1024,256]{1,0:T(8,128)(2,1)}, bf16[1024,256]{1,0:T(8,128)(2,1)S(1)}, u32[]{:S(2)}, u32[]{:S(2)}) collective-permute-start(bf16[1024,256]{1,0:T(8,128)(2,1)} %param.5), channel_id=1, source_target_pairs={{0,1},{1,2},{2,3},{3,4},{4,5},{5,6},{6,7},{7,8},{8,9},{9,10},{10,1... | collective-permute-start | bytes 1572872 | tf_op jit(solution)/shard_map/ppermute | solution.py:31
  16.5 0.8 copy-start.10
  17.4 1.2 copy-start.6
  17.4 1.2 copy-start.15
  17.8 0.8 copy-start
  19.0 31.3 %copy-start.2 = (bf16[1024,256]{1,0:T(8,128)(2,1)}, bf16[1024,256]{1,0:T(8,128)(2,1)S(1)}, u32[]{:S(2)}) copy-start(bf16[1024,256]{1,0:T(8,128)(2,1)S(1)} %fusion) | copy-start | bytes 1572868
  19.0 28.6 %collective-permute-start.1 = (bf16[1024,256]{1,0:T(8,128)(2,1)S(1)}, bf16[1024,256]{1,0:T(8,128)(2,1)}, u32[]{:S(2)}, u32[]{:S(2)}) collective-permute-start(bf16[1024,256]{1,0:T(8,128)(2,1)S(1)} %fusion), channel_id=1, source_target_pairs={{0,64},{32,96},{64,128},{96,160},{128,192},{160,224},{192,256},{22... | collective-permute-start | bytes 1572872 | tf_op jit(solution)/shard_map/ppermute | solution.py:31
  34.4 14.7 %copy-start.12 = (bf16[1024,256]{1,0:T(8,128)(2,1)S(1)}, bf16[1024,256]{1,0:T(8,128)(2,1)}, u32[]{:S(2)}) copy-start(bf16[1024,256]{1,0:T(8,128)(2,1)} %param.9) | copy-start | bytes 1572868
  49.9 2.4 copy-start.4
  49.9 2.4 copy-start.17
  49.9 2.4 copy-start.19
  53.4 55.1 %collective-permute-start.18 = (f32[64,1280]{1,0:T(8,128)}, f32[64,1280]{1,0:T(8,128)}, u32[]{:S(2)}, u32[]{:S(2)}) collective-permute-start(f32[64,1280]{1,0:T(8,128)} %get-tuple-element.13), channel_id=1, source_target_pairs={{0,8},{8,16},{16,24},{24,0},{1,9},{9,17},{17,25},{25,1},{2,10},{10... | collective-permute-start | bytes 983048 | tf_op jit(solution)/shard_map/ppermute | solution.py:41
  56.8 51.7 %collective-permute-start.19 = (f32[64,1280]{1,0:T(8,128)}, f32[64,1280]{1,0:T(8,128)}, u32[]{:S(2)}, u32[]{:S(2)}) collective-permute-start(f32[64,1280]{1,0:T(8,128)} %get-tuple-element.15), channel_id=1, source_target_pairs={{0,16},{8,24},{16,0},{24,8},{1,17},{9,25},{17,1},{25,9},{2,18},{10... | collective-permute-start | bytes 983048 | tf_op jit(solution)/shard_map/ppermute | solution.py:41
  60.1 48.5 %collective-permute-start.20 = (f32[64,1280]{1,0:T(8,128)}, f32[64,1280]{1,0:T(8,128)}, u32[]{:S(2)}, u32[]{:S(2)}) collective-permute-start(f32[64,1280]{1,0:T(8,128)} %get-tuple-element.14), channel_id=1, source_target_pairs={{0,24},{8,0},{16,8},{24,16},{1,25},{9,1},{17,9},{25,17},{2,26},{10... | collective-permute-start | bytes 983048 | tf_op jit(solution)/shard_map/ppermute | solution.py:41
  63.9 89.3 %copy-start.13 = (bf16[1024,256]{1,0:T(8,128)(2,1)S(1)}, bf16[1024,256]{1,0:T(8,128)(2,1)}, u32[]{:S(2)}) copy-start(bf16[1024,256]{1,0:T(8,128)(2,1)} %param.9) | copy-start | bytes 1572868
  63.9 89.3 %copy-start.14 = (bf16[2,256,512]{2,1,0:T(8,128)(2,1)S(1)}, bf16[2,256,512]{2,1,0:T(8,128)(2,1)}, u32[]{:S(2)}) copy-start(bf16[2,256,512]{2,1,0:T(8,128)(2,1)} %param.7) | copy-start | bytes 1572868
  63.9 89.3 %copy-start.18 = (bf16[1024,256]{0,1:T(8,128)(2,1)S(1)}, bf16[1024,256]{0,1:T(8,128)(2,1)}, u32[]{:S(2)}) copy-start(bf16[1024,256]{0,1:T(8,128)(2,1)} %copy-done.17) | copy-start | bytes 1572868
  63.9 89.3 %copy-start.20 = (bf16[1024,256]{0,1:T(8,128)(2,1)S(1)}, bf16[1024,256]{0,1:T(8,128)(2,1)}, u32[]{:S(2)}) copy-start(bf16[1024,256]{0,1:T(8,128)(2,1)} %copy-done.19) | copy-start | bytes 1572868
  65.9 78.1 %collective-permute-start.2 = (bf16[1024,256]{1,0:T(8,128)(2,1)S(1)}, bf16[1024,256]{1,0:T(8,128)(2,1)S(1)}, u32[]{:S(2)}, u32[]{:S(2)}) collective-permute-start(bf16[1024,256]{1,0:T(8,128)(2,1)S(1)} %convolution_convert_fusion.1), channel_id=1, source_target_pairs={{64,0},{96,32},{128,64},{160,96},{192,128},{224,160},{256,192},{28... | collective-permute-start | bytes 1572872 | tf_op jit(solution)/shard_map/ppermute | solution.py:31
  109.8 44.0 %copy-start.16 = (bf16[2,256,256]{2,1,0:T(8,128)(2,1)S(1)}, bf16[2,256,256]{2,1,0:T(8,128)(2,1)}, u32[]{:S(2)}) copy-start(bf16[2,256,256]{2,1,0:T(8,128)(2,1)} %param.8) | copy-start | bytes 786436
  109.9 46.7 %collective-permute-start.21 = (f32[8,1280]{1,0:T(8,128)S(1)}, f32[8,1280]{1,0:T(8,128)S(1)}, u32[]{:S(2)}, u32[]{:S(2)}) collective-permute-start(f32[8,1280]{1,0:T(8,128)S(1)} %get-tuple-element.23), channel_id=1, source_target_pairs={{0,1},{1,2},{2,3},{3,4},{4,5},{5,6},{6,7},{7,0},{8,9},{9,10},{10,1... | collective-permute-start | bytes 122888 | tf_op jit(solution)/shard_map/ppermute | solution.py:41
  111.9 46.5 %collective-permute-start.22 = (f32[8,1280]{1,0:T(8,128)S(1)}, f32[8,1280]{1,0:T(8,128)S(1)}, u32[]{:S(2)}, u32[]{:S(2)}) collective-permute-start(f32[8,1280]{1,0:T(8,128)S(1)} %get-tuple-element.29), channel_id=1, source_target_pairs={{0,2},{1,3},{2,4},{3,5},{4,6},{5,7},{6,0},{7,1},{8,10},{9,11},{10,... | collective-permute-start | bytes 122888 | tf_op jit(solution)/shard_map/ppermute | solution.py:41
  113.9 48.2 %collective-permute-start.23 = (f32[8,1280]{1,0:T(8,128)S(1)}, f32[8,1280]{1,0:T(8,128)S(1)}, u32[]{:S(2)}, u32[]{:S(2)}) collective-permute-start(f32[8,1280]{1,0:T(8,128)S(1)} %get-tuple-element.28), channel_id=1, source_target_pairs={{0,3},{1,4},{2,5},{3,6},{4,7},{5,0},{6,1},{7,2},{8,11},{9,12},{10,... | collective-permute-start | bytes 122888 | tf_op jit(solution)/shard_map/ppermute | solution.py:41
  128.3 35.7 %collective-permute-start.24 = (f32[8,1280]{1,0:T(8,128)S(1)}, f32[8,1280]{1,0:T(8,128)S(1)}, u32[]{:S(2)}, u32[]{:S(2)}) collective-permute-start(f32[8,1280]{1,0:T(8,128)S(1)} %get-tuple-element.27), channel_id=1, source_target_pairs={{0,4},{1,5},{2,6},{3,7},{4,0},{5,1},{6,2},{7,3},{8,12},{9,13},{10,... | collective-permute-start | bytes 122888 | tf_op jit(solution)/shard_map/ppermute | solution.py:41
  143.9 24.1 %collective-permute-start.25 = (f32[8,1280]{1,0:T(8,128)S(1)}, f32[8,1280]{1,0:T(8,128)S(1)}, u32[]{:S(2)}, u32[]{:S(2)}) collective-permute-start(f32[8,1280]{1,0:T(8,128)S(1)} %get-tuple-element.26), channel_id=1, source_target_pairs={{0,5},{1,6},{2,7},{3,0},{4,1},{5,2},{6,3},{7,4},{8,13},{9,14},{10,... | collective-permute-start | bytes 122888 | tf_op jit(solution)/shard_map/ppermute | solution.py:41
  153.8 1.0 copy-start.1
  153.8 1.3 copy-start.7
  154.8 1.1 copy-start.11
  156.5 13.5 %collective-permute-start.26 = (f32[8,1280]{1,0:T(8,128)S(1)}, f32[8,1280]{1,0:T(8,128)S(1)}, u32[]{:S(2)}, u32[]{:S(2)}) collective-permute-start(f32[8,1280]{1,0:T(8,128)S(1)} %get-tuple-element.25), channel_id=1, source_target_pairs={{0,6},{1,7},{2,0},{3,1},{4,2},{5,3},{6,4},{7,5},{8,14},{9,15},{10,... | collective-permute-start | bytes 122888 | tf_op jit(solution)/shard_map/ppermute | solution.py:41
  158.5 69.5 %copy-start.9 = (bf16[2,256,512]{2,1,0:T(8,128)(2,1)S(1)}, bf16[2,256,512]{2,1,0:T(8,128)(2,1)}, u32[]{:S(2)}) copy-start(bf16[2,256,512]{2,1,0:T(8,128)(2,1)} %param.6) | copy-start | bytes 1572868
  158.5 11.5 %collective-permute-start.27 = (f32[8,1280]{1,0:T(8,128)S(1)}, f32[8,1280]{1,0:T(8,128)S(1)}, u32[]{:S(2)}, u32[]{:S(2)}) collective-permute-start(f32[8,1280]{1,0:T(8,128)S(1)} %get-tuple-element.24), channel_id=1, source_target_pairs={{0,7},{1,0},{2,1},{3,2},{4,3},{5,4},{6,5},{7,6},{8,15},{9,8},{10,9... | collective-permute-start | bytes 122888 | tf_op jit(solution)/shard_map/ppermute | solution.py:41
  162.1 27.7 %collective-permute-start.4 = (f32[64,1280]{1,0:T(8,128)S(1)}, f32[64,1280]{1,0:T(8,128)S(1)}, u32[]{:S(2)}, u32[]{:S(2)}) collective-permute-start(f32[64,1280]{1,0:T(8,128)S(1)} %get-tuple-element.10), channel_id=1, source_target_pairs={{0,8},{8,16},{16,24},{24,0},{1,9},{9,17},{17,25},{25,1},{2,10},{10... | collective-permute-start | bytes 983048 | tf_op jit(solution)/shard_map/ppermute | solution.py:41
  164.0 25.8 %collective-permute-start.5 = (f32[64,1280]{1,0:T(8,128)S(1)}, f32[64,1280]{1,0:T(8,128)S(1)}, u32[]{:S(2)}, u32[]{:S(2)}) collective-permute-start(f32[64,1280]{1,0:T(8,128)S(1)} %get-tuple-element.12), channel_id=1, source_target_pairs={{0,16},{8,24},{16,0},{24,8},{1,17},{9,25},{17,1},{25,9},{2,18},{10... | collective-permute-start | bytes 983048 | tf_op jit(solution)/shard_map/ppermute | solution.py:41
  168.0 21.8 %collective-permute-start.6 = (f32[64,1280]{1,0:T(8,128)S(1)}, f32[64,1280]{1,0:T(8,128)S(1)}, u32[]{:S(2)}, u32[]{:S(2)}) collective-permute-start(f32[64,1280]{1,0:T(8,128)S(1)} %get-tuple-element.11), channel_id=1, source_target_pairs={{0,24},{8,0},{16,8},{24,16},{1,25},{9,1},{17,9},{25,17},{2,26},{10... | collective-permute-start | bytes 983048 | tf_op jit(solution)/shard_map/ppermute | solution.py:41
  170.0 3.1 %collective-permute-start.28 = (f32[8,1280]{1,0:T(8,128)S(1)}, f32[8,1280]{1,0:T(8,128)S(1)}, u32[]{:S(2)}, u32[]{:S(2)}) collective-permute-start(f32[8,1280]{1,0:T(8,128)S(1)} %fusion.50), channel_id=1, source_target_pairs={{0,32},{32,0},{64,96},{96,64},{128,160},{160,128},{192,224},{224,1... | collective-permute-start | bytes 122888 | tf_op jit(solution)/shard_map/ppermute | solution.py:49
  173.2 14.7 %collective-permute-start.29 = (f32[8,1280]{1,0:T(8,128)S(1)}, f32[8,1280]{1,0:T(8,128)S(1)}, u32[]{:S(2)}, u32[]{:S(2)}) collective-permute-start(f32[8,1280]{1,0:T(8,128)S(1)} %add.311), channel_id=1, source_target_pairs={{0,64},{32,96},{64,0},{96,32},{128,192},{160,224},{192,128},{224,1... | collective-permute-start | bytes 122888 | tf_op jit(solution)/shard_map/ppermute | solution.py:49
  187.9 14.3 %collective-permute-start.30 = (f32[8,1280]{1,0:T(8,128)S(1)}, f32[8,1280]{1,0:T(8,128)S(1)}, u32[]{:S(2)}, u32[]{:S(2)}) collective-permute-start(f32[8,1280]{1,0:T(8,128)S(1)} %add.312), channel_id=1, source_target_pairs={{0,128},{32,160},{64,192},{96,224},{128,0},{160,32},{192,64},{224,... | collective-permute-start | bytes 122888 | tf_op jit(solution)/shard_map/ppermute | solution.py:49
  189.9 48.2 %copy-start.3 = (bf16[1024,256]{1,0:T(8,128)(2,1)S(1)}, bf16[1024,256]{1,0:T(8,128)(2,1)}, u32[]{:S(2)}) copy-start(bf16[1024,256]{1,0:T(8,128)(2,1)} %copy-done.2) | copy-start | bytes 1572868
  189.9 48.2 %copy-start.5 = (bf16[1024,256]{0,1:T(8,128)(2,1)S(1)}, bf16[1024,256]{0,1:T(8,128)(2,1)}, u32[]{:S(2)}) copy-start(bf16[1024,256]{0,1:T(8,128)(2,1)} %copy-done.4) | copy-start | bytes 1572868
  190.0 26.6 %collective-permute-start.10 = (f32[8,1280]{1,0:T(8,128)S(1)}, f32[8,1280]{1,0:T(8,128)S(1)}, u32[]{:S(2)}, u32[]{:S(2)}) collective-permute-start(f32[8,1280]{1,0:T(8,128)S(1)} %get-tuple-element.20), channel_id=1, source_target_pairs={{0,4},{1,5},{2,6},{3,7},{4,0},{5,1},{6,2},{7,3},{8,12},{9,13},{10,... | collective-permute-start | bytes 122888 | tf_op jit(solution)/shard_map/ppermute | solution.py:41
  198.3 20.2 %collective-permute-start.11 = (f32[8,1280]{1,0:T(8,128)S(1)}, f32[8,1280]{1,0:T(8,128)S(1)}, u32[]{:S(2)}, u32[]{:S(2)}) collective-permute-start(f32[8,1280]{1,0:T(8,128)S(1)} %get-tuple-element.19), channel_id=1, source_target_pairs={{0,5},{1,6},{2,7},{3,0},{4,1},{5,2},{6,3},{7,4},{8,13},{9,14},{10,... | collective-permute-start | bytes 122888 | tf_op jit(solution)/shard_map/ppermute | solution.py:41
  202.2 26.3 %collective-permute-start.12 = (f32[8,1280]{1,0:T(8,128)S(1)}, f32[8,1280]{1,0:T(8,128)S(1)}, u32[]{:S(2)}, u32[]{:S(2)}) collective-permute-start(f32[8,1280]{1,0:T(8,128)S(1)} %get-tuple-element.18), channel_id=1, source_target_pairs={{0,6},{1,7},{2,0},{3,1},{4,2},{5,3},{6,4},{7,5},{8,14},{9,15},{10,... | collective-permute-start | bytes 122888 | tf_op jit(solution)/shard_map/ppermute | solution.py:41
  210.7 23.5 %collective-permute-start.13 = (f32[8,1280]{1,0:T(8,128)S(1)}, f32[8,1280]{1,0:T(8,128)S(1)}, u32[]{:S(2)}, u32[]{:S(2)}) collective-permute-start(f32[8,1280]{1,0:T(8,128)S(1)} %get-tuple-element.17), channel_id=1, source_target_pairs={{0,7},{1,0},{2,1},{3,2},{4,3},{5,4},{6,5},{7,6},{8,15},{9,8},{10,9... | collective-permute-start | bytes 122888 | tf_op jit(solution)/shard_map/ppermute | solution.py:41
  214.5 21.7 %collective-permute-start.7 = (f32[8,1280]{1,0:T(8,128)S(1)}, f32[8,1280]{1,0:T(8,128)S(1)}, u32[]{:S(2)}, u32[]{:S(2)}) collective-permute-start(f32[8,1280]{1,0:T(8,128)S(1)} %get-tuple-element.16), channel_id=1, source_target_pairs={{0,1},{1,2},{2,3},{3,4},{4,5},{5,6},{6,7},{7,0},{8,9},{9,10},{10,1... | collective-permute-start | bytes 122888 | tf_op jit(solution)/shard_map/ppermute | solution.py:41
  216.6 19.6 %collective-permute-start.8 = (f32[8,1280]{1,0:T(8,128)S(1)}, f32[8,1280]{1,0:T(8,128)S(1)}, u32[]{:S(2)}, u32[]{:S(2)}) collective-permute-start(f32[8,1280]{1,0:T(8,128)S(1)} %get-tuple-element.22), channel_id=1, source_target_pairs={{0,2},{1,3},{2,4},{3,5},{4,6},{5,7},{6,0},{7,1},{8,10},{9,11},{10,... | collective-permute-start | bytes 122888 | tf_op jit(solution)/shard_map/ppermute | solution.py:41
  218.5 17.7 %collective-permute-start.9 = (f32[8,1280]{1,0:T(8,128)S(1)}, f32[8,1280]{1,0:T(8,128)S(1)}, u32[]{:S(2)}, u32[]{:S(2)}) collective-permute-start(f32[8,1280]{1,0:T(8,128)S(1)} %get-tuple-element.21), channel_id=1, source_target_pairs={{0,3},{1,4},{2,5},{3,6},{4,7},{5,0},{6,1},{7,2},{8,11},{9,12},{10,... | collective-permute-start | bytes 122888 | tf_op jit(solution)/shard_map/ppermute | solution.py:41
  228.5 10.8 %collective-permute-start.31 = (f32[8,1280]{1,0:T(8,128)S(1)}, f32[8,1280]{1,0:T(8,128)S(1)}, u32[]{:S(2)}, u32[]{:S(2)}) collective-permute-start(f32[8,1280]{1,0:T(8,128)S(1)} %add.313), channel_id=1, source_target_pairs={{0,256},{32,288},{64,320},{96,352},{128,384},{160,416},{192,448},{... | collective-permute-start | bytes 122888 | tf_op jit(solution)/shard_map/ppermute | solution.py:49
  234.2 35.9 %collective-permute-start.3 = (bf16[1024,256]{1,0:T(8,128)(2,1)S(1)}, bf16[1024,256]{1,0:T(8,128)(2,1)S(1)}, u32[]{:S(2)}, u32[]{:S(2)}) collective-permute-start(bf16[1024,256]{1,0:T(8,128)(2,1)S(1)} %convolution_convert_fusion), channel_id=1, source_target_pairs={{1,0},{2,1},{3,2},{4,3},{5,4},{6,5},{7,6},{8,7},{9,8},{10,9},{11,1... | collective-permute-start | bytes 1572872 | tf_op jit(solution)/shard_map/ppermute | solution.py:31
  236.2 3.1 %collective-permute-start.14 = (f32[8,1280]{1,0:T(8,128)S(1)}, f32[8,1280]{1,0:T(8,128)S(1)}, u32[]{:S(2)}, u32[]{:S(2)}) collective-permute-start(f32[8,1280]{1,0:T(8,128)S(1)} %fusion.56), channel_id=1, source_target_pairs={{0,32},{32,0},{64,96},{96,64},{128,160},{160,128},{192,224},{224,1... | collective-permute-start | bytes 122888 | tf_op jit(solution)/shard_map/ppermute | solution.py:49
  239.4 22.7 %collective-permute-start.15 = (f32[8,1280]{1,0:T(8,128)S(1)}, f32[8,1280]{1,0:T(8,128)S(1)}, u32[]{:S(2)}, u32[]{:S(2)}) collective-permute-start(f32[8,1280]{1,0:T(8,128)S(1)} %add.297), channel_id=1, source_target_pairs={{0,64},{32,96},{64,0},{96,32},{128,192},{160,224},{192,128},{224,1... | collective-permute-start | bytes 122888 | tf_op jit(solution)/shard_map/ppermute | solution.py:49
  262.0 5.9 %collective-permute-start.16 = (f32[8,1280]{1,0:T(8,128)S(1)}, f32[8,1280]{1,0:T(8,128)S(1)}, u32[]{:S(2)}, u32[]{:S(2)}) collective-permute-start(f32[8,1280]{1,0:T(8,128)S(1)} %add.298), channel_id=1, source_target_pairs={{0,128},{32,160},{64,192},{96,224},{128,0},{160,32},{192,64},{224,... | collective-permute-start | bytes 122888 | tf_op jit(solution)/shard_map/ppermute | solution.py:49
  267.9 7.4 %collective-permute-start.17 = (f32[8,1280]{1,0:T(8,128)S(1)}, f32[8,1280]{1,0:T(8,128)S(1)}, u32[]{:S(2)}, u32[]{:S(2)}) collective-permute-start(f32[8,1280]{1,0:T(8,128)S(1)} %add.299), channel_id=1, source_target_pairs={{0,256},{32,288},{64,320},{96,352},{128,384},{160,416},{192,448},{... | collective-permute-start | bytes 122888 | tf_op jit(solution)/shard_map/ppermute | solution.py:49

commit v2 on v1

--- a/solution.py
+++ b/solution.py
@@ -42,6 +42,20 @@
     return summed
 
 
+def halving_sum(total, axes):
+    size = group_size(axes)
+    own = group_index(axes)
+    step = size // 2
+    while step >= 1:
+        halves = total.reshape(2, total.shape[0] // 2, *total.shape[1:])
+        keep = (own // step) % 2
+        kept = lax.dynamic_index_in_dim(halves, keep, 0, keepdims=False)
+        given = lax.dynamic_index_in_dim(halves, 1 - keep, 0, keepdims=False)
+        total = kept + lax.ppermute(given, axes, [(i, i ^ step) for i in range(size)])
+        step //= 2
+    return total
+
+
 def everyone_sum(total, axes):
     size = group_size(axes)
     step = 1
@@ -52,9 +66,19 @@
 
 
 def weight_sum(term):
-    for axis in INNER:
-        term = scatter_sum(term, (axis,))
-    return everyone_sum(term, OUTER)
+    own_core = lax.axis_index("core")
+    halves = term.reshape(term.shape[0], 2, term.shape[1] // 2)
+    kept = lax.dynamic_index_in_dim(halves, own_core, 1, keepdims=False)
+    given = lax.dynamic_index_in_dim(halves, 1 - own_core, 1, keepdims=False)
+    term = kept + lax.ppermute(given, "core", [(0, 1), (1, 0)])
+    term = scatter_sum(term, ("x",))
+    term = halving_sum(term, ("z_lo",))
+    term = everyone_sum(term, ("y", "z_hi"))
+    other = lax.ppermute(term, "core", [(0, 1), (1, 0)])
+    pair = jnp.stack([term, other])
+    first = lax.dynamic_index_in_dim(pair, own_core, 0, keepdims=False)
+    second = lax.dynamic_index_in_dim(pair, 1 - own_core, 0, keepdims=False)
+    return jnp.concatenate([first, second], 1)
 
 
 def gating(current, earlier, w_past, w_now):
@@ -132,11 +156,17 @@
         ).astype(jnp.bfloat16)
         arrived = return_past(sent_back, layer_at)
         operands = (earlier, current, gated_out, grad_preact, upstream)
-        summed_list[layer_at] = weight_sum(layer_term(operands, grad_scale))
+        summed_list[layer_at] = layer_term(operands, grad_scale)
         local_grad = upstream.astype(jnp.float32) + jnp.dot(
             grad_preact, conv_now[layer_at].T, preferred_element_type=jnp.float32
         )
         upstream = (local_grad + arrived.astype(jnp.float32)).astype(jnp.bfloat16)
+    term_width = summed_list[0].shape[1]
+    whole = weight_sum(jnp.concatenate(summed_list, 1))
+    summed_list = [
+        whole[:, layer_at * term_width : (layer_at + 1) * term_width]
+        for layer_at in range(layer_count)
+    ]
     past_list = [summed[:, :gate_width] for summed in summed_list]
     now_list = [summed[:, gate_width : 2 * gate_width] for summed in summed_list]
     out_list = [summed[:, 2 * gate_width :] for summed in summed_list]

time: 278 us -> 247 us (0.89)
  the two profiles are of different devices: /device:TPU:82 before, /device:TPU:11 now
where the time goes in v2:
time: 247 us; the launch traced here: 246 us
  waiting for transfers between devices  136 us (55%)
  starting transfers between devices  83.7 us (34%)
  matrix products  15.5 us (6%)
  other arithmetic  5.68 us (2%)
  local copies, waits for them, and re-layouts  4.51 us (2%)
    ppermute x4, waiting for transfers between devices, from_behind(): return lax.ppermute(array, axes, pairs)  94.6 us
    ppermute x4, starting transfers between devices, from_behind(): return lax.ppermute(array, axes, pairs)  32.2 us
    ppermute x3, starting transfers between devices, halving_sum(): lax.ppermute(given, axes, [(i, i ^ step) for i in range(size)])  17.9 us
    ppermute x3, waiting for transfers between devices, everyone_sum(): lax.ppermute(total, axes, [(i, i ^ step) for i in range(size)])  16.9 us
    ppermute x3, starting transfers between devices, everyone_sum(): lax.ppermute(total, axes, [(i, i ^ step) for i in range(size)])  14.1 us
    ppermute x3, waiting for transfers between devices, scatter_sum(): lax.ppermute(piece, axes, [(i, (i + shift) % size) for i in range(size)])  11.7 us
    ppermute x3, waiting for transfers between devices, halving_sum(): lax.ppermute(given, axes, [(i, i ^ step) for i in range(size)])  9.79 us
    ppermute x3, starting transfers between devices, scatter_sum(): lax.ppermute(piece, axes, [(i, (i + shift) % size) for i in range(size)])  9.59 us
  transfers between devices with their start and end apart: 15, of which 12 were waited for; matrix products, arithmetic and copies ran while one was open for 4% of the time, Pallas kernels for 0%

profile of v2, /device:TPU:11, one launch (start us, length us, event | category | flops | bytes accessed | tf_op | source)
XLA Modules:
  0.0 246.2 jit_solution(15665298463937150734)
XLA Ops:
  0.6 3.7 %collective-permute-start = (bf16[1024,256]{1,0:T(8,128)(2,1)}, bf16[1024,256]{1,0:T(8,128)(2,1)S(1)}, u32[]{:S(2)}, u32[]{:S(2)}) collective-permute-start(bf16[1024,256]{1,0:T(8,128)(2,1)} %param.5), channel_id=1, source_target_pairs={{0,1},{1,2},{2,3},{3,4},{4,5},{5,6},{6,7},{7,8},{8,9},{9,10},{10,1... | collective-permute-start | bytes 1572872 | tf_op jit(solution)/shard_map/ppermute | solution.py:31
  4.3 1.6 fusion.19
  5.9 19.6 %collective-permute-done = bf16[1024,256]{1,0:T(8,128)(2,1)S(1)} collective-permute-done((bf16[1024,256]{1,0:T(8,128)(2,1)}, bf16[1024,256]{1,0:T(8,128)(2,1)S(1)}, u32[]{:S(2)}, u32[]{:S(2)}) %collective-permute-start) | collective-permute-done | bytes 524320 | tf_op jit(solution)/shard_map/ppermute | solution.py:31
  25.5 0.5 convolution_add_fusion.1
  26.0 0.3 copy-done.7
  26.3 0.4 multiply_convert_fusion.5
  26.7 0.6 copy-done.2
  27.3 0.1 copy-done.14
  27.4 0.4 fusion.2
  27.7 13.1 %collective-permute-start.1 = (bf16[1024,256]{1,0:T(8,128)(2,1)S(1)}, bf16[1024,256]{1,0:T(8,128)(2,1)}, u32[]{:S(2)}, u32[]{:S(2)}) collective-permute-start(bf16[1024,256]{1,0:T(8,128)(2,1)S(1)} %fusion.2), channel_id=1, source_target_pairs={{0,64},{32,96},{64,128},{96,160},{128,192},{160,224},{192,256},{22... | collective-permute-start | bytes 1572872 | tf_op jit(solution)/shard_map/ppermute | solution.py:31
  40.9 1.5 fusion.13
  42.4 43.0 %collective-permute-done.1 = bf16[1024,256]{1,0:T(8,128)(2,1)} collective-permute-done((bf16[1024,256]{1,0:T(8,128)(2,1)S(1)}, bf16[1024,256]{1,0:T(8,128)(2,1)}, u32[]{:S(2)}, u32[]{:S(2)}) %collective-permute-start.1) | collective-permute-done | bytes 524320 | tf_op jit(solution)/shard_map/ppermute | solution.py:31
  85.4 1.5 convolution_add_fusion
  86.9 0.8 multiply_convert_fusion.3
  87.7 0.5 convolution_convert_fusion.1
  88.2 0.5 convolution_bitcast_fusion
  88.7 5.2 %collective-permute-start.2 = (bf16[1024,256]{1,0:T(8,128)(2,1)S(1)}, bf16[1024,256]{1,0:T(8,128)(2,1)S(1)}, u32[]{:S(2)}, u32[]{:S(2)}) collective-permute-start(bf16[1024,256]{1,0:T(8,128)(2,1)S(1)} %convolution_convert_fusion.1), channel_id=1, source_target_pairs={{64,0},{96,32},{128,64},{160,96},{192,128},{224,160},{256,192},{28... | collective-permute-start | bytes 1572872 | tf_op jit(solution)/shard_map/ppermute | solution.py:31
  93.9 0.4 convolution_bitcast_fusion.4
  94.3 1.6 convolution_bitcast_fusion.1
  95.8 0.1 maximum_multiply_fusion.1
  96.0 32.0 %collective-permute-done.2 = bf16[1024,256]{1,0:T(8,128)(2,1)S(1)} collective-permute-done((bf16[1024,256]{1,0:T(8,128)(2,1)S(1)}, bf16[1024,256]{1,0:T(8,128)(2,1)S(1)}, u32[]{:S(2)}, u32[]{:S(2)}) %collective-permute-start.2) | collective-permute-done | bytes 524320 | tf_op jit(solution)/shard_map/ppermute | solution.py:31
  128.0 0.5 add_convert_fusion.1
  128.5 0.7 multiply_convert_fusion.1
  129.2 0.1 copy-done.10
  129.3 0.3 convolution_bitcast_fusion.5
  129.6 0.1 copy-done.3
  129.7 0.4 convolution_bitcast_fusion.2
  130.2 0.1 copy-done.18
  130.3 0.5 copy-done.8
  130.7 0.4 convolution_bitcast_fusion.3
  131.2 0.1 maximum_multiply_fusion
  131.3 0.5 fusion.1
  131.8 1.5 copy.17
  133.3 2.4 collective-permute-start.4
  135.8 0.4 copy.16
  136.2 2.5 %collective-permute-done.4 = f32[256,1280]{1,0:T(8,128)} collective-permute-done((f32[256,1280]{1,0:T(8,128)}, f32[256,1280]{1,0:T(8,128)}, u32[]{:S(2)}, u32[]{:S(2)}) %collective-permute-start.4) | collective-permute-done | bytes 1310752 | tf_op jit(solution)/shard_map/ppermute | solution.py:73
  138.8 1.5 bitcast_add_fusion
  140.2 0.8 dynamic-slice_bitcast_fusion.2
  141.0 2.1 collective-permute-start.7
  143.2 4.1 %collective-permute-start.6 = (f32[64,1280]{1,0:T(8,128)S(1)}, f32[64,1280]{1,0:T(8,128)}, u32[]{:S(2)}, u32[]{:S(2)}) collective-permute-start(f32[64,1280]{1,0:T(8,128)S(1)} %get-tuple-element.14), channel_id=1, source_target_pairs={{0,16},{8,24},{16,0},{24,8},{1,17},{9,25},{17,1},{25,9},{2,18},{10... | collective-permute-start | bytes 983048 | tf_op jit(solution)/shard_map/ppermute | solution.py:41
  147.3 3.4 %collective-permute-start.5 = (f32[64,1280]{1,0:T(8,128)S(1)}, f32[64,1280]{1,0:T(8,128)}, u32[]{:S(2)}, u32[]{:S(2)}) collective-permute-start(f32[64,1280]{1,0:T(8,128)S(1)} %get-tuple-element.12), channel_id=1, source_target_pairs={{0,8},{8,16},{16,24},{24,0},{1,9},{9,17},{17,25},{25,1},{2,10},{10... | collective-permute-start | bytes 983048 | tf_op jit(solution)/shard_map/ppermute | solution.py:41
  150.7 1.4 collective-permute-done.7
  152.1 8.1 %collective-permute-done.6 = f32[64,1280]{1,0:T(8,128)} collective-permute-done((f32[64,1280]{1,0:T(8,128)S(1)}, f32[64,1280]{1,0:T(8,128)}, u32[]{:S(2)}, u32[]{:S(2)}) %collective-permute-start.6) | collective-permute-done | bytes 327712 | tf_op jit(solution)/shard_map/ppermute | solution.py:41
  160.1 2.3 collective-permute-done.5
  162.4 1.1 fusion.11
  163.6 1.9 collective-permute-start.8
  165.6 8.0 %collective-permute-done.8 = f32[32,1280]{1,0:T(8,128)S(1)} collective-permute-done((f32[32,1280]{1,0:T(8,128)S(1)}, f32[32,1280]{1,0:T(8,128)S(1)}, u32[]{:S(2)}, u32[]{:S(2)}) %collective-permute-start.8) | collective-permute-done | bytes 163872 | tf_op jit(solution)/shard_map/ppermute | solution.py:54
  173.6 13.9 %collective-permute-start.9 = (f32[16,1280]{1,0:T(8,128)S(1)}, f32[16,1280]{1,0:T(8,128)S(1)}, u32[]{:S(2)}, u32[]{:S(2)}) collective-permute-start(f32[16,1280]{1,0:T(8,128)S(1)} %dynamic-slice_bitcast_fusion.4), channel_id=1, source_target_pairs={{0,2},{1,3},{2,0},{3,1},{4,6},{5,7},{6,4},{7,5},{8,10},{9,11},{10,... | collective-permute-start | bytes 245768 | tf_op jit(solution)/shard_map/ppermute | solution.py:54
  187.5 1.8 collective-permute-done.9
  189.4 2.1 collective-permute-start.10
  191.5 1.5 convolution_convert_fusion
  193.0 10.2 %collective-permute-start.3 = (bf16[1024,256]{1,0:T(8,128)(2,1)S(1)}, bf16[1024,256]{1,0:T(8,128)(2,1)S(1)}, u32[]{:S(2)}, u32[]{:S(2)}) collective-permute-start(bf16[1024,256]{1,0:T(8,128)(2,1)S(1)} %convolution_convert_fusion), channel_id=1, source_target_pairs={{1,0},{2,1},{3,2},{4,3},{5,4},{6,5},{7,6},{8,7},{9,8},{10,9},{11,1... | collective-permute-start | bytes 1572872 | tf_op jit(solution)/shard_map/ppermute | solution.py:31
  203.2 10.3 %collective-permute-start.11 = (f32[8,1280]{1,0:T(8,128)S(1)}, f32[8,1280]{1,0:T(8,128)S(1)}, u32[]{:S(2)}, u32[]{:S(2)}) collective-permute-start(f32[8,1280]{1,0:T(8,128)S(1)} %bitcast_add_fusion.4), channel_id=1, source_target_pairs={{0,64},{64,0},{128,192},{192,128},{256,320},{320,256},{384,448},{4... | collective-permute-start | bytes 122888 | tf_op jit(solution)/shard_map/ppermute | solution.py:63
  213.6 11.0 %collective-permute-done.11 = f32[8,1280]{1,0:T(8,128)S(1)} collective-permute-done((f32[8,1280]{1,0:T(8,128)S(1)}, f32[8,1280]{1,0:T(8,128)S(1)}, u32[]{:S(2)}, u32[]{:S(2)}) %collective-permute-start.11) | collective-permute-done | bytes 40992 | tf_op jit(solution)/shard_map/ppermute | solution.py:63
  224.5 1.9 collective-permute-start.12
  226.5 2.8 %collective-permute-done.12 = f32[8,1280]{1,0:T(8,128)S(1)} collective-permute-done((f32[8,1280]{1,0:T(8,128)S(1)}, f32[8,1280]{1,0:T(8,128)S(1)}, u32[]{:S(2)}, u32[]{:S(2)}) %collective-permute-start.12) | collective-permute-done | bytes 40992 | tf_op jit(solution)/shard_map/ppermute | solution.py:63
  229.3 1.9 collective-permute-start.13
  231.2 1.1 fusion.3
  232.4 3.2 %collective-permute-done.13 = f32[8,1280]{1,0:T(8,128)S(1)} collective-permute-done((f32[8,1280]{1,0:T(8,128)S(1)}, f32[8,1280]{1,0:T(8,128)S(1)}, u32[]{:S(2)}, u32[]{:S(2)}) %collective-permute-start.13) | collective-permute-done | bytes 40992 | tf_op jit(solution)/shard_map/ppermute | solution.py:63
  235.5 7.4 %collective-permute-start.14 = (f32[8,1280]{1,0:T(8,128)S(1)}, f32[8,1280]{1,0:T(8,128)S(1)}, u32[]{:S(2)}, u32[]{:S(2)}) collective-permute-start(f32[8,1280]{1,0:T(8,128)S(1)} %add.178), channel_id=1, source_target_pairs={{0,32},{32,0},{1,33},{33,1},{2,34},{34,2},{3,35},{35,3},{4,36},{36... | collective-permute-start | bytes 122888 | tf_op jit(solution)/shard_map/ppermute | solution.py:77
  243.0 1.3 add_convert_fusion
  244.4 0.6 pad_maximum_fusion.2
  245.0 0.6 pad_maximum_fusion.3
  245.6 0.6 pad_maximum_fusion.4
  (48 shorter events, 0.2 us)
Async XLA Ops:
  0.6 24.9 %copy-start.4 = (bf16[2,256,512]{2,1,0:T(8,128)(2,1)S(1)}, bf16[2,256,512]{2,1,0:T(8,128)(2,1)}, u32[]{:S(2)}) copy-start(bf16[2,256,512]{2,1,0:T(8,128)(2,1)} %param.6) | copy-start | bytes 1572868
  0.6 24.8 %collective-permute-start = (bf16[1024,256]{1,0:T(8,128)(2,1)}, bf16[1024,256]{1,0:T(8,128)(2,1)S(1)}, u32[]{:S(2)}, u32[]{:S(2)}) collective-permute-start(bf16[1024,256]{1,0:T(8,128)(2,1)} %param.5), channel_id=1, source_target_pairs={{0,1},{1,2},{2,3},{3,4},{4,5},{5,6},{6,7},{7,8},{8,9},{9,10},{10,1... | collective-permute-start | bytes 1572872 | tf_op jit(solution)/shard_map/ppermute | solution.py:31
  25.5 0.8 copy-start.7
  26.3 1.0 copy-start.2
  26.3 1.1 copy-start.14
  27.7 57.6 %collective-permute-start.1 = (bf16[1024,256]{1,0:T(8,128)(2,1)S(1)}, bf16[1024,256]{1,0:T(8,128)(2,1)}, u32[]{:S(2)}, u32[]{:S(2)}) collective-permute-start(bf16[1024,256]{1,0:T(8,128)(2,1)S(1)} %fusion.2), channel_id=1, source_target_pairs={{0,64},{32,96},{64,128},{96,160},{128,192},{160,224},{192,256},{22... | collective-permute-start | bytes 1572872 | tf_op jit(solution)/shard_map/ppermute | solution.py:31
  40.9 44.5 %copy-start.5 = (bf16[2,256,512]{2,1,0:T(8,128)(2,1)S(1)}, bf16[2,256,512]{2,1,0:T(8,128)(2,1)}, u32[]{:S(2)}) copy-start(bf16[2,256,512]{2,1,0:T(8,128)(2,1)} %param.6) | copy-start | bytes 1572868
  42.4 44.5 %copy-start.9 = (bf16[1024,256]{1,0:T(8,128)(2,1)S(1)}, bf16[1024,256]{1,0:T(8,128)(2,1)}, u32[]{:S(2)}) copy-start(bf16[1024,256]{1,0:T(8,128)(2,1)} %param.9) | copy-start | bytes 1572868
  87.7 6.2 %copy-start = (bf16[1024,256]{0,1:T(8,128)(2,1)}, bf16[1024,256]{0,1:T(8,128)(2,1)S(1)}, u32[]{:S(2)}) copy-start(bf16[1024,256]{0,1:T(8,128)(2,1)S(1)} %get-tuple-element.11) | copy-start | bytes 1572868
  88.7 39.3 %collective-permute-start.2 = (bf16[1024,256]{1,0:T(8,128)(2,1)S(1)}, bf16[1024,256]{1,0:T(8,128)(2,1)S(1)}, u32[]{:S(2)}, u32[]{:S(2)}) collective-permute-start(bf16[1024,256]{1,0:T(8,128)(2,1)S(1)} %convolution_convert_fusion.1), channel_id=1, source_target_pairs={{64,0},{96,32},{128,64},{160,96},{192,128},{224,160},{256,192},{28... | collective-permute-start | bytes 1572872 | tf_op jit(solution)/shard_map/ppermute | solution.py:31
  94.3 33.7 %copy-start.12 = (bf16[2,256,512]{2,1,0:T(8,128)(2,1)S(1)}, bf16[2,256,512]{2,1,0:T(8,128)(2,1)}, u32[]{:S(2)}) copy-start(bf16[2,256,512]{2,1,0:T(8,128)(2,1)} %param.7) | copy-start | bytes 1572868
  128.5 0.8 copy-start.10
  128.5 1.2 copy-start.3
  129.3 0.9 copy-start.16
  129.3 1.0 copy-start.18
  129.3 1.4 copy-start.8
  133.3 5.4 %collective-permute-start.4 = (f32[256,1280]{1,0:T(8,128)}, f32[256,1280]{1,0:T(8,128)}, u32[]{:S(2)}, u32[]{:S(2)}) collective-permute-start(f32[256,1280]{1,0:T(8,128)} %bitcast.122), channel_id=1, source_target_pairs={{0,32},{32,0},{1,33},{33,1},{2,34},{34,2},{3,35},{35,3},{4,36},{36... | collective-permute-start | bytes 3932168 | tf_op jit(solution)/shard_map/ppermute | solution.py:73
  140.2 51.2 %copy-start.6 = (bf16[2,256,512]{2,1,0:T(8,128)(2,1)S(1)}, bf16[2,256,512]{2,1,0:T(8,128)(2,1)}, u32[]{:S(2)}) copy-start(bf16[2,256,512]{2,1,0:T(8,128)(2,1)} %param.6) | copy-start | bytes 1572868
  141.0 11.0 %collective-permute-start.7 = (f32[64,1280]{1,0:T(8,128)}, f32[64,1280]{1,0:T(8,128)S(1)}, u32[]{:S(2)}, u32[]{:S(2)}) collective-permute-start(f32[64,1280]{1,0:T(8,128)} %get-tuple-element.13), channel_id=1, source_target_pairs={{0,24},{8,0},{16,8},{24,16},{1,25},{9,1},{17,9},{25,17},{2,26},{10... | collective-permute-start | bytes 983048 | tf_op jit(solution)/shard_map/ppermute | solution.py:41
  143.2 17.0 %collective-permute-start.6 = (f32[64,1280]{1,0:T(8,128)S(1)}, f32[64,1280]{1,0:T(8,128)}, u32[]{:S(2)}, u32[]{:S(2)}) collective-permute-start(f32[64,1280]{1,0:T(8,128)S(1)} %get-tuple-element.14), channel_id=1, source_target_pairs={{0,16},{8,24},{16,0},{24,8},{1,17},{9,25},{17,1},{25,9},{2,18},{10... | collective-permute-start | bytes 983048 | tf_op jit(solution)/shard_map/ppermute | solution.py:41
  147.3 15.1 %collective-permute-start.5 = (f32[64,1280]{1,0:T(8,128)S(1)}, f32[64,1280]{1,0:T(8,128)}, u32[]{:S(2)}, u32[]{:S(2)}) collective-permute-start(f32[64,1280]{1,0:T(8,128)S(1)} %get-tuple-element.12), channel_id=1, source_target_pairs={{0,8},{8,16},{16,24},{24,0},{1,9},{9,17},{17,25},{25,1},{2,10},{10... | collective-permute-start | bytes 983048 | tf_op jit(solution)/shard_map/ppermute | solution.py:41
  160.1 31.4 %copy-start.17 = (bf16[1024,256]{0,1:T(8,128)(2,1)S(1)}, bf16[1024,256]{0,1:T(8,128)(2,1)}, u32[]{:S(2)}) copy-start(bf16[1024,256]{0,1:T(8,128)(2,1)} %copy-done.16) | copy-start | bytes 1572868
  163.6 10.0 %collective-permute-start.8 = (f32[32,1280]{1,0:T(8,128)S(1)}, f32[32,1280]{1,0:T(8,128)S(1)}, u32[]{:S(2)}, u32[]{:S(2)}) collective-permute-start(f32[32,1280]{1,0:T(8,128)S(1)} %dynamic-slice_bitcast_fusion.3), channel_id=1, source_target_pairs={{0,4},{1,5},{2,6},{3,7},{4,0},{5,1},{6,2},{7,3},{8,12},{9,13},{10,... | collective-permute-start | bytes 491528 | tf_op jit(solution)/shard_map/ppermute | solution.py:54
  165.5 65.7 %copy-start.1 = (bf16[1024,256]{0,1:T(8,128)(2,1)S(1)}, bf16[1024,256]{0,1:T(8,128)(2,1)}, u32[]{:S(2)}) copy-start(bf16[1024,256]{0,1:T(8,128)(2,1)} %copy-done) | copy-start | bytes 1572868
  165.5 65.7 %copy-start.15 = (bf16[2,256,256]{2,1,0:T(8,128)(2,1)S(1)}, bf16[2,256,256]{2,1,0:T(8,128)(2,1)}, u32[]{:S(2)}) copy-start(bf16[2,256,256]{2,1,0:T(8,128)(2,1)} %param.8) | copy-start | bytes 786436
  173.6 15.7 %collective-permute-start.9 = (f32[16,1280]{1,0:T(8,128)S(1)}, f32[16,1280]{1,0:T(8,128)S(1)}, u32[]{:S(2)}, u32[]{:S(2)}) collective-permute-start(f32[16,1280]{1,0:T(8,128)S(1)} %dynamic-slice_bitcast_fusion.4), channel_id=1, source_target_pairs={{0,2},{1,3},{2,0},{3,1},{4,6},{5,7},{6,4},{7,5},{8,10},{9,11},{10,... | collective-permute-start | bytes 245768 | tf_op jit(solution)/shard_map/ppermute | solution.py:54
  189.4 53.6 %copy-start.11 = (bf16[1024,256]{1,0:T(8,128)(2,1)S(1)}, bf16[1024,256]{1,0:T(8,128)(2,1)}, u32[]{:S(2)}) copy-start(bf16[1024,256]{1,0:T(8,128)(2,1)} %copy-done.10) | copy-start | bytes 1572868
  189.4 53.6 %copy-start.13 = (bf16[2,256,512]{2,1,0:T(8,128)(2,1)S(1)}, bf16[2,256,512]{2,1,0:T(8,128)(2,1)}, u32[]{:S(2)}) copy-start(bf16[2,256,512]{2,1,0:T(8,128)(2,1)} %param.7) | copy-start | bytes 1572868
  189.4 53.6 %copy-start.19 = (bf16[1024,256]{0,1:T(8,128)(2,1)S(1)}, bf16[1024,256]{0,1:T(8,128)(2,1)}, u32[]{:S(2)}) copy-start(bf16[1024,256]{0,1:T(8,128)(2,1)} %copy-done.18) | copy-start | bytes 1572868
  189.4 13.8 %collective-permute-start.10 = (f32[8,1280]{1,0:T(8,128)S(1)}, f32[8,1280]{1,0:T(8,128)S(1)}, u32[]{:S(2)}, u32[]{:S(2)}) collective-permute-start(f32[8,1280]{1,0:T(8,128)S(1)} %dynamic-slice_bitcast_fusion.5), channel_id=1, source_target_pairs={{0,1},{1,0},{2,3},{3,2},{4,5},{5,4},{6,7},{7,6},{8,9},{9,8},{10,11... | collective-permute-start | bytes 122888 | tf_op jit(solution)/shard_map/ppermute | solution.py:54
  193.0 50.0 %collective-permute-start.3 = (bf16[1024,256]{1,0:T(8,128)(2,1)S(1)}, bf16[1024,256]{1,0:T(8,128)(2,1)S(1)}, u32[]{:S(2)}, u32[]{:S(2)}) collective-permute-start(bf16[1024,256]{1,0:T(8,128)(2,1)S(1)} %convolution_convert_fusion), channel_id=1, source_target_pairs={{1,0},{2,1},{3,2},{4,3},{5,4},{6,5},{7,6},{8,7},{9,8},{10,9},{11,1... | collective-permute-start | bytes 1572872 | tf_op jit(solution)/shard_map/ppermute | solution.py:31
  203.2 21.3 %collective-permute-start.11 = (f32[8,1280]{1,0:T(8,128)S(1)}, f32[8,1280]{1,0:T(8,128)S(1)}, u32[]{:S(2)}, u32[]{:S(2)}) collective-permute-start(f32[8,1280]{1,0:T(8,128)S(1)} %bitcast_add_fusion.4), channel_id=1, source_target_pairs={{0,64},{64,0},{128,192},{192,128},{256,320},{320,256},{384,448},{4... | collective-permute-start | bytes 122888 | tf_op jit(solution)/shard_map/ppermute | solution.py:63
  224.5 4.7 %collective-permute-start.12 = (f32[8,1280]{1,0:T(8,128)S(1)}, f32[8,1280]{1,0:T(8,128)S(1)}, u32[]{:S(2)}, u32[]{:S(2)}) collective-permute-start(f32[8,1280]{1,0:T(8,128)S(1)} %add.176), channel_id=1, source_target_pairs={{0,128},{64,192},{128,0},{192,64},{256,384},{320,448},{384,256},{4... | collective-permute-start | bytes 122888 | tf_op jit(solution)/shard_map/ppermute | solution.py:63
  229.3 6.2 %collective-permute-start.13 = (f32[8,1280]{1,0:T(8,128)S(1)}, f32[8,1280]{1,0:T(8,128)S(1)}, u32[]{:S(2)}, u32[]{:S(2)}) collective-permute-start(f32[8,1280]{1,0:T(8,128)S(1)} %add.177), channel_id=1, source_target_pairs={{0,256},{64,320},{128,384},{192,448},{256,0},{320,64},{384,128},{4... | collective-permute-start | bytes 122888 | tf_op jit(solution)/shard_map/ppermute | solution.py:63
  235.5 8.8 %collective-permute-start.14 = (f32[8,1280]{1,0:T(8,128)S(1)}, f32[8,1280]{1,0:T(8,128)S(1)}, u32[]{:S(2)}, u32[]{:S(2)}) collective-permute-start(f32[8,1280]{1,0:T(8,128)S(1)} %add.178), channel_id=1, source_target_pairs={{0,32},{32,0},{1,33},{33,1},{2,34},{34,2},{3,35},{35,3},{4,36},{36... | collective-permute-start | bytes 122888 | tf_op jit(solution)/shard_map/ppermute | solution.py:77

commit v3 on v2

--- a/solution.py
+++ b/solution.py
@@ -65,20 +65,26 @@
     return total
 
 
-def weight_sum(term):
+def near_sum(term):
     own_core = lax.axis_index("core")
     halves = term.reshape(term.shape[0], 2, term.shape[1] // 2)
     kept = lax.dynamic_index_in_dim(halves, own_core, 1, keepdims=False)
     given = lax.dynamic_index_in_dim(halves, 1 - own_core, 1, keepdims=False)
     term = kept + lax.ppermute(given, "core", [(0, 1), (1, 0)])
-    term = scatter_sum(term, ("x",))
-    term = halving_sum(term, ("z_lo",))
+    return scatter_sum(term, ("x",))
+
+
+def far_sum(term):
+    size = lax.axis_size("z_lo")
+    pieces = term.reshape(size, term.shape[0] // size, term.shape[1])
+    term = lax.all_to_all(pieces, "z_lo", 0, 0, tiled=True).sum(0)
     term = everyone_sum(term, ("y", "z_hi"))
     other = lax.ppermute(term, "core", [(0, 1), (1, 0)])
+    own_core = lax.axis_index("core")
     pair = jnp.stack([term, other])
     first = lax.dynamic_index_in_dim(pair, own_core, 0, keepdims=False)
     second = lax.dynamic_index_in_dim(pair, 1 - own_core, 0, keepdims=False)
-    return jnp.concatenate([first, second], 1)
+    return first, second
 
 
 def gating(current, earlier, w_past, w_now):
@@ -142,7 +148,7 @@
         ).astype(jnp.bfloat16)
     result = current
     upstream = cotangent
-    summed_list = [None] * layer_count
+    near_list = [None] * layer_count
     for layer_at in reversed(range(layer_count)):
         current = inputs[layer_at]
         earlier = earliers[layer_at]
@@ -156,15 +162,22 @@
         ).astype(jnp.bfloat16)
         arrived = return_past(sent_back, layer_at)
         operands = (earlier, current, gated_out, grad_preact, upstream)
-        summed_list[layer_at] = layer_term(operands, grad_scale)
+        near_list[layer_at] = near_sum(layer_term(operands, grad_scale))
+        near_list, arrived = lax.optimization_barrier((near_list, arrived))
         local_grad = upstream.astype(jnp.float32) + jnp.dot(
             grad_preact, conv_now[layer_at].T, preferred_element_type=jnp.float32
         )
         upstream = (local_grad + arrived.astype(jnp.float32)).astype(jnp.bfloat16)
-    term_width = summed_list[0].shape[1]
-    whole = weight_sum(jnp.concatenate(summed_list, 1))
+    first, second = far_sum(jnp.concatenate(near_list, 1))
+    half_width = near_list[0].shape[1]
     summed_list = [
-        whole[:, layer_at * term_width : (layer_at + 1) * term_width]
+        jnp.concatenate(
+            [
+                first[:, layer_at * half_width : (layer_at + 1) * half_width],
+                second[:, layer_at * half_width : (layer_at + 1) * half_width],
+            ],
+            1,
+        )
         for layer_at in range(layer_count)
     ]
     past_list = [summed[:, :gate_width] for summed in summed_list]

time: 247 us -> 247 us (level)
  the two profiles are of different devices: /device:TPU:11 before, /device:TPU:1 now
where the time goes in v3:
time: 247 us; the launch traced here: 245 us
  starting transfers between devices  92.7 us (38%)
  waiting for transfers between devices  87.6 us (35%)
  blocking collectives  32 us (13%)
  matrix products  16.8 us (7%)
  local copies, waits for them, and re-layouts  9.57 us (4%)
  other arithmetic  4.68 us (2%)
    ppermute x4, waiting for transfers between devices, from_behind(): return lax.ppermute(array, axes, pairs)  75.6 us
    ppermute x3, starting transfers between devices, everyone_sum(): lax.ppermute(total, axes, [(i, i ^ step) for i in range(size)])  36.6 us
    all_to_all x1, blocking collectives, far_sum(): term = lax.all_to_all(pieces, 'z_lo', 0, 0, tiled=True).sum(0)  32 us
    ppermute x4, starting transfers between devices, from_behind(): return lax.ppermute(array, axes, pairs)  22.1 us
    ppermute x6, starting transfers between devices, scatter_sum(): lax.ppermute(piece, axes, [(i, (i + shift) % size) for i in range(size)])  21.2 us
    ppermute x6, waiting for transfers between devices, scatter_sum(): lax.ppermute(piece, axes, [(i, (i + shift) % size) for i in range(size)])  8.66 us
    ppermute x1, starting transfers between devices, far_sum(): other = lax.ppermute(term, 'core', [(0, 1), (1, 0)])  8.04 us
  transfers between devices with their start and end apart: 16, of which 11 were waited for; matrix products, arithmetic and copies ran while one was open for 5% of the time, Pallas kernels for 0%

profile of v3, /device:TPU:1, one launch (start us, length us, event | category | flops | bytes accessed | tf_op | source)
XLA Modules:
  0.0 244.8 jit_solution(16341975920086013837)
XLA Ops:
  0.6 4.5 %collective-permute-start = (bf16[1024,256]{1,0:T(8,128)(2,1)}, bf16[1024,256]{1,0:T(8,128)(2,1)S(1)}, u32[]{:S(2)}, u32[]{:S(2)}) collective-permute-start(bf16[1024,256]{1,0:T(8,128)(2,1)} %param.5), channel_id=1, source_target_pairs={{0,1},{1,2},{2,3},{3,4},{4,5},{5,6},{6,7},{7,8},{8,9},{9,10},{10,1... | collective-permute-start | bytes 1572872 | tf_op jit(solution)/shard_map/ppermute | solution.py:31
  5.2 1.6 fusion.14
  6.8 20.6 %collective-permute-done = bf16[1024,256]{1,0:T(8,128)(2,1)S(1)} collective-permute-done((bf16[1024,256]{1,0:T(8,128)(2,1)}, bf16[1024,256]{1,0:T(8,128)(2,1)S(1)}, u32[]{:S(2)}, u32[]{:S(2)}) %collective-permute-start) | collective-permute-done | bytes 524320 | tf_op jit(solution)/shard_map/ppermute | solution.py:31
  27.3 0.5 convolution_add_fusion.1
  27.8 0.3 copy-done.13
  28.1 0.4 multiply_convert_fusion.5
  28.5 0.8 copy-done
  29.3 0.4 fusion
  29.7 10.2 %collective-permute-start.1 = (bf16[1024,256]{1,0:T(8,128)(2,1)S(1)}, bf16[1024,256]{1,0:T(8,128)(2,1)}, u32[]{:S(2)}, u32[]{:S(2)}) collective-permute-start(bf16[1024,256]{1,0:T(8,128)(2,1)S(1)} %fusion), channel_id=1, source_target_pairs={{0,64},{32,96},{64,128},{96,160},{128,192},{160,224},{192,256},{22... | collective-permute-start | bytes 1572872 | tf_op jit(solution)/shard_map/ppermute | solution.py:31
  39.9 1.4 fusion.9
  41.3 37.4 %collective-permute-done.1 = bf16[1024,256]{1,0:T(8,128)(2,1)} collective-permute-done((bf16[1024,256]{1,0:T(8,128)(2,1)S(1)}, bf16[1024,256]{1,0:T(8,128)(2,1)}, u32[]{:S(2)}, u32[]{:S(2)}) %collective-permute-start.1) | collective-permute-done | bytes 524320 | tf_op jit(solution)/shard_map/ppermute | solution.py:31
  78.7 1.5 convolution_add_fusion
  80.3 0.8 multiply_convert_fusion.3
  81.1 0.3 fusion.52
  81.4 0.5 fusion.48
  81.9 0.1 copy-done.22
  82.0 0.2 copy-done.24
  82.2 1.5 fusion.49
  83.7 0.1 maximum_multiply_fusion
  83.9 1.8 mul.65
  85.7 3.1 %constant_dynamic-slice_fusion.3 = (f32[256,1,640]{2,1,0:T(1,128)S(1)}, f32[256,1,640]{2,1,0:T(1,128)S(1)}) fusion(f32[256,2,640]{2,1,0:T(2,128)} %mul.65, s32[]{:T(128)S(6)} %select_n.50, s32[]{:T(128)S(6)} %select_n.51), kind=kLoop, calls=%fused_computation.101 | loop fusion | bytes 2621448 | tf_op jit(solution)/shard_map/jit(dynamic_index_in_dim)/dynamic_slice | solution.py:71
  88.8 2.1 collective-permute-start.2
  91.0 1.8 convolution_convert_fusion.1
  92.8 1.4 collective-permute-start.6
  94.2 1.2 bitcast_add_fusion.1
  95.5 3.2 %collective-permute-start.3 = (f32[64,640]{1,0:T(8,128)S(1)}, f32[64,640]{1,0:T(8,128)S(1)}, u32[]{:S(2)}, u32[]{:S(2)}) collective-permute-start(f32[64,640]{1,0:T(8,128)S(1)} %get-tuple-element.27), channel_id=1, source_target_pairs={{0,8},{8,16},{16,24},{24,0},{1,9},{9,17},{17,25},{25,1},{2,10},{10... | collective-permute-start | bytes 491528 | tf_op jit(solution)/shard_map/ppermute | solution.py:41
  98.7 4.4 %collective-permute-start.4 = (f32[64,640]{1,0:T(8,128)S(1)}, f32[64,640]{1,0:T(8,128)S(1)}, u32[]{:S(2)}, u32[]{:S(2)}) collective-permute-start(f32[64,640]{1,0:T(8,128)S(1)} %get-tuple-element.29), channel_id=1, source_target_pairs={{0,16},{8,24},{16,0},{24,8},{1,17},{9,25},{17,1},{25,9},{2,18},{10... | collective-permute-start | bytes 491528 | tf_op jit(solution)/shard_map/ppermute | solution.py:41
  103.1 3.2 %collective-permute-start.5 = (f32[64,640]{1,0:T(8,128)S(1)}, f32[64,640]{1,0:T(8,128)S(1)}, u32[]{:S(2)}, u32[]{:S(2)}) collective-permute-start(f32[64,640]{1,0:T(8,128)S(1)} %get-tuple-element.28), channel_id=1, source_target_pairs={{0,24},{8,0},{16,8},{24,16},{1,25},{9,1},{17,9},{25,17},{2,26},{10... | collective-permute-start | bytes 491528 | tf_op jit(solution)/shard_map/ppermute | solution.py:41
  106.3 0.5 convolution_add_fusion.5
  106.9 2.1 collective-permute-done.4
  109.0 1.2 collective-permute-done.5
  110.1 0.7 fusion.31
  110.8 7.5 %collective-permute-done.6 = bf16[1024,256]{1,0:T(8,128)(2,1)S(1)} collective-permute-done((bf16[1024,256]{1,0:T(8,128)(2,1)S(1)}, bf16[1024,256]{1,0:T(8,128)(2,1)S(1)}, u32[]{:S(2)}, u32[]{:S(2)}) %collective-permute-start.6) | collective-permute-done | bytes 524320 | tf_op jit(solution)/shard_map/ppermute | solution.py:31
  118.5 0.7 multiply_convert_fusion.1
  119.2 0.5 copy-done.1
  119.7 0.3 fusion.53
  120.0 0.5 convolution_bitcast_fusion
  120.5 0.6 copy-done.14
  121.1 0.5 convolution_bitcast_fusion.1
  121.6 0.1 maximum_multiply_fusion.1
  121.7 0.7 mul.73
  122.5 1.1 constant_dynamic-slice_fusion.1
  123.7 2.7 %collective-permute-start.7 = (f32[256,640]{1,0:T(8,128)S(1)}, f32[256,640]{1,0:T(8,128)S(1)}, u32[]{:S(2)}, u32[]{:S(2)}) collective-permute-start(f32[256,640]{1,0:T(8,128)S(1)} %bitcast.117), channel_id=1, source_target_pairs={{0,32},{32,0},{1,33},{33,1},{2,34},{34,2},{3,35},{35,3},{4,36},{36... | collective-permute-start | bytes 1966088 | tf_op jit(solution)/shard_map/ppermute | solution.py:73
  126.4 0.5 convolution_convert_fusion
  126.9 6.0 %collective-permute-start.11 = (bf16[1024,256]{1,0:T(8,128)(2,1)S(1)}, bf16[1024,256]{1,0:T(8,128)(2,1)S(1)}, u32[]{:S(2)}, u32[]{:S(2)}) collective-permute-start(bf16[1024,256]{1,0:T(8,128)(2,1)S(1)} %convolution_convert_fusion), channel_id=1, source_target_pairs={{1,0},{2,1},{3,2},{4,3},{5,4},{6,5},{7,6},{8,7},{9,8},{10,9},{11,1... | collective-permute-start | bytes 1572872 | tf_op jit(solution)/shard_map/ppermute | solution.py:31
  133.1 4.6 %collective-permute-start.10 = (f32[64,640]{1,0:T(8,128)S(1)}, f32[64,640]{1,0:T(8,128)S(1)}, u32[]{:S(2)}, u32[]{:S(2)}) collective-permute-start(f32[64,640]{1,0:T(8,128)S(1)} %get-tuple-element.25), channel_id=1, source_target_pairs={{0,24},{8,0},{16,8},{24,16},{1,25},{9,1},{17,9},{25,17},{2,26},{10... | collective-permute-start | bytes 491528 | tf_op jit(solution)/shard_map/ppermute | solution.py:41
  137.8 1.9 collective-permute-start.8
  139.7 3.8 %collective-permute-start.9 = (f32[64,640]{1,0:T(8,128)S(1)}, f32[64,640]{1,0:T(8,128)S(1)}, u32[]{:S(2)}, u32[]{:S(2)}) collective-permute-start(f32[64,640]{1,0:T(8,128)S(1)} %get-tuple-element.26), channel_id=1, source_target_pairs={{0,16},{8,24},{16,0},{24,8},{1,17},{9,25},{17,1},{25,9},{2,18},{10... | collective-permute-start | bytes 491528 | tf_op jit(solution)/shard_map/ppermute | solution.py:41
  143.5 2.6 %collective-permute-done.8 = f32[64,640]{1,0:T(8,128)S(1)} collective-permute-done((f32[64,640]{1,0:T(8,128)S(1)}, f32[64,640]{1,0:T(8,128)S(1)}, u32[]{:S(2)}, u32[]{:S(2)}) %collective-permute-start.8) | collective-permute-done | bytes 163872 | tf_op jit(solution)/shard_map/ppermute | solution.py:41
  146.1 2.8 %collective-permute-done.9 = f32[64,640]{1,0:T(8,128)S(1)} collective-permute-done((f32[64,640]{1,0:T(8,128)S(1)}, f32[64,640]{1,0:T(8,128)S(1)}, u32[]{:S(2)}, u32[]{:S(2)}) %collective-permute-start.9) | collective-permute-done | bytes 163872 | tf_op jit(solution)/shard_map/ppermute | solution.py:41
  148.9 10.1 %collective-permute-done.11 = bf16[1024,256]{1,0:T(8,128)(2,1)S(1)} collective-permute-done((bf16[1024,256]{1,0:T(8,128)(2,1)S(1)}, bf16[1024,256]{1,0:T(8,128)(2,1)S(1)}, u32[]{:S(2)}, u32[]{:S(2)}) %collective-permute-start.11) | collective-permute-done | bytes 524320 | tf_op jit(solution)/shard_map/ppermute | solution.py:31
  159.1 32.0 %all_to_all.5 = f32[8,8,1280]{2,1,0:T(8,128)S(1)} all-to-all(f32[8,8,1280]{2,1,0:T(8,128)S(1)} %maximum_bitcast_fusion), channel_id=1, replica_groups=mesh['y'=4,'z_hi'=2,'core'=2,'x'=4,'z_lo'=8] {'z_lo'}, dimensions={0} | all-to-all | bytes 655360 | tf_op jit(solution)/shard_map/all_to_all | solution.py:80
  191.1 15.4 %collective-permute-start.12 = (f32[8,1280]{1,0:T(8,128)S(1)}, f32[8,1280]{1,0:T(8,128)S(1)}, u32[]{:S(2)}, u32[]{:S(2)}) collective-permute-start(f32[8,1280]{1,0:T(8,128)S(1)} %reduce_sum.9), channel_id=1, source_target_pairs={{0,64},{64,0},{128,192},{192,128},{256,320},{320,256},{384,448},{4... | collective-permute-start | bytes 122888 | tf_op jit(solution)/shard_map/ppermute | solution.py:63
  206.5 1.4 collective-permute-done.12
  207.9 16.7 %collective-permute-start.13 = (f32[8,1280]{1,0:T(8,128)S(1)}, f32[8,1280]{1,0:T(8,128)S(1)}, u32[]{:S(2)}, u32[]{:S(2)}) collective-permute-start(f32[8,1280]{1,0:T(8,128)S(1)} %add.148), channel_id=1, source_target_pairs={{0,128},{64,192},{128,0},{192,64},{256,384},{320,448},{384,256},{4... | collective-permute-start | bytes 122888 | tf_op jit(solution)/shard_map/ppermute | solution.py:63
  224.6 1.4 collective-permute-done.13
  226.0 4.5 %collective-permute-start.14 = (f32[8,1280]{1,0:T(8,128)S(1)}, f32[8,1280]{1,0:T(8,128)S(1)}, u32[]{:S(2)}, u32[]{:S(2)}) collective-permute-start(f32[8,1280]{1,0:T(8,128)S(1)} %add.149), channel_id=1, source_target_pairs={{0,256},{64,320},{128,384},{192,448},{256,0},{320,64},{384,128},{4... | collective-permute-start | bytes 122888 | tf_op jit(solution)/shard_map/ppermute | solution.py:63
  230.5 1.1 fusion.1
  231.7 0.6 collective-permute-done.14
  232.3 8.0 %collective-permute-start.15 = (f32[8,1280]{1,0:T(8,128)S(1)}, f32[8,1280]{1,0:T(8,128)S(1)}, u32[]{:S(2)}, u32[]{:S(2)}) collective-permute-start(f32[8,1280]{1,0:T(8,128)S(1)} %add.150), channel_id=1, source_target_pairs={{0,32},{32,0},{1,33},{33,1},{2,34},{34,2},{3,35},{35,3},{4,36},{36... | collective-permute-start | bytes 122888 | tf_op jit(solution)/shard_map/ppermute | solution.py:82
  240.4 2.5 %add_convert_fusion = bf16[1024,256]{1,0:T(8,128)(2,1)} fusion(bf16[1024,256]{1,0:T(8,128)(2,1)S(1)} %collective-permute-done.11, bf16[1024,256]{1,0:T(8,128)(2,1)S(1)} %copy-done.9, bf16[2,256,512]{2,1,0:T(8,128)(2,1)S(1)} %copy-done.18, bf16[1024,256]{0,1:T(8,128)(2,1)} %copy-done.28, bf16[1024,256]{0,1:T(8,128)(2,1)} %copy-done.26), kind=kOutput, calls=%fused_computation.26 | convolution fusion | flops 271843328 | bytes 2883584 | tf_op jit(solution)/shard_map/dot_general | solution.py:167
  243.0 0.6 pad_maximum_fusion.6
  243.6 0.6 pad_maximum_fusion.3
  244.2 0.6 pad_maximum_fusion.2
  (77 shorter events, 0.7 us)
Async XLA Ops:
  0.6 26.7 %copy-start.11 = (bf16[2,256,512]{2,1,0:T(8,128)(2,1)S(1)}, bf16[2,256,512]{2,1,0:T(8,128)(2,1)}, u32[]{:S(2)}) copy-start(bf16[2,256,512]{2,1,0:T(8,128)(2,1)} %param.6) | copy-start | bytes 1572868
  0.6 26.7 %collective-permute-start = (bf16[1024,256]{1,0:T(8,128)(2,1)}, bf16[1024,256]{1,0:T(8,128)(2,1)S(1)}, u32[]{:S(2)}, u32[]{:S(2)}) collective-permute-start(bf16[1024,256]{1,0:T(8,128)(2,1)} %param.5), channel_id=1, source_target_pairs={{0,1},{1,2},{2,3},{3,4},{4,5},{5,6},{6,7},{7,8},{8,9},{9,10},{10,1... | collective-permute-start | bytes 1572872 | tf_op jit(solution)/shard_map/ppermute | solution.py:31
  27.3 0.8 copy-start.13
  28.1 1.2 copy-start.6
  28.1 1.2 copy-start.19
  28.5 0.8 copy-start
  29.7 51.7 %copy-start.2 = (bf16[1024,256]{1,0:T(8,128)(2,1)}, bf16[1024,256]{1,0:T(8,128)(2,1)S(1)}, u32[]{:S(2)}) copy-start(bf16[1024,256]{1,0:T(8,128)(2,1)S(1)} %fusion) | copy-start | bytes 1572868
  29.7 49.0 %collective-permute-start.1 = (bf16[1024,256]{1,0:T(8,128)(2,1)S(1)}, bf16[1024,256]{1,0:T(8,128)(2,1)}, u32[]{:S(2)}, u32[]{:S(2)}) collective-permute-start(bf16[1024,256]{1,0:T(8,128)(2,1)S(1)} %fusion), channel_id=1, source_target_pairs={{0,64},{32,96},{64,128},{96,160},{128,192},{160,224},{192,256},{22... | collective-permute-start | bytes 1572872 | tf_op jit(solution)/shard_map/ppermute | solution.py:31
  41.3 39.0 %copy-start.15 = (bf16[1024,256]{1,0:T(8,128)(2,1)S(1)}, bf16[1024,256]{1,0:T(8,128)(2,1)}, u32[]{:S(2)}) copy-start(bf16[1024,256]{1,0:T(8,128)(2,1)} %param.9) | copy-start | bytes 1572868
  81.1 0.8 copy-start.4
  81.1 1.0 copy-start.22
  81.1 1.1 copy-start.24
  88.8 5.4 %collective-permute-start.2 = (f32[256,640]{1,0:T(8,128)S(1)}, f32[256,640]{1,0:T(8,128)}, u32[]{:S(2)}, u32[]{:S(2)}) collective-permute-start(f32[256,640]{1,0:T(8,128)S(1)} %bitcast.116), channel_id=1, source_target_pairs={{0,32},{32,0},{1,33},{33,1},{2,34},{34,2},{3,35},{35,3},{4,36},{36... | collective-permute-start | bytes 1966088 | tf_op jit(solution)/shard_map/ppermute | solution.py:73
  92.8 13.6 %copy-start.16 = (bf16[1024,256]{1,0:T(8,128)(2,1)S(1)}, bf16[1024,256]{1,0:T(8,128)(2,1)}, u32[]{:S(2)}) copy-start(bf16[1024,256]{1,0:T(8,128)(2,1)} %param.9) | copy-start | bytes 1572868
  92.8 13.6 %copy-start.17 = (bf16[2,256,512]{2,1,0:T(8,128)(2,1)S(1)}, bf16[2,256,512]{2,1,0:T(8,128)(2,1)}, u32[]{:S(2)}) copy-start(bf16[2,256,512]{2,1,0:T(8,128)(2,1)} %param.7) | copy-start | bytes 1572868
  92.8 13.5 %copy-start.23 = (bf16[1024,256]{0,1:T(8,128)(2,1)S(1)}, bf16[1024,256]{0,1:T(8,128)(2,1)}, u32[]{:S(2)}) copy-start(bf16[1024,256]{0,1:T(8,128)(2,1)} %copy-done.22) | copy-start | bytes 1572868
  92.8 13.5 %copy-start.25 = (bf16[1024,256]{0,1:T(8,128)(2,1)S(1)}, bf16[1024,256]{0,1:T(8,128)(2,1)}, u32[]{:S(2)}) copy-start(bf16[1024,256]{0,1:T(8,128)(2,1)} %copy-done.24) | copy-start | bytes 1572868
  92.8 25.5 %collective-permute-start.6 = (bf16[1024,256]{1,0:T(8,128)(2,1)S(1)}, bf16[1024,256]{1,0:T(8,128)(2,1)S(1)}, u32[]{:S(2)}, u32[]{:S(2)}) collective-permute-start(bf16[1024,256]{1,0:T(8,128)(2,1)S(1)} %convolution_convert_fusion.1), channel_id=1, source_target_pairs={{64,0},{96,32},{128,64},{160,96},{192,128},{224,160},{256,192},{28... | collective-permute-start | bytes 1572872 | tf_op jit(solution)/shard_map/ppermute | solution.py:31
  95.5 11.4 %collective-permute-start.3 = (f32[64,640]{1,0:T(8,128)S(1)}, f32[64,640]{1,0:T(8,128)S(1)}, u32[]{:S(2)}, u32[]{:S(2)}) collective-permute-start(f32[64,640]{1,0:T(8,128)S(1)} %get-tuple-element.27), channel_id=1, source_target_pairs={{0,8},{8,16},{16,24},{24,0},{1,9},{9,17},{17,25},{25,1},{2,10},{10... | collective-permute-start | bytes 491528 | tf_op jit(solution)/shard_map/ppermute | solution.py:41
  98.7 10.3 %collective-permute-start.4 = (f32[64,640]{1,0:T(8,128)S(1)}, f32[64,640]{1,0:T(8,128)S(1)}, u32[]{:S(2)}, u32[]{:S(2)}) collective-permute-start(f32[64,640]{1,0:T(8,128)S(1)} %get-tuple-element.29), channel_id=1, source_target_pairs={{0,16},{8,24},{16,0},{24,8},{1,17},{9,25},{17,1},{25,9},{2,18},{10... | collective-permute-start | bytes 491528 | tf_op jit(solution)/shard_map/ppermute | solution.py:41
  103.1 7.1 %collective-permute-start.5 = (f32[64,640]{1,0:T(8,128)S(1)}, f32[64,640]{1,0:T(8,128)S(1)}, u32[]{:S(2)}, u32[]{:S(2)}) collective-permute-start(f32[64,640]{1,0:T(8,128)S(1)} %get-tuple-element.28), channel_id=1, source_target_pairs={{0,24},{8,0},{16,8},{24,16},{1,25},{9,1},{17,9},{25,17},{2,26},{10... | collective-permute-start | bytes 491528 | tf_op jit(solution)/shard_map/ppermute | solution.py:41
  106.8 11.6 %copy-start.20 = (bf16[2,256,256]{2,1,0:T(8,128)(2,1)S(1)}, bf16[2,256,256]{2,1,0:T(8,128)(2,1)}, u32[]{:S(2)}) copy-start(bf16[2,256,256]{2,1,0:T(8,128)(2,1)} %param.8) | copy-start | bytes 786436
  118.4 0.8 copy-start.8
  118.4 1.2 copy-start.1
  118.5 1.5 copy-start.7
  119.7 0.8 copy-start.26
  119.7 1.9 copy-start.28
  119.7 1.4 copy-start.14
  122.4 3.9 %copy-start.12 = (bf16[2,256,512]{2,1,0:T(8,128)(2,1)S(1)}, bf16[2,256,512]{2,1,0:T(8,128)(2,1)}, u32[]{:S(2)}) copy-start(bf16[2,256,512]{2,1,0:T(8,128)(2,1)} %param.6) | copy-start | bytes 1572868
  122.5 3.9 %copy-start.27 = (bf16[1024,256]{0,1:T(8,128)(2,1)S(1)}, bf16[1024,256]{0,1:T(8,128)(2,1)}, u32[]{:S(2)}) copy-start(bf16[1024,256]{0,1:T(8,128)(2,1)} %copy-done.26) | copy-start | bytes 1572868
  122.5 3.9 %copy-start.29 = (bf16[1024,256]{0,1:T(8,128)(2,1)S(1)}, bf16[1024,256]{0,1:T(8,128)(2,1)}, u32[]{:S(2)}) copy-start(bf16[1024,256]{0,1:T(8,128)(2,1)} %copy-done.28) | copy-start | bytes 1572868
  123.7 9.3 %collective-permute-start.7 = (f32[256,640]{1,0:T(8,128)S(1)}, f32[256,640]{1,0:T(8,128)S(1)}, u32[]{:S(2)}, u32[]{:S(2)}) collective-permute-start(f32[256,640]{1,0:T(8,128)S(1)} %bitcast.117), channel_id=1, source_target_pairs={{0,32},{32,0},{1,33},{33,1},{2,34},{34,2},{3,35},{35,3},{4,36},{36... | collective-permute-start | bytes 1966088 | tf_op jit(solution)/shard_map/ppermute | solution.py:73
  126.9 32.2 %copy-start.10 = (f32[64,640]{1,0:T(8,128)S(1)}, f32[64,640]{1,0:T(8,128)}, u32[]{:S(2)}) copy-start(f32[64,640]{1,0:T(8,128)} %fusion.31) | copy-start | bytes 491524
  126.9 32.2 %collective-permute-start.11 = (bf16[1024,256]{1,0:T(8,128)(2,1)S(1)}, bf16[1024,256]{1,0:T(8,128)(2,1)S(1)}, u32[]{:S(2)}, u32[]{:S(2)}) collective-permute-start(bf16[1024,256]{1,0:T(8,128)(2,1)S(1)} %convolution_convert_fusion), channel_id=1, source_target_pairs={{1,0},{2,1},{3,2},{4,3},{5,4},{6,5},{7,6},{8,7},{9,8},{10,9},{11,1... | collective-permute-start | bytes 1572872 | tf_op jit(solution)/shard_map/ppermute | solution.py:31
  133.0 97.5 %copy-start.3 = (bf16[1024,256]{1,0:T(8,128)(2,1)S(1)}, bf16[1024,256]{1,0:T(8,128)(2,1)}, u32[]{:S(2)}) copy-start(bf16[1024,256]{1,0:T(8,128)(2,1)} %copy-done.2) | copy-start | bytes 1572868
  133.0 97.5 %copy-start.5 = (bf16[1024,256]{0,1:T(8,128)(2,1)S(1)}, bf16[1024,256]{0,1:T(8,128)(2,1)}, u32[]{:S(2)}) copy-start(bf16[1024,256]{0,1:T(8,128)(2,1)} %copy-done.4) | copy-start | bytes 1572868
  133.0 97.5 %copy-start.21 = (bf16[2,256,256]{2,1,0:T(8,128)(2,1)S(1)}, bf16[2,256,256]{2,1,0:T(8,128)(2,1)}, u32[]{:S(2)}) copy-start(bf16[2,256,256]{2,1,0:T(8,128)(2,1)} %param.8) | copy-start | bytes 786436
  133.1 10.4 %collective-permute-start.10 = (f32[64,640]{1,0:T(8,128)S(1)}, f32[64,640]{1,0:T(8,128)S(1)}, u32[]{:S(2)}, u32[]{:S(2)}) collective-permute-start(f32[64,640]{1,0:T(8,128)S(1)} %get-tuple-element.25), channel_id=1, source_target_pairs={{0,24},{8,0},{16,8},{24,16},{1,25},{9,1},{17,9},{25,17},{2,26},{10... | collective-permute-start | bytes 491528 | tf_op jit(solution)/shard_map/ppermute | solution.py:41
  137.8 8.3 %collective-permute-start.8 = (f32[64,640]{1,0:T(8,128)S(1)}, f32[64,640]{1,0:T(8,128)S(1)}, u32[]{:S(2)}, u32[]{:S(2)}) collective-permute-start(f32[64,640]{1,0:T(8,128)S(1)} %get-tuple-element.24), channel_id=1, source_target_pairs={{0,8},{8,16},{16,24},{24,0},{1,9},{9,17},{17,25},{25,1},{2,10},{10... | collective-permute-start | bytes 491528 | tf_op jit(solution)/shard_map/ppermute | solution.py:41
  139.7 100.7 %copy-start.9 = (bf16[1024,256]{1,0:T(8,128)(2,1)S(1)}, bf16[1024,256]{1,0:T(8,128)(2,1)}, u32[]{:S(2)}) copy-start(bf16[1024,256]{1,0:T(8,128)(2,1)} %copy-done.8) | copy-start | bytes 1572868
  139.7 100.7 %copy-start.18 = (bf16[2,256,512]{2,1,0:T(8,128)(2,1)S(1)}, bf16[2,256,512]{2,1,0:T(8,128)(2,1)}, u32[]{:S(2)}) copy-start(bf16[2,256,512]{2,1,0:T(8,128)(2,1)} %param.7) | copy-start | bytes 1572868
  139.7 9.2 %collective-permute-start.9 = (f32[64,640]{1,0:T(8,128)S(1)}, f32[64,640]{1,0:T(8,128)S(1)}, u32[]{:S(2)}, u32[]{:S(2)}) collective-permute-start(f32[64,640]{1,0:T(8,128)S(1)} %get-tuple-element.26), channel_id=1, source_target_pairs={{0,16},{8,24},{16,0},{24,8},{1,17},{9,25},{17,1},{25,9},{2,18},{10... | collective-permute-start | bytes 491528 | tf_op jit(solution)/shard_map/ppermute | solution.py:41
  191.1 16.8 %collective-permute-start.12 = (f32[8,1280]{1,0:T(8,128)S(1)}, f32[8,1280]{1,0:T(8,128)S(1)}, u32[]{:S(2)}, u32[]{:S(2)}) collective-permute-start(f32[8,1280]{1,0:T(8,128)S(1)} %reduce_sum.9), channel_id=1, source_target_pairs={{0,64},{64,0},{128,192},{192,128},{256,320},{320,256},{384,448},{4... | collective-permute-start | bytes 122888 | tf_op jit(solution)/shard_map/ppermute | solution.py:63
  207.9 18.1 %collective-permute-start.13 = (f32[8,1280]{1,0:T(8,128)S(1)}, f32[8,1280]{1,0:T(8,128)S(1)}, u32[]{:S(2)}, u32[]{:S(2)}) collective-permute-start(f32[8,1280]{1,0:T(8,128)S(1)} %add.148), channel_id=1, source_target_pairs={{0,128},{64,192},{128,0},{192,64},{256,384},{320,448},{384,256},{4... | collective-permute-start | bytes 122888 | tf_op jit(solution)/shard_map/ppermute | solution.py:63
  226.0 6.3 %collective-permute-start.14 = (f32[8,1280]{1,0:T(8,128)S(1)}, f32[8,1280]{1,0:T(8,128)S(1)}, u32[]{:S(2)}, u32[]{:S(2)}) collective-permute-start(f32[8,1280]{1,0:T(8,128)S(1)} %add.149), channel_id=1, source_target_pairs={{0,256},{64,320},{128,384},{192,448},{256,0},{320,64},{384,128},{4... | collective-permute-start | bytes 122888 | tf_op jit(solution)/shard_map/ppermute | solution.py:63
  232.3 10.6 %collective-permute-start.15 = (f32[8,1280]{1,0:T(8,128)S(1)}, f32[8,1280]{1,0:T(8,128)S(1)}, u32[]{:S(2)}, u32[]{:S(2)}) collective-permute-start(f32[8,1280]{1,0:T(8,128)S(1)} %add.150), channel_id=1, source_target_pairs={{0,32},{32,0},{1,33},{33,1},{2,34},{34,2},{3,35},{35,3},{4,36},{36... | collective-permute-start | bytes 122888 | tf_op jit(solution)/shard_map/ppermute | solution.py:82

commit v4 on v3

--- a/solution.py
+++ b/solution.py
@@ -75,10 +75,13 @@
 
 
 def far_sum(term):
-    size = lax.axis_size("z_lo")
-    pieces = term.reshape(size, term.shape[0] // size, term.shape[1])
-    term = lax.all_to_all(pieces, "z_lo", 0, 0, tiled=True).sum(0)
-    term = everyone_sum(term, ("y", "z_hi"))
+    lo_size = lax.axis_size("z_lo")
+    hi_size = lax.axis_size("y") * lax.axis_size("z_hi")
+    rows = term.reshape(lo_size, hi_size, term.shape[1]).transpose(1, 0, 2)
+    rows = rows.reshape(hi_size * lo_size, 1, term.shape[1])
+    row = lax.all_to_all(rows, ("y", "z_hi", "z_lo"), 0, 0, tiled=True).sum(0)
+    spread = jnp.broadcast_to(row[None], (hi_size, *row.shape))
+    term = lax.all_to_all(spread, ("y", "z_hi"), 0, 0, tiled=True).reshape(hi_size, term.shape[1])
     other = lax.ppermute(term, "core", [(0, 1), (1, 0)])
     own_core = lax.axis_index("core")
     pair = jnp.stack([term, other])

time: 247 us -> 247 us (level)
  starting transfers between devices: 92.7 us -> 60.2 us
  blocking collectives: 32 us -> 56.2 us
  waiting for transfers between devices: 87.6 us -> 96.2 us
    ppermute x3 -> x0, starting transfers between devices: 36.6 us -> none  [everyone_sum(): lax.ppermute(total, axes, [(i, i ^ step) for i in range(size)])]
    all_to_all x1, blocking collectives: 32 us -> 56.2 us  [far_sum(): row = lax.all_to_all(rows, ('y', 'z_hi', 'z_lo'), 0, 0, tiled=True).sum(0)]
    all_to_all x0 -> x1, waiting for transfers between devices: none -> 12.7 us  [far_sum(): lax.all_to_all(spread, ('y', 'z_hi'), 0, 0, tiled=True)]
    all_to_all x0 -> x1, starting transfers between devices: none -> 6.88 us  [far_sum(): lax.all_to_all(spread, ('y', 'z_hi'), 0, 0, tiled=True)]
    ppermute x3 -> x0, waiting for transfers between devices: 3.41 us -> none  [everyone_sum(): lax.ppermute(total, axes, [(i, i ^ step) for i in range(size)])]
    ppermute x1, starting transfers between devices: 8.04 us -> 5.44 us  [far_sum(): other = lax.ppermute(term, 'core', [(0, 1), (1, 0)])]
  transfers between devices with their start and end apart: 16 -> 14, of which waited for: 11 -> 9; matrix products, arithmetic and copies ran while one was open for 5% -> 5% of each run, Pallas kernels for 0% -> 0%
where the time goes in v4:
time: 247 us; the launch traced here: 246 us
  waiting for transfers between devices  96.2 us (39%)
  starting transfers between devices  60.2 us (24%)
  blocking collectives  56.2 us (23%)
  matrix products  16.8 us (7%)
  local copies, waits for them, and re-layouts  10.6 us (4%)
  other arithmetic  4.86 us (2%)
    ppermute x4, waiting for transfers between devices, from_behind(): return lax.ppermute(array, axes, pairs)  74.6 us
    all_to_all x1, blocking collectives, far_sum(): row = lax.all_to_all(rows, ('y', 'z_hi', 'z_lo'), 0, 0, tiled=True).sum(0)  56.2 us
    ppermute x4, starting transfers between devices, from_behind(): return lax.ppermute(array, axes, pairs)  22.1 us
    ppermute x6, starting transfers between devices, scatter_sum(): lax.ppermute(piece, axes, [(i, (i + shift) % size) for i in range(size)])  21 us
    all_to_all x1, waiting for transfers between devices, far_sum(): lax.all_to_all(spread, ('y', 'z_hi'), 0, 0, tiled=True)  12.7 us
    ppermute x6, waiting for transfers between devices, scatter_sum(): lax.ppermute(piece, axes, [(i, (i + shift) % size) for i in range(size)])  8.91 us
    all_to_all x1, starting transfers between devices, far_sum(): lax.all_to_all(spread, ('y', 'z_hi'), 0, 0, tiled=True)  6.88 us
    ppermute x1, starting transfers between devices, far_sum(): other = lax.ppermute(term, 'core', [(0, 1), (1, 0)])  5.44 us
  transfers between devices with their start and end apart: 14, of which 9 were waited for; matrix products, arithmetic and copies ran while one was open for 5% of the time, Pallas kernels for 0%

profile of v4, /device:TPU:1, one launch (start us, length us, event | category | flops | bytes accessed | tf_op | source)
XLA Modules:
  0.0 246.4 jit_solution(2572239531708573130)
XLA Ops:
  0.6 4.5 %collective-permute-start = (bf16[1024,256]{1,0:T(8,128)(2,1)}, bf16[1024,256]{1,0:T(8,128)(2,1)S(1)}, u32[]{:S(2)}, u32[]{:S(2)}) collective-permute-start(bf16[1024,256]{1,0:T(8,128)(2,1)} %param.5), channel_id=1, source_target_pairs={{0,1},{1,2},{2,3},{3,4},{4,5},{5,6},{6,7},{7,8},{8,9},{9,10},{10,1... | collective-permute-start | bytes 1572872 | tf_op jit(solution)/shard_map/ppermute | solution.py:31
  5.2 1.6 fusion.14
  6.8 20.6 %collective-permute-done = bf16[1024,256]{1,0:T(8,128)(2,1)S(1)} collective-permute-done((bf16[1024,256]{1,0:T(8,128)(2,1)}, bf16[1024,256]{1,0:T(8,128)(2,1)S(1)}, u32[]{:S(2)}, u32[]{:S(2)}) %collective-permute-start) | collective-permute-done | bytes 524320 | tf_op jit(solution)/shard_map/ppermute | solution.py:31
  27.3 0.5 convolution_add_fusion.1
  27.8 0.3 copy-done.13
  28.1 0.4 multiply_convert_fusion.5
  28.5 0.8 copy-done
  29.3 0.4 fusion
  29.7 10.2 %collective-permute-start.1 = (bf16[1024,256]{1,0:T(8,128)(2,1)S(1)}, bf16[1024,256]{1,0:T(8,128)(2,1)}, u32[]{:S(2)}, u32[]{:S(2)}) collective-permute-start(bf16[1024,256]{1,0:T(8,128)(2,1)S(1)} %fusion), channel_id=1, source_target_pairs={{0,64},{32,96},{64,128},{96,160},{128,192},{160,224},{192,256},{22... | collective-permute-start | bytes 1572872 | tf_op jit(solution)/shard_map/ppermute | solution.py:31
  39.9 1.4 fusion.9
  41.3 37.4 %collective-permute-done.1 = bf16[1024,256]{1,0:T(8,128)(2,1)} collective-permute-done((bf16[1024,256]{1,0:T(8,128)(2,1)S(1)}, bf16[1024,256]{1,0:T(8,128)(2,1)}, u32[]{:S(2)}, u32[]{:S(2)}) %collective-permute-start.1) | collective-permute-done | bytes 524320 | tf_op jit(solution)/shard_map/ppermute | solution.py:31
  78.7 1.5 convolution_add_fusion
  80.3 0.8 multiply_convert_fusion.3
  81.1 0.3 fusion.52
  81.4 0.5 fusion.48
  81.9 0.1 copy-done.22
  82.0 0.2 copy-done.24
  82.2 1.5 fusion.49
  83.7 0.1 maximum_multiply_fusion
  83.9 1.8 mul.65
  85.7 3.1 %constant_dynamic-slice_fusion.3 = (f32[256,1,640]{2,1,0:T(1,128)S(1)}, f32[256,1,640]{2,1,0:T(1,128)S(1)}) fusion(f32[256,2,640]{2,1,0:T(2,128)} %mul.65, s32[]{:T(128)S(6)} %select_n.50, s32[]{:T(128)S(6)} %select_n.51), kind=kLoop, calls=%fused_computation.104 | loop fusion | bytes 2621448 | tf_op jit(solution)/shard_map/jit(dynamic_index_in_dim)/dynamic_slice | solution.py:71
  88.8 2.1 collective-permute-start.2
  90.9 1.8 convolution_convert_fusion.1
  92.7 1.4 collective-permute-start.6
  94.2 1.2 bitcast_add_fusion.1
  95.4 3.2 %collective-permute-start.3 = (f32[64,640]{1,0:T(8,128)S(1)}, f32[64,640]{1,0:T(8,128)S(1)}, u32[]{:S(2)}, u32[]{:S(2)}) collective-permute-start(f32[64,640]{1,0:T(8,128)S(1)} %get-tuple-element.27), channel_id=1, source_target_pairs={{0,8},{8,16},{16,24},{24,0},{1,9},{9,17},{17,25},{25,1},{2,10},{10... | collective-permute-start | bytes 491528 | tf_op jit(solution)/shard_map/ppermute | solution.py:41
  98.6 4.4 %collective-permute-start.4 = (f32[64,640]{1,0:T(8,128)S(1)}, f32[64,640]{1,0:T(8,128)S(1)}, u32[]{:S(2)}, u32[]{:S(2)}) collective-permute-start(f32[64,640]{1,0:T(8,128)S(1)} %get-tuple-element.29), channel_id=1, source_target_pairs={{0,16},{8,24},{16,0},{24,8},{1,17},{9,25},{17,1},{25,9},{2,18},{10... | collective-permute-start | bytes 491528 | tf_op jit(solution)/shard_map/ppermute | solution.py:41
  103.0 3.2 %collective-permute-start.5 = (f32[64,640]{1,0:T(8,128)S(1)}, f32[64,640]{1,0:T(8,128)S(1)}, u32[]{:S(2)}, u32[]{:S(2)}) collective-permute-start(f32[64,640]{1,0:T(8,128)S(1)} %get-tuple-element.28), channel_id=1, source_target_pairs={{0,24},{8,0},{16,8},{24,16},{1,25},{9,1},{17,9},{25,17},{2,26},{10... | collective-permute-start | bytes 491528 | tf_op jit(solution)/shard_map/ppermute | solution.py:41
  106.3 0.5 convolution_add_fusion.5
  106.8 2.1 collective-permute-done.4
  108.9 1.1 collective-permute-done.5
  110.0 0.7 fusion.31
  110.8 7.5 %collective-permute-done.6 = bf16[1024,256]{1,0:T(8,128)(2,1)S(1)} collective-permute-done((bf16[1024,256]{1,0:T(8,128)(2,1)S(1)}, bf16[1024,256]{1,0:T(8,128)(2,1)S(1)}, u32[]{:S(2)}, u32[]{:S(2)}) %collective-permute-start.6) | collective-permute-done | bytes 524320 | tf_op jit(solution)/shard_map/ppermute | solution.py:31
  118.2 0.1 add_convert_fusion.1
  118.4 0.7 multiply_convert_fusion.1
  119.2 0.4 copy-done.1
  119.6 0.3 fusion.53
  119.9 0.5 convolution_bitcast_fusion
  120.4 0.6 copy-done.14
  121.0 0.5 convolution_bitcast_fusion.1
  121.5 0.1 maximum_multiply_fusion.1
  121.7 0.7 mul.73
  122.4 1.1 constant_dynamic-slice_fusion.1
  123.6 2.7 %collective-permute-start.7 = (f32[256,640]{1,0:T(8,128)S(1)}, f32[256,640]{1,0:T(8,128)S(1)}, u32[]{:S(2)}, u32[]{:S(2)}) collective-permute-start(f32[256,640]{1,0:T(8,128)S(1)} %bitcast.127), channel_id=1, source_target_pairs={{0,32},{32,0},{1,33},{33,1},{2,34},{34,2},{3,35},{35,3},{4,36},{36... | collective-permute-start | bytes 1966088 | tf_op jit(solution)/shard_map/ppermute | solution.py:73
  126.3 0.5 convolution_convert_fusion
  126.9 6.0 %collective-permute-start.11 = (bf16[1024,256]{1,0:T(8,128)(2,1)S(1)}, bf16[1024,256]{1,0:T(8,128)(2,1)S(1)}, u32[]{:S(2)}, u32[]{:S(2)}) collective-permute-start(bf16[1024,256]{1,0:T(8,128)(2,1)S(1)} %convolution_convert_fusion), channel_id=1, source_target_pairs={{1,0},{2,1},{3,2},{4,3},{5,4},{6,5},{7,6},{8,7},{9,8},{10,9},{11,1... | collective-permute-start | bytes 1572872 | tf_op jit(solution)/shard_map/ppermute | solution.py:31
  133.0 4.6 %collective-permute-start.10 = (f32[64,640]{1,0:T(8,128)S(1)}, f32[64,640]{1,0:T(8,128)S(1)}, u32[]{:S(2)}, u32[]{:S(2)}) collective-permute-start(f32[64,640]{1,0:T(8,128)S(1)} %get-tuple-element.25), channel_id=1, source_target_pairs={{0,24},{8,0},{16,8},{24,16},{1,25},{9,1},{17,9},{25,17},{2,26},{10... | collective-permute-start | bytes 491528 | tf_op jit(solution)/shard_map/ppermute | solution.py:41
  137.7 1.9 collective-permute-start.8
  139.6 3.6 %collective-permute-start.9 = (f32[64,640]{1,0:T(8,128)S(1)}, f32[64,640]{1,0:T(8,128)S(1)}, u32[]{:S(2)}, u32[]{:S(2)}) collective-permute-start(f32[64,640]{1,0:T(8,128)S(1)} %get-tuple-element.26), channel_id=1, source_target_pairs={{0,16},{8,24},{16,0},{24,8},{1,17},{9,25},{17,1},{25,9},{2,18},{10... | collective-permute-start | bytes 491528 | tf_op jit(solution)/shard_map/ppermute | solution.py:41
  143.3 2.9 %collective-permute-done.8 = f32[64,640]{1,0:T(8,128)S(1)} collective-permute-done((f32[64,640]{1,0:T(8,128)S(1)}, f32[64,640]{1,0:T(8,128)S(1)}, u32[]{:S(2)}, u32[]{:S(2)}) %collective-permute-start.8) | collective-permute-done | bytes 163872 | tf_op jit(solution)/shard_map/ppermute | solution.py:41
  146.2 2.8 %collective-permute-done.9 = f32[64,640]{1,0:T(8,128)S(1)} collective-permute-done((f32[64,640]{1,0:T(8,128)S(1)}, f32[64,640]{1,0:T(8,128)S(1)}, u32[]{:S(2)}, u32[]{:S(2)}) %collective-permute-start.9) | collective-permute-done | bytes 163872 | tf_op jit(solution)/shard_map/ppermute | solution.py:41
  149.0 9.2 %collective-permute-done.11 = bf16[1024,256]{1,0:T(8,128)(2,1)S(1)} collective-permute-done((bf16[1024,256]{1,0:T(8,128)(2,1)S(1)}, bf16[1024,256]{1,0:T(8,128)(2,1)S(1)}, u32[]{:S(2)}, u32[]{:S(2)}) %collective-permute-start.11) | collective-permute-done | bytes 524320 | tf_op jit(solution)/shard_map/ppermute | solution.py:31
  158.3 0.3 copy.28
  158.7 56.2 %all_to_all.10 = f32[64,1,1280]{2,1,0:T(1,128)S(1)} all-to-all(f32[64,1,1280]{2,1,0:T(1,128)S(1)} %copy.28), channel_id=1, replica_groups=mesh['y'=4,'z_hi'=2,'core'=2,'x'=4,'z_lo'=8] {'y','z_hi','z_lo'}, dimensions={0} | all-to-all | bytes 655360 | tf_op jit(solution)/shard_map/all_to_all | solution.py:82
  214.9 0.2 reduce_sum.9
  215.1 0.6 broadcast_in_dim.2
  215.8 6.9 %all-to-all-start.1 = ((f32[8,1,1280]{2,1,0:T(1,128)}), f32[8,1,1280]{2,1,0:T(1,128)S(1)}, u32[]{:S(2)}, u32[]{:S(2)}) async-start(f32[8,1,1280]{2,1,0:T(1,128)} %broadcast_in_dim.2), calls=%async_computation.1 | async-start | bytes 81920 | tf_op jit(solution)/shard_map/all_to_all | solution.py:84
  222.7 1.1 fusion.1
  223.8 12.7 %all-to-all-done.1 = f32[8,1,1280]{2,1,0:T(1,128)S(1)} async-done(((f32[8,1,1280]{2,1,0:T(1,128)}), f32[8,1,1280]{2,1,0:T(1,128)S(1)}, u32[]{:S(2)}, u32[]{:S(2)}) %all-to-all-start.1) | async-done | bytes 40992 | tf_op jit(solution)/shard_map/all_to_all | solution.py:84
  236.5 5.4 %collective-permute-start.12 = (f32[8,1280]{1,0:T(8,128)S(1)}, f32[8,1280]{1,0:T(8,128)S(1)}, u32[]{:S(2)}, u32[]{:S(2)}) collective-permute-start(f32[8,1280]{1,0:T(8,128)S(1)} %bitcast.128), channel_id=1, source_target_pairs={{0,32},{32,0},{1,33},{33,1},{2,34},{34,2},{3,35},{35,3},{4,36},{36... | collective-permute-start | bytes 122888 | tf_op jit(solution)/shard_map/ppermute | solution.py:85
  242.0 2.5 %add_convert_fusion = bf16[1024,256]{1,0:T(8,128)(2,1)} fusion(bf16[1024,256]{1,0:T(8,128)(2,1)S(1)} %collective-permute-done.11, bf16[1024,256]{1,0:T(8,128)(2,1)S(1)} %copy-done.9, bf16[2,256,512]{2,1,0:T(8,128)(2,1)S(1)} %copy-done.18, bf16[1024,256]{0,1:T(8,128)(2,1)} %copy-done.28, bf16[1024,256]{0,1:T(8,128)(2,1)} %copy-done.26), kind=kOutput, calls=%fused_computation.26 | convolution fusion | flops 271843328 | bytes 2883584 | tf_op jit(solution)/shard_map/dot_general | solution.py:170
  244.5 0.6 pad_maximum_fusion.6
  245.1 0.6 pad_maximum_fusion.3
  245.8 0.6 pad_maximum_fusion.2
  (74 shorter events, 0.7 us)
Async XLA Ops:
  0.6 26.7 %copy-start.11 = (bf16[2,256,512]{2,1,0:T(8,128)(2,1)S(1)}, bf16[2,256,512]{2,1,0:T(8,128)(2,1)}, u32[]{:S(2)}) copy-start(bf16[2,256,512]{2,1,0:T(8,128)(2,1)} %param.6) | copy-start | bytes 1572868
  0.6 26.7 %collective-permute-start = (bf16[1024,256]{1,0:T(8,128)(2,1)}, bf16[1024,256]{1,0:T(8,128)(2,1)S(1)}, u32[]{:S(2)}, u32[]{:S(2)}) collective-permute-start(bf16[1024,256]{1,0:T(8,128)(2,1)} %param.5), channel_id=1, source_target_pairs={{0,1},{1,2},{2,3},{3,4},{4,5},{5,6},{6,7},{7,8},{8,9},{9,10},{10,1... | collective-permute-start | bytes 1572872 | tf_op jit(solution)/shard_map/ppermute | solution.py:31
  27.3 0.8 copy-start.13
  28.1 1.2 copy-start.6
  28.1 1.2 copy-start.19
  28.5 0.8 copy-start
  29.7 51.7 %copy-start.2 = (bf16[1024,256]{1,0:T(8,128)(2,1)}, bf16[1024,256]{1,0:T(8,128)(2,1)S(1)}, u32[]{:S(2)}) copy-start(bf16[1024,256]{1,0:T(8,128)(2,1)S(1)} %fusion) | copy-start | bytes 1572868
  29.7 49.0 %collective-permute-start.1 = (bf16[1024,256]{1,0:T(8,128)(2,1)S(1)}, bf16[1024,256]{1,0:T(8,128)(2,1)}, u32[]{:S(2)}, u32[]{:S(2)}) collective-permute-start(bf16[1024,256]{1,0:T(8,128)(2,1)S(1)} %fusion), channel_id=1, source_target_pairs={{0,64},{32,96},{64,128},{96,160},{128,192},{160,224},{192,256},{22... | collective-permute-start | bytes 1572872 | tf_op jit(solution)/shard_map/ppermute | solution.py:31
  41.3 39.0 %copy-start.15 = (bf16[1024,256]{1,0:T(8,128)(2,1)S(1)}, bf16[1024,256]{1,0:T(8,128)(2,1)}, u32[]{:S(2)}) copy-start(bf16[1024,256]{1,0:T(8,128)(2,1)} %param.9) | copy-start | bytes 1572868
  81.1 0.8 copy-start.4
  81.1 1.0 copy-start.22
  81.1 1.1 copy-start.24
  88.8 5.4 %collective-permute-start.2 = (f32[256,640]{1,0:T(8,128)S(1)}, f32[256,640]{1,0:T(8,128)}, u32[]{:S(2)}, u32[]{:S(2)}) collective-permute-start(f32[256,640]{1,0:T(8,128)S(1)} %bitcast.126), channel_id=1, source_target_pairs={{0,32},{32,0},{1,33},{33,1},{2,34},{34,2},{3,35},{35,3},{4,36},{36... | collective-permute-start | bytes 1966088 | tf_op jit(solution)/shard_map/ppermute | solution.py:73
  92.7 13.5 %copy-start.16 = (bf16[1024,256]{1,0:T(8,128)(2,1)S(1)}, bf16[1024,256]{1,0:T(8,128)(2,1)}, u32[]{:S(2)}) copy-start(bf16[1024,256]{1,0:T(8,128)(2,1)} %param.9) | copy-start | bytes 1572868
  92.7 13.5 %copy-start.17 = (bf16[2,256,512]{2,1,0:T(8,128)(2,1)S(1)}, bf16[2,256,512]{2,1,0:T(8,128)(2,1)}, u32[]{:S(2)}) copy-start(bf16[2,256,512]{2,1,0:T(8,128)(2,1)} %param.7) | copy-start | bytes 1572868
  92.7 13.5 %copy-start.23 = (bf16[1024,256]{0,1:T(8,128)(2,1)S(1)}, bf16[1024,256]{0,1:T(8,128)(2,1)}, u32[]{:S(2)}) copy-start(bf16[1024,256]{0,1:T(8,128)(2,1)} %copy-done.22) | copy-start | bytes 1572868
  92.7 13.5 %copy-start.25 = (bf16[1024,256]{0,1:T(8,128)(2,1)S(1)}, bf16[1024,256]{0,1:T(8,128)(2,1)}, u32[]{:S(2)}) copy-start(bf16[1024,256]{0,1:T(8,128)(2,1)} %copy-done.24) | copy-start | bytes 1572868
  92.7 25.5 %collective-permute-start.6 = (bf16[1024,256]{1,0:T(8,128)(2,1)S(1)}, bf16[1024,256]{1,0:T(8,128)(2,1)S(1)}, u32[]{:S(2)}, u32[]{:S(2)}) collective-permute-start(bf16[1024,256]{1,0:T(8,128)(2,1)S(1)} %convolution_convert_fusion.1), channel_id=1, source_target_pairs={{64,0},{96,32},{128,64},{160,96},{192,128},{224,160},{256,192},{28... | collective-permute-start | bytes 1572872 | tf_op jit(solution)/shard_map/ppermute | solution.py:31
  95.4 11.4 %collective-permute-start.3 = (f32[64,640]{1,0:T(8,128)S(1)}, f32[64,640]{1,0:T(8,128)S(1)}, u32[]{:S(2)}, u32[]{:S(2)}) collective-permute-start(f32[64,640]{1,0:T(8,128)S(1)} %get-tuple-element.27), channel_id=1, source_target_pairs={{0,8},{8,16},{16,24},{24,0},{1,9},{9,17},{17,25},{25,1},{2,10},{10... | collective-permute-start | bytes 491528 | tf_op jit(solution)/shard_map/ppermute | solution.py:41
  98.6 10.3 %collective-permute-start.4 = (f32[64,640]{1,0:T(8,128)S(1)}, f32[64,640]{1,0:T(8,128)S(1)}, u32[]{:S(2)}, u32[]{:S(2)}) collective-permute-start(f32[64,640]{1,0:T(8,128)S(1)} %get-tuple-element.29), channel_id=1, source_target_pairs={{0,16},{8,24},{16,0},{24,8},{1,17},{9,25},{17,1},{25,9},{2,18},{10... | collective-permute-start | bytes 491528 | tf_op jit(solution)/shard_map/ppermute | solution.py:41
  103.0 7.1 %collective-permute-start.5 = (f32[64,640]{1,0:T(8,128)S(1)}, f32[64,640]{1,0:T(8,128)S(1)}, u32[]{:S(2)}, u32[]{:S(2)}) collective-permute-start(f32[64,640]{1,0:T(8,128)S(1)} %get-tuple-element.28), channel_id=1, source_target_pairs={{0,24},{8,0},{16,8},{24,16},{1,25},{9,1},{17,9},{25,17},{2,26},{10... | collective-permute-start | bytes 491528 | tf_op jit(solution)/shard_map/ppermute | solution.py:41
  106.8 11.6 %copy-start.20 = (bf16[2,256,256]{2,1,0:T(8,128)(2,1)S(1)}, bf16[2,256,256]{2,1,0:T(8,128)(2,1)}, u32[]{:S(2)}) copy-start(bf16[2,256,256]{2,1,0:T(8,128)(2,1)} %param.8) | copy-start | bytes 786436
  118.4 0.8 copy-start.8
  118.4 1.2 copy-start.1
  118.4 1.5 copy-start.7
  119.6 0.8 copy-start.26
  119.6 1.9 copy-start.28
  119.6 1.4 copy-start.14
  122.4 3.9 %copy-start.12 = (bf16[2,256,512]{2,1,0:T(8,128)(2,1)S(1)}, bf16[2,256,512]{2,1,0:T(8,128)(2,1)}, u32[]{:S(2)}) copy-start(bf16[2,256,512]{2,1,0:T(8,128)(2,1)} %param.6) | copy-start | bytes 1572868
  122.4 3.9 %copy-start.27 = (bf16[1024,256]{0,1:T(8,128)(2,1)S(1)}, bf16[1024,256]{0,1:T(8,128)(2,1)}, u32[]{:S(2)}) copy-start(bf16[1024,256]{0,1:T(8,128)(2,1)} %copy-done.26) | copy-start | bytes 1572868
  122.4 3.9 %copy-start.29 = (bf16[1024,256]{0,1:T(8,128)(2,1)S(1)}, bf16[1024,256]{0,1:T(8,128)(2,1)}, u32[]{:S(2)}) copy-start(bf16[1024,256]{0,1:T(8,128)(2,1)} %copy-done.28) | copy-start | bytes 1572868
  123.6 9.3 %collective-permute-start.7 = (f32[256,640]{1,0:T(8,128)S(1)}, f32[256,640]{1,0:T(8,128)S(1)}, u32[]{:S(2)}, u32[]{:S(2)}) collective-permute-start(f32[256,640]{1,0:T(8,128)S(1)} %bitcast.127), channel_id=1, source_target_pairs={{0,32},{32,0},{1,33},{33,1},{2,34},{34,2},{3,35},{35,3},{4,36},{36... | collective-permute-start | bytes 1966088 | tf_op jit(solution)/shard_map/ppermute | solution.py:73
  126.8 31.3 %copy-start.10 = (f32[64,640]{1,0:T(8,128)S(1)}, f32[64,640]{1,0:T(8,128)}, u32[]{:S(2)}) copy-start(f32[64,640]{1,0:T(8,128)} %fusion.31) | copy-start | bytes 491524
  126.9 31.3 %collective-permute-start.11 = (bf16[1024,256]{1,0:T(8,128)(2,1)S(1)}, bf16[1024,256]{1,0:T(8,128)(2,1)S(1)}, u32[]{:S(2)}, u32[]{:S(2)}) collective-permute-start(bf16[1024,256]{1,0:T(8,128)(2,1)S(1)} %convolution_convert_fusion), channel_id=1, source_target_pairs={{1,0},{2,1},{3,2},{4,3},{5,4},{6,5},{7,6},{8,7},{9,8},{10,9},{11,1... | collective-permute-start | bytes 1572872 | tf_op jit(solution)/shard_map/ppermute | solution.py:31
  133.0 89.7 %copy-start.3 = (bf16[1024,256]{1,0:T(8,128)(2,1)S(1)}, bf16[1024,256]{1,0:T(8,128)(2,1)}, u32[]{:S(2)}) copy-start(bf16[1024,256]{1,0:T(8,128)(2,1)} %copy-done.2) | copy-start | bytes 1572868
  133.0 89.6 %copy-start.5 = (bf16[1024,256]{0,1:T(8,128)(2,1)S(1)}, bf16[1024,256]{0,1:T(8,128)(2,1)}, u32[]{:S(2)}) copy-start(bf16[1024,256]{0,1:T(8,128)(2,1)} %copy-done.4) | copy-start | bytes 1572868
  133.0 89.6 %copy-start.21 = (bf16[2,256,256]{2,1,0:T(8,128)(2,1)S(1)}, bf16[2,256,256]{2,1,0:T(8,128)(2,1)}, u32[]{:S(2)}) copy-start(bf16[2,256,256]{2,1,0:T(8,128)(2,1)} %param.8) | copy-start | bytes 786436
  133.0 10.2 %collective-permute-start.10 = (f32[64,640]{1,0:T(8,128)S(1)}, f32[64,640]{1,0:T(8,128)S(1)}, u32[]{:S(2)}, u32[]{:S(2)}) collective-permute-start(f32[64,640]{1,0:T(8,128)S(1)} %get-tuple-element.25), channel_id=1, source_target_pairs={{0,24},{8,0},{16,8},{24,16},{1,25},{9,1},{17,9},{25,17},{2,26},{10... | collective-permute-start | bytes 491528 | tf_op jit(solution)/shard_map/ppermute | solution.py:41
  137.7 8.5 %collective-permute-start.8 = (f32[64,640]{1,0:T(8,128)S(1)}, f32[64,640]{1,0:T(8,128)S(1)}, u32[]{:S(2)}, u32[]{:S(2)}) collective-permute-start(f32[64,640]{1,0:T(8,128)S(1)} %get-tuple-element.24), channel_id=1, source_target_pairs={{0,8},{8,16},{16,24},{24,0},{1,9},{9,17},{17,25},{25,1},{2,10},{10... | collective-permute-start | bytes 491528 | tf_op jit(solution)/shard_map/ppermute | solution.py:41
  139.6 9.3 %collective-permute-start.9 = (f32[64,640]{1,0:T(8,128)S(1)}, f32[64,640]{1,0:T(8,128)S(1)}, u32[]{:S(2)}, u32[]{:S(2)}) collective-permute-start(f32[64,640]{1,0:T(8,128)S(1)} %get-tuple-element.26), channel_id=1, source_target_pairs={{0,16},{8,24},{16,0},{24,8},{1,17},{9,25},{17,1},{25,9},{2,18},{10... | collective-permute-start | bytes 491528 | tf_op jit(solution)/shard_map/ppermute | solution.py:41
  158.2 83.8 %copy-start.9 = (bf16[1024,256]{1,0:T(8,128)(2,1)S(1)}, bf16[1024,256]{1,0:T(8,128)(2,1)}, u32[]{:S(2)}) copy-start(bf16[1024,256]{1,0:T(8,128)(2,1)} %copy-done.8) | copy-start | bytes 1572868
  158.2 83.8 %copy-start.18 = (bf16[2,256,512]{2,1,0:T(8,128)(2,1)S(1)}, bf16[2,256,512]{2,1,0:T(8,128)(2,1)}, u32[]{:S(2)}) copy-start(bf16[2,256,512]{2,1,0:T(8,128)(2,1)} %param.7) | copy-start | bytes 1572868
  215.8 20.7 %all-to-all-start.1 = ((f32[8,1,1280]{2,1,0:T(1,128)}), f32[8,1,1280]{2,1,0:T(1,128)S(1)}, u32[]{:S(2)}, u32[]{:S(2)}) async-start(f32[8,1,1280]{2,1,0:T(1,128)} %broadcast_in_dim.2), calls=%async_computation.1 | async-start | bytes 81920 | tf_op jit(solution)/shard_map/all_to_all | solution.py:84
  236.5 8.0 %collective-permute-start.12 = (f32[8,1280]{1,0:T(8,128)S(1)}, f32[8,1280]{1,0:T(8,128)S(1)}, u32[]{:S(2)}, u32[]{:S(2)}) collective-permute-start(f32[8,1280]{1,0:T(8,128)S(1)} %bitcast.128), channel_id=1, source_target_pairs={{0,32},{32,0},{1,33},{33,1},{2,34},{34,2},{3,35},{35,3},{4,36},{36... | collective-permute-start | bytes 122888 | tf_op jit(solution)/shard_map/ppermute | solution.py:85

commit v5 on v4

--- a/solution.py
+++ b/solution.py
@@ -38,7 +38,8 @@
     summed = lax.dynamic_index_in_dim(pieces, own, 0, keepdims=False)
     for shift in range(1, size):
         piece = lax.dynamic_index_in_dim(pieces, (own + shift) % size, 0, keepdims=False)
-        summed = summed + lax.ppermute(piece, axes, [(i, (i + shift) % size) for i in range(size)])
+        moved = lax.ppermute(piece.astype(jnp.bfloat16), axes, [(i, (i + shift) % size) for i in range(size)])
+        summed = summed + moved.astype(jnp.float32)
     return summed
 
 
@@ -70,8 +71,8 @@
     halves = term.reshape(term.shape[0], 2, term.shape[1] // 2)
     kept = lax.dynamic_index_in_dim(halves, own_core, 1, keepdims=False)
     given = lax.dynamic_index_in_dim(halves, 1 - own_core, 1, keepdims=False)
-    term = kept + lax.ppermute(given, "core", [(0, 1), (1, 0)])
-    return scatter_sum(term, ("x",))
+    moved = lax.ppermute(given.astype(jnp.bfloat16), "core", [(0, 1), (1, 0)])
+    return scatter_sum(kept + moved.astype(jnp.float32), ("x",))
 
 
 def far_sum(term):
@@ -79,7 +80,8 @@
     hi_size = lax.axis_size("y") * lax.axis_size("z_hi")
     rows = term.reshape(lo_size, hi_size, term.shape[1]).transpose(1, 0, 2)
     rows = rows.reshape(hi_size * lo_size, 1, term.shape[1])
-    row = lax.all_to_all(rows, ("y", "z_hi", "z_lo"), 0, 0, tiled=True).sum(0)
+    row = lax.all_to_all(rows.astype(jnp.bfloat16), ("y", "z_hi", "z_lo"), 0, 0, tiled=True)
+    row = row.astype(jnp.float32).sum(0)
     spread = jnp.broadcast_to(row[None], (hi_size, *row.shape))
     term = lax.all_to_all(spread, ("y", "z_hi"), 0, 0, tiled=True).reshape(hi_size, term.shape[1])
     other = lax.ppermute(term, "core", [(0, 1), (1, 0)])
@@ -166,7 +168,8 @@
         arrived = return_past(sent_back, layer_at)
         operands = (earlier, current, gated_out, grad_preact, upstream)
         near_list[layer_at] = near_sum(layer_term(operands, grad_scale))
-        near_list, arrived = lax.optimization_barrier((near_list, arrived))
+        if layer_at > 0:
+            near_list, arrived = lax.optimization_barrier((near_list, arrived))
         local_grad = upstream.astype(jnp.float32) + jnp.dot(
             grad_preact, conv_now[layer_at].T, preferred_element_type=jnp.float32
         )

time: 247 us -> 228 us (0.923)
  blocking collectives: 56.2 us -> 0 us
  starting transfers between devices: 60.2 us -> 106 us
  waiting for transfers between devices: 96.2 us -> 87.3 us
    all_to_all x1 -> x0, blocking collectives: 56.2 us -> none  [far_sum(): row = lax.all_to_all(rows, ('y', 'z_hi', 'z_lo'), 0, 0, tiled=True).sum(0)]
    all_to_all x0 -> x1, starting transfers between devices: none -> 41 us  [far_sum(): lax.all_to_all(rows.astype(jnp.bfloat16), ('y', 'z_hi', 'z_lo'), 0, 0, ti...]
    ppermute x4, waiting for transfers between devices: 74.6 us -> 68.2 us  [from_behind(): return lax.ppermute(array, axes, pairs)]
    ppermute x4, starting transfers between devices: 22.1 us -> 27.6 us  [from_behind(): return lax.ppermute(array, axes, pairs)]
    dynamic_slice x2, local copies, waits for them, and re-layouts: 4.19 us -> 1.13 us  [near_sum(): kept = lax.dynamic_index_in_dim(halves, own_core, 1, keepdims=False)]
    ppermute x8, waiting for transfers between devices: 8.92 us -> 6.14 us  [the longest x6 5.67 us: scatter_sum(): lax.ppermute(piece.astype(jnp.bfloat16), axes, [(i, (i + shift) % size) f...]
  transfers between devices with their start and end apart: 14 -> 15, of which waited for: 9 -> 8; matrix products, arithmetic and copies ran while one was open for 5% -> 6% of each run, Pallas kernels for 0% -> 0%
where the time goes in v5:
time: 228 us; the launch traced here: 227 us
  starting transfers between devices  106 us (46%)
  waiting for transfers between devices  87.3 us (38%)
  matrix products  17.6 us (8%)
  local copies, waits for them, and re-layouts  9.47 us (4%)
  other arithmetic  4.96 us (2%)
    ppermute x4, waiting for transfers between devices, from_behind(): return lax.ppermute(array, axes, pairs)  68.2 us
    all_to_all x1, starting transfers between devices, far_sum(): lax.all_to_all(rows.astype(jnp.bfloat16), ('y', 'z_hi', 'z_lo'), 0, 0, ti...  41 us
    ppermute x4, starting transfers between devices, from_behind(): return lax.ppermute(array, axes, pairs)  27.6 us
    ppermute x6, starting transfers between devices, scatter_sum(): lax.ppermute(piece.astype(jnp.bfloat16), axes, [(i, (i + shift) % size) f...  20.7 us
    all_to_all x1, waiting for transfers between devices, far_sum(): lax.all_to_all(spread, ('y', 'z_hi'), 0, 0, tiled=True)  12.8 us
    all_to_all x1, starting transfers between devices, far_sum(): lax.all_to_all(spread, ('y', 'z_hi'), 0, 0, tiled=True)  6.2 us
    ppermute x1, starting transfers between devices, far_sum(): other = lax.ppermute(term, 'core', [(0, 1), (1, 0)])  5.97 us
    ppermute x6, waiting for transfers between devices, scatter_sum(): lax.ppermute(piece.astype(jnp.bfloat16), axes, [(i, (i + shift) % size) f...  5.67 us
  transfers between devices with their start and end apart: 15, of which 8 were waited for; matrix products, arithmetic and copies ran while one was open for 6% of the time, Pallas kernels for 0%

profile of v5, /device:TPU:1, one launch (start us, length us, event | category | flops | bytes accessed | tf_op | source)
XLA Modules:
  0.0 227.1 jit_solution(4619315852986312054)
XLA Ops:
  0.6 4.5 %collective-permute-start = (bf16[1024,256]{1,0:T(8,128)(2,1)}, bf16[1024,256]{1,0:T(8,128)(2,1)S(1)}, u32[]{:S(2)}, u32[]{:S(2)}) collective-permute-start(bf16[1024,256]{1,0:T(8,128)(2,1)} %param.5), channel_id=1, source_target_pairs={{0,1},{1,2},{2,3},{3,4},{4,5},{5,6},{6,7},{7,8},{8,9},{9,10},{10,1... | collective-permute-start | bytes 1572872 | tf_op jit(solution)/shard_map/ppermute | solution.py:31
  5.2 1.6 fusion.16
  6.8 20.6 %collective-permute-done = bf16[1024,256]{1,0:T(8,128)(2,1)S(1)} collective-permute-done((bf16[1024,256]{1,0:T(8,128)(2,1)}, bf16[1024,256]{1,0:T(8,128)(2,1)S(1)}, u32[]{:S(2)}, u32[]{:S(2)}) %collective-permute-start) | collective-permute-done | bytes 524320 | tf_op jit(solution)/shard_map/ppermute | solution.py:31
  27.3 0.5 convolution_add_fusion.1
  27.8 0.3 copy-done.11
  28.1 0.4 multiply_convert_fusion.5
  28.5 0.8 copy-done
  29.3 0.4 fusion
  29.7 10.2 %collective-permute-start.1 = (bf16[1024,256]{1,0:T(8,128)(2,1)S(1)}, bf16[1024,256]{1,0:T(8,128)(2,1)}, u32[]{:S(2)}, u32[]{:S(2)}) collective-permute-start(bf16[1024,256]{1,0:T(8,128)(2,1)S(1)} %fusion), channel_id=1, source_target_pairs={{0,64},{32,96},{64,128},{96,160},{128,192},{160,224},{192,256},{22... | collective-permute-start | bytes 1572872 | tf_op jit(solution)/shard_map/ppermute | solution.py:31
  39.9 1.4 fusion.11
  41.3 37.4 %collective-permute-done.1 = bf16[1024,256]{1,0:T(8,128)(2,1)} collective-permute-done((bf16[1024,256]{1,0:T(8,128)(2,1)S(1)}, bf16[1024,256]{1,0:T(8,128)(2,1)}, u32[]{:S(2)}, u32[]{:S(2)}) %collective-permute-start.1) | collective-permute-done | bytes 524320 | tf_op jit(solution)/shard_map/ppermute | solution.py:31
  78.7 1.5 convolution_add_fusion
  80.3 0.8 multiply_convert_fusion.3
  81.1 0.3 fusion.59
  81.4 0.5 fusion.55
  81.9 0.1 copy-done.21
  82.0 1.5 fusion.56
  83.6 1.2 maximum_multiply_fusion
  84.8 2.0 mul.65
  86.8 0.6 constant_dynamic-slice_fusion.2
  87.5 2.1 collective-permute-start.2
  89.6 0.5 convolution_convert_fusion.1
  90.1 1.4 collective-permute-start.6
  91.6 0.6 constant_dynamic-slice_fusion.3
  92.3 3.2 %collective-permute-start.3 = (bf16[64,640]{1,0:T(8,128)(2,1)S(1)}, bf16[64,640]{1,0:T(8,128)(2,1)S(1)}, u32[]{:S(2)}, u32[]{:S(2)}) collective-permute-start(bf16[64,640]{1,0:T(8,128)(2,1)S(1)} %get-tuple-element.17), channel_id=1, source_target_pairs={{0,8},{8,16},{16,24},{24,0},{1,9},{9,17},{17,25},{25,1},{2,10},{10... | collective-permute-start | bytes 245768 | tf_op jit(solution)/shard_map/ppermute | solution.py:41
  95.5 4.4 %collective-permute-start.4 = (bf16[64,640]{1,0:T(8,128)(2,1)S(1)}, bf16[64,640]{1,0:T(8,128)(2,1)S(1)}, u32[]{:S(2)}, u32[]{:S(2)}) collective-permute-start(bf16[64,640]{1,0:T(8,128)(2,1)S(1)} %get-tuple-element.19), channel_id=1, source_target_pairs={{0,16},{8,24},{16,0},{24,8},{1,17},{9,25},{17,1},{25,9},{2,18},{10... | collective-permute-start | bytes 245768 | tf_op jit(solution)/shard_map/ppermute | solution.py:41
  99.9 3.1 %collective-permute-start.5 = (bf16[64,640]{1,0:T(8,128)(2,1)S(1)}, bf16[64,640]{1,0:T(8,128)(2,1)S(1)}, u32[]{:S(2)}, u32[]{:S(2)}) collective-permute-start(bf16[64,640]{1,0:T(8,128)(2,1)S(1)} %get-tuple-element.18), channel_id=1, source_target_pairs={{0,24},{8,0},{16,8},{24,16},{1,25},{9,1},{17,9},{25,17},{2,26},{10... | collective-permute-start | bytes 245768 | tf_op jit(solution)/shard_map/ppermute | solution.py:41
  103.0 0.5 convolution_add_fusion.5
  103.5 1.8 collective-permute-done.5
  105.4 10.3 %collective-permute-done.6 = bf16[1024,256]{1,0:T(8,128)(2,1)S(1)} collective-permute-done((bf16[1024,256]{1,0:T(8,128)(2,1)S(1)}, bf16[1024,256]{1,0:T(8,128)(2,1)S(1)}, u32[]{:S(2)}, u32[]{:S(2)}) %collective-permute-start.6) | collective-permute-done | bytes 524320 | tf_op jit(solution)/shard_map/ppermute | solution.py:31
  115.6 0.1 add_convert_fusion.1
  115.8 0.7 multiply_convert_fusion.1
  116.5 0.3 copy-done.1
  116.8 0.3 fusion.60
  117.1 0.5 convolution_bitcast_fusion
  117.6 0.2 copy-done.24
  117.8 0.5 copy-done.12
  118.3 0.5 convolution_bitcast_fusion.1
  118.9 0.7 mul.73
  119.6 0.6 constant_dynamic-slice_fusion
  120.2 2.9 %collective-permute-start.8 = (bf16[256,640]{1,0:T(8,128)(2,1)S(1)}, bf16[256,640]{1,0:T(8,128)(2,1)S(1)}, u32[]{:S(2)}, u32[]{:S(2)}) collective-permute-start(bf16[256,640]{1,0:T(8,128)(2,1)S(1)} %bitcast.127), channel_id=1, source_target_pairs={{0,32},{32,0},{1,33},{33,1},{2,34},{34,2},{3,35},{35,3},{4,36},{36... | collective-permute-start | bytes 983048 | tf_op jit(solution)/shard_map/ppermute | solution.py:74
  123.1 0.6 constant_dynamic-slice_fusion.1
  123.7 0.5 collective-permute-done.8
  124.3 4.8 %collective-permute-start.10 = (bf16[64,640]{1,0:T(8,128)(2,1)S(1)}, bf16[64,640]{1,0:T(8,128)(2,1)S(1)}, u32[]{:S(2)}, u32[]{:S(2)}) collective-permute-start(bf16[64,640]{1,0:T(8,128)(2,1)S(1)} %get-tuple-element.16), channel_id=1, source_target_pairs={{0,16},{8,24},{16,0},{24,8},{1,17},{9,25},{17,1},{25,9},{2,18},{10... | collective-permute-start | bytes 245768 | tf_op jit(solution)/shard_map/ppermute | solution.py:41
  129.1 2.7 %collective-permute-start.11 = (bf16[64,640]{1,0:T(8,128)(2,1)S(1)}, bf16[64,640]{1,0:T(8,128)(2,1)S(1)}, u32[]{:S(2)}, u32[]{:S(2)}) collective-permute-start(bf16[64,640]{1,0:T(8,128)(2,1)S(1)} %get-tuple-element.15), channel_id=1, source_target_pairs={{0,24},{8,0},{16,8},{24,16},{1,25},{9,1},{17,9},{25,17},{2,26},{10... | collective-permute-start | bytes 245768 | tf_op jit(solution)/shard_map/ppermute | solution.py:41
  131.8 2.5 %collective-permute-start.9 = (bf16[64,640]{1,0:T(8,128)(2,1)S(1)}, bf16[64,640]{1,0:T(8,128)(2,1)S(1)}, u32[]{:S(2)}, u32[]{:S(2)}) collective-permute-start(bf16[64,640]{1,0:T(8,128)(2,1)S(1)} %get-tuple-element.14), channel_id=1, source_target_pairs={{0,8},{8,16},{16,24},{24,0},{1,9},{9,17},{17,25},{25,1},{2,10},{10... | collective-permute-start | bytes 245768 | tf_op jit(solution)/shard_map/ppermute | solution.py:41
  134.4 3.8 %collective-permute-done.9 = bf16[64,640]{1,0:T(8,128)(2,1)S(1)} collective-permute-done((bf16[64,640]{1,0:T(8,128)(2,1)S(1)}, bf16[64,640]{1,0:T(8,128)(2,1)S(1)}, u32[]{:S(2)}, u32[]{:S(2)}) %collective-permute-start.9) | collective-permute-done | bytes 81952 | tf_op jit(solution)/shard_map/ppermute | solution.py:41
  138.3 0.5 broadcast.38
  138.8 0.7 reduce.1
  139.5 0.7 reshape.59
  140.2 41.0 %all-to-all-start = ((bf16[64,2,640]{2,1,0:T(2,128)(2,1)}), bf16[64,2,640]{2,1,0:T(2,128)(2,1)S(1)}, u32[]{:S(2)}, u32[]{:S(2)}) async-start(bf16[64,2,640]{2,1,0:T(2,128)(2,1)} %reshape.59), calls=%async_computation | async-start | bytes 327680 | tf_op jit(solution)/shard_map/all_to_all | solution.py:83
  181.2 2.6 %convolution_convert_fusion = bf16[1024,256]{1,0:T(8,128)(2,1)} fusion(bf16[2,256,512]{2,1,0:T(8,128)(2,1)S(1)} %copy-done.10, bf16[1024,256]{0,1:T(8,128)(2,1)} %copy-done.24, bf16[1024,256]{0,1:T(8,128)(2,1)} %copy-done.23), kind=kOutput, calls=%fused_computation.8 | convolution fusion | flops 270794752 | bytes 1835008 | tf_op jit(solution)/shard_map/dot_general | solution.py:165
  183.8 11.5 %collective-permute-start.7 = (bf16[1024,256]{1,0:T(8,128)(2,1)}, bf16[1024,256]{1,0:T(8,128)(2,1)S(1)}, u32[]{:S(2)}, u32[]{:S(2)}) collective-permute-start(bf16[1024,256]{1,0:T(8,128)(2,1)} %convolution_convert_fusion), channel_id=1, source_target_pairs={{1,0},{2,1},{3,2},{4,3},{5,4},{6,5},{7,6},{8,7},{9,8},{10,9},{11,1... | collective-permute-start | bytes 1572872 | tf_op jit(solution)/shard_map/ppermute | solution.py:31
  195.3 0.2 all-to-all-done
  195.6 0.3 convert_reduce_fusion
  195.9 0.6 broadcast_in_dim.2
  196.6 6.2 %all-to-all-start.1 = ((f32[8,1,1280]{2,1,0:T(1,128)}), f32[8,1,1280]{2,1,0:T(1,128)S(1)}, u32[]{:S(2)}, u32[]{:S(2)}) async-start(f32[8,1,1280]{2,1,0:T(1,128)} %broadcast_in_dim.2), calls=%async_computation.1 | async-start | bytes 81920 | tf_op jit(solution)/shard_map/all_to_all | solution.py:86
  202.8 1.1 fusion.1
  203.9 12.8 %all-to-all-done.1 = f32[8,1,1280]{2,1,0:T(1,128)S(1)} async-done(((f32[8,1,1280]{2,1,0:T(1,128)}), f32[8,1,1280]{2,1,0:T(1,128)S(1)}, u32[]{:S(2)}, u32[]{:S(2)}) %all-to-all-start.1) | async-done | bytes 40992 | tf_op jit(solution)/shard_map/all_to_all | solution.py:86
  216.7 6.0 %collective-permute-start.12 = (f32[8,1280]{1,0:T(8,128)S(1)}, f32[8,1280]{1,0:T(8,128)S(1)}, u32[]{:S(2)}, u32[]{:S(2)}) collective-permute-start(f32[8,1280]{1,0:T(8,128)S(1)} %bitcast.128), channel_id=1, source_target_pairs={{0,32},{32,0},{1,33},{33,1},{2,34},{34,2},{3,35},{35,3},{4,36},{36... | collective-permute-start | bytes 122888 | tf_op jit(solution)/shard_map/ppermute | solution.py:87
  222.7 2.5 %add_convert_fusion = bf16[1024,256]{1,0:T(8,128)(2,1)} fusion(bf16[1024,256]{1,0:T(8,128)(2,1)S(1)} %collective-permute-done.7, bf16[1024,256]{1,0:T(8,128)(2,1)S(1)} %add_convert_fusion.1, bf16[2,256,512]{2,1,0:T(8,128)(2,1)S(1)} %copy-done.16, bf16[1024,256]{0,1:T(8,128)(2,1)} %copy-done.24, bf16[1024,256]{0,1:T(8,128)(2,1)} %copy-done.23), kind=kOutput, calls=%fused_computation.26 | convolution fusion | flops 271843328 | bytes 2883584 | tf_op jit(solution)/shard_map/dot_general | solution.py:173
  225.2 0.6 pad_maximum_fusion.6
  225.9 0.6 pad_maximum_fusion.3
  226.5 0.6 pad_maximum_fusion.2
  (70 shorter events, 0.8 us)
Async XLA Ops:
  0.6 26.7 %copy-start.8 = (bf16[2,256,512]{2,1,0:T(8,128)(2,1)S(1)}, bf16[2,256,512]{2,1,0:T(8,128)(2,1)}, u32[]{:S(2)}) copy-start(bf16[2,256,512]{2,1,0:T(8,128)(2,1)} %param.6) | copy-start | bytes 1572868
  0.6 26.7 %collective-permute-start = (bf16[1024,256]{1,0:T(8,128)(2,1)}, bf16[1024,256]{1,0:T(8,128)(2,1)S(1)}, u32[]{:S(2)}, u32[]{:S(2)}) collective-permute-start(bf16[1024,256]{1,0:T(8,128)(2,1)} %param.5), channel_id=1, source_target_pairs={{0,1},{1,2},{2,3},{3,4},{4,5},{5,6},{6,7},{7,8},{8,9},{9,10},{10,1... | collective-permute-start | bytes 1572872 | tf_op jit(solution)/shard_map/ppermute | solution.py:31
  27.3 0.8 copy-start.11
  28.1 1.2 copy-start.6
  28.1 1.2 copy-start.17
  28.5 0.8 copy-start
  29.7 51.7 %copy-start.2 = (bf16[1024,256]{1,0:T(8,128)(2,1)}, bf16[1024,256]{1,0:T(8,128)(2,1)S(1)}, u32[]{:S(2)}) copy-start(bf16[1024,256]{1,0:T(8,128)(2,1)S(1)} %fusion) | copy-start | bytes 1572868
  29.7 49.0 %collective-permute-start.1 = (bf16[1024,256]{1,0:T(8,128)(2,1)S(1)}, bf16[1024,256]{1,0:T(8,128)(2,1)}, u32[]{:S(2)}, u32[]{:S(2)}) collective-permute-start(bf16[1024,256]{1,0:T(8,128)(2,1)S(1)} %fusion), channel_id=1, source_target_pairs={{0,64},{32,96},{64,128},{96,160},{128,192},{160,224},{192,256},{22... | collective-permute-start | bytes 1572872 | tf_op jit(solution)/shard_map/ppermute | solution.py:31
  41.3 39.0 %copy-start.13 = (bf16[1024,256]{1,0:T(8,128)(2,1)S(1)}, bf16[1024,256]{1,0:T(8,128)(2,1)}, u32[]{:S(2)}) copy-start(bf16[1024,256]{1,0:T(8,128)(2,1)} %param.9) | copy-start | bytes 1572868
  81.1 0.8 copy-start.4
  81.1 1.0 copy-start.21
  81.1 2.5 %copy-start.19 = (bf16[1024,256]{0,1:T(8,128)(2,1)}, bf16[1024,256]{0,1:T(8,128)(2,1)S(1)}, u32[]{:S(2)}) copy-start(bf16[1024,256]{0,1:T(8,128)(2,1)S(1)} %get-tuple-element.11) | copy-start | bytes 1572868
  86.8 2.8 %copy-start.9 = (bf16[2,256,512]{2,1,0:T(8,128)(2,1)S(1)}, bf16[2,256,512]{2,1,0:T(8,128)(2,1)}, u32[]{:S(2)}) copy-start(bf16[2,256,512]{2,1,0:T(8,128)(2,1)} %param.6) | copy-start | bytes 1572868
  86.8 2.8 %copy-start.20 = (bf16[1024,256]{0,1:T(8,128)(2,1)S(1)}, bf16[1024,256]{0,1:T(8,128)(2,1)}, u32[]{:S(2)}) copy-start(bf16[1024,256]{0,1:T(8,128)(2,1)} %copy-done.19) | copy-start | bytes 1572868
  86.8 2.8 %copy-start.22 = (bf16[1024,256]{0,1:T(8,128)(2,1)S(1)}, bf16[1024,256]{0,1:T(8,128)(2,1)}, u32[]{:S(2)}) copy-start(bf16[1024,256]{0,1:T(8,128)(2,1)} %copy-done.21) | copy-start | bytes 1572868
  87.5 4.7 %collective-permute-start.2 = (bf16[256,640]{1,0:T(8,128)(2,1)S(1)}, bf16[256,640]{1,0:T(8,128)(2,1)S(1)}, u32[]{:S(2)}, u32[]{:S(2)}) collective-permute-start(bf16[256,640]{1,0:T(8,128)(2,1)S(1)} %bitcast.126), channel_id=1, source_target_pairs={{0,32},{32,0},{1,33},{33,1},{2,34},{34,2},{3,35},{35,3},{4,36},{36... | collective-permute-start | bytes 983048 | tf_op jit(solution)/shard_map/ppermute | solution.py:74
  90.1 12.8 %copy-start.14 = (bf16[1024,256]{1,0:T(8,128)(2,1)S(1)}, bf16[1024,256]{1,0:T(8,128)(2,1)}, u32[]{:S(2)}) copy-start(bf16[1024,256]{1,0:T(8,128)(2,1)} %param.9) | copy-start | bytes 1572868
  90.1 12.8 %copy-start.15 = (bf16[2,256,512]{2,1,0:T(8,128)(2,1)S(1)}, bf16[2,256,512]{2,1,0:T(8,128)(2,1)}, u32[]{:S(2)}) copy-start(bf16[2,256,512]{2,1,0:T(8,128)(2,1)} %param.7) | copy-start | bytes 1572868
  90.1 25.5 %collective-permute-start.6 = (bf16[1024,256]{1,0:T(8,128)(2,1)S(1)}, bf16[1024,256]{1,0:T(8,128)(2,1)S(1)}, u32[]{:S(2)}, u32[]{:S(2)}) collective-permute-start(bf16[1024,256]{1,0:T(8,128)(2,1)S(1)} %convolution_convert_fusion.1), channel_id=1, source_target_pairs={{64,0},{96,32},{128,64},{160,96},{192,128},{224,160},{256,192},{28... | collective-permute-start | bytes 1572872 | tf_op jit(solution)/shard_map/ppermute | solution.py:31
  92.3 11.2 %collective-permute-start.3 = (bf16[64,640]{1,0:T(8,128)(2,1)S(1)}, bf16[64,640]{1,0:T(8,128)(2,1)S(1)}, u32[]{:S(2)}, u32[]{:S(2)}) collective-permute-start(bf16[64,640]{1,0:T(8,128)(2,1)S(1)} %get-tuple-element.17), channel_id=1, source_target_pairs={{0,8},{8,16},{16,24},{24,0},{1,9},{9,17},{17,25},{25,1},{2,10},{10... | collective-permute-start | bytes 245768 | tf_op jit(solution)/shard_map/ppermute | solution.py:41
  95.5 8.0 %collective-permute-start.4 = (bf16[64,640]{1,0:T(8,128)(2,1)S(1)}, bf16[64,640]{1,0:T(8,128)(2,1)S(1)}, u32[]{:S(2)}, u32[]{:S(2)}) collective-permute-start(bf16[64,640]{1,0:T(8,128)(2,1)S(1)} %get-tuple-element.19), channel_id=1, source_target_pairs={{0,16},{8,24},{16,0},{24,8},{1,17},{9,25},{17,1},{25,9},{2,18},{10... | collective-permute-start | bytes 245768 | tf_op jit(solution)/shard_map/ppermute | solution.py:41
  99.9 5.5 %collective-permute-start.5 = (bf16[64,640]{1,0:T(8,128)(2,1)S(1)}, bf16[64,640]{1,0:T(8,128)(2,1)S(1)}, u32[]{:S(2)}, u32[]{:S(2)}) collective-permute-start(bf16[64,640]{1,0:T(8,128)(2,1)S(1)} %get-tuple-element.18), channel_id=1, source_target_pairs={{0,24},{8,0},{16,8},{24,16},{1,25},{9,1},{17,9},{25,17},{2,26},{10... | collective-permute-start | bytes 245768 | tf_op jit(solution)/shard_map/ppermute | solution.py:41
  103.5 12.3 %copy-start.18 = (bf16[2,256,256]{2,1,0:T(8,128)(2,1)S(1)}, bf16[2,256,256]{2,1,0:T(8,128)(2,1)}, u32[]{:S(2)}) copy-start(bf16[2,256,256]{2,1,0:T(8,128)(2,1)} %param.8) | copy-start | bytes 786436
  115.8 1.0 copy-start.1
  115.8 1.3 copy-start.7
  116.8 0.8 copy-start.23
  116.8 1.0 copy-start.24
  116.8 1.4 copy-start.12
  120.2 3.9 %collective-permute-start.8 = (bf16[256,640]{1,0:T(8,128)(2,1)S(1)}, bf16[256,640]{1,0:T(8,128)(2,1)S(1)}, u32[]{:S(2)}, u32[]{:S(2)}) collective-permute-start(bf16[256,640]{1,0:T(8,128)(2,1)S(1)} %bitcast.127), channel_id=1, source_target_pairs={{0,32},{32,0},{1,33},{33,1},{2,34},{34,2},{3,35},{35,3},{4,36},{36... | collective-permute-start | bytes 983048 | tf_op jit(solution)/shard_map/ppermute | solution.py:74
  123.7 57.5 %copy-start.10 = (bf16[2,256,512]{2,1,0:T(8,128)(2,1)S(1)}, bf16[2,256,512]{2,1,0:T(8,128)(2,1)}, u32[]{:S(2)}) copy-start(bf16[2,256,512]{2,1,0:T(8,128)(2,1)} %param.6) | copy-start | bytes 1572868
  124.3 10.1 %collective-permute-start.10 = (bf16[64,640]{1,0:T(8,128)(2,1)S(1)}, bf16[64,640]{1,0:T(8,128)(2,1)S(1)}, u32[]{:S(2)}, u32[]{:S(2)}) collective-permute-start(bf16[64,640]{1,0:T(8,128)(2,1)S(1)} %get-tuple-element.16), channel_id=1, source_target_pairs={{0,16},{8,24},{16,0},{24,8},{1,17},{9,25},{17,1},{25,9},{2,18},{10... | collective-permute-start | bytes 245768 | tf_op jit(solution)/shard_map/ppermute | solution.py:41
  129.1 5.3 %collective-permute-start.11 = (bf16[64,640]{1,0:T(8,128)(2,1)S(1)}, bf16[64,640]{1,0:T(8,128)(2,1)S(1)}, u32[]{:S(2)}, u32[]{:S(2)}) collective-permute-start(bf16[64,640]{1,0:T(8,128)(2,1)S(1)} %get-tuple-element.15), channel_id=1, source_target_pairs={{0,24},{8,0},{16,8},{24,16},{1,25},{9,1},{17,9},{25,17},{2,26},{10... | collective-permute-start | bytes 245768 | tf_op jit(solution)/shard_map/ppermute | solution.py:41
  131.8 6.4 %collective-permute-start.9 = (bf16[64,640]{1,0:T(8,128)(2,1)S(1)}, bf16[64,640]{1,0:T(8,128)(2,1)S(1)}, u32[]{:S(2)}, u32[]{:S(2)}) collective-permute-start(bf16[64,640]{1,0:T(8,128)(2,1)S(1)} %get-tuple-element.14), channel_id=1, source_target_pairs={{0,8},{8,16},{16,24},{24,0},{1,9},{9,17},{17,25},{25,1},{2,10},{10... | collective-permute-start | bytes 245768 | tf_op jit(solution)/shard_map/ppermute | solution.py:41
  140.2 62.5 %copy-start.3 = (bf16[1024,256]{1,0:T(8,128)(2,1)S(1)}, bf16[1024,256]{1,0:T(8,128)(2,1)}, u32[]{:S(2)}) copy-start(bf16[1024,256]{1,0:T(8,128)(2,1)} %copy-done.2) | copy-start | bytes 1572868
  140.2 62.5 %copy-start.5 = (bf16[1024,256]{0,1:T(8,128)(2,1)S(1)}, bf16[1024,256]{0,1:T(8,128)(2,1)}, u32[]{:S(2)}) copy-start(bf16[1024,256]{0,1:T(8,128)(2,1)} %copy-done.4) | copy-start | bytes 1572868
  140.2 55.3 %all-to-all-start = ((bf16[64,2,640]{2,1,0:T(2,128)(2,1)}), bf16[64,2,640]{2,1,0:T(2,128)(2,1)S(1)}, u32[]{:S(2)}, u32[]{:S(2)}) async-start(bf16[64,2,640]{2,1,0:T(2,128)(2,1)} %reshape.59), calls=%async_computation | async-start | bytes 327680 | tf_op jit(solution)/shard_map/all_to_all | solution.py:83
  181.2 41.5 %copy-start.16 = (bf16[2,256,512]{2,1,0:T(8,128)(2,1)S(1)}, bf16[2,256,512]{2,1,0:T(8,128)(2,1)}, u32[]{:S(2)}) copy-start(bf16[2,256,512]{2,1,0:T(8,128)(2,1)} %param.7) | copy-start | bytes 1572868
  183.8 38.9 %collective-permute-start.7 = (bf16[1024,256]{1,0:T(8,128)(2,1)}, bf16[1024,256]{1,0:T(8,128)(2,1)S(1)}, u32[]{:S(2)}, u32[]{:S(2)}) collective-permute-start(bf16[1024,256]{1,0:T(8,128)(2,1)} %convolution_convert_fusion), channel_id=1, source_target_pairs={{1,0},{2,1},{3,2},{4,3},{5,4},{6,5},{7,6},{8,7},{9,8},{10,9},{11,1... | collective-permute-start | bytes 1572872 | tf_op jit(solution)/shard_map/ppermute | solution.py:31
  196.6 20.1 %all-to-all-start.1 = ((f32[8,1,1280]{2,1,0:T(1,128)}), f32[8,1,1280]{2,1,0:T(1,128)S(1)}, u32[]{:S(2)}, u32[]{:S(2)}) async-start(f32[8,1,1280]{2,1,0:T(1,128)} %broadcast_in_dim.2), calls=%async_computation.1 | async-start | bytes 81920 | tf_op jit(solution)/shard_map/all_to_all | solution.py:86
  216.7 8.5 %collective-permute-start.12 = (f32[8,1280]{1,0:T(8,128)S(1)}, f32[8,1280]{1,0:T(8,128)S(1)}, u32[]{:S(2)}, u32[]{:S(2)}) collective-permute-start(f32[8,1280]{1,0:T(8,128)S(1)} %bitcast.128), channel_id=1, source_target_pairs={{0,32},{32,0},{1,33},{33,1},{2,34},{34,2},{3,35},{35,3},{4,36},{36... | collective-permute-start | bytes 122888 | tf_op jit(solution)/shard_map/ppermute | solution.py:87

commit v6 on v5

--- a/solution.py
+++ b/solution.py
@@ -78,18 +78,14 @@
 def far_sum(term):
     lo_size = lax.axis_size("z_lo")
     hi_size = lax.axis_size("y") * lax.axis_size("z_hi")
+    core_size = lax.axis_size("core")
     rows = term.reshape(lo_size, hi_size, term.shape[1]).transpose(1, 0, 2)
     rows = rows.reshape(hi_size * lo_size, 1, term.shape[1])
     row = lax.all_to_all(rows.astype(jnp.bfloat16), ("y", "z_hi", "z_lo"), 0, 0, tiled=True)
     row = row.astype(jnp.float32).sum(0)
-    spread = jnp.broadcast_to(row[None], (hi_size, *row.shape))
-    term = lax.all_to_all(spread, ("y", "z_hi"), 0, 0, tiled=True).reshape(hi_size, term.shape[1])
-    other = lax.ppermute(term, "core", [(0, 1), (1, 0)])
-    own_core = lax.axis_index("core")
-    pair = jnp.stack([term, other])
-    first = lax.dynamic_index_in_dim(pair, own_core, 0, keepdims=False)
-    second = lax.dynamic_index_in_dim(pair, 1 - own_core, 0, keepdims=False)
-    return first, second
+    spread = jnp.broadcast_to(row[None], (hi_size * core_size, *row.shape))
+    gathered = lax.all_to_all(spread, ("y", "z_hi", "core"), 0, 0, tiled=True)
+    return gathered.reshape(hi_size, core_size, term.shape[1])
 
 
 def gating(current, earlier, w_past, w_now):
@@ -174,15 +170,11 @@
             grad_preact, conv_now[layer_at].T, preferred_element_type=jnp.float32
         )
         upstream = (local_grad + arrived.astype(jnp.float32)).astype(jnp.bfloat16)
-    first, second = far_sum(jnp.concatenate(near_list, 1))
+    whole = far_sum(jnp.concatenate(near_list, 1))
     half_width = near_list[0].shape[1]
     summed_list = [
-        jnp.concatenate(
-            [
-                first[:, layer_at * half_width : (layer_at + 1) * half_width],
-                second[:, layer_at * half_width : (layer_at + 1) * half_width],
-            ],
-            1,
+        whole[:, :, layer_at * half_width : (layer_at + 1) * half_width].reshape(
+            whole.shape[0], 2 * half_width
         )
         for layer_at in range(layer_count)
     ]

time: 228 us -> 223 us (0.978)
    ppermute x1 -> x0, starting transfers between devices: 5.97 us -> none  [far_sum(): other = lax.ppermute(term, 'core', [(0, 1), (1, 0)])]
    all_to_all x1, starting transfers between devices: 6.2 us -> 9.36 us  [far_sum(): gathered = lax.all_to_all(spread, ('y', 'z_hi', 'core'), 0, 0, tiled=True)]
  transfers between devices with their start and end apart: 15 -> 14, of which waited for: 8 -> 8; matrix products, arithmetic and copies ran while one was open for 6% -> 5% of each run, Pallas kernels for 0% -> 0%
where the time goes in v6:
time: 223 us
  starting transfers between devices  104 us (47%)
  waiting for transfers between devices  86.8 us (39%)
  matrix products  16.3 us (7%)
  local copies, waits for them, and re-layouts  9.97 us (4%)
  other arithmetic  4.55 us (2%)
    ppermute x4, waiting for transfers between devices, from_behind(): return lax.ppermute(array, axes, pairs)  68.2 us
    all_to_all x1, starting transfers between devices, far_sum(): lax.all_to_all(rows.astype(jnp.bfloat16), ('y', 'z_hi', 'z_lo'), 0, 0, ti...  41 us
    ppermute x4, starting transfers between devices, from_behind(): return lax.ppermute(array, axes, pairs)  27.6 us
    ppermute x6, starting transfers between devices, scatter_sum(): lax.ppermute(piece.astype(jnp.bfloat16), axes, [(i, (i + shift) % size) f...  20.7 us
    all_to_all x1, waiting for transfers between devices, far_sum(): gathered = lax.all_to_all(spread, ('y', 'z_hi', 'core'), 0, 0, tiled=True)  10.9 us
    all_to_all x1, starting transfers between devices, far_sum(): gathered = lax.all_to_all(spread, ('y', 'z_hi', 'core'), 0, 0, tiled=True)  9.36 us
    ppermute x6, waiting for transfers between devices, scatter_sum(): lax.ppermute(piece.astype(jnp.bfloat16), axes, [(i, (i + shift) % size) f...  5.72 us
    ppermute x2, starting transfers between devices, near_sum(): moved = lax.ppermute(given.astype(jnp.bfloat16), 'core', [(0, 1), (1, 0)])  4.99 us
  transfers between devices with their start and end apart: 14, of which 8 were waited for; matrix products, arithmetic and copies ran while one was open for 5% of the time, Pallas kernels for 0%

profile of v6, /device:TPU:1, one launch (start us, length us, event | category | flops | bytes accessed | tf_op | source)
XLA Modules:
  0.0 222.5 jit_solution(708121455494834143)
XLA Ops:
  0.6 4.5 %collective-permute-start = (bf16[1024,256]{1,0:T(8,128)(2,1)}, bf16[1024,256]{1,0:T(8,128)(2,1)S(1)}, u32[]{:S(2)}, u32[]{:S(2)}) collective-permute-start(bf16[1024,256]{1,0:T(8,128)(2,1)} %param.5), channel_id=1, source_target_pairs={{0,1},{1,2},{2,3},{3,4},{4,5},{5,6},{6,7},{7,8},{8,9},{9,10},{10,1... | collective-permute-start | bytes 1572872 | tf_op jit(solution)/shard_map/ppermute | solution.py:31
  5.2 1.6 fusion.16
  6.8 20.6 %collective-permute-done = bf16[1024,256]{1,0:T(8,128)(2,1)S(1)} collective-permute-done((bf16[1024,256]{1,0:T(8,128)(2,1)}, bf16[1024,256]{1,0:T(8,128)(2,1)S(1)}, u32[]{:S(2)}, u32[]{:S(2)}) %collective-permute-start) | collective-permute-done | bytes 524320 | tf_op jit(solution)/shard_map/ppermute | solution.py:31
  27.3 0.5 convolution_add_fusion.1
  27.8 0.3 copy-done.13
  28.1 0.4 multiply_convert_fusion.5
  28.5 0.8 copy-done
  29.4 0.4 fusion
  29.7 10.2 %collective-permute-start.1 = (bf16[1024,256]{1,0:T(8,128)(2,1)S(1)}, bf16[1024,256]{1,0:T(8,128)(2,1)}, u32[]{:S(2)}, u32[]{:S(2)}) collective-permute-start(bf16[1024,256]{1,0:T(8,128)(2,1)S(1)} %fusion), channel_id=1, source_target_pairs={{0,64},{32,96},{64,128},{96,160},{128,192},{160,224},{192,256},{22... | collective-permute-start | bytes 1572872 | tf_op jit(solution)/shard_map/ppermute | solution.py:31
  39.9 1.4 fusion.11
  41.4 37.4 %collective-permute-done.1 = bf16[1024,256]{1,0:T(8,128)(2,1)} collective-permute-done((bf16[1024,256]{1,0:T(8,128)(2,1)S(1)}, bf16[1024,256]{1,0:T(8,128)(2,1)}, u32[]{:S(2)}, u32[]{:S(2)}) %collective-permute-start.1) | collective-permute-done | bytes 524320 | tf_op jit(solution)/shard_map/ppermute | solution.py:31
  78.8 1.5 convolution_add_fusion
  80.3 0.8 multiply_convert_fusion.3
  81.1 0.3 fusion.51
  81.4 0.5 fusion.49
  81.9 0.1 copy-done.22
  82.1 0.1 copy-done.24
  82.2 1.5 fusion.50
  83.7 1.2 maximum_multiply_fusion
  85.0 2.0 mul.65
  87.0 0.6 constant_dynamic-slice_fusion.2
  87.7 2.1 collective-permute-start.2
  89.8 0.5 convolution_convert_fusion.1
  90.3 1.4 collective-permute-start.6
  91.8 0.6 constant_dynamic-slice_fusion.3
  92.5 3.2 %collective-permute-start.3 = (bf16[64,640]{1,0:T(8,128)(2,1)S(1)}, bf16[64,640]{1,0:T(8,128)(2,1)S(1)}, u32[]{:S(2)}, u32[]{:S(2)}) collective-permute-start(bf16[64,640]{1,0:T(8,128)(2,1)S(1)} %get-tuple-element.17), channel_id=1, source_target_pairs={{0,8},{8,16},{16,24},{24,0},{1,9},{9,17},{17,25},{25,1},{2,10},{10... | collective-permute-start | bytes 245768 | tf_op jit(solution)/shard_map/ppermute | solution.py:41
  95.7 4.3 %collective-permute-start.4 = (bf16[64,640]{1,0:T(8,128)(2,1)S(1)}, bf16[64,640]{1,0:T(8,128)(2,1)S(1)}, u32[]{:S(2)}, u32[]{:S(2)}) collective-permute-start(bf16[64,640]{1,0:T(8,128)(2,1)S(1)} %get-tuple-element.19), channel_id=1, source_target_pairs={{0,16},{8,24},{16,0},{24,8},{1,17},{9,25},{17,1},{25,9},{2,18},{10... | collective-permute-start | bytes 245768 | tf_op jit(solution)/shard_map/ppermute | solution.py:41
  100.0 3.1 %collective-permute-start.5 = (bf16[64,640]{1,0:T(8,128)(2,1)S(1)}, bf16[64,640]{1,0:T(8,128)(2,1)S(1)}, u32[]{:S(2)}, u32[]{:S(2)}) collective-permute-start(bf16[64,640]{1,0:T(8,128)(2,1)S(1)} %get-tuple-element.18), channel_id=1, source_target_pairs={{0,24},{8,0},{16,8},{24,16},{1,25},{9,1},{17,9},{25,17},{2,26},{10... | collective-permute-start | bytes 245768 | tf_op jit(solution)/shard_map/ppermute | solution.py:41
  103.1 0.5 convolution_add_fusion.5
  103.7 1.8 collective-permute-done.5
  105.6 10.2 %collective-permute-done.6 = bf16[1024,256]{1,0:T(8,128)(2,1)S(1)} collective-permute-done((bf16[1024,256]{1,0:T(8,128)(2,1)S(1)}, bf16[1024,256]{1,0:T(8,128)(2,1)S(1)}, u32[]{:S(2)}, u32[]{:S(2)}) %collective-permute-start.6) | collective-permute-done | bytes 524320 | tf_op jit(solution)/shard_map/ppermute | solution.py:31
  115.8 0.1 add_convert_fusion.1
  116.0 0.7 multiply_convert_fusion.1
  116.8 0.4 copy-done.1
  117.2 0.3 fusion.52
  117.5 0.5 convolution_bitcast_fusion
  118.0 0.2 copy-done.28
  118.2 0.4 copy-done.14
  118.6 0.5 convolution_bitcast_fusion.1
  119.2 0.7 mul.73
  120.0 0.6 constant_dynamic-slice_fusion
  120.6 2.9 %collective-permute-start.8 = (bf16[256,640]{1,0:T(8,128)(2,1)S(1)}, bf16[256,640]{1,0:T(8,128)(2,1)S(1)}, u32[]{:S(2)}, u32[]{:S(2)}) collective-permute-start(bf16[256,640]{1,0:T(8,128)(2,1)S(1)} %bitcast.123), channel_id=1, source_target_pairs={{0,32},{32,0},{1,33},{33,1},{2,34},{34,2},{3,35},{35,3},{4,36},{36... | collective-permute-start | bytes 983048 | tf_op jit(solution)/shard_map/ppermute | solution.py:74
  123.5 0.6 constant_dynamic-slice_fusion.1
  124.1 0.4 collective-permute-done.8
  124.7 4.8 %collective-permute-start.10 = (bf16[64,640]{1,0:T(8,128)(2,1)S(1)}, bf16[64,640]{1,0:T(8,128)(2,1)S(1)}, u32[]{:S(2)}, u32[]{:S(2)}) collective-permute-start(bf16[64,640]{1,0:T(8,128)(2,1)S(1)} %get-tuple-element.16), channel_id=1, source_target_pairs={{0,16},{8,24},{16,0},{24,8},{1,17},{9,25},{17,1},{25,9},{2,18},{10... | collective-permute-start | bytes 245768 | tf_op jit(solution)/shard_map/ppermute | solution.py:41
  129.4 2.8 %collective-permute-start.11 = (bf16[64,640]{1,0:T(8,128)(2,1)S(1)}, bf16[64,640]{1,0:T(8,128)(2,1)S(1)}, u32[]{:S(2)}, u32[]{:S(2)}) collective-permute-start(bf16[64,640]{1,0:T(8,128)(2,1)S(1)} %get-tuple-element.15), channel_id=1, source_target_pairs={{0,24},{8,0},{16,8},{24,16},{1,25},{9,1},{17,9},{25,17},{2,26},{10... | collective-permute-start | bytes 245768 | tf_op jit(solution)/shard_map/ppermute | solution.py:41
  132.2 2.5 %collective-permute-start.9 = (bf16[64,640]{1,0:T(8,128)(2,1)S(1)}, bf16[64,640]{1,0:T(8,128)(2,1)S(1)}, u32[]{:S(2)}, u32[]{:S(2)}) collective-permute-start(bf16[64,640]{1,0:T(8,128)(2,1)S(1)} %get-tuple-element.14), channel_id=1, source_target_pairs={{0,8},{8,16},{16,24},{24,0},{1,9},{9,17},{17,25},{25,1},{2,10},{10... | collective-permute-start | bytes 245768 | tf_op jit(solution)/shard_map/ppermute | solution.py:41
  134.8 3.9 %collective-permute-done.9 = bf16[64,640]{1,0:T(8,128)(2,1)S(1)} collective-permute-done((bf16[64,640]{1,0:T(8,128)(2,1)S(1)}, bf16[64,640]{1,0:T(8,128)(2,1)S(1)}, u32[]{:S(2)}, u32[]{:S(2)}) %collective-permute-start.9) | collective-permute-done | bytes 81952 | tf_op jit(solution)/shard_map/ppermute | solution.py:41
  138.7 0.5 broadcast.39
  139.2 0.7 reduce.2
  139.9 0.7 reshape.68
  140.7 41.0 %all-to-all-start = ((bf16[64,2,640]{2,1,0:T(2,128)(2,1)}), bf16[64,2,640]{2,1,0:T(2,128)(2,1)S(1)}, u32[]{:S(2)}, u32[]{:S(2)}) async-start(bf16[64,2,640]{2,1,0:T(2,128)(2,1)} %reshape.68), calls=%async_computation | async-start | bytes 327680 | tf_op jit(solution)/shard_map/all_to_all | solution.py:84
  181.6 1.3 convolution_convert_fusion
  182.9 11.4 %collective-permute-start.7 = (bf16[1024,256]{1,0:T(8,128)(2,1)}, bf16[1024,256]{1,0:T(8,128)(2,1)S(1)}, u32[]{:S(2)}, u32[]{:S(2)}) collective-permute-start(bf16[1024,256]{1,0:T(8,128)(2,1)} %convolution_convert_fusion), channel_id=1, source_target_pairs={{1,0},{2,1},{3,2},{4,3},{5,4},{6,5},{7,6},{8,7},{9,8},{10,9},{11,1... | collective-permute-start | bytes 1572872 | tf_op jit(solution)/shard_map/ppermute | solution.py:31
  194.4 1.5 all-to-all-done
  196.0 0.3 convert_reduce_fusion
  196.3 0.7 broadcast_in_dim.2
  197.0 9.4 %all-to-all-start.1 = ((f32[16,1,1280]{2,1,0:T(1,128)}), f32[16,1,1280]{2,1,0:T(1,128)S(1)}, u32[]{:S(2)}, u32[]{:S(2)}) async-start(f32[16,1,1280]{2,1,0:T(1,128)} %broadcast_in_dim.2), calls=%async_computation.1 | async-start | bytes 163840 | tf_op jit(solution)/shard_map/all_to_all | solution.py:87
  206.4 1.2 fusion.1
  207.6 2.5 %add_convert_fusion = bf16[1024,256]{1,0:T(8,128)(2,1)} fusion(bf16[1024,256]{1,0:T(8,128)(2,1)S(1)} %collective-permute-done.7, bf16[1024,256]{1,0:T(8,128)(2,1)S(1)} %copy-done.9, bf16[2,256,512]{2,1,0:T(8,128)(2,1)S(1)} %copy-done.18, bf16[1024,256]{0,1:T(8,128)(2,1)} %copy-done.28, bf16[1024,256]{0,1:T(8,128)(2,1)} %copy-done.26), kind=kOutput, calls=%fused_computation.26 | convolution fusion | flops 271843328 | bytes 2883584 | tf_op jit(solution)/shard_map/dot_general | solution.py:169
  210.0 10.9 %all-to-all-done.1 = f32[16,1,1280]{2,1,0:T(1,128)S(1)} async-done(((f32[16,1,1280]{2,1,0:T(1,128)}), f32[16,1,1280]{2,1,0:T(1,128)S(1)}, u32[]{:S(2)}, u32[]{:S(2)}) %all-to-all-start.1) | async-done | bytes 81952 | tf_op jit(solution)/shard_map/all_to_all | solution.py:87
  221.0 0.2 reduce.1
  221.3 0.6 pad_maximum_fusion.4
  221.9 0.6 pad_maximum_fusion.2
  (78 shorter events, 1.0 us)
Async XLA Ops:
  0.6 26.7 %copy-start.10 = (bf16[2,256,512]{2,1,0:T(8,128)(2,1)S(1)}, bf16[2,256,512]{2,1,0:T(8,128)(2,1)}, u32[]{:S(2)}) copy-start(bf16[2,256,512]{2,1,0:T(8,128)(2,1)} %param.6) | copy-start | bytes 1572868
  0.6 26.7 %collective-permute-start = (bf16[1024,256]{1,0:T(8,128)(2,1)}, bf16[1024,256]{1,0:T(8,128)(2,1)S(1)}, u32[]{:S(2)}, u32[]{:S(2)}) collective-permute-start(bf16[1024,256]{1,0:T(8,128)(2,1)} %param.5), channel_id=1, source_target_pairs={{0,1},{1,2},{2,3},{3,4},{4,5},{5,6},{6,7},{7,8},{8,9},{9,10},{10,1... | collective-permute-start | bytes 1572872 | tf_op jit(solution)/shard_map/ppermute | solution.py:31
  27.3 0.8 copy-start.13
  28.1 1.2 copy-start.6
  28.1 1.2 copy-start.19
  28.5 0.8 copy-start
  29.7 51.7 %copy-start.2 = (bf16[1024,256]{1,0:T(8,128)(2,1)}, bf16[1024,256]{1,0:T(8,128)(2,1)S(1)}, u32[]{:S(2)}) copy-start(bf16[1024,256]{1,0:T(8,128)(2,1)S(1)} %fusion) | copy-start | bytes 1572868
  29.7 49.0 %collective-permute-start.1 = (bf16[1024,256]{1,0:T(8,128)(2,1)S(1)}, bf16[1024,256]{1,0:T(8,128)(2,1)}, u32[]{:S(2)}, u32[]{:S(2)}) collective-permute-start(bf16[1024,256]{1,0:T(8,128)(2,1)S(1)} %fusion), channel_id=1, source_target_pairs={{0,64},{32,96},{64,128},{96,160},{128,192},{160,224},{192,256},{22... | collective-permute-start | bytes 1572872 | tf_op jit(solution)/shard_map/ppermute | solution.py:31
  41.3 39.0 %copy-start.15 = (bf16[1024,256]{1,0:T(8,128)(2,1)S(1)}, bf16[1024,256]{1,0:T(8,128)(2,1)}, u32[]{:S(2)}) copy-start(bf16[1024,256]{1,0:T(8,128)(2,1)} %param.9) | copy-start | bytes 1572868
  81.1 0.8 copy-start.4
  81.1 1.0 copy-start.22
  81.1 1.1 copy-start.24
  87.0 2.8 %copy-start.11 = (bf16[2,256,512]{2,1,0:T(8,128)(2,1)S(1)}, bf16[2,256,512]{2,1,0:T(8,128)(2,1)}, u32[]{:S(2)}) copy-start(bf16[2,256,512]{2,1,0:T(8,128)(2,1)} %param.6) | copy-start | bytes 1572868
  87.0 2.8 %copy-start.23 = (bf16[1024,256]{0,1:T(8,128)(2,1)S(1)}, bf16[1024,256]{0,1:T(8,128)(2,1)}, u32[]{:S(2)}) copy-start(bf16[1024,256]{0,1:T(8,128)(2,1)} %copy-done.22) | copy-start | bytes 1572868
  87.0 2.8 %copy-start.25 = (bf16[1024,256]{0,1:T(8,128)(2,1)S(1)}, bf16[1024,256]{0,1:T(8,128)(2,1)}, u32[]{:S(2)}) copy-start(bf16[1024,256]{0,1:T(8,128)(2,1)} %copy-done.24) | copy-start | bytes 1572868
  87.7 4.7 %collective-permute-start.2 = (bf16[256,640]{1,0:T(8,128)(2,1)S(1)}, bf16[256,640]{1,0:T(8,128)(2,1)S(1)}, u32[]{:S(2)}, u32[]{:S(2)}) collective-permute-start(bf16[256,640]{1,0:T(8,128)(2,1)S(1)} %bitcast.122), channel_id=1, source_target_pairs={{0,32},{32,0},{1,33},{33,1},{2,34},{34,2},{3,35},{35,3},{4,36},{36... | collective-permute-start | bytes 983048 | tf_op jit(solution)/shard_map/ppermute | solution.py:74
  90.3 12.8 %copy-start.16 = (bf16[1024,256]{1,0:T(8,128)(2,1)S(1)}, bf16[1024,256]{1,0:T(8,128)(2,1)}, u32[]{:S(2)}) copy-start(bf16[1024,256]{1,0:T(8,128)(2,1)} %param.9) | copy-start | bytes 1572868
  90.3 12.8 %copy-start.17 = (bf16[2,256,512]{2,1,0:T(8,128)(2,1)S(1)}, bf16[2,256,512]{2,1,0:T(8,128)(2,1)}, u32[]{:S(2)}) copy-start(bf16[2,256,512]{2,1,0:T(8,128)(2,1)} %param.7) | copy-start | bytes 1572868
  90.3 25.5 %collective-permute-start.6 = (bf16[1024,256]{1,0:T(8,128)(2,1)S(1)}, bf16[1024,256]{1,0:T(8,128)(2,1)S(1)}, u32[]{:S(2)}, u32[]{:S(2)}) collective-permute-start(bf16[1024,256]{1,0:T(8,128)(2,1)S(1)} %convolution_convert_fusion.1), channel_id=1, source_target_pairs={{64,0},{96,32},{128,64},{160,96},{192,128},{224,160},{256,192},{28... | collective-permute-start | bytes 1572872 | tf_op jit(solution)/shard_map/ppermute | solution.py:31
  92.5 11.2 %collective-permute-start.3 = (bf16[64,640]{1,0:T(8,128)(2,1)S(1)}, bf16[64,640]{1,0:T(8,128)(2,1)S(1)}, u32[]{:S(2)}, u32[]{:S(2)}) collective-permute-start(bf16[64,640]{1,0:T(8,128)(2,1)S(1)} %get-tuple-element.17), channel_id=1, source_target_pairs={{0,8},{8,16},{16,24},{24,0},{1,9},{9,17},{17,25},{25,1},{2,10},{10... | collective-permute-start | bytes 245768 | tf_op jit(solution)/shard_map/ppermute | solution.py:41
  95.7 8.0 %collective-permute-start.4 = (bf16[64,640]{1,0:T(8,128)(2,1)S(1)}, bf16[64,640]{1,0:T(8,128)(2,1)S(1)}, u32[]{:S(2)}, u32[]{:S(2)}) collective-permute-start(bf16[64,640]{1,0:T(8,128)(2,1)S(1)} %get-tuple-element.19), channel_id=1, source_target_pairs={{0,16},{8,24},{16,0},{24,8},{1,17},{9,25},{17,1},{25,9},{2,18},{10... | collective-permute-start | bytes 245768 | tf_op jit(solution)/shard_map/ppermute | solution.py:41
  100.0 5.5 %collective-permute-start.5 = (bf16[64,640]{1,0:T(8,128)(2,1)S(1)}, bf16[64,640]{1,0:T(8,128)(2,1)S(1)}, u32[]{:S(2)}, u32[]{:S(2)}) collective-permute-start(bf16[64,640]{1,0:T(8,128)(2,1)S(1)} %get-tuple-element.18), channel_id=1, source_target_pairs={{0,24},{8,0},{16,8},{24,16},{1,25},{9,1},{17,9},{25,17},{2,26},{10... | collective-permute-start | bytes 245768 | tf_op jit(solution)/shard_map/ppermute | solution.py:41
  103.6 12.3 %copy-start.20 = (bf16[2,256,256]{2,1,0:T(8,128)(2,1)S(1)}, bf16[2,256,256]{2,1,0:T(8,128)(2,1)}, u32[]{:S(2)}) copy-start(bf16[2,256,256]{2,1,0:T(8,128)(2,1)} %param.8) | copy-start | bytes 786436
  116.0 0.8 copy-start.8
  116.0 1.2 copy-start.1
  116.0 1.5 copy-start.7
  117.2 0.8 copy-start.26
  117.2 1.0 copy-start.28
  117.2 1.4 copy-start.14
  120.6 3.9 %collective-permute-start.8 = (bf16[256,640]{1,0:T(8,128)(2,1)S(1)}, bf16[256,640]{1,0:T(8,128)(2,1)S(1)}, u32[]{:S(2)}, u32[]{:S(2)}) collective-permute-start(bf16[256,640]{1,0:T(8,128)(2,1)S(1)} %bitcast.123), channel_id=1, source_target_pairs={{0,32},{32,0},{1,33},{33,1},{2,34},{34,2},{3,35},{35,3},{4,36},{36... | collective-permute-start | bytes 983048 | tf_op jit(solution)/shard_map/ppermute | solution.py:74
  124.1 57.5 %copy-start.12 = (bf16[2,256,512]{2,1,0:T(8,128)(2,1)S(1)}, bf16[2,256,512]{2,1,0:T(8,128)(2,1)}, u32[]{:S(2)}) copy-start(bf16[2,256,512]{2,1,0:T(8,128)(2,1)} %param.6) | copy-start | bytes 1572868
  124.1 57.5 %copy-start.27 = (bf16[1024,256]{0,1:T(8,128)(2,1)S(1)}, bf16[1024,256]{0,1:T(8,128)(2,1)}, u32[]{:S(2)}) copy-start(bf16[1024,256]{0,1:T(8,128)(2,1)} %copy-done.26) | copy-start | bytes 1572868
  124.1 57.5 %copy-start.29 = (bf16[1024,256]{0,1:T(8,128)(2,1)S(1)}, bf16[1024,256]{0,1:T(8,128)(2,1)}, u32[]{:S(2)}) copy-start(bf16[1024,256]{0,1:T(8,128)(2,1)} %copy-done.28) | copy-start | bytes 1572868
  124.7 10.1 %collective-permute-start.10 = (bf16[64,640]{1,0:T(8,128)(2,1)S(1)}, bf16[64,640]{1,0:T(8,128)(2,1)S(1)}, u32[]{:S(2)}, u32[]{:S(2)}) collective-permute-start(bf16[64,640]{1,0:T(8,128)(2,1)S(1)} %get-tuple-element.16), channel_id=1, source_target_pairs={{0,16},{8,24},{16,0},{24,8},{1,17},{9,25},{17,1},{25,9},{2,18},{10... | collective-permute-start | bytes 245768 | tf_op jit(solution)/shard_map/ppermute | solution.py:41
  129.4 5.3 %collective-permute-start.11 = (bf16[64,640]{1,0:T(8,128)(2,1)S(1)}, bf16[64,640]{1,0:T(8,128)(2,1)S(1)}, u32[]{:S(2)}, u32[]{:S(2)}) collective-permute-start(bf16[64,640]{1,0:T(8,128)(2,1)S(1)} %get-tuple-element.15), channel_id=1, source_target_pairs={{0,24},{8,0},{16,8},{24,16},{1,25},{9,1},{17,9},{25,17},{2,26},{10... | collective-permute-start | bytes 245768 | tf_op jit(solution)/shard_map/ppermute | solution.py:41
  132.2 6.4 %collective-permute-start.9 = (bf16[64,640]{1,0:T(8,128)(2,1)S(1)}, bf16[64,640]{1,0:T(8,128)(2,1)S(1)}, u32[]{:S(2)}, u32[]{:S(2)}) collective-permute-start(bf16[64,640]{1,0:T(8,128)(2,1)S(1)} %get-tuple-element.14), channel_id=1, source_target_pairs={{0,8},{8,16},{16,24},{24,0},{1,9},{9,17},{17,25},{25,1},{2,10},{10... | collective-permute-start | bytes 245768 | tf_op jit(solution)/shard_map/ppermute | solution.py:41
  140.6 65.7 %copy-start.3 = (bf16[1024,256]{1,0:T(8,128)(2,1)S(1)}, bf16[1024,256]{1,0:T(8,128)(2,1)}, u32[]{:S(2)}) copy-start(bf16[1024,256]{1,0:T(8,128)(2,1)} %copy-done.2) | copy-start | bytes 1572868
  140.6 65.7 %copy-start.5 = (bf16[1024,256]{0,1:T(8,128)(2,1)S(1)}, bf16[1024,256]{0,1:T(8,128)(2,1)}, u32[]{:S(2)}) copy-start(bf16[1024,256]{0,1:T(8,128)(2,1)} %copy-done.4) | copy-start | bytes 1572868
  140.6 65.7 %copy-start.21 = (bf16[2,256,256]{2,1,0:T(8,128)(2,1)S(1)}, bf16[2,256,256]{2,1,0:T(8,128)(2,1)}, u32[]{:S(2)}) copy-start(bf16[2,256,256]{2,1,0:T(8,128)(2,1)} %param.8) | copy-start | bytes 786436
  140.7 55.2 %all-to-all-start = ((bf16[64,2,640]{2,1,0:T(2,128)(2,1)}), bf16[64,2,640]{2,1,0:T(2,128)(2,1)S(1)}, u32[]{:S(2)}, u32[]{:S(2)}) async-start(bf16[64,2,640]{2,1,0:T(2,128)(2,1)} %reshape.68), calls=%async_computation | async-start | bytes 327680 | tf_op jit(solution)/shard_map/all_to_all | solution.py:84
  182.9 24.6 %copy-start.9 = (bf16[1024,256]{1,0:T(8,128)(2,1)S(1)}, bf16[1024,256]{1,0:T(8,128)(2,1)}, u32[]{:S(2)}) copy-start(bf16[1024,256]{1,0:T(8,128)(2,1)} %copy-done.8) | copy-start | bytes 1572868
  182.9 24.6 %copy-start.18 = (bf16[2,256,512]{2,1,0:T(8,128)(2,1)S(1)}, bf16[2,256,512]{2,1,0:T(8,128)(2,1)}, u32[]{:S(2)}) copy-start(bf16[2,256,512]{2,1,0:T(8,128)(2,1)} %param.7) | copy-start | bytes 1572868
  182.9 24.6 %collective-permute-start.7 = (bf16[1024,256]{1,0:T(8,128)(2,1)}, bf16[1024,256]{1,0:T(8,128)(2,1)S(1)}, u32[]{:S(2)}, u32[]{:S(2)}) collective-permute-start(bf16[1024,256]{1,0:T(8,128)(2,1)} %convolution_convert_fusion), channel_id=1, source_target_pairs={{1,0},{2,1},{3,2},{4,3},{5,4},{6,5},{7,6},{8,7},{9,8},{10,9},{11,1... | collective-permute-start | bytes 1572872 | tf_op jit(solution)/shard_map/ppermute | solution.py:31
  197.0 24.0 %all-to-all-start.1 = ((f32[16,1,1280]{2,1,0:T(1,128)}), f32[16,1,1280]{2,1,0:T(1,128)S(1)}, u32[]{:S(2)}, u32[]{:S(2)}) async-start(f32[16,1,1280]{2,1,0:T(1,128)} %broadcast_in_dim.2), calls=%async_computation.1 | async-start | bytes 163840 | tf_op jit(solution)/shard_map/all_to_all | solution.py:87

commit v7 on v6

--- a/solution.py
+++ b/solution.py
@@ -66,13 +66,18 @@
     return total
 
 
-def near_sum(term):
+def near_sum(term, by_exchange):
     own_core = lax.axis_index("core")
     halves = term.reshape(term.shape[0], 2, term.shape[1] // 2)
     kept = lax.dynamic_index_in_dim(halves, own_core, 1, keepdims=False)
     given = lax.dynamic_index_in_dim(halves, 1 - own_core, 1, keepdims=False)
     moved = lax.ppermute(given.astype(jnp.bfloat16), "core", [(0, 1), (1, 0)])
-    return scatter_sum(kept + moved.astype(jnp.float32), ("x",))
+    term = kept + moved.astype(jnp.float32)
+    if not by_exchange:
+        return scatter_sum(term, ("x",))
+    size = lax.axis_size("x")
+    pieces = term.reshape(size, term.shape[0] // size, term.shape[1]).astype(jnp.bfloat16)
+    return lax.all_to_all(pieces, "x", 0, 0, tiled=True).astype(jnp.float32).sum(0)
 
 
 def far_sum(term):
@@ -163,7 +168,7 @@
         ).astype(jnp.bfloat16)
         arrived = return_past(sent_back, layer_at)
         operands = (earlier, current, gated_out, grad_preact, upstream)
-        near_list[layer_at] = near_sum(layer_term(operands, grad_scale))
+        near_list[layer_at] = near_sum(layer_term(operands, grad_scale), layer_at == 0)
         if layer_at > 0:
             near_list, arrived = lax.optimization_barrier((near_list, arrived))
         local_grad = upstream.astype(jnp.float32) + jnp.dot(

time: 223 us -> 220 us (0.987)
  blocking collectives: 0 us -> 10.7 us
  starting transfers between devices: 104 us -> 93.9 us
  waiting for transfers between devices: 86.8 us -> 81.5 us
    all_to_all x0 -> x1, blocking collectives: none -> 10.7 us  [near_sum(): lax.all_to_all(pieces, 'x', 0, 0, tiled=True).astype(jnp.float32).sum(0)]
    ppermute x6 -> x3, starting transfers between devices: 20.7 us -> 10.6 us  [scatter_sum(): lax.ppermute(piece.astype(jnp.bfloat16), axes, [(i, (i + shift) % size) f...]
    ppermute x6 -> x3, waiting for transfers between devices: 5.72 us -> 1.86 us  [scatter_sum(): lax.ppermute(piece.astype(jnp.bfloat16), axes, [(i, (i + shift) % size) f...]
  transfers between devices with their start and end apart: 14 -> 11, of which waited for: 8 -> 6; matrix products, arithmetic and copies ran while one was open for 5% -> 6% of each run, Pallas kernels for 0% -> 0%
where the time goes in v7:
time: 220 us; the launch traced here: 219 us
  starting transfers between devices  93.9 us (43%)
  waiting for transfers between devices  81.5 us (37%)
  matrix products  17.5 us (8%)
  blocking collectives  10.7 us (5%)
  local copies, waits for them, and re-layouts  9.57 us (4%)
  other arithmetic  4.52 us (2%)
    ppermute x4, waiting for transfers between devices, from_behind(): return lax.ppermute(array, axes, pairs)  68.2 us
    all_to_all x1, starting transfers between devices, far_sum(): lax.all_to_all(rows.astype(jnp.bfloat16), ('y', 'z_hi', 'z_lo'), 0, 0, ti...  41.2 us
    ppermute x4, starting transfers between devices, from_behind(): return lax.ppermute(array, axes, pairs)  28.3 us
    all_to_all x1, waiting for transfers between devices, far_sum(): gathered = lax.all_to_all(spread, ('y', 'z_hi', 'core'), 0, 0, tiled=True)  10.9 us
    all_to_all x1, blocking collectives, near_sum(): lax.all_to_all(pieces, 'x', 0, 0, tiled=True).astype(jnp.float32).sum(0)  10.7 us
    ppermute x3, starting transfers between devices, scatter_sum(): lax.ppermute(piece.astype(jnp.bfloat16), axes, [(i, (i + shift) % size) f...  10.6 us
    all_to_all x1, starting transfers between devices, far_sum(): gathered = lax.all_to_all(spread, ('y', 'z_hi', 'core'), 0, 0, tiled=True)  8.7 us
    ppermute x2, starting transfers between devices, near_sum(): moved = lax.ppermute(given.astype(jnp.bfloat16), 'core', [(0, 1), (1, 0)])  4.99 us
  transfers between devices with their start and end apart: 11, of which 6 were waited for; matrix products, arithmetic and copies ran while one was open for 6% of the time, Pallas kernels for 0%

profile of v7, /device:TPU:1, one launch (start us, length us, event | category | flops | bytes accessed | tf_op | source)
XLA Modules:
  0.0 219.0 jit_solution(5225265576856643569)
XLA Ops:
  0.6 4.5 %collective-permute-start = (bf16[1024,256]{1,0:T(8,128)(2,1)}, bf16[1024,256]{1,0:T(8,128)(2,1)S(1)}, u32[]{:S(2)}, u32[]{:S(2)}) collective-permute-start(bf16[1024,256]{1,0:T(8,128)(2,1)} %param.5), channel_id=1, source_target_pairs={{0,1},{1,2},{2,3},{3,4},{4,5},{5,6},{6,7},{7,8},{8,9},{9,10},{10,1... | collective-permute-start | bytes 1572872 | tf_op jit(solution)/shard_map/ppermute | solution.py:31
  5.2 1.6 fusion.17
  6.8 20.6 %collective-permute-done = bf16[1024,256]{1,0:T(8,128)(2,1)S(1)} collective-permute-done((bf16[1024,256]{1,0:T(8,128)(2,1)}, bf16[1024,256]{1,0:T(8,128)(2,1)S(1)}, u32[]{:S(2)}, u32[]{:S(2)}) %collective-permute-start) | collective-permute-done | bytes 524320 | tf_op jit(solution)/shard_map/ppermute | solution.py:31
  27.3 0.5 convolution_add_fusion.1
  27.8 0.3 copy-done.11
  28.1 0.4 multiply_convert_fusion.5
  28.6 0.8 copy-done
  29.4 0.4 fusion
  29.7 10.2 %collective-permute-start.1 = (bf16[1024,256]{1,0:T(8,128)(2,1)S(1)}, bf16[1024,256]{1,0:T(8,128)(2,1)}, u32[]{:S(2)}, u32[]{:S(2)}) collective-permute-start(bf16[1024,256]{1,0:T(8,128)(2,1)S(1)} %fusion), channel_id=1, source_target_pairs={{0,64},{32,96},{64,128},{96,160},{128,192},{160,224},{192,256},{22... | collective-permute-start | bytes 1572872 | tf_op jit(solution)/shard_map/ppermute | solution.py:31
  39.9 1.4 fusion.12
  41.4 37.4 %collective-permute-done.1 = bf16[1024,256]{1,0:T(8,128)(2,1)} collective-permute-done((bf16[1024,256]{1,0:T(8,128)(2,1)S(1)}, bf16[1024,256]{1,0:T(8,128)(2,1)}, u32[]{:S(2)}, u32[]{:S(2)}) %collective-permute-start.1) | collective-permute-done | bytes 524320 | tf_op jit(solution)/shard_map/ppermute | solution.py:31
  78.8 1.5 convolution_add_fusion
  80.3 0.8 multiply_convert_fusion.3
  81.1 0.3 fusion.46
  81.4 0.5 fusion.44
  81.9 0.1 copy-done.21
  82.1 1.5 fusion.45
  83.6 1.2 maximum_multiply_fusion
  84.8 2.0 mul.65
  86.8 0.6 constant_dynamic-slice_fusion.2
  87.5 2.1 collective-permute-start.2
  89.6 0.5 convolution_convert_fusion.1
  90.1 1.4 collective-permute-start.6
  91.6 0.6 constant_dynamic-slice_fusion.3
  92.2 0.1 bitcast_add_fusion.1
  92.3 3.2 %collective-permute-start.3 = (bf16[64,640]{1,0:T(8,128)(2,1)S(1)}, bf16[64,640]{1,0:T(8,128)(2,1)S(1)}, u32[]{:S(2)}, u32[]{:S(2)}) collective-permute-start(bf16[64,640]{1,0:T(8,128)(2,1)S(1)} %get-tuple-element.14), channel_id=1, source_target_pairs={{0,8},{8,16},{16,24},{24,0},{1,9},{9,17},{17,25},{25,1},{2,10},{10... | collective-permute-start | bytes 245768 | tf_op jit(solution)/shard_map/ppermute | solution.py:41
  95.5 4.4 %collective-permute-start.4 = (bf16[64,640]{1,0:T(8,128)(2,1)S(1)}, bf16[64,640]{1,0:T(8,128)(2,1)S(1)}, u32[]{:S(2)}, u32[]{:S(2)}) collective-permute-start(bf16[64,640]{1,0:T(8,128)(2,1)S(1)} %get-tuple-element.16), channel_id=1, source_target_pairs={{0,16},{8,24},{16,0},{24,8},{1,17},{9,25},{17,1},{25,9},{2,18},{10... | collective-permute-start | bytes 245768 | tf_op jit(solution)/shard_map/ppermute | solution.py:41
  99.9 3.1 %collective-permute-start.5 = (bf16[64,640]{1,0:T(8,128)(2,1)S(1)}, bf16[64,640]{1,0:T(8,128)(2,1)S(1)}, u32[]{:S(2)}, u32[]{:S(2)}) collective-permute-start(bf16[64,640]{1,0:T(8,128)(2,1)S(1)} %get-tuple-element.15), channel_id=1, source_target_pairs={{0,24},{8,0},{16,8},{24,16},{1,25},{9,1},{17,9},{25,17},{2,26},{10... | collective-permute-start | bytes 245768 | tf_op jit(solution)/shard_map/ppermute | solution.py:41
  103.0 0.5 convolution_add_fusion.5
  103.5 1.9 collective-permute-done.5
  105.4 10.2 %collective-permute-done.6 = bf16[1024,256]{1,0:T(8,128)(2,1)S(1)} collective-permute-done((bf16[1024,256]{1,0:T(8,128)(2,1)S(1)}, bf16[1024,256]{1,0:T(8,128)(2,1)S(1)}, u32[]{:S(2)}, u32[]{:S(2)}) %collective-permute-start.6) | collective-permute-done | bytes 524320 | tf_op jit(solution)/shard_map/ppermute | solution.py:31
  115.6 0.1 add_convert_fusion.1
  115.8 0.7 multiply_convert_fusion.1
  116.5 0.3 copy-done.1
  116.8 0.3 fusion.47
  117.2 0.5 convolution_bitcast_fusion
  117.7 0.2 copy-done.24
  117.8 0.4 copy-done.12
  118.3 0.5 convolution_bitcast_fusion.1
  118.8 0.1 maximum_multiply_fusion.1
  118.9 0.7 mul.73
  119.6 0.6 constant_dynamic-slice_fusion
  120.2 2.9 %collective-permute-start.8 = (bf16[256,640]{1,0:T(8,128)(2,1)S(1)}, bf16[256,640]{1,0:T(8,128)(2,1)S(1)}, u32[]{:S(2)}, u32[]{:S(2)}) collective-permute-start(bf16[256,640]{1,0:T(8,128)(2,1)S(1)} %bitcast.110), channel_id=1, source_target_pairs={{0,32},{32,0},{1,33},{33,1},{2,34},{34,2},{3,35},{35,3},{4,36},{36... | collective-permute-start | bytes 983048 | tf_op jit(solution)/shard_map/ppermute | solution.py:74
  123.1 0.6 constant_dynamic-slice_fusion.1
  123.7 0.5 collective-permute-done.8
  124.2 0.1 fusion.8
  124.3 10.7 %all_to_all.15 = bf16[4,64,640]{2,1,0:T(8,128)(2,1)S(1)} all-to-all(bf16[4,64,640]{2,1,0:T(8,128)(2,1)S(1)} %bitcast.107), channel_id=1, replica_groups=mesh['y'=4,'z_hi'=2,'core'=2,'x'=4,'z_lo'=8] {'x'}, dimensions={0} | all-to-all | bytes 655360 | tf_op jit(solution)/shard_map/all_to_all | solution.py:80
  135.1 0.5 broadcast.39
  135.6 0.7 reduce.3
  136.3 0.7 reshape.63
  137.0 41.2 %all-to-all-start.1 = ((bf16[64,2,640]{2,1,0:T(2,128)(2,1)}), bf16[64,2,640]{2,1,0:T(2,128)(2,1)S(1)}, u32[]{:S(2)}, u32[]{:S(2)}) async-start(bf16[64,2,640]{2,1,0:T(2,128)(2,1)} %reshape.63), calls=%async_computation.1 | async-start | bytes 327680 | tf_op jit(solution)/shard_map/all_to_all | solution.py:89
  178.3 2.5 %convolution_convert_fusion = bf16[1024,256]{1,0:T(8,128)(2,1)} fusion(bf16[2,256,512]{2,1,0:T(8,128)(2,1)S(1)} %copy-done.10, bf16[1024,256]{0,1:T(8,128)(2,1)} %copy-done.24, bf16[1024,256]{0,1:T(8,128)(2,1)} %copy-done.23), kind=kOutput, calls=%fused_computation.8 | convolution fusion | flops 270794752 | bytes 1835008 | tf_op jit(solution)/shard_map/dot_general | solution.py:166
  180.8 12.2 %collective-permute-start.7 = (bf16[1024,256]{1,0:T(8,128)(2,1)}, bf16[1024,256]{1,0:T(8,128)(2,1)S(1)}, u32[]{:S(2)}, u32[]{:S(2)}) collective-permute-start(bf16[1024,256]{1,0:T(8,128)(2,1)} %convolution_convert_fusion), channel_id=1, source_target_pairs={{1,0},{2,1},{3,2},{4,3},{5,4},{6,5},{7,6},{8,7},{9,8},{10,9},{11,1... | collective-permute-start | bytes 1572872 | tf_op jit(solution)/shard_map/ppermute | solution.py:31
  193.0 0.1 reshape.64
  193.1 0.3 convert_reduce_fusion
  193.5 0.7 broadcast_in_dim.2
  194.1 8.7 %all-to-all-start.2 = ((f32[16,1,1280]{2,1,0:T(1,128)}), f32[16,1,1280]{2,1,0:T(1,128)S(1)}, u32[]{:S(2)}, u32[]{:S(2)}) async-start(f32[16,1,1280]{2,1,0:T(1,128)} %broadcast_in_dim.2), calls=%async_computation.2 | async-start | bytes 163840 | tf_op jit(solution)/shard_map/all_to_all | solution.py:92
  202.8 1.1 fusion.1
  204.0 2.5 %add_convert_fusion = bf16[1024,256]{1,0:T(8,128)(2,1)} fusion(bf16[1024,256]{1,0:T(8,128)(2,1)S(1)} %collective-permute-done.7, bf16[1024,256]{1,0:T(8,128)(2,1)S(1)} %add_convert_fusion.1, bf16[2,256,512]{2,1,0:T(8,128)(2,1)S(1)} %copy-done.16, bf16[1024,256]{0,1:T(8,128)(2,1)} %copy-done.24, bf16[1024,256]{0,1:T(8,128)(2,1)} %copy-done.23), kind=kOutput, calls=%fused_computation.26 | convolution fusion | flops 271843328 | bytes 2883584 | tf_op jit(solution)/shard_map/dot_general | solution.py:174
  206.5 10.9 %all-to-all-done.2 = f32[16,1,1280]{2,1,0:T(1,128)S(1)} async-done(((f32[16,1,1280]{2,1,0:T(1,128)}), f32[16,1,1280]{2,1,0:T(1,128)S(1)}, u32[]{:S(2)}, u32[]{:S(2)}) %all-to-all-start.2) | async-done | bytes 81952 | tf_op jit(solution)/shard_map/all_to_all | solution.py:92
  217.4 0.2 reduce.2
  217.6 0.1 reshape.59
  217.7 0.6 pad_maximum_fusion.4
  218.4 0.6 pad_maximum_fusion.2
  (62 shorter events, 0.4 us)
Async XLA Ops:
  0.6 26.7 %copy-start.8 = (bf16[2,256,512]{2,1,0:T(8,128)(2,1)S(1)}, bf16[2,256,512]{2,1,0:T(8,128)(2,1)}, u32[]{:S(2)}) copy-start(bf16[2,256,512]{2,1,0:T(8,128)(2,1)} %param.6) | copy-start | bytes 1572868
  0.6 26.7 %collective-permute-start = (bf16[1024,256]{1,0:T(8,128)(2,1)}, bf16[1024,256]{1,0:T(8,128)(2,1)S(1)}, u32[]{:S(2)}, u32[]{:S(2)}) collective-permute-start(bf16[1024,256]{1,0:T(8,128)(2,1)} %param.5), channel_id=1, source_target_pairs={{0,1},{1,2},{2,3},{3,4},{4,5},{5,6},{6,7},{7,8},{8,9},{9,10},{10,1... | collective-permute-start | bytes 1572872 | tf_op jit(solution)/shard_map/ppermute | solution.py:31
  27.3 0.8 copy-start.11
  28.1 1.2 copy-start.6
  28.1 1.2 copy-start.17
  28.6 0.8 copy-start
  29.7 51.7 %copy-start.2 = (bf16[1024,256]{1,0:T(8,128)(2,1)}, bf16[1024,256]{1,0:T(8,128)(2,1)S(1)}, u32[]{:S(2)}) copy-start(bf16[1024,256]{1,0:T(8,128)(2,1)S(1)} %fusion) | copy-start | bytes 1572868
  29.7 49.0 %collective-permute-start.1 = (bf16[1024,256]{1,0:T(8,128)(2,1)S(1)}, bf16[1024,256]{1,0:T(8,128)(2,1)}, u32[]{:S(2)}, u32[]{:S(2)}) collective-permute-start(bf16[1024,256]{1,0:T(8,128)(2,1)S(1)} %fusion), channel_id=1, source_target_pairs={{0,64},{32,96},{64,128},{96,160},{128,192},{160,224},{192,256},{22... | collective-permute-start | bytes 1572872 | tf_op jit(solution)/shard_map/ppermute | solution.py:31
  41.3 39.0 %copy-start.13 = (bf16[1024,256]{1,0:T(8,128)(2,1)S(1)}, bf16[1024,256]{1,0:T(8,128)(2,1)}, u32[]{:S(2)}) copy-start(bf16[1024,256]{1,0:T(8,128)(2,1)} %param.9) | copy-start | bytes 1572868
  81.1 0.8 copy-start.4
  81.1 1.0 copy-start.21
  81.1 2.5 %copy-start.19 = (bf16[1024,256]{0,1:T(8,128)(2,1)}, bf16[1024,256]{0,1:T(8,128)(2,1)S(1)}, u32[]{:S(2)}) copy-start(bf16[1024,256]{0,1:T(8,128)(2,1)S(1)} %get-tuple-element.11) | copy-start | bytes 1572868
  86.8 2.8 %copy-start.9 = (bf16[2,256,512]{2,1,0:T(8,128)(2,1)S(1)}, bf16[2,256,512]{2,1,0:T(8,128)(2,1)}, u32[]{:S(2)}) copy-start(bf16[2,256,512]{2,1,0:T(8,128)(2,1)} %param.6) | copy-start | bytes 1572868
  86.8 2.8 %copy-start.20 = (bf16[1024,256]{0,1:T(8,128)(2,1)S(1)}, bf16[1024,256]{0,1:T(8,128)(2,1)}, u32[]{:S(2)}) copy-start(bf16[1024,256]{0,1:T(8,128)(2,1)} %copy-done.19) | copy-start | bytes 1572868
  86.8 2.8 %copy-start.22 = (bf16[1024,256]{0,1:T(8,128)(2,1)S(1)}, bf16[1024,256]{0,1:T(8,128)(2,1)}, u32[]{:S(2)}) copy-start(bf16[1024,256]{0,1:T(8,128)(2,1)} %copy-done.21) | copy-start | bytes 1572868
  87.5 4.7 %collective-permute-start.2 = (bf16[256,640]{1,0:T(8,128)(2,1)S(1)}, bf16[256,640]{1,0:T(8,128)(2,1)S(1)}, u32[]{:S(2)}, u32[]{:S(2)}) collective-permute-start(bf16[256,640]{1,0:T(8,128)(2,1)S(1)} %bitcast.109), channel_id=1, source_target_pairs={{0,32},{32,0},{1,33},{33,1},{2,34},{34,2},{3,35},{35,3},{4,36},{36... | collective-permute-start | bytes 983048 | tf_op jit(solution)/shard_map/ppermute | solution.py:74
  90.1 12.8 %copy-start.14 = (bf16[1024,256]{1,0:T(8,128)(2,1)S(1)}, bf16[1024,256]{1,0:T(8,128)(2,1)}, u32[]{:S(2)}) copy-start(bf16[1024,256]{1,0:T(8,128)(2,1)} %param.9) | copy-start | bytes 1572868
  90.1 12.8 %copy-start.15 = (bf16[2,256,512]{2,1,0:T(8,128)(2,1)S(1)}, bf16[2,256,512]{2,1,0:T(8,128)(2,1)}, u32[]{:S(2)}) copy-start(bf16[2,256,512]{2,1,0:T(8,128)(2,1)} %param.7) | copy-start | bytes 1572868
  90.1 25.5 %collective-permute-start.6 = (bf16[1024,256]{1,0:T(8,128)(2,1)S(1)}, bf16[1024,256]{1,0:T(8,128)(2,1)S(1)}, u32[]{:S(2)}, u32[]{:S(2)}) collective-permute-start(bf16[1024,256]{1,0:T(8,128)(2,1)S(1)} %convolution_convert_fusion.1), channel_id=1, source_target_pairs={{64,0},{96,32},{128,64},{160,96},{192,128},{224,160},{256,192},{28... | collective-permute-start | bytes 1572872 | tf_op jit(solution)/shard_map/ppermute | solution.py:31
  92.3 11.2 %collective-permute-start.3 = (bf16[64,640]{1,0:T(8,128)(2,1)S(1)}, bf16[64,640]{1,0:T(8,128)(2,1)S(1)}, u32[]{:S(2)}, u32[]{:S(2)}) collective-permute-start(bf16[64,640]{1,0:T(8,128)(2,1)S(1)} %get-tuple-element.14), channel_id=1, source_target_pairs={{0,8},{8,16},{16,24},{24,0},{1,9},{9,17},{17,25},{25,1},{2,10},{10... | collective-permute-start | bytes 245768 | tf_op jit(solution)/shard_map/ppermute | solution.py:41
  95.5 8.0 %collective-permute-start.4 = (bf16[64,640]{1,0:T(8,128)(2,1)S(1)}, bf16[64,640]{1,0:T(8,128)(2,1)S(1)}, u32[]{:S(2)}, u32[]{:S(2)}) collective-permute-start(bf16[64,640]{1,0:T(8,128)(2,1)S(1)} %get-tuple-element.16), channel_id=1, source_target_pairs={{0,16},{8,24},{16,0},{24,8},{1,17},{9,25},{17,1},{25,9},{2,18},{10... | collective-permute-start | bytes 245768 | tf_op jit(solution)/shard_map/ppermute | solution.py:41
  99.9 5.5 %collective-permute-start.5 = (bf16[64,640]{1,0:T(8,128)(2,1)S(1)}, bf16[64,640]{1,0:T(8,128)(2,1)S(1)}, u32[]{:S(2)}, u32[]{:S(2)}) collective-permute-start(bf16[64,640]{1,0:T(8,128)(2,1)S(1)} %get-tuple-element.15), channel_id=1, source_target_pairs={{0,24},{8,0},{16,8},{24,16},{1,25},{9,1},{17,9},{25,17},{2,26},{10... | collective-permute-start | bytes 245768 | tf_op jit(solution)/shard_map/ppermute | solution.py:41
  103.5 12.3 %copy-start.18 = (bf16[2,256,256]{2,1,0:T(8,128)(2,1)S(1)}, bf16[2,256,256]{2,1,0:T(8,128)(2,1)}, u32[]{:S(2)}) copy-start(bf16[2,256,256]{2,1,0:T(8,128)(2,1)} %param.8) | copy-start | bytes 786436
  115.8 1.0 copy-start.1
  115.8 1.3 copy-start.7
  116.8 0.8 copy-start.23
  116.8 1.0 copy-start.24
  116.8 1.4 copy-start.12
  120.2 3.9 %collective-permute-start.8 = (bf16[256,640]{1,0:T(8,128)(2,1)S(1)}, bf16[256,640]{1,0:T(8,128)(2,1)S(1)}, u32[]{:S(2)}, u32[]{:S(2)}) collective-permute-start(bf16[256,640]{1,0:T(8,128)(2,1)S(1)} %bitcast.110), channel_id=1, source_target_pairs={{0,32},{32,0},{1,33},{33,1},{2,34},{34,2},{3,35},{35,3},{4,36},{36... | collective-permute-start | bytes 983048 | tf_op jit(solution)/shard_map/ppermute | solution.py:74
  123.7 54.6 %copy-start.10 = (bf16[2,256,512]{2,1,0:T(8,128)(2,1)S(1)}, bf16[2,256,512]{2,1,0:T(8,128)(2,1)}, u32[]{:S(2)}) copy-start(bf16[2,256,512]{2,1,0:T(8,128)(2,1)} %param.6) | copy-start | bytes 1572868
  137.0 65.8 %copy-start.3 = (bf16[1024,256]{1,0:T(8,128)(2,1)S(1)}, bf16[1024,256]{1,0:T(8,128)(2,1)}, u32[]{:S(2)}) copy-start(bf16[1024,256]{1,0:T(8,128)(2,1)} %copy-done.2) | copy-start | bytes 1572868
  137.0 65.8 %copy-start.5 = (bf16[1024,256]{0,1:T(8,128)(2,1)S(1)}, bf16[1024,256]{0,1:T(8,128)(2,1)}, u32[]{:S(2)}) copy-start(bf16[1024,256]{0,1:T(8,128)(2,1)} %copy-done.4) | copy-start | bytes 1572868
  137.0 56.0 %all-to-all-start.1 = ((bf16[64,2,640]{2,1,0:T(2,128)(2,1)}), bf16[64,2,640]{2,1,0:T(2,128)(2,1)S(1)}, u32[]{:S(2)}, u32[]{:S(2)}) async-start(bf16[64,2,640]{2,1,0:T(2,128)(2,1)} %reshape.63), calls=%async_computation.1 | async-start | bytes 327680 | tf_op jit(solution)/shard_map/all_to_all | solution.py:89
  180.8 23.2 %copy-start.16 = (bf16[2,256,512]{2,1,0:T(8,128)(2,1)S(1)}, bf16[2,256,512]{2,1,0:T(8,128)(2,1)}, u32[]{:S(2)}) copy-start(bf16[2,256,512]{2,1,0:T(8,128)(2,1)} %param.7) | copy-start | bytes 1572868
  180.8 23.2 %collective-permute-start.7 = (bf16[1024,256]{1,0:T(8,128)(2,1)}, bf16[1024,256]{1,0:T(8,128)(2,1)S(1)}, u32[]{:S(2)}, u32[]{:S(2)}) collective-permute-start(bf16[1024,256]{1,0:T(8,128)(2,1)} %convolution_convert_fusion), channel_id=1, source_target_pairs={{1,0},{2,1},{3,2},{4,3},{5,4},{6,5},{7,6},{8,7},{9,8},{10,9},{11,1... | collective-permute-start | bytes 1572872 | tf_op jit(solution)/shard_map/ppermute | solution.py:31
  194.1 23.3 %all-to-all-start.2 = ((f32[16,1,1280]{2,1,0:T(1,128)}), f32[16,1,1280]{2,1,0:T(1,128)S(1)}, u32[]{:S(2)}, u32[]{:S(2)}) async-start(f32[16,1,1280]{2,1,0:T(1,128)} %broadcast_in_dim.2), calls=%async_computation.2 | async-start | bytes 163840 | tf_op jit(solution)/shard_map/all_to_all | solution.py:92

commit v8 on v6

--- a/solution.py
+++ b/solution.py
@@ -72,16 +72,17 @@
     kept = lax.dynamic_index_in_dim(halves, own_core, 1, keepdims=False)
     given = lax.dynamic_index_in_dim(halves, 1 - own_core, 1, keepdims=False)
     moved = lax.ppermute(given.astype(jnp.bfloat16), "core", [(0, 1), (1, 0)])
-    return scatter_sum(kept + moved.astype(jnp.float32), ("x",))
+    return kept + moved.astype(jnp.float32)
 
 
 def far_sum(term):
+    x_size = lax.axis_size("x")
     lo_size = lax.axis_size("z_lo")
     hi_size = lax.axis_size("y") * lax.axis_size("z_hi")
     core_size = lax.axis_size("core")
-    rows = term.reshape(lo_size, hi_size, term.shape[1]).transpose(1, 0, 2)
-    rows = rows.reshape(hi_size * lo_size, 1, term.shape[1])
-    row = lax.all_to_all(rows.astype(jnp.bfloat16), ("y", "z_hi", "z_lo"), 0, 0, tiled=True)
+    rows = term.reshape(x_size, lo_size, hi_size, term.shape[1]).transpose(2, 0, 1, 3)
+    rows = rows.reshape(hi_size * x_size * lo_size, 1, term.shape[1])
+    row = lax.all_to_all(rows.astype(jnp.bfloat16), ("y", "z_hi", "x", "z_lo"), 0, 0, tiled=True)
     row = row.astype(jnp.float32).sum(0)
     spread = jnp.broadcast_to(row[None], (hi_size * core_size, *row.shape))
     gathered = lax.all_to_all(spread, ("y", "z_hi", "core"), 0, 0, tiled=True)

time: 223 us -> 245 us (1.099)
  waiting for transfers between devices: 86.8 us -> 114 us
  starting transfers between devices: 104 us -> 92.1 us
  matrix products: 16.3 us -> 19.2 us
    all_to_all x1, waiting for transfers between devices: 1.49 us -> 22.3 us  [far_sum(): lax.all_to_all(rows.astype(jnp.bfloat16), ('y', 'z_hi', 'x', 'z_lo'), 0,...]
    ppermute x6 -> x0, starting transfers between devices: 20.7 us -> none  [scatter_sum(): lax.ppermute(piece.astype(jnp.bfloat16), axes, [(i, (i + shift) % size) f...]
    ppermute x4, waiting for transfers between devices: 68.2 us -> 81.4 us  [from_behind(): return lax.ppermute(array, axes, pairs)]
    all_to_all x1, starting transfers between devices: 41 us -> 47.3 us  [far_sum(): lax.all_to_all(rows.astype(jnp.bfloat16), ('y', 'z_hi', 'x', 'z_lo'), 0,...]
    ppermute x6 -> x0, waiting for transfers between devices: 5.72 us -> none  [scatter_sum(): lax.ppermute(piece.astype(jnp.bfloat16), axes, [(i, (i + shift) % size) f...]
    all_to_all x1, starting transfers between devices: 9.36 us -> 12.3 us  [far_sum(): gathered = lax.all_to_all(spread, ('y', 'z_hi', 'core'), 0, 0, tiled=True)]
  transfers between devices with their start and end apart: 14 -> 8, of which waited for: 8 -> 6; matrix products, arithmetic and copies ran while one was open for 5% -> 6% of each run, Pallas kernels for 0% -> 0%
where the time goes in v8:
time: 245 us; the launch traced here: 242 us
  waiting for transfers between devices  114 us (47%)
  starting transfers between devices  92.1 us (38%)
  matrix products  19.2 us (8%)
  local copies, waits for them, and re-layouts  10.2 us (4%)
  other arithmetic  5.76 us (2%)
    ppermute x4, waiting for transfers between devices, from_behind(): return lax.ppermute(array, axes, pairs)  81.4 us
    all_to_all x1, starting transfers between devices, far_sum(): lax.all_to_all(rows.astype(jnp.bfloat16), ('y', 'z_hi', 'x', 'z_lo'), 0,...  47.3 us
    ppermute x4, starting transfers between devices, from_behind(): return lax.ppermute(array, axes, pairs)  27.3 us
    all_to_all x1, waiting for transfers between devices, far_sum(): lax.all_to_all(rows.astype(jnp.bfloat16), ('y', 'z_hi', 'x', 'z_lo'), 0,...  22.3 us
    all_to_all x1, starting transfers between devices, far_sum(): gathered = lax.all_to_all(spread, ('y', 'z_hi', 'core'), 0, 0, tiled=True)  12.3 us
    all_to_all x1, waiting for transfers between devices, far_sum(): gathered = lax.all_to_all(spread, ('y', 'z_hi', 'core'), 0, 0, tiled=True)  9.83 us
    ppermute x2, starting transfers between devices, near_sum(): moved = lax.ppermute(given.astype(jnp.bfloat16), 'core', [(0, 1), (1, 0)])  5.12 us
  transfers between devices with their start and end apart: 8, of which 6 were waited for; matrix products, arithmetic and copies ran while one was open for 6% of the time, Pallas kernels for 0%

profile of v8, /device:TPU:1, one launch (start us, length us, event | category | flops | bytes accessed | tf_op | source)
XLA Modules:
  0.0 242.5 jit_solution(8740682643671560659)
XLA Ops:
  0.6 4.5 %collective-permute-start = (bf16[1024,256]{1,0:T(8,128)(2,1)}, bf16[1024,256]{1,0:T(8,128)(2,1)S(1)}, u32[]{:S(2)}, u32[]{:S(2)}) collective-permute-start(bf16[1024,256]{1,0:T(8,128)(2,1)} %param.5), channel_id=1, source_target_pairs={{0,1},{1,2},{2,3},{3,4},{4,5},{5,6},{6,7},{7,8},{8,9},{9,10},{10,1... | collective-permute-start | bytes 1572872 | tf_op jit(solution)/shard_map/ppermute | solution.py:31
  5.2 1.6 fusion.17
  6.8 20.6 %collective-permute-done = bf16[1024,256]{1,0:T(8,128)(2,1)S(1)} collective-permute-done((bf16[1024,256]{1,0:T(8,128)(2,1)}, bf16[1024,256]{1,0:T(8,128)(2,1)S(1)}, u32[]{:S(2)}, u32[]{:S(2)}) %collective-permute-start) | collective-permute-done | bytes 524320 | tf_op jit(solution)/shard_map/ppermute | solution.py:31
  27.3 0.5 convolution_add_fusion.1
  27.8 0.3 copy-done.10
  28.1 0.4 multiply_convert_fusion.5
  28.6 0.8 copy-done
  29.4 0.4 fusion
  29.7 10.2 %collective-permute-start.1 = (bf16[1024,256]{1,0:T(8,128)(2,1)S(1)}, bf16[1024,256]{1,0:T(8,128)(2,1)}, u32[]{:S(2)}, u32[]{:S(2)}) collective-permute-start(bf16[1024,256]{1,0:T(8,128)(2,1)S(1)} %fusion), channel_id=1, source_target_pairs={{0,64},{32,96},{64,128},{96,160},{128,192},{160,224},{192,256},{22... | collective-permute-start | bytes 1572872 | tf_op jit(solution)/shard_map/ppermute | solution.py:31
  39.9 1.4 fusion.12
  41.4 37.4 %collective-permute-done.1 = bf16[1024,256]{1,0:T(8,128)(2,1)} collective-permute-done((bf16[1024,256]{1,0:T(8,128)(2,1)S(1)}, bf16[1024,256]{1,0:T(8,128)(2,1)}, u32[]{:S(2)}, u32[]{:S(2)}) %collective-permute-start.1) | collective-permute-done | bytes 524320 | tf_op jit(solution)/shard_map/ppermute | solution.py:31
  78.8 1.5 convolution_add_fusion
  80.3 0.8 multiply_convert_fusion.3
  81.1 0.0 copy-start.4
  81.1 0.5 fusion.39
  81.6 1.3 convolution_convert_fusion.1
  82.9 0.3 fusion.41
  83.2 1.5 fusion.40
  84.8 1.2 maximum_multiply_fusion
  86.0 2.0 mul.65
  88.0 0.0 copy-start.13
  88.0 0.6 constant_dynamic-slice_fusion.2
  88.7 2.2 collective-permute-start.2
  90.9 0.6 constant_dynamic-slice_fusion.3
  91.5 1.3 collective-permute-start.3
  92.8 0.5 convolution_add_fusion.5
  93.4 0.0 copy-start.17
  93.4 0.1 bitcast_add_fusion.1
  93.4 23.4 %collective-permute-done.3 = bf16[1024,256]{1,0:T(8,128)(2,1)S(1)} collective-permute-done((bf16[1024,256]{1,0:T(8,128)(2,1)S(1)}, bf16[1024,256]{1,0:T(8,128)(2,1)S(1)}, u32[]{:S(2)}, u32[]{:S(2)}) %collective-permute-start.3) | collective-permute-done | bytes 524320 | tf_op jit(solution)/shard_map/ppermute | solution.py:31
  116.9 0.1 add_convert_fusion.1
  117.0 0.7 multiply_convert_fusion.1
  117.7 0.3 copy-done.1
  118.0 0.3 fusion.42
  118.4 0.5 convolution_bitcast_fusion
  118.9 0.2 copy-done.25
  119.0 0.4 copy-done.11
  119.5 0.5 convolution_bitcast_fusion.1
  120.0 0.1 maximum_multiply_fusion.1
  120.1 0.7 mul.73
  120.8 0.6 constant_dynamic-slice_fusion
  121.5 2.9 %collective-permute-start.5 = (bf16[256,640]{1,0:T(8,128)(2,1)S(1)}, bf16[256,640]{1,0:T(8,128)(2,1)S(1)}, u32[]{:S(2)}, u32[]{:S(2)}) collective-permute-start(bf16[256,640]{1,0:T(8,128)(2,1)S(1)} %bitcast.91), channel_id=1, source_target_pairs={{0,32},{32,0},{1,33},{33,1},{2,34},{34,2},{3,35},{35,3},{4,36},{36... | collective-permute-start | bytes 983048 | tf_op jit(solution)/shard_map/ppermute | solution.py:74
  124.3 0.6 constant_dynamic-slice_fusion.1
  124.9 0.5 collective-permute-done.5
  125.4 0.1 fusion.8
  125.5 0.1 pad_maximum_fusion.2
  125.5 0.1 copy.28
  125.7 0.5 broadcast.36
  126.2 1.1 reduce.2
  127.3 1.0 reshape.54
  128.3 47.3 %all-to-all-start = ((bf16[256,2,640]{2,1,0:T(2,128)(2,1)}), bf16[256,2,640]{2,1,0:T(2,128)(2,1)S(1)}, u32[]{:S(2)}, u32[]{:S(2)}) async-start(bf16[256,2,640]{2,1,0:T(2,128)(2,1)} %reshape.54), calls=%async_computation | async-start | bytes 1310720 | tf_op jit(solution)/shard_map/all_to_all | solution.py:85
  175.6 2.3 convolution_convert_fusion
  177.9 11.4 %collective-permute-start.4 = (bf16[1024,256]{1,0:T(8,128)(2,1)}, bf16[1024,256]{1,0:T(8,128)(2,1)}, u32[]{:S(2)}, u32[]{:S(2)}) collective-permute-start(bf16[1024,256]{1,0:T(8,128)(2,1)} %convolution_convert_fusion), channel_id=1, source_target_pairs={{1,0},{2,1},{3,2},{4,3},{5,4},{6,5},{7,6},{8,7},{9,8},{10,9},{11,1... | collective-permute-start | bytes 1572872 | tf_op jit(solution)/shard_map/ppermute | solution.py:31
  189.3 22.3 %all-to-all-done = bf16[256,2,640]{2,1,0:T(2,128)(2,1)S(1)} async-done(((bf16[256,2,640]{2,1,0:T(2,128)(2,1)}), bf16[256,2,640]{2,1,0:T(2,128)(2,1)S(1)}, u32[]{:S(2)}, u32[]{:S(2)}) %all-to-all-start) | async-done | bytes 655392 | tf_op jit(solution)/shard_map/all_to_all | solution.py:85
  211.6 0.5 reshape.55
  212.2 1.2 convert_reduce_fusion
  213.4 0.7 broadcast_in_dim.2
  214.0 12.3 %all-to-all-start.1 = ((f32[16,1,1280]{2,1,0:T(1,128)}), f32[16,1,1280]{2,1,0:T(1,128)S(1)}, u32[]{:S(2)}, u32[]{:S(2)}) async-start(f32[16,1,1280]{2,1,0:T(1,128)} %broadcast_in_dim.2), calls=%async_computation.1 | async-start | bytes 163840 | tf_op jit(solution)/shard_map/all_to_all | solution.py:88
  226.4 2.1 fusion.1
  228.4 2.6 %add_convert_fusion = bf16[1024,256]{1,0:T(8,128)(2,1)} fusion(bf16[1024,256]{1,0:T(8,128)(2,1)} %collective-permute-done.4, bf16[1024,256]{1,0:T(8,128)(2,1)S(1)} %add_convert_fusion.1, bf16[2,256,512]{2,1,0:T(8,128)(2,1)S(1)} %copy-done.15, bf16[1024,256]{0,1:T(8,128)(2,1)} %copy-done.25, bf16[1024,256]{0,1:T(8,128)(2,1)} %copy-done.23), kind=kOutput, calls=%fused_computation.27 | convolution fusion | flops 271843328 | bytes 2883584 | tf_op jit(solution)/shard_map/dot_general | solution.py:170
  231.1 9.8 %all-to-all-done.1 = f32[16,1,1280]{2,1,0:T(1,128)S(1)} async-done(((f32[16,1,1280]{2,1,0:T(1,128)}), f32[16,1,1280]{2,1,0:T(1,128)S(1)}, u32[]{:S(2)}, u32[]{:S(2)}) %all-to-all-start.1) | async-done | bytes 81952 | tf_op jit(solution)/shard_map/all_to_all | solution.py:88
  240.9 0.2 reduce.1
  241.1 0.1 reshape.50
  241.2 0.6 pad_maximum_fusion.5
  241.8 0.6 pad_maximum_fusion.3
  (54 shorter events, 0.2 us)
Async XLA Ops:
  0.6 26.7 %copy-start.8 = (bf16[2,256,512]{2,1,0:T(8,128)(2,1)S(1)}, bf16[2,256,512]{2,1,0:T(8,128)(2,1)}, u32[]{:S(2)}) copy-start(bf16[2,256,512]{2,1,0:T(8,128)(2,1)} %param.6) | copy-start | bytes 1572868
  0.6 26.7 %collective-permute-start = (bf16[1024,256]{1,0:T(8,128)(2,1)}, bf16[1024,256]{1,0:T(8,128)(2,1)S(1)}, u32[]{:S(2)}, u32[]{:S(2)}) collective-permute-start(bf16[1024,256]{1,0:T(8,128)(2,1)} %param.5), channel_id=1, source_target_pairs={{0,1},{1,2},{2,3},{3,4},{4,5},{5,6},{6,7},{7,8},{8,9},{9,10},{10,1... | collective-permute-start | bytes 1572872 | tf_op jit(solution)/shard_map/ppermute | solution.py:31
  27.3 0.8 copy-start.10
  28.1 1.2 copy-start.6
  28.1 1.2 copy-start.16
  28.6 0.8 copy-start
  29.7 51.4 %copy-start.2 = (bf16[1024,256]{1,0:T(8,128)(2,1)}, bf16[1024,256]{1,0:T(8,128)(2,1)S(1)}, u32[]{:S(2)}) copy-start(bf16[1024,256]{1,0:T(8,128)(2,1)S(1)} %fusion) | copy-start | bytes 1572868
  29.7 49.0 %collective-permute-start.1 = (bf16[1024,256]{1,0:T(8,128)(2,1)S(1)}, bf16[1024,256]{1,0:T(8,128)(2,1)}, u32[]{:S(2)}, u32[]{:S(2)}) collective-permute-start(bf16[1024,256]{1,0:T(8,128)(2,1)S(1)} %fusion), channel_id=1, source_target_pairs={{0,64},{32,96},{64,128},{96,160},{128,192},{160,224},{192,256},{22... | collective-permute-start | bytes 1572872 | tf_op jit(solution)/shard_map/ppermute | solution.py:31
  41.3 39.0 %copy-start.12 = (bf16[1024,256]{1,0:T(8,128)(2,1)S(1)}, bf16[1024,256]{1,0:T(8,128)(2,1)}, u32[]{:S(2)}) copy-start(bf16[1024,256]{1,0:T(8,128)(2,1)} %param.9) | copy-start | bytes 1572868
  81.1 1.8 copy-start.4
  81.1 2.1 copy-start.19
  81.1 2.1 copy-start.21
  88.0 3.5 %copy-start.18 = (bf16[1024,256]{1,0:T(8,128)(2,1)S(1)}, bf16[1024,256]{1,0:T(8,128)(2,1)}, u32[]{:S(2)}) copy-start(bf16[1024,256]{1,0:T(8,128)(2,1)} %convolution_convert_fusion.1) | copy-start | bytes 1572868
  88.0 4.8 %copy-start.13 = (bf16[1024,256]{1,0:T(8,128)(2,1)S(1)}, bf16[1024,256]{1,0:T(8,128)(2,1)}, u32[]{:S(2)}) copy-start(bf16[1024,256]{1,0:T(8,128)(2,1)} %param.9) | copy-start | bytes 1572868
  88.0 4.8 %copy-start.14 = (bf16[2,256,512]{2,1,0:T(8,128)(2,1)S(1)}, bf16[2,256,512]{2,1,0:T(8,128)(2,1)}, u32[]{:S(2)}) copy-start(bf16[2,256,512]{2,1,0:T(8,128)(2,1)} %param.7) | copy-start | bytes 1572868
  88.0 4.8 %copy-start.20 = (bf16[1024,256]{0,1:T(8,128)(2,1)S(1)}, bf16[1024,256]{0,1:T(8,128)(2,1)}, u32[]{:S(2)}) copy-start(bf16[1024,256]{0,1:T(8,128)(2,1)} %copy-done.19) | copy-start | bytes 1572868
  88.0 4.8 %copy-start.22 = (bf16[1024,256]{0,1:T(8,128)(2,1)S(1)}, bf16[1024,256]{0,1:T(8,128)(2,1)}, u32[]{:S(2)}) copy-start(bf16[1024,256]{0,1:T(8,128)(2,1)} %copy-done.21) | copy-start | bytes 1572868
  88.7 4.7 %collective-permute-start.2 = (bf16[256,640]{1,0:T(8,128)(2,1)S(1)}, bf16[256,640]{1,0:T(8,128)(2,1)S(1)}, u32[]{:S(2)}, u32[]{:S(2)}) collective-permute-start(bf16[256,640]{1,0:T(8,128)(2,1)S(1)} %bitcast.90), channel_id=1, source_target_pairs={{0,32},{32,0},{1,33},{33,1},{2,34},{34,2},{3,35},{35,3},{4,36},{36... | collective-permute-start | bytes 983048 | tf_op jit(solution)/shard_map/ppermute | solution.py:74
  91.5 25.4 %collective-permute-start.3 = (bf16[1024,256]{1,0:T(8,128)(2,1)S(1)}, bf16[1024,256]{1,0:T(8,128)(2,1)S(1)}, u32[]{:S(2)}, u32[]{:S(2)}) collective-permute-start(bf16[1024,256]{1,0:T(8,128)(2,1)S(1)} %copy-done.18), channel_id=1, source_target_pairs={{64,0},{96,32},{128,64},{160,96},{192,128},{224,160},{256,192},{28... | collective-permute-start | bytes 1572872 | tf_op jit(solution)/shard_map/ppermute | solution.py:31
  93.4 23.6 %copy-start.17 = (bf16[2,256,256]{2,1,0:T(8,128)(2,1)S(1)}, bf16[2,256,256]{2,1,0:T(8,128)(2,1)}, u32[]{:S(2)}) copy-start(bf16[2,256,256]{2,1,0:T(8,128)(2,1)} %param.8) | copy-start | bytes 786436
  117.0 1.0 copy-start.1
  117.0 1.3 copy-start.7
  118.0 0.8 copy-start.23
  118.0 1.0 copy-start.25
  118.0 1.4 copy-start.11
  121.5 3.9 %collective-permute-start.5 = (bf16[256,640]{1,0:T(8,128)(2,1)S(1)}, bf16[256,640]{1,0:T(8,128)(2,1)S(1)}, u32[]{:S(2)}, u32[]{:S(2)}) collective-permute-start(bf16[256,640]{1,0:T(8,128)(2,1)S(1)} %bitcast.91), channel_id=1, source_target_pairs={{0,32},{32,0},{1,33},{33,1},{2,34},{34,2},{3,35},{35,3},{4,36},{36... | collective-permute-start | bytes 983048 | tf_op jit(solution)/shard_map/ppermute | solution.py:74
  125.6 49.9 %copy-start.9 = (bf16[2,256,512]{2,1,0:T(8,128)(2,1)S(1)}, bf16[2,256,512]{2,1,0:T(8,128)(2,1)}, u32[]{:S(2)}) copy-start(bf16[2,256,512]{2,1,0:T(8,128)(2,1)} %param.6) | copy-start | bytes 1572868
  125.7 49.9 %copy-start.24 = (bf16[1024,256]{0,1:T(8,128)(2,1)S(1)}, bf16[1024,256]{0,1:T(8,128)(2,1)}, u32[]{:S(2)}) copy-start(bf16[1024,256]{0,1:T(8,128)(2,1)} %copy-done.23) | copy-start | bytes 1572868
  128.3 83.3 %all-to-all-start = ((bf16[256,2,640]{2,1,0:T(2,128)(2,1)}), bf16[256,2,640]{2,1,0:T(2,128)(2,1)S(1)}, u32[]{:S(2)}, u32[]{:S(2)}) async-start(bf16[256,2,640]{2,1,0:T(2,128)(2,1)} %reshape.54), calls=%async_computation | async-start | bytes 1310720 | tf_op jit(solution)/shard_map/all_to_all | solution.py:85
  177.9 48.4 %copy-start.3 = (bf16[1024,256]{1,0:T(8,128)(2,1)S(1)}, bf16[1024,256]{1,0:T(8,128)(2,1)}, u32[]{:S(2)}) copy-start(bf16[1024,256]{1,0:T(8,128)(2,1)} %copy-done.2) | copy-start | bytes 1572868
  177.9 48.4 %copy-start.5 = (bf16[1024,256]{0,1:T(8,128)(2,1)S(1)}, bf16[1024,256]{0,1:T(8,128)(2,1)}, u32[]{:S(2)}) copy-start(bf16[1024,256]{0,1:T(8,128)(2,1)} %copy-done.4) | copy-start | bytes 1572868
  177.9 50.5 %collective-permute-start.4 = (bf16[1024,256]{1,0:T(8,128)(2,1)}, bf16[1024,256]{1,0:T(8,128)(2,1)}, u32[]{:S(2)}, u32[]{:S(2)}) collective-permute-start(bf16[1024,256]{1,0:T(8,128)(2,1)} %convolution_convert_fusion), channel_id=1, source_target_pairs={{1,0},{2,1},{3,2},{4,3},{5,4},{6,5},{7,6},{8,7},{9,8},{10,9},{11,1... | collective-permute-start | bytes 1572872 | tf_op jit(solution)/shard_map/ppermute | solution.py:31
  212.1 16.3 %copy-start.15 = (bf16[2,256,512]{2,1,0:T(8,128)(2,1)S(1)}, bf16[2,256,512]{2,1,0:T(8,128)(2,1)}, u32[]{:S(2)}) copy-start(bf16[2,256,512]{2,1,0:T(8,128)(2,1)} %param.7) | copy-start | bytes 1572868
  214.0 26.9 %all-to-all-start.1 = ((f32[16,1,1280]{2,1,0:T(1,128)}), f32[16,1,1280]{2,1,0:T(1,128)S(1)}, u32[]{:S(2)}, u32[]{:S(2)}) async-start(f32[16,1,1280]{2,1,0:T(1,128)} %broadcast_in_dim.2), calls=%async_computation.1 | async-start | bytes 163840 | tf_op jit(solution)/shard_map/all_to_all | solution.py:88

commit v9 on v7

--- a/solution.py
+++ b/solution.py
@@ -166,6 +166,7 @@
         sent_back = jnp.dot(
             grad_preact, conv_past[layer_at].T, preferred_element_type=jnp.float32
         ).astype(jnp.bfloat16)
+        grad_preact, sent_back = lax.optimization_barrier((grad_preact, sent_back))
         arrived = return_past(sent_back, layer_at)
         operands = (earlier, current, gated_out, grad_preact, upstream)
         near_list[layer_at] = near_sum(layer_term(operands, grad_scale), layer_at == 0)

time: 220 us -> 227 us (1.032)
  local copies, waits for them, and re-layouts: 9.57 us -> 16.5 us
    unnamed x57 -> x55, local copies, waits for them, and re-layouts: 3.24 us -> 5.34 us
  transfers between devices with their start and end apart: 11 -> 11, of which waited for: 6 -> 7; matrix products, arithmetic and copies ran while one was open for 6% -> 6% of each run, Pallas kernels for 0% -> 0%
where the time goes in v9:
time: 227 us; the launch traced here: 226 us
  starting transfers between devices  93.2 us (41%)
  waiting for transfers between devices  82 us (36%)
  local copies, waits for them, and re-layouts  16.5 us (7%)
  matrix products  15.9 us (7%)
  blocking collectives  10.9 us (5%)
  other arithmetic  6.7 us (3%)
    ppermute x4, waiting for transfers between devices, from_behind(): return lax.ppermute(array, axes, pairs)  66.2 us
    all_to_all x1, starting transfers between devices, far_sum(): lax.all_to_all(rows.astype(jnp.bfloat16), ('y', 'z_hi', 'z_lo'), 0, 0, ti...  41.3 us
    ppermute x4, starting transfers between devices, from_behind(): return lax.ppermute(array, axes, pairs)  27.4 us
    all_to_all x1, blocking collectives, near_sum(): lax.all_to_all(pieces, 'x', 0, 0, tiled=True).astype(jnp.float32).sum(0)  10.9 us
    ppermute x3, starting transfers between devices, scatter_sum(): lax.ppermute(piece.astype(jnp.bfloat16), axes, [(i, (i + shift) % size) f...  10.3 us
    all_to_all x1, waiting for transfers between devices, far_sum(): gathered = lax.all_to_all(spread, ('y', 'z_hi', 'core'), 0, 0, tiled=True)  10.2 us
    all_to_all x1, starting transfers between devices, far_sum(): gathered = lax.all_to_all(spread, ('y', 'z_hi', 'core'), 0, 0, tiled=True)  9.38 us
    unnamed x55, local copies, waits for them, and re-layouts  5.34 us
  transfers between devices with their start and end apart: 11, of which 7 were waited for; matrix products, arithmetic and copies ran while one was open for 6% of the time, Pallas kernels for 0%

profile of v9, /device:TPU:1, one launch (start us, length us, event | category | flops | bytes accessed | tf_op | source)
XLA Modules:
  0.0 226.4 jit_solution(11691802781207076049)
XLA Ops:
  0.6 4.5 %collective-permute-start = (bf16[1024,256]{1,0:T(8,128)(2,1)}, bf16[1024,256]{1,0:T(8,128)(2,1)S(1)}, u32[]{:S(2)}, u32[]{:S(2)}) collective-permute-start(bf16[1024,256]{1,0:T(8,128)(2,1)} %param.5), channel_id=1, source_target_pairs={{0,1},{1,2},{2,3},{3,4},{4,5},{5,6},{6,7},{7,8},{8,9},{9,10},{10,1... | collective-permute-start | bytes 1572872 | tf_op jit(solution)/shard_map/ppermute | solution.py:31
  5.2 1.6 fusion.17
  6.8 20.6 %collective-permute-done = bf16[1024,256]{1,0:T(8,128)(2,1)S(1)} collective-permute-done((bf16[1024,256]{1,0:T(8,128)(2,1)}, bf16[1024,256]{1,0:T(8,128)(2,1)S(1)}, u32[]{:S(2)}, u32[]{:S(2)}) %collective-permute-start) | collective-permute-done | bytes 524320 | tf_op jit(solution)/shard_map/ppermute | solution.py:31
  27.3 0.5 convolution_add_fusion.1
  27.8 0.3 copy-done.11
  28.1 0.4 multiply_convert_fusion.5
  28.5 0.8 copy-done.3
  29.3 0.4 fusion
  29.7 9.4 %collective-permute-start.1 = (bf16[1024,256]{1,0:T(8,128)(2,1)S(1)}, bf16[1024,256]{1,0:T(8,128)(2,1)S(1)}, u32[]{:S(2)}, u32[]{:S(2)}) collective-permute-start(bf16[1024,256]{1,0:T(8,128)(2,1)S(1)} %fusion), channel_id=1, source_target_pairs={{0,64},{32,96},{64,128},{96,160},{128,192},{160,224},{192,256},{22... | collective-permute-start | bytes 1572872 | tf_op jit(solution)/shard_map/ppermute | solution.py:31
  39.1 1.5 fusion.12
  40.6 38.1 %collective-permute-done.1 = bf16[1024,256]{1,0:T(8,128)(2,1)S(1)} collective-permute-done((bf16[1024,256]{1,0:T(8,128)(2,1)S(1)}, bf16[1024,256]{1,0:T(8,128)(2,1)S(1)}, u32[]{:S(2)}, u32[]{:S(2)}) %collective-permute-start.1) | collective-permute-done | bytes 524320 | tf_op jit(solution)/shard_map/ppermute | solution.py:31
  78.7 0.5 convolution_add_fusion
  79.3 0.3 copy-done.13
  79.5 0.8 multiply_convert_fusion.3
  80.3 1.3 convolution_convert_fusion.1
  81.7 0.3 fusion.46
  82.0 0.6 copy-done.1
  82.6 0.5 fusion.45
  83.1 0.5 fusion.44
  83.6 1.2 maximum_multiply_fusion
  84.8 2.9 %mul.65 = f32[256,2,640]{2,1,0:T(2,128)} reshape(f32[256,1280]{1,0:T(8,128)} %maximum_multiply_fusion) | data formatting | bytes 2621440 | tf_op jit(solution)/shard_map/mul | solution.py:125
  87.7 1.9 constant_dynamic-slice_fusion.2
  89.7 2.1 collective-permute-start.2
  91.9 1.4 collective-permute-start.6
  93.3 1.9 constant_dynamic-slice_fusion.3
  95.2 1.0 bitcast_add_fusion.1
  96.3 3.2 %collective-permute-start.3 = (bf16[64,640]{1,0:T(8,128)(2,1)S(1)}, bf16[64,640]{1,0:T(8,128)(2,1)S(1)}, u32[]{:S(2)}, u32[]{:S(2)}) collective-permute-start(bf16[64,640]{1,0:T(8,128)(2,1)S(1)} %get-tuple-element.22), channel_id=1, source_target_pairs={{0,8},{8,16},{16,24},{24,0},{1,9},{9,17},{17,25},{25,1},{2,10},{10... | collective-permute-start | bytes 245768 | tf_op jit(solution)/shard_map/ppermute | solution.py:41
  99.5 3.3 %collective-permute-start.5 = (bf16[64,640]{1,0:T(8,128)(2,1)S(1)}, bf16[64,640]{1,0:T(8,128)(2,1)S(1)}, u32[]{:S(2)}, u32[]{:S(2)}) collective-permute-start(bf16[64,640]{1,0:T(8,128)(2,1)S(1)} %get-tuple-element.23), channel_id=1, source_target_pairs={{0,24},{8,0},{16,8},{24,16},{1,25},{9,1},{17,9},{25,17},{2,26},{10... | collective-permute-start | bytes 245768 | tf_op jit(solution)/shard_map/ppermute | solution.py:41
  102.8 3.8 %collective-permute-start.4 = (bf16[64,640]{1,0:T(8,128)(2,1)S(1)}, bf16[64,640]{1,0:T(8,128)(2,1)S(1)}, u32[]{:S(2)}, u32[]{:S(2)}) collective-permute-start(bf16[64,640]{1,0:T(8,128)(2,1)S(1)} %get-tuple-element.24), channel_id=1, source_target_pairs={{0,16},{8,24},{16,0},{24,8},{1,17},{9,25},{17,1},{25,9},{2,18},{10... | collective-permute-start | bytes 245768 | tf_op jit(solution)/shard_map/ppermute | solution.py:41
  106.7 0.5 convolution_add_fusion.5
  107.2 2.7 %collective-permute-done.4 = bf16[64,640]{1,0:T(8,128)(2,1)S(1)} collective-permute-done((bf16[64,640]{1,0:T(8,128)(2,1)S(1)}, bf16[64,640]{1,0:T(8,128)(2,1)S(1)}, u32[]{:S(2)}, u32[]{:S(2)}) %collective-permute-start.4) | collective-permute-done | bytes 81952 | tf_op jit(solution)/shard_map/ppermute | solution.py:41
  110.0 7.5 %collective-permute-done.6 = bf16[1024,256]{1,0:T(8,128)(2,1)S(1)} collective-permute-done((bf16[1024,256]{1,0:T(8,128)(2,1)}, bf16[1024,256]{1,0:T(8,128)(2,1)S(1)}, u32[]{:S(2)}, u32[]{:S(2)}) %collective-permute-start.6) | collective-permute-done | bytes 524320 | tf_op jit(solution)/shard_map/ppermute | solution.py:31
  117.5 0.1 add_convert_fusion.1
  117.6 0.7 multiply_convert_fusion.1
  118.3 0.1 copy-done.7
  118.4 0.4 copy-done.4
  118.8 0.3 fusion.47
  119.2 1.3 convolution_convert_fusion
  120.6 0.5 convolution_bitcast_fusion
  121.1 0.5 copy-done.12
  121.5 0.5 convolution_bitcast_fusion.1
  122.0 1.2 maximum_multiply_fusion.1
  123.2 2.0 mul.73
  125.2 0.6 constant_dynamic-slice_fusion
  125.9 2.7 %collective-permute-start.8 = (bf16[256,640]{1,0:T(8,128)(2,1)S(1)}, bf16[256,640]{1,0:T(8,128)(2,1)S(1)}, u32[]{:S(2)}, u32[]{:S(2)}) collective-permute-start(bf16[256,640]{1,0:T(8,128)(2,1)S(1)} %bitcast.116), channel_id=1, source_target_pairs={{0,32},{32,0},{1,33},{33,1},{2,34},{34,2},{3,35},{35,3},{4,36},{36... | collective-permute-start | bytes 983048 | tf_op jit(solution)/shard_map/ppermute | solution.py:74
  128.6 0.6 constant_dynamic-slice_fusion.1
  129.2 0.7 collective-permute-done.8
  129.9 10.9 %all_to_all.15 = bf16[4,64,640]{2,1,0:T(8,128)(2,1)S(1)} all-to-all(bf16[4,64,640]{2,1,0:T(8,128)(2,1)S(1)} %bitcast.113), channel_id=1, replica_groups=mesh['y'=4,'z_hi'=2,'core'=2,'x'=4,'z_lo'=8] {'x'}, dimensions={0} | all-to-all | bytes 655360 | tf_op jit(solution)/shard_map/all_to_all | solution.py:80
  140.9 0.5 broadcast.39
  141.4 0.7 reduce.3
  142.1 0.7 reshape.63
  142.8 41.3 %all-to-all-start.1 = ((bf16[64,2,640]{2,1,0:T(2,128)(2,1)}), bf16[64,2,640]{2,1,0:T(2,128)(2,1)}, u32[]{:S(2)}, u32[]{:S(2)}) async-start(bf16[64,2,640]{2,1,0:T(2,128)(2,1)} %reshape.63), calls=%async_computation.1 | async-start | bytes 327680 | tf_op jit(solution)/shard_map/all_to_all | solution.py:89
  184.2 12.0 %collective-permute-start.7 = (bf16[1024,256]{1,0:T(8,128)(2,1)}, bf16[1024,256]{1,0:T(8,128)(2,1)}, u32[]{:S(2)}, u32[]{:S(2)}) collective-permute-start(bf16[1024,256]{1,0:T(8,128)(2,1)} %convolution_convert_fusion), channel_id=1, source_target_pairs={{1,0},{2,1},{3,2},{4,3},{5,4},{6,5},{7,6},{8,7},{9,8},{10,9},{11,1... | collective-permute-start | bytes 1572872 | tf_op jit(solution)/shard_map/ppermute | solution.py:31
  196.2 2.2 all-to-all-done.1
  198.4 1.4 reshape.64
  199.9 0.3 convert_reduce_fusion
  200.2 0.7 broadcast_in_dim.2
  200.9 9.4 %all-to-all-start.2 = ((f32[16,1,1280]{2,1,0:T(1,128)}), f32[16,1,1280]{2,1,0:T(1,128)S(1)}, u32[]{:S(2)}, u32[]{:S(2)}) async-start(f32[16,1,1280]{2,1,0:T(1,128)} %broadcast_in_dim.2), calls=%async_computation.2 | async-start | bytes 163840 | tf_op jit(solution)/shard_map/all_to_all | solution.py:92
  210.3 2.1 fusion.1
  212.3 2.3 %add_convert_fusion = bf16[1024,256]{1,0:T(8,128)(2,1)} fusion(bf16[1024,256]{1,0:T(8,128)(2,1)} %collective-permute-done.7, bf16[1024,512]{0,1:T(8,128)(2,1)S(1)} %pad_maximum_fusion.1, bf16[1024,256]{1,0:T(8,128)(2,1)S(1)} %copy-done.8, bf16[2,256,512]{2,1,0:T(8,128)(2,1)S(1)} %copy-done.18), kind=kOutput, calls=%fused_computation.26 | convolution fusion | flops 269746176 | bytes 2883584 | tf_op jit(solution)/shard_map/dot_general | solution.py:175
  214.7 10.2 %all-to-all-done.2 = f32[16,1,1280]{2,1,0:T(1,128)S(1)} async-done(((f32[16,1,1280]{2,1,0:T(1,128)}), f32[16,1,1280]{2,1,0:T(1,128)S(1)}, u32[]{:S(2)}, u32[]{:S(2)}) %all-to-all-start.2) | async-done | bytes 81952 | tf_op jit(solution)/shard_map/all_to_all | solution.py:92
  224.9 0.2 reduce.2
  225.2 0.6 pad_maximum_fusion.4
  225.8 0.6 pad_maximum_fusion.2
  (62 shorter events, 0.7 us)
Async XLA Ops:
  0.6 26.7 %copy-start.19 = (bf16[2,256,512]{2,1,0:T(8,128)(2,1)S(1)}, bf16[2,256,512]{2,1,0:T(8,128)(2,1)}, u32[]{:S(2)}) copy-start(bf16[2,256,512]{2,1,0:T(8,128)(2,1)} %param.6) | copy-start | bytes 1572868
  0.6 26.7 %collective-permute-start = (bf16[1024,256]{1,0:T(8,128)(2,1)}, bf16[1024,256]{1,0:T(8,128)(2,1)S(1)}, u32[]{:S(2)}, u32[]{:S(2)}) collective-permute-start(bf16[1024,256]{1,0:T(8,128)(2,1)} %param.5), channel_id=1, source_target_pairs={{0,1},{1,2},{2,3},{3,4},{4,5},{5,6},{6,7},{7,8},{8,9},{9,10},{10,1... | collective-permute-start | bytes 1572872 | tf_op jit(solution)/shard_map/ppermute | solution.py:31
  27.3 0.8 copy-start.11
  28.1 1.2 copy-start.5
  28.1 1.2 copy-start.22
  28.5 0.8 copy-start.3
  29.7 49.5 %copy-start = (bf16[1024,256]{1,0:T(8,128)(2,1)}, bf16[1024,256]{1,0:T(8,128)(2,1)S(1)}, u32[]{:S(2)}) copy-start(bf16[1024,256]{1,0:T(8,128)(2,1)S(1)} %fusion) | copy-start | bytes 1572868
  29.7 49.0 %collective-permute-start.1 = (bf16[1024,256]{1,0:T(8,128)(2,1)S(1)}, bf16[1024,256]{1,0:T(8,128)(2,1)S(1)}, u32[]{:S(2)}, u32[]{:S(2)}) collective-permute-start(bf16[1024,256]{1,0:T(8,128)(2,1)S(1)} %fusion), channel_id=1, source_target_pairs={{0,64},{32,96},{64,128},{96,160},{128,192},{160,224},{192,256},{22... | collective-permute-start | bytes 1572872 | tf_op jit(solution)/shard_map/ppermute | solution.py:31
  39.1 39.6 %copy-start.20 = (bf16[2,256,512]{2,1,0:T(8,128)(2,1)S(1)}, bf16[2,256,512]{2,1,0:T(8,128)(2,1)}, u32[]{:S(2)}) copy-start(bf16[2,256,512]{2,1,0:T(8,128)(2,1)} %param.6) | copy-start | bytes 1572868
  40.6 38.9 %copy-start.15 = (bf16[1024,256]{1,0:T(8,128)(2,1)S(1)}, bf16[1024,256]{1,0:T(8,128)(2,1)}, u32[]{:S(2)}) copy-start(bf16[1024,256]{1,0:T(8,128)(2,1)} %param.9) | copy-start | bytes 1572868
  78.7 0.8 copy-start.13
  80.3 1.4 copy-start.9
  81.6 1.0 copy-start.1
  81.7 1.5 copy-start.14
  89.7 5.5 %collective-permute-start.2 = (bf16[256,640]{1,0:T(8,128)(2,1)S(1)}, bf16[256,640]{1,0:T(8,128)(2,1)}, u32[]{:S(2)}, u32[]{:S(2)}) collective-permute-start(bf16[256,640]{1,0:T(8,128)(2,1)S(1)} %bitcast.115), channel_id=1, source_target_pairs={{0,32},{32,0},{1,33},{33,1},{2,34},{34,2},{3,35},{35,3},{4,36},{36... | collective-permute-start | bytes 983048 | tf_op jit(solution)/shard_map/ppermute | solution.py:74
  91.8 14.8 %copy-start.16 = (bf16[1024,256]{1,0:T(8,128)(2,1)S(1)}, bf16[1024,256]{1,0:T(8,128)(2,1)}, u32[]{:S(2)}) copy-start(bf16[1024,256]{1,0:T(8,128)(2,1)} %param.9) | copy-start | bytes 1572868
  91.9 14.8 %copy-start.17 = (bf16[2,256,512]{2,1,0:T(8,128)(2,1)S(1)}, bf16[2,256,512]{2,1,0:T(8,128)(2,1)}, u32[]{:S(2)}) copy-start(bf16[2,256,512]{2,1,0:T(8,128)(2,1)} %param.7) | copy-start | bytes 1572868
  91.9 25.6 %collective-permute-start.6 = (bf16[1024,256]{1,0:T(8,128)(2,1)}, bf16[1024,256]{1,0:T(8,128)(2,1)S(1)}, u32[]{:S(2)}, u32[]{:S(2)}) collective-permute-start(bf16[1024,256]{1,0:T(8,128)(2,1)} %convolution_convert_fusion.1), channel_id=1, source_target_pairs={{64,0},{96,32},{128,64},{160,96},{192,128},{224,160},{256,192},{28... | collective-permute-start | bytes 1572872 | tf_op jit(solution)/shard_map/ppermute | solution.py:31
  96.3 10.9 %collective-permute-start.3 = (bf16[64,640]{1,0:T(8,128)(2,1)S(1)}, bf16[64,640]{1,0:T(8,128)(2,1)S(1)}, u32[]{:S(2)}, u32[]{:S(2)}) collective-permute-start(bf16[64,640]{1,0:T(8,128)(2,1)S(1)} %get-tuple-element.22), channel_id=1, source_target_pairs={{0,8},{8,16},{16,24},{24,0},{1,9},{9,17},{17,25},{25,1},{2,10},{10... | collective-permute-start | bytes 245768 | tf_op jit(solution)/shard_map/ppermute | solution.py:41
  99.5 7.7 %collective-permute-start.5 = (bf16[64,640]{1,0:T(8,128)(2,1)S(1)}, bf16[64,640]{1,0:T(8,128)(2,1)S(1)}, u32[]{:S(2)}, u32[]{:S(2)}) collective-permute-start(bf16[64,640]{1,0:T(8,128)(2,1)S(1)} %get-tuple-element.23), channel_id=1, source_target_pairs={{0,24},{8,0},{16,8},{24,16},{1,25},{9,1},{17,9},{25,17},{2,26},{10... | collective-permute-start | bytes 245768 | tf_op jit(solution)/shard_map/ppermute | solution.py:41
  102.8 14.8 %copy-start.23 = (bf16[2,256,256]{2,1,0:T(8,128)(2,1)S(1)}, bf16[2,256,256]{2,1,0:T(8,128)(2,1)}, u32[]{:S(2)}) copy-start(bf16[2,256,256]{2,1,0:T(8,128)(2,1)} %param.8) | copy-start | bytes 786436
  102.8 7.1 %collective-permute-start.4 = (bf16[64,640]{1,0:T(8,128)(2,1)S(1)}, bf16[64,640]{1,0:T(8,128)(2,1)S(1)}, u32[]{:S(2)}, u32[]{:S(2)}) collective-permute-start(bf16[64,640]{1,0:T(8,128)(2,1)S(1)} %get-tuple-element.24), channel_id=1, source_target_pairs={{0,16},{8,24},{16,0},{24,8},{1,17},{9,25},{17,1},{25,9},{2,18},{10... | collective-permute-start | bytes 245768 | tf_op jit(solution)/shard_map/ppermute | solution.py:41
  117.6 0.8 copy-start.7
  117.6 1.2 copy-start.4
  117.6 1.5 copy-start.21
  119.2 1.4 copy-start.6
  120.5 1.0 copy-start.12
  125.9 3.9 %collective-permute-start.8 = (bf16[256,640]{1,0:T(8,128)(2,1)S(1)}, bf16[256,640]{1,0:T(8,128)(2,1)S(1)}, u32[]{:S(2)}, u32[]{:S(2)}) collective-permute-start(bf16[256,640]{1,0:T(8,128)(2,1)S(1)} %bitcast.116), channel_id=1, source_target_pairs={{0,32},{32,0},{1,33},{33,1},{2,34},{34,2},{3,35},{35,3},{4,36},{36... | collective-permute-start | bytes 983048 | tf_op jit(solution)/shard_map/ppermute | solution.py:74
  129.9 80.4 %copy-start.2 = (bf16[1024,256]{1,0:T(8,128)(2,1)S(1)}, bf16[1024,256]{1,0:T(8,128)(2,1)}, u32[]{:S(2)}) copy-start(bf16[1024,256]{1,0:T(8,128)(2,1)} %copy-done) | copy-start | bytes 1572868
  129.9 80.4 %copy-start.10 = (bf16[1024,256]{0,1:T(8,128)(2,1)S(1)}, bf16[1024,256]{0,1:T(8,128)(2,1)}, u32[]{:S(2)}) copy-start(bf16[1024,256]{0,1:T(8,128)(2,1)} %copy-done.9) | copy-start | bytes 1572868
  140.9 71.5 %copy-start.8 = (bf16[1024,256]{1,0:T(8,128)(2,1)S(1)}, bf16[1024,256]{1,0:T(8,128)(2,1)}, u32[]{:S(2)}) copy-start(bf16[1024,256]{1,0:T(8,128)(2,1)} %copy-done.7) | copy-start | bytes 1572868
  140.9 71.5 %copy-start.18 = (bf16[2,256,512]{2,1,0:T(8,128)(2,1)S(1)}, bf16[2,256,512]{2,1,0:T(8,128)(2,1)}, u32[]{:S(2)}) copy-start(bf16[2,256,512]{2,1,0:T(8,128)(2,1)} %param.7) | copy-start | bytes 1572868
  142.8 55.6 %all-to-all-start.1 = ((bf16[64,2,640]{2,1,0:T(2,128)(2,1)}), bf16[64,2,640]{2,1,0:T(2,128)(2,1)}, u32[]{:S(2)}, u32[]{:S(2)}) async-start(bf16[64,2,640]{2,1,0:T(2,128)(2,1)} %reshape.63), calls=%async_computation.1 | async-start | bytes 327680 | tf_op jit(solution)/shard_map/all_to_all | solution.py:89
  184.2 28.2 %collective-permute-start.7 = (bf16[1024,256]{1,0:T(8,128)(2,1)}, bf16[1024,256]{1,0:T(8,128)(2,1)}, u32[]{:S(2)}, u32[]{:S(2)}) collective-permute-start(bf16[1024,256]{1,0:T(8,128)(2,1)} %convolution_convert_fusion), channel_id=1, source_target_pairs={{1,0},{2,1},{3,2},{4,3},{5,4},{6,5},{7,6},{8,7},{9,8},{10,9},{11,1... | collective-permute-start | bytes 1572872 | tf_op jit(solution)/shard_map/ppermute | solution.py:31
  200.9 24.0 %all-to-all-start.2 = ((f32[16,1,1280]{2,1,0:T(1,128)}), f32[16,1,1280]{2,1,0:T(1,128)S(1)}, u32[]{:S(2)}, u32[]{:S(2)}) async-start(f32[16,1,1280]{2,1,0:T(1,128)} %broadcast_in_dim.2), calls=%async_computation.2 | async-start | bytes 163840 | tf_op jit(solution)/shard_map/all_to_all | solution.py:92

commit v10 on v6

--- a/solution.py
+++ b/solution.py
@@ -66,7 +66,14 @@
     return total
 
 
-def near_sum(term):
+def near_sum(term, by_exchange):
+    if by_exchange:
+        core_size = lax.axis_size("core")
+        x_size = lax.axis_size("x")
+        pieces = term.reshape(x_size, term.shape[0] // x_size, core_size, term.shape[1] // core_size)
+        pieces = pieces.transpose(2, 0, 1, 3).reshape(core_size * x_size, term.shape[0] // x_size, -1)
+        moved = lax.all_to_all(pieces.astype(jnp.bfloat16), ("core", "x"), 0, 0, tiled=True)
+        return moved.astype(jnp.float32).sum(0)
     own_core = lax.axis_index("core")
     halves = term.reshape(term.shape[0], 2, term.shape[1] // 2)
     kept = lax.dynamic_index_in_dim(halves, own_core, 1, keepdims=False)
@@ -163,7 +170,7 @@
         ).astype(jnp.bfloat16)
         arrived = return_past(sent_back, layer_at)
         operands = (earlier, current, gated_out, grad_preact, upstream)
-        near_list[layer_at] = near_sum(layer_term(operands, grad_scale))
+        near_list[layer_at] = near_sum(layer_term(operands, grad_scale), layer_at == 0)
         if layer_at > 0:
             near_list, arrived = lax.optimization_barrier((near_list, arrived))
         local_grad = upstream.astype(jnp.float32) + jnp.dot(

time: 223 us -> 220 us (0.987)
  blocking collectives: 0 us -> 15.9 us
  starting transfers between devices: 104 us -> 89.3 us
  waiting for transfers between devices: 86.8 us -> 82.7 us
    all_to_all x0 -> x1, blocking collectives: none -> 15.9 us  [near_sum(): lax.all_to_all(pieces.astype(jnp.bfloat16), ('core', 'x'), 0, 0, tiled=True)]
    ppermute x6 -> x3, starting transfers between devices: 20.7 us -> 10.6 us  [scatter_sum(): lax.ppermute(piece.astype(jnp.bfloat16), axes, [(i, (i + shift) % size) f...]
    ppermute x6 -> x3, waiting for transfers between devices: 5.72 us -> 1.86 us  [scatter_sum(): lax.ppermute(piece.astype(jnp.bfloat16), axes, [(i, (i + shift) % size) f...]
    ppermute x2 -> x1, starting transfers between devices: 4.99 us -> 2.11 us  [near_sum(): moved = lax.ppermute(given.astype(jnp.bfloat16), 'core', [(0, 1), (1, 0)])]
  transfers between devices with their start and end apart: 14 -> 10, of which waited for: 8 -> 6; matrix products, arithmetic and copies ran while one was open for 5% -> 5% of each run, Pallas kernels for 0% -> 0%
where the time goes in v10:
time: 220 us; the launch traced here: 219 us
  starting transfers between devices  89.3 us (41%)
  waiting for transfers between devices  82.7 us (38%)
  matrix products  17.5 us (8%)
  blocking collectives  15.9 us (7%)
  local copies, waits for them, and re-layouts  8.09 us (4%)
  other arithmetic  4.48 us (2%)
    ppermute x4, waiting for transfers between devices, from_behind(): return lax.ppermute(array, axes, pairs)  68.2 us
    all_to_all x1, starting transfers between devices, far_sum(): lax.all_to_all(rows.astype(jnp.bfloat16), ('y', 'z_hi', 'z_lo'), 0, 0, ti...  41.4 us
    ppermute x4, starting transfers between devices, from_behind(): return lax.ppermute(array, axes, pairs)  27.6 us
    all_to_all x1, blocking collectives, near_sum(): lax.all_to_all(pieces.astype(jnp.bfloat16), ('core', 'x'), 0, 0, tiled=True)  15.9 us
    all_to_all x1, waiting for transfers between devices, far_sum(): gathered = lax.all_to_all(spread, ('y', 'z_hi', 'core'), 0, 0, tiled=True)  11 us
    ppermute x3, starting transfers between devices, scatter_sum(): lax.ppermute(piece.astype(jnp.bfloat16), axes, [(i, (i + shift) % size) f...  10.6 us
    all_to_all x1, starting transfers between devices, far_sum(): gathered = lax.all_to_all(spread, ('y', 'z_hi', 'core'), 0, 0, tiled=True)  7.5 us
  transfers between devices with their start and end apart: 10, of which 6 were waited for; matrix products, arithmetic and copies ran while one was open for 5% of the time, Pallas kernels for 0%

profile of v10, /device:TPU:1, one launch (start us, length us, event | category | flops | bytes accessed | tf_op | source)
XLA Modules:
  0.0 219.2 jit_solution(844347319716718993)
XLA Ops:
  0.6 4.5 %collective-permute-start = (bf16[1024,256]{1,0:T(8,128)(2,1)}, bf16[1024,256]{1,0:T(8,128)(2,1)S(1)}, u32[]{:S(2)}, u32[]{:S(2)}) collective-permute-start(bf16[1024,256]{1,0:T(8,128)(2,1)} %param.5), channel_id=1, source_target_pairs={{0,1},{1,2},{2,3},{3,4},{4,5},{5,6},{6,7},{7,8},{8,9},{9,10},{10,1... | collective-permute-start | bytes 1572872 | tf_op jit(solution)/shard_map/ppermute | solution.py:31
  5.2 1.6 fusion.16
  6.8 20.6 %collective-permute-done = bf16[1024,256]{1,0:T(8,128)(2,1)S(1)} collective-permute-done((bf16[1024,256]{1,0:T(8,128)(2,1)}, bf16[1024,256]{1,0:T(8,128)(2,1)S(1)}, u32[]{:S(2)}, u32[]{:S(2)}) %collective-permute-start) | collective-permute-done | bytes 524320 | tf_op jit(solution)/shard_map/ppermute | solution.py:31
  27.3 0.5 convolution_add_fusion.1
  27.8 0.3 copy-done.11
  28.1 0.4 multiply_convert_fusion.5
  28.6 0.8 copy-done
  29.4 0.4 fusion.1
  29.8 10.2 %collective-permute-start.1 = (bf16[1024,256]{1,0:T(8,128)(2,1)S(1)}, bf16[1024,256]{1,0:T(8,128)(2,1)}, u32[]{:S(2)}, u32[]{:S(2)}) collective-permute-start(bf16[1024,256]{1,0:T(8,128)(2,1)S(1)} %fusion.1), channel_id=1, source_target_pairs={{0,64},{32,96},{64,128},{96,160},{128,192},{160,224},{192,256},{22... | collective-permute-start | bytes 1572872 | tf_op jit(solution)/shard_map/ppermute | solution.py:31
  39.9 1.4 fusion.11
  41.4 37.4 %collective-permute-done.1 = bf16[1024,256]{1,0:T(8,128)(2,1)} collective-permute-done((bf16[1024,256]{1,0:T(8,128)(2,1)S(1)}, bf16[1024,256]{1,0:T(8,128)(2,1)}, u32[]{:S(2)}, u32[]{:S(2)}) %collective-permute-start.1) | collective-permute-done | bytes 524320 | tf_op jit(solution)/shard_map/ppermute | solution.py:31
  78.8 1.5 convolution_add_fusion
  80.3 0.8 multiply_convert_fusion.3
  81.1 0.0 copy-start.4
  81.1 0.3 fusion.45
  81.5 0.5 fusion.43
  82.0 0.1 copy-done.19
  82.1 0.2 copy-done.21
  82.3 1.5 fusion.44
  83.8 1.2 maximum_multiply_fusion
  85.0 2.0 mul.63
  87.0 0.6 constant_dynamic-slice_fusion
  87.6 2.1 collective-permute-start.2
  89.8 0.5 convolution_convert_fusion.1
  90.3 1.4 collective-permute-start.6
  91.7 0.6 constant_dynamic-slice_fusion.1
  92.3 0.1 bitcast_add_fusion
  92.4 3.2 %collective-permute-start.3 = (bf16[64,640]{1,0:T(8,128)(2,1)S(1)}, bf16[64,640]{1,0:T(8,128)(2,1)S(1)}, u32[]{:S(2)}, u32[]{:S(2)}) collective-permute-start(bf16[64,640]{1,0:T(8,128)(2,1)S(1)} %get-tuple-element.14), channel_id=1, source_target_pairs={{0,8},{8,16},{16,24},{24,0},{1,9},{9,17},{17,25},{25,1},{2,10},{10... | collective-permute-start | bytes 245768 | tf_op jit(solution)/shard_map/ppermute | solution.py:41
  95.7 4.4 %collective-permute-start.4 = (bf16[64,640]{1,0:T(8,128)(2,1)S(1)}, bf16[64,640]{1,0:T(8,128)(2,1)S(1)}, u32[]{:S(2)}, u32[]{:S(2)}) collective-permute-start(bf16[64,640]{1,0:T(8,128)(2,1)S(1)} %get-tuple-element.16), channel_id=1, source_target_pairs={{0,16},{8,24},{16,0},{24,8},{1,17},{9,25},{17,1},{25,9},{2,18},{10... | collective-permute-start | bytes 245768 | tf_op jit(solution)/shard_map/ppermute | solution.py:41
  100.1 3.1 %collective-permute-start.5 = (bf16[64,640]{1,0:T(8,128)(2,1)S(1)}, bf16[64,640]{1,0:T(8,128)(2,1)S(1)}, u32[]{:S(2)}, u32[]{:S(2)}) collective-permute-start(bf16[64,640]{1,0:T(8,128)(2,1)S(1)} %get-tuple-element.15), channel_id=1, source_target_pairs={{0,24},{8,0},{16,8},{24,16},{1,25},{9,1},{17,9},{25,17},{2,26},{10... | collective-permute-start | bytes 245768 | tf_op jit(solution)/shard_map/ppermute | solution.py:41
  103.1 0.5 convolution_add_fusion.5
  103.7 1.9 collective-permute-done.5
  105.6 10.2 %collective-permute-done.6 = bf16[1024,256]{1,0:T(8,128)(2,1)S(1)} collective-permute-done((bf16[1024,256]{1,0:T(8,128)(2,1)S(1)}, bf16[1024,256]{1,0:T(8,128)(2,1)S(1)}, u32[]{:S(2)}, u32[]{:S(2)}) %collective-permute-start.6) | collective-permute-done | bytes 524320 | tf_op jit(solution)/shard_map/ppermute | solution.py:31
  115.8 0.1 add_convert_fusion.1
  116.0 0.7 multiply_convert_fusion.1
  116.7 0.3 copy-done.1
  117.0 0.3 fusion.46
  117.3 0.5 convolution_bitcast_fusion
  117.8 0.2 copy-done.24
  118.0 0.4 copy-done.12
  118.4 0.5 convolution_bitcast_fusion.1
  118.9 0.1 fusion
  119.0 0.1 convert_element_type.143
  119.2 0.1 copy.32
  119.3 15.9 %all_to_all.15 = bf16[8,64,640]{2,1,0:T(8,128)(2,1)S(1)} all-to-all(bf16[8,64,640]{2,1,0:T(8,128)(2,1)S(1)} %bitcast.100), channel_id=1, replica_groups=mesh['y'=4,'z_hi'=2,'core'=2,'x'=4,'z_lo'=8] {'core','x'}, dimensions={0} | all-to-all | bytes 1310720 | tf_op jit(solution)/shard_map/all_to_all | solution.py:75
  135.2 0.1 reduce.1
  135.4 0.5 broadcast.40
  135.9 0.7 reduce.3
  136.6 0.7 reshape.63
  137.3 41.4 %all-to-all-start.1 = ((bf16[64,2,640]{2,1,0:T(2,128)(2,1)}), bf16[64,2,640]{2,1,0:T(2,128)(2,1)S(1)}, u32[]{:S(2)}, u32[]{:S(2)}) async-start(bf16[64,2,640]{2,1,0:T(2,128)(2,1)} %reshape.63), calls=%async_computation.1 | async-start | bytes 327680 | tf_op jit(solution)/shard_map/all_to_all | solution.py:91
  178.7 2.5 %convolution_convert_fusion = bf16[1024,256]{1,0:T(8,128)(2,1)} fusion(bf16[2,256,512]{2,1,0:T(8,128)(2,1)S(1)} %copy-done.10, bf16[1024,256]{0,1:T(8,128)(2,1)} %copy-done.24, bf16[1024,256]{0,1:T(8,128)(2,1)} %copy-done.23), kind=kOutput, calls=%fused_computation.9 | convolution fusion | flops 270794752 | bytes 1835008 | tf_op jit(solution)/shard_map/dot_general | solution.py:168
  181.2 11.5 %collective-permute-start.7 = (bf16[1024,256]{1,0:T(8,128)(2,1)}, bf16[1024,256]{1,0:T(8,128)(2,1)S(1)}, u32[]{:S(2)}, u32[]{:S(2)}) collective-permute-start(bf16[1024,256]{1,0:T(8,128)(2,1)} %convolution_convert_fusion), channel_id=1, source_target_pairs={{1,0},{2,1},{3,2},{4,3},{5,4},{6,5},{7,6},{8,7},{9,8},{10,9},{11,1... | collective-permute-start | bytes 1572872 | tf_op jit(solution)/shard_map/ppermute | solution.py:31
  192.7 1.6 all-to-all-done.1
  194.4 0.1 reshape.64
  194.5 0.3 convert_reduce_fusion
  194.8 0.7 broadcast_in_dim.2
  195.5 7.5 %all-to-all-start.2 = ((f32[16,1,1280]{2,1,0:T(1,128)}), f32[16,1,1280]{2,1,0:T(1,128)S(1)}, u32[]{:S(2)}, u32[]{:S(2)}) async-start(f32[16,1,1280]{2,1,0:T(1,128)} %broadcast_in_dim.2), calls=%async_computation.2 | async-start | bytes 163840 | tf_op jit(solution)/shard_map/all_to_all | solution.py:94
  203.0 1.2 fusion.2
  204.2 2.5 %add_convert_fusion = bf16[1024,256]{1,0:T(8,128)(2,1)} fusion(bf16[1024,256]{1,0:T(8,128)(2,1)S(1)} %collective-permute-done.7, bf16[1024,256]{1,0:T(8,128)(2,1)S(1)} %add_convert_fusion.1, bf16[2,256,512]{2,1,0:T(8,128)(2,1)S(1)} %copy-done.16, bf16[1024,256]{0,1:T(8,128)(2,1)} %copy-done.24, bf16[1024,256]{0,1:T(8,128)(2,1)} %copy-done.23), kind=kOutput, calls=%fused_computation.27 | convolution fusion | flops 271843328 | bytes 2883584 | tf_op jit(solution)/shard_map/dot_general | solution.py:176
  206.7 11.0 %all-to-all-done.2 = f32[16,1,1280]{2,1,0:T(1,128)S(1)} async-done(((f32[16,1,1280]{2,1,0:T(1,128)}), f32[16,1,1280]{2,1,0:T(1,128)S(1)}, u32[]{:S(2)}, u32[]{:S(2)}) %all-to-all-start.2) | async-done | bytes 81952 | tf_op jit(solution)/shard_map/all_to_all | solution.py:94
  217.6 0.2 reduce.2
  217.8 0.1 reshape.59
  218.0 0.6 pad_maximum_fusion.4
  218.6 0.6 pad_maximum_fusion.2
  (57 shorter events, 0.3 us)
Async XLA Ops:
  0.6 26.7 %copy-start.8 = (bf16[2,256,512]{2,1,0:T(8,128)(2,1)S(1)}, bf16[2,256,512]{2,1,0:T(8,128)(2,1)}, u32[]{:S(2)}) copy-start(bf16[2,256,512]{2,1,0:T(8,128)(2,1)} %param.6) | copy-start | bytes 1572868
  0.6 26.7 %collective-permute-start = (bf16[1024,256]{1,0:T(8,128)(2,1)}, bf16[1024,256]{1,0:T(8,128)(2,1)S(1)}, u32[]{:S(2)}, u32[]{:S(2)}) collective-permute-start(bf16[1024,256]{1,0:T(8,128)(2,1)} %param.5), channel_id=1, source_target_pairs={{0,1},{1,2},{2,3},{3,4},{4,5},{5,6},{6,7},{7,8},{8,9},{9,10},{10,1... | collective-permute-start | bytes 1572872 | tf_op jit(solution)/shard_map/ppermute | solution.py:31
  27.3 0.8 copy-start.11
  28.1 1.2 copy-start.6
  28.1 1.2 copy-start.17
  28.6 0.8 copy-start
  29.7 51.7 %copy-start.2 = (bf16[1024,256]{1,0:T(8,128)(2,1)}, bf16[1024,256]{1,0:T(8,128)(2,1)S(1)}, u32[]{:S(2)}) copy-start(bf16[1024,256]{1,0:T(8,128)(2,1)S(1)} %fusion.1) | copy-start | bytes 1572868
  29.8 49.0 %collective-permute-start.1 = (bf16[1024,256]{1,0:T(8,128)(2,1)S(1)}, bf16[1024,256]{1,0:T(8,128)(2,1)}, u32[]{:S(2)}, u32[]{:S(2)}) collective-permute-start(bf16[1024,256]{1,0:T(8,128)(2,1)S(1)} %fusion.1), channel_id=1, source_target_pairs={{0,64},{32,96},{64,128},{96,160},{128,192},{160,224},{192,256},{22... | collective-permute-start | bytes 1572872 | tf_op jit(solution)/shard_map/ppermute | solution.py:31
  41.4 39.0 %copy-start.13 = (bf16[1024,256]{1,0:T(8,128)(2,1)S(1)}, bf16[1024,256]{1,0:T(8,128)(2,1)}, u32[]{:S(2)}) copy-start(bf16[1024,256]{1,0:T(8,128)(2,1)} %param.9) | copy-start | bytes 1572868
  81.1 0.8 copy-start.4
  81.1 1.0 copy-start.19
  81.1 1.1 copy-start.21
  87.0 2.8 %copy-start.9 = (bf16[2,256,512]{2,1,0:T(8,128)(2,1)S(1)}, bf16[2,256,512]{2,1,0:T(8,128)(2,1)}, u32[]{:S(2)}) copy-start(bf16[2,256,512]{2,1,0:T(8,128)(2,1)} %param.6) | copy-start | bytes 1572868
  87.0 2.8 %copy-start.20 = (bf16[1024,256]{0,1:T(8,128)(2,1)S(1)}, bf16[1024,256]{0,1:T(8,128)(2,1)}, u32[]{:S(2)}) copy-start(bf16[1024,256]{0,1:T(8,128)(2,1)} %copy-done.19) | copy-start | bytes 1572868
  87.0 2.8 %copy-start.22 = (bf16[1024,256]{0,1:T(8,128)(2,1)S(1)}, bf16[1024,256]{0,1:T(8,128)(2,1)}, u32[]{:S(2)}) copy-start(bf16[1024,256]{0,1:T(8,128)(2,1)} %copy-done.21) | copy-start | bytes 1572868
  87.6 4.7 %collective-permute-start.2 = (bf16[256,640]{1,0:T(8,128)(2,1)S(1)}, bf16[256,640]{1,0:T(8,128)(2,1)S(1)}, u32[]{:S(2)}, u32[]{:S(2)}) collective-permute-start(bf16[256,640]{1,0:T(8,128)(2,1)S(1)} %bitcast.104), channel_id=1, source_target_pairs={{0,32},{32,0},{1,33},{33,1},{2,34},{34,2},{3,35},{35,3},{4,36},{36... | collective-permute-start | bytes 983048 | tf_op jit(solution)/shard_map/ppermute | solution.py:81
  90.3 12.8 %copy-start.14 = (bf16[1024,256]{1,0:T(8,128)(2,1)S(1)}, bf16[1024,256]{1,0:T(8,128)(2,1)}, u32[]{:S(2)}) copy-start(bf16[1024,256]{1,0:T(8,128)(2,1)} %param.9) | copy-start | bytes 1572868
  90.3 12.8 %copy-start.15 = (bf16[2,256,512]{2,1,0:T(8,128)(2,1)S(1)}, bf16[2,256,512]{2,1,0:T(8,128)(2,1)}, u32[]{:S(2)}) copy-start(bf16[2,256,512]{2,1,0:T(8,128)(2,1)} %param.7) | copy-start | bytes 1572868
  90.3 25.5 %collective-permute-start.6 = (bf16[1024,256]{1,0:T(8,128)(2,1)S(1)}, bf16[1024,256]{1,0:T(8,128)(2,1)S(1)}, u32[]{:S(2)}, u32[]{:S(2)}) collective-permute-start(bf16[1024,256]{1,0:T(8,128)(2,1)S(1)} %convolution_convert_fusion.1), channel_id=1, source_target_pairs={{64,0},{96,32},{128,64},{160,96},{192,128},{224,160},{256,192},{28... | collective-permute-start | bytes 1572872 | tf_op jit(solution)/shard_map/ppermute | solution.py:31
  92.4 11.2 %collective-permute-start.3 = (bf16[64,640]{1,0:T(8,128)(2,1)S(1)}, bf16[64,640]{1,0:T(8,128)(2,1)S(1)}, u32[]{:S(2)}, u32[]{:S(2)}) collective-permute-start(bf16[64,640]{1,0:T(8,128)(2,1)S(1)} %get-tuple-element.14), channel_id=1, source_target_pairs={{0,8},{8,16},{16,24},{24,0},{1,9},{9,17},{17,25},{25,1},{2,10},{10... | collective-permute-start | bytes 245768 | tf_op jit(solution)/shard_map/ppermute | solution.py:41
  95.7 8.0 %collective-permute-start.4 = (bf16[64,640]{1,0:T(8,128)(2,1)S(1)}, bf16[64,640]{1,0:T(8,128)(2,1)S(1)}, u32[]{:S(2)}, u32[]{:S(2)}) collective-permute-start(bf16[64,640]{1,0:T(8,128)(2,1)S(1)} %get-tuple-element.16), channel_id=1, source_target_pairs={{0,16},{8,24},{16,0},{24,8},{1,17},{9,25},{17,1},{25,9},{2,18},{10... | collective-permute-start | bytes 245768 | tf_op jit(solution)/shard_map/ppermute | solution.py:41
  100.1 5.5 %collective-permute-start.5 = (bf16[64,640]{1,0:T(8,128)(2,1)S(1)}, bf16[64,640]{1,0:T(8,128)(2,1)S(1)}, u32[]{:S(2)}, u32[]{:S(2)}) collective-permute-start(bf16[64,640]{1,0:T(8,128)(2,1)S(1)} %get-tuple-element.15), channel_id=1, source_target_pairs={{0,24},{8,0},{16,8},{24,16},{1,25},{9,1},{17,9},{25,17},{2,26},{10... | collective-permute-start | bytes 245768 | tf_op jit(solution)/shard_map/ppermute | solution.py:41
  103.6 12.3 %copy-start.18 = (bf16[2,256,256]{2,1,0:T(8,128)(2,1)S(1)}, bf16[2,256,256]{2,1,0:T(8,128)(2,1)}, u32[]{:S(2)}) copy-start(bf16[2,256,256]{2,1,0:T(8,128)(2,1)} %param.8) | copy-start | bytes 786436
  116.0 1.0 copy-start.1
  116.0 1.3 copy-start.7
  117.0 0.8 copy-start.23
  117.0 1.0 copy-start.24
  117.0 1.4 copy-start.12
  119.3 59.5 %copy-start.10 = (bf16[2,256,512]{2,1,0:T(8,128)(2,1)S(1)}, bf16[2,256,512]{2,1,0:T(8,128)(2,1)}, u32[]{:S(2)}) copy-start(bf16[2,256,512]{2,1,0:T(8,128)(2,1)} %param.6) | copy-start | bytes 1572868
  137.3 65.7 %copy-start.3 = (bf16[1024,256]{1,0:T(8,128)(2,1)S(1)}, bf16[1024,256]{1,0:T(8,128)(2,1)}, u32[]{:S(2)}) copy-start(bf16[1024,256]{1,0:T(8,128)(2,1)} %copy-done.2) | copy-start | bytes 1572868
  137.3 65.7 %copy-start.5 = (bf16[1024,256]{0,1:T(8,128)(2,1)S(1)}, bf16[1024,256]{0,1:T(8,128)(2,1)}, u32[]{:S(2)}) copy-start(bf16[1024,256]{0,1:T(8,128)(2,1)} %copy-done.4) | copy-start | bytes 1572868
  137.3 57.1 %all-to-all-start.1 = ((bf16[64,2,640]{2,1,0:T(2,128)(2,1)}), bf16[64,2,640]{2,1,0:T(2,128)(2,1)S(1)}, u32[]{:S(2)}, u32[]{:S(2)}) async-start(bf16[64,2,640]{2,1,0:T(2,128)(2,1)} %reshape.63), calls=%async_computation.1 | async-start | bytes 327680 | tf_op jit(solution)/shard_map/all_to_all | solution.py:91
  181.2 22.9 %copy-start.16 = (bf16[2,256,512]{2,1,0:T(8,128)(2,1)S(1)}, bf16[2,256,512]{2,1,0:T(8,128)(2,1)}, u32[]{:S(2)}) copy-start(bf16[2,256,512]{2,1,0:T(8,128)(2,1)} %param.7) | copy-start | bytes 1572868
  181.2 22.9 %collective-permute-start.7 = (bf16[1024,256]{1,0:T(8,128)(2,1)}, bf16[1024,256]{1,0:T(8,128)(2,1)S(1)}, u32[]{:S(2)}, u32[]{:S(2)}) collective-permute-start(bf16[1024,256]{1,0:T(8,128)(2,1)} %convolution_convert_fusion), channel_id=1, source_target_pairs={{1,0},{2,1},{3,2},{4,3},{5,4},{6,5},{7,6},{8,7},{9,8},{10,9},{11,1... | collective-permute-start | bytes 1572872 | tf_op jit(solution)/shard_map/ppermute | solution.py:31
  195.5 22.1 %all-to-all-start.2 = ((f32[16,1,1280]{2,1,0:T(1,128)}), f32[16,1,1280]{2,1,0:T(1,128)S(1)}, u32[]{:S(2)}, u32[]{:S(2)}) async-start(f32[16,1,1280]{2,1,0:T(1,128)} %broadcast_in_dim.2), calls=%async_computation.2 | async-start | bytes 163840 | tf_op jit(solution)/shard_map/all_to_all | solution.py:94

commit v11 on v7

--- a/solution.py
+++ b/solution.py
@@ -86,8 +86,7 @@
     core_size = lax.axis_size("core")
     rows = term.reshape(lo_size, hi_size, term.shape[1]).transpose(1, 0, 2)
     rows = rows.reshape(hi_size * lo_size, 1, term.shape[1])
-    row = lax.all_to_all(rows.astype(jnp.bfloat16), ("y", "z_hi", "z_lo"), 0, 0, tiled=True)
-    row = row.astype(jnp.float32).sum(0)
+    row = lax.all_to_all(rows, ("y", "z_hi", "z_lo"), 0, 0, tiled=True).sum(0)
     spread = jnp.broadcast_to(row[None], (hi_size * core_size, *row.shape))
     gathered = lax.all_to_all(spread, ("y", "z_hi", "core"), 0, 0, tiled=True)
     return gathered.reshape(hi_size, core_size, term.shape[1])

time: 220 us -> 226 us (1.027)
  waiting for transfers between devices: 81.5 us -> 87.6 us
    all_to_all x1, waiting for transfers between devices: 0.01 us -> 6.13 us  [far_sum(): row = lax.all_to_all(rows, ('y', 'z_hi', 'z_lo'), 0, 0, tiled=True).sum(0)]
  transfers between devices with their start and end apart: 11 -> 11, of which waited for: 6 -> 7; matrix products, arithmetic and copies ran while one was open for 6% -> 5% of each run, Pallas kernels for 0% -> 0%
where the time goes in v11:
time: 226 us; the launch traced here: 225 us
  starting transfers between devices  95 us (42%)
  waiting for transfers between devices  87.6 us (39%)
  matrix products  17.6 us (8%)
  blocking collectives  10.8 us (5%)
  local copies, waits for them, and re-layouts  9.33 us (4%)
  other arithmetic  3.72 us (2%)
    ppermute x4, waiting for transfers between devices, from_behind(): return lax.ppermute(array, axes, pairs)  68.2 us
    all_to_all x1, starting transfers between devices, far_sum(): row = lax.all_to_all(rows, ('y', 'z_hi', 'z_lo'), 0, 0, tiled=True).sum(0)  41.3 us
    ppermute x4, starting transfers between devices, from_behind(): return lax.ppermute(array, axes, pairs)  28.2 us
    all_to_all x1, waiting for transfers between devices, far_sum(): gathered = lax.all_to_all(spread, ('y', 'z_hi', 'core'), 0, 0, tiled=True)  10.9 us
    all_to_all x1, blocking collectives, near_sum(): lax.all_to_all(pieces, 'x', 0, 0, tiled=True).astype(jnp.float32).sum(0)  10.8 us
    ppermute x3, starting transfers between devices, scatter_sum(): lax.ppermute(piece.astype(jnp.bfloat16), axes, [(i, (i + shift) % size) f...  10.6 us
    all_to_all x1, starting transfers between devices, far_sum(): gathered = lax.all_to_all(spread, ('y', 'z_hi', 'core'), 0, 0, tiled=True)  9.93 us
    all_to_all x1, waiting for transfers between devices, far_sum(): row = lax.all_to_all(rows, ('y', 'z_hi', 'z_lo'), 0, 0, tiled=True).sum(0)  6.13 us
  transfers between devices with their start and end apart: 11, of which 7 were waited for; matrix products, arithmetic and copies ran while one was open for 5% of the time, Pallas kernels for 0%

profile of v11, /device:TPU:1, one launch (start us, length us, event | category | flops | bytes accessed | tf_op | source)
XLA Modules:
  0.0 225.4 jit_solution(13985531943315286220)
XLA Ops:
  0.6 4.5 %collective-permute-start = (bf16[1024,256]{1,0:T(8,128)(2,1)}, bf16[1024,256]{1,0:T(8,128)(2,1)S(1)}, u32[]{:S(2)}, u32[]{:S(2)}) collective-permute-start(bf16[1024,256]{1,0:T(8,128)(2,1)} %param.5), channel_id=1, source_target_pairs={{0,1},{1,2},{2,3},{3,4},{4,5},{5,6},{6,7},{7,8},{8,9},{9,10},{10,1... | collective-permute-start | bytes 1572872 | tf_op jit(solution)/shard_map/ppermute | solution.py:31
  5.2 1.6 fusion.17
  6.8 20.6 %collective-permute-done = bf16[1024,256]{1,0:T(8,128)(2,1)S(1)} collective-permute-done((bf16[1024,256]{1,0:T(8,128)(2,1)}, bf16[1024,256]{1,0:T(8,128)(2,1)S(1)}, u32[]{:S(2)}, u32[]{:S(2)}) %collective-permute-start) | collective-permute-done | bytes 524320 | tf_op jit(solution)/shard_map/ppermute | solution.py:31
  27.3 0.5 convolution_add_fusion.1
  27.8 0.3 copy-done.11
  28.1 0.4 multiply_convert_fusion.5
  28.6 0.8 copy-done
  29.3 0.4 fusion
  29.7 10.2 %collective-permute-start.1 = (bf16[1024,256]{1,0:T(8,128)(2,1)S(1)}, bf16[1024,256]{1,0:T(8,128)(2,1)}, u32[]{:S(2)}, u32[]{:S(2)}) collective-permute-start(bf16[1024,256]{1,0:T(8,128)(2,1)S(1)} %fusion), channel_id=1, source_target_pairs={{0,64},{32,96},{64,128},{96,160},{128,192},{160,224},{192,256},{22... | collective-permute-start | bytes 1572872 | tf_op jit(solution)/shard_map/ppermute | solution.py:31
  39.9 1.4 fusion.12
  41.3 0.0 copy-start.13
  41.3 37.4 %collective-permute-done.1 = bf16[1024,256]{1,0:T(8,128)(2,1)} collective-permute-done((bf16[1024,256]{1,0:T(8,128)(2,1)S(1)}, bf16[1024,256]{1,0:T(8,128)(2,1)}, u32[]{:S(2)}, u32[]{:S(2)}) %collective-permute-start.1) | collective-permute-done | bytes 524320 | tf_op jit(solution)/shard_map/ppermute | solution.py:31
  78.7 1.5 convolution_add_fusion
  80.3 0.8 multiply_convert_fusion.3
  81.1 0.3 fusion.46
  81.4 0.5 fusion.44
  81.9 0.1 copy-done.22
  82.0 1.5 fusion.45
  83.6 1.2 maximum_multiply_fusion
  84.8 2.0 mul.65
  86.8 0.6 constant_dynamic-slice_fusion.2
  87.4 2.1 collective-permute-start.2
  89.6 0.5 convolution_convert_fusion.1
  90.1 1.4 collective-permute-start.6
  91.5 0.6 constant_dynamic-slice_fusion.3
  92.1 0.1 bitcast_add_fusion.1
  92.2 3.2 %collective-permute-start.3 = (bf16[64,640]{1,0:T(8,128)(2,1)S(1)}, bf16[64,640]{1,0:T(8,128)(2,1)S(1)}, u32[]{:S(2)}, u32[]{:S(2)}) collective-permute-start(bf16[64,640]{1,0:T(8,128)(2,1)S(1)} %get-tuple-element.14), channel_id=1, source_target_pairs={{0,8},{8,16},{16,24},{24,0},{1,9},{9,17},{17,25},{25,1},{2,10},{10... | collective-permute-start | bytes 245768 | tf_op jit(solution)/shard_map/ppermute | solution.py:41
  95.5 4.4 %collective-permute-start.4 = (bf16[64,640]{1,0:T(8,128)(2,1)S(1)}, bf16[64,640]{1,0:T(8,128)(2,1)S(1)}, u32[]{:S(2)}, u32[]{:S(2)}) collective-permute-start(bf16[64,640]{1,0:T(8,128)(2,1)S(1)} %get-tuple-element.16), channel_id=1, source_target_pairs={{0,16},{8,24},{16,0},{24,8},{1,17},{9,25},{17,1},{25,9},{2,18},{10... | collective-permute-start | bytes 245768 | tf_op jit(solution)/shard_map/ppermute | solution.py:41
  99.8 3.1 %collective-permute-start.5 = (bf16[64,640]{1,0:T(8,128)(2,1)S(1)}, bf16[64,640]{1,0:T(8,128)(2,1)S(1)}, u32[]{:S(2)}, u32[]{:S(2)}) collective-permute-start(bf16[64,640]{1,0:T(8,128)(2,1)S(1)} %get-tuple-element.15), channel_id=1, source_target_pairs={{0,24},{8,0},{16,8},{24,16},{1,25},{9,1},{17,9},{25,17},{2,26},{10... | collective-permute-start | bytes 245768 | tf_op jit(solution)/shard_map/ppermute | solution.py:41
  102.9 0.5 convolution_add_fusion.5
  103.5 1.8 collective-permute-done.5
  105.3 10.3 %collective-permute-done.6 = bf16[1024,256]{1,0:T(8,128)(2,1)S(1)} collective-permute-done((bf16[1024,256]{1,0:T(8,128)(2,1)S(1)}, bf16[1024,256]{1,0:T(8,128)(2,1)S(1)}, u32[]{:S(2)}, u32[]{:S(2)}) %collective-permute-start.6) | collective-permute-done | bytes 524320 | tf_op jit(solution)/shard_map/ppermute | solution.py:31
  115.6 0.1 add_convert_fusion.1
  115.8 0.7 multiply_convert_fusion.1
  116.5 0.3 copy-done.1
  116.8 0.3 fusion.47
  117.1 0.5 convolution_bitcast_fusion
  117.6 0.1 copy-done.25
  117.8 0.5 copy-done.12
  118.2 0.5 convolution_bitcast_fusion.1
  118.7 0.1 maximum_multiply_fusion.1
  118.8 0.7 mul.73
  119.6 0.6 constant_dynamic-slice_fusion
  120.2 2.9 %collective-permute-start.8 = (bf16[256,640]{1,0:T(8,128)(2,1)S(1)}, bf16[256,640]{1,0:T(8,128)(2,1)S(1)}, u32[]{:S(2)}, u32[]{:S(2)}) collective-permute-start(bf16[256,640]{1,0:T(8,128)(2,1)S(1)} %bitcast.110), channel_id=1, source_target_pairs={{0,32},{32,0},{1,33},{33,1},{2,34},{34,2},{3,35},{35,3},{4,36},{36... | collective-permute-start | bytes 983048 | tf_op jit(solution)/shard_map/ppermute | solution.py:74
  123.1 0.6 constant_dynamic-slice_fusion.1
  123.7 0.5 collective-permute-done.8
  124.2 0.1 fusion.8
  124.2 10.8 %all_to_all.15 = bf16[4,64,640]{2,1,0:T(8,128)(2,1)S(1)} all-to-all(bf16[4,64,640]{2,1,0:T(8,128)(2,1)S(1)} %bitcast.107), channel_id=1, replica_groups=mesh['y'=4,'z_hi'=2,'core'=2,'x'=4,'z_lo'=8] {'x'}, dimensions={0} | all-to-all | bytes 655360 | tf_op jit(solution)/shard_map/all_to_all | solution.py:80
  135.2 0.1 copy.57
  135.3 1.1 copy.34
  136.3 41.3 %all-to-all-start.1 = ((f32[64,1,1280]{2,1,0:T(1,128)}), f32[64,1,1280]{2,1,0:T(1,128)S(1)}, u32[]{:S(2)}, u32[]{:S(2)}) async-start(f32[64,1,1280]{2,1,0:T(1,128)} %copy.34), calls=%async_computation.1 | async-start | bytes 655360 | tf_op jit(solution)/shard_map/all_to_all | solution.py:89
  177.6 2.5 %convolution_convert_fusion = bf16[1024,256]{1,0:T(8,128)(2,1)} fusion(bf16[2,256,512]{2,1,0:T(8,128)(2,1)S(1)} %copy-done.10, bf16[1024,256]{0,1:T(8,128)(2,1)} %copy-done.25, bf16[1024,256]{0,1:T(8,128)(2,1)} %copy-done.24), kind=kOutput, calls=%fused_computation.8 | convolution fusion | flops 270794752 | bytes 1835008 | tf_op jit(solution)/shard_map/dot_general | solution.py:165
  180.2 12.1 %collective-permute-start.7 = (bf16[1024,256]{1,0:T(8,128)(2,1)}, bf16[1024,256]{1,0:T(8,128)(2,1)S(1)}, u32[]{:S(2)}, u32[]{:S(2)}) collective-permute-start(bf16[1024,256]{1,0:T(8,128)(2,1)} %convolution_convert_fusion), channel_id=1, source_target_pairs={{1,0},{2,1},{3,2},{4,3},{5,4},{6,5},{7,6},{8,7},{9,8},{10,9},{11,1... | collective-permute-start | bytes 1572872 | tf_op jit(solution)/shard_map/ppermute | solution.py:31
  192.3 6.1 %all-to-all-done.1 = f32[64,1,1280]{2,1,0:T(1,128)S(1)} async-done(((f32[64,1,1280]{2,1,0:T(1,128)}), f32[64,1,1280]{2,1,0:T(1,128)S(1)}, u32[]{:S(2)}, u32[]{:S(2)}) %all-to-all-start.1) | async-done | bytes 327712 | tf_op jit(solution)/shard_map/all_to_all | solution.py:89
  198.4 0.2 reduce_sum.19
  198.6 0.7 broadcast_in_dim.2
  199.3 9.9 %all-to-all-start.2 = ((f32[16,1,1280]{2,1,0:T(1,128)}), f32[16,1,1280]{2,1,0:T(1,128)S(1)}, u32[]{:S(2)}, u32[]{:S(2)}) async-start(f32[16,1,1280]{2,1,0:T(1,128)} %broadcast_in_dim.2), calls=%async_computation.2 | async-start | bytes 163840 | tf_op jit(solution)/shard_map/all_to_all | solution.py:91
  209.2 1.1 fusion.1
  210.4 2.5 %add_convert_fusion = bf16[1024,256]{1,0:T(8,128)(2,1)} fusion(bf16[1024,256]{1,0:T(8,128)(2,1)S(1)} %collective-permute-done.7, bf16[1024,256]{1,0:T(8,128)(2,1)S(1)} %add_convert_fusion.1, bf16[2,256,512]{2,1,0:T(8,128)(2,1)S(1)} %copy-done.16, bf16[1024,256]{0,1:T(8,128)(2,1)} %copy-done.25, bf16[1024,256]{0,1:T(8,128)(2,1)} %copy-done.24), kind=kOutput, calls=%fused_computation.26 | convolution fusion | flops 271843328 | bytes 2883584 | tf_op jit(solution)/shard_map/dot_general | solution.py:173
  212.9 10.9 %all-to-all-done.2 = f32[16,1,1280]{2,1,0:T(1,128)S(1)} async-done(((f32[16,1,1280]{2,1,0:T(1,128)}), f32[16,1,1280]{2,1,0:T(1,128)S(1)}, u32[]{:S(2)}, u32[]{:S(2)}) %all-to-all-start.2) | async-done | bytes 81952 | tf_op jit(solution)/shard_map/all_to_all | solution.py:91
  223.8 0.2 reduce.1
  224.0 0.1 reshape.51
  224.1 0.6 pad_maximum_fusion.4
  224.8 0.6 pad_maximum_fusion.2
  (61 shorter events, 0.4 us)
Async XLA Ops:
  0.6 26.7 %copy-start.8 = (bf16[2,256,512]{2,1,0:T(8,128)(2,1)S(1)}, bf16[2,256,512]{2,1,0:T(8,128)(2,1)}, u32[]{:S(2)}) copy-start(bf16[2,256,512]{2,1,0:T(8,128)(2,1)} %param.6) | copy-start | bytes 1572868
  0.6 26.7 %collective-permute-start = (bf16[1024,256]{1,0:T(8,128)(2,1)}, bf16[1024,256]{1,0:T(8,128)(2,1)S(1)}, u32[]{:S(2)}, u32[]{:S(2)}) collective-permute-start(bf16[1024,256]{1,0:T(8,128)(2,1)} %param.5), channel_id=1, source_target_pairs={{0,1},{1,2},{2,3},{3,4},{4,5},{5,6},{6,7},{7,8},{8,9},{9,10},{10,1... | collective-permute-start | bytes 1572872 | tf_op jit(solution)/shard_map/ppermute | solution.py:31
  27.3 0.8 copy-start.11
  28.1 1.2 copy-start.6
  28.1 1.2 copy-start.17
  28.6 0.8 copy-start
  29.7 51.7 %copy-start.2 = (bf16[1024,256]{1,0:T(8,128)(2,1)}, bf16[1024,256]{1,0:T(8,128)(2,1)S(1)}, u32[]{:S(2)}) copy-start(bf16[1024,256]{1,0:T(8,128)(2,1)S(1)} %fusion) | copy-start | bytes 1572868
  29.7 49.0 %collective-permute-start.1 = (bf16[1024,256]{1,0:T(8,128)(2,1)S(1)}, bf16[1024,256]{1,0:T(8,128)(2,1)}, u32[]{:S(2)}, u32[]{:S(2)}) collective-permute-start(bf16[1024,256]{1,0:T(8,128)(2,1)S(1)} %fusion), channel_id=1, source_target_pairs={{0,64},{32,96},{64,128},{96,160},{128,192},{160,224},{192,256},{22... | collective-permute-start | bytes 1572872 | tf_op jit(solution)/shard_map/ppermute | solution.py:31
  41.3 39.0 %copy-start.13 = (bf16[1024,256]{1,0:T(8,128)(2,1)S(1)}, bf16[1024,256]{1,0:T(8,128)(2,1)}, u32[]{:S(2)}) copy-start(bf16[1024,256]{1,0:T(8,128)(2,1)} %param.9) | copy-start | bytes 1572868
  81.1 0.8 copy-start.4
  81.1 1.0 copy-start.22
  81.1 2.5 %copy-start.20 = (bf16[1024,256]{0,1:T(8,128)(2,1)}, bf16[1024,256]{0,1:T(8,128)(2,1)S(1)}, u32[]{:S(2)}) copy-start(bf16[1024,256]{0,1:T(8,128)(2,1)S(1)} %get-tuple-element.11) | copy-start | bytes 1572868
  86.8 2.8 %copy-start.9 = (bf16[2,256,512]{2,1,0:T(8,128)(2,1)S(1)}, bf16[2,256,512]{2,1,0:T(8,128)(2,1)}, u32[]{:S(2)}) copy-start(bf16[2,256,512]{2,1,0:T(8,128)(2,1)} %param.6) | copy-start | bytes 1572868
  86.8 2.8 %copy-start.21 = (bf16[1024,256]{0,1:T(8,128)(2,1)S(1)}, bf16[1024,256]{0,1:T(8,128)(2,1)}, u32[]{:S(2)}) copy-start(bf16[1024,256]{0,1:T(8,128)(2,1)} %copy-done.20) | copy-start | bytes 1572868
  86.8 2.8 %copy-start.23 = (bf16[1024,256]{0,1:T(8,128)(2,1)S(1)}, bf16[1024,256]{0,1:T(8,128)(2,1)}, u32[]{:S(2)}) copy-start(bf16[1024,256]{0,1:T(8,128)(2,1)} %copy-done.22) | copy-start | bytes 1572868
  87.4 4.7 %collective-permute-start.2 = (bf16[256,640]{1,0:T(8,128)(2,1)S(1)}, bf16[256,640]{1,0:T(8,128)(2,1)S(1)}, u32[]{:S(2)}, u32[]{:S(2)}) collective-permute-start(bf16[256,640]{1,0:T(8,128)(2,1)S(1)} %bitcast.109), channel_id=1, source_target_pairs={{0,32},{32,0},{1,33},{33,1},{2,34},{34,2},{3,35},{35,3},{4,36},{36... | collective-permute-start | bytes 983048 | tf_op jit(solution)/shard_map/ppermute | solution.py:74
  90.1 12.8 %copy-start.14 = (bf16[1024,256]{1,0:T(8,128)(2,1)S(1)}, bf16[1024,256]{1,0:T(8,128)(2,1)}, u32[]{:S(2)}) copy-start(bf16[1024,256]{1,0:T(8,128)(2,1)} %param.9) | copy-start | bytes 1572868
  90.1 12.8 %copy-start.15 = (bf16[2,256,512]{2,1,0:T(8,128)(2,1)S(1)}, bf16[2,256,512]{2,1,0:T(8,128)(2,1)}, u32[]{:S(2)}) copy-start(bf16[2,256,512]{2,1,0:T(8,128)(2,1)} %param.7) | copy-start | bytes 1572868
  90.1 25.5 %collective-permute-start.6 = (bf16[1024,256]{1,0:T(8,128)(2,1)S(1)}, bf16[1024,256]{1,0:T(8,128)(2,1)S(1)}, u32[]{:S(2)}, u32[]{:S(2)}) collective-permute-start(bf16[1024,256]{1,0:T(8,128)(2,1)S(1)} %convolution_convert_fusion.1), channel_id=1, source_target_pairs={{64,0},{96,32},{128,64},{160,96},{192,128},{224,160},{256,192},{28... | collective-permute-start | bytes 1572872 | tf_op jit(solution)/shard_map/ppermute | solution.py:31
  92.2 11.2 %collective-permute-start.3 = (bf16[64,640]{1,0:T(8,128)(2,1)S(1)}, bf16[64,640]{1,0:T(8,128)(2,1)S(1)}, u32[]{:S(2)}, u32[]{:S(2)}) collective-permute-start(bf16[64,640]{1,0:T(8,128)(2,1)S(1)} %get-tuple-element.14), channel_id=1, source_target_pairs={{0,8},{8,16},{16,24},{24,0},{1,9},{9,17},{17,25},{25,1},{2,10},{10... | collective-permute-start | bytes 245768 | tf_op jit(solution)/shard_map/ppermute | solution.py:41
  95.5 8.0 %collective-permute-start.4 = (bf16[64,640]{1,0:T(8,128)(2,1)S(1)}, bf16[64,640]{1,0:T(8,128)(2,1)S(1)}, u32[]{:S(2)}, u32[]{:S(2)}) collective-permute-start(bf16[64,640]{1,0:T(8,128)(2,1)S(1)} %get-tuple-element.16), channel_id=1, source_target_pairs={{0,16},{8,24},{16,0},{24,8},{1,17},{9,25},{17,1},{25,9},{2,18},{10... | collective-permute-start | bytes 245768 | tf_op jit(solution)/shard_map/ppermute | solution.py:41
  99.8 5.5 %collective-permute-start.5 = (bf16[64,640]{1,0:T(8,128)(2,1)S(1)}, bf16[64,640]{1,0:T(8,128)(2,1)S(1)}, u32[]{:S(2)}, u32[]{:S(2)}) collective-permute-start(bf16[64,640]{1,0:T(8,128)(2,1)S(1)} %get-tuple-element.15), channel_id=1, source_target_pairs={{0,24},{8,0},{16,8},{24,16},{1,25},{9,1},{17,9},{25,17},{2,26},{10... | collective-permute-start | bytes 245768 | tf_op jit(solution)/shard_map/ppermute | solution.py:41
  103.4 12.3 %copy-start.18 = (bf16[2,256,256]{2,1,0:T(8,128)(2,1)S(1)}, bf16[2,256,256]{2,1,0:T(8,128)(2,1)}, u32[]{:S(2)}) copy-start(bf16[2,256,256]{2,1,0:T(8,128)(2,1)} %param.8) | copy-start | bytes 786436
  115.7 1.0 copy-start.1
  115.8 1.3 copy-start.7
  116.8 0.8 copy-start.24
  116.8 1.0 copy-start.25
  116.8 1.4 copy-start.12
  120.2 3.9 %collective-permute-start.8 = (bf16[256,640]{1,0:T(8,128)(2,1)S(1)}, bf16[256,640]{1,0:T(8,128)(2,1)S(1)}, u32[]{:S(2)}, u32[]{:S(2)}) collective-permute-start(bf16[256,640]{1,0:T(8,128)(2,1)S(1)} %bitcast.110), channel_id=1, source_target_pairs={{0,32},{32,0},{1,33},{33,1},{2,34},{34,2},{3,35},{35,3},{4,36},{36... | collective-permute-start | bytes 983048 | tf_op jit(solution)/shard_map/ppermute | solution.py:74
  124.2 53.4 %copy-start.10 = (bf16[2,256,512]{2,1,0:T(8,128)(2,1)S(1)}, bf16[2,256,512]{2,1,0:T(8,128)(2,1)}, u32[]{:S(2)}) copy-start(bf16[2,256,512]{2,1,0:T(8,128)(2,1)} %param.6) | copy-start | bytes 1572868
  136.3 72.9 %copy-start.3 = (bf16[1024,256]{1,0:T(8,128)(2,1)S(1)}, bf16[1024,256]{1,0:T(8,128)(2,1)}, u32[]{:S(2)}) copy-start(bf16[1024,256]{1,0:T(8,128)(2,1)} %copy-done.2) | copy-start | bytes 1572868
  136.3 72.9 %copy-start.5 = (bf16[1024,256]{0,1:T(8,128)(2,1)S(1)}, bf16[1024,256]{0,1:T(8,128)(2,1)}, u32[]{:S(2)}) copy-start(bf16[1024,256]{0,1:T(8,128)(2,1)} %copy-done.4) | copy-start | bytes 1572868
  136.3 72.9 %copy-start.19 = (bf16[2,256,256]{2,1,0:T(8,128)(2,1)S(1)}, bf16[2,256,256]{2,1,0:T(8,128)(2,1)}, u32[]{:S(2)}) copy-start(bf16[2,256,256]{2,1,0:T(8,128)(2,1)} %param.8) | copy-start | bytes 786436
  136.3 62.1 %all-to-all-start.1 = ((f32[64,1,1280]{2,1,0:T(1,128)}), f32[64,1,1280]{2,1,0:T(1,128)S(1)}, u32[]{:S(2)}, u32[]{:S(2)}) async-start(f32[64,1,1280]{2,1,0:T(1,128)} %copy.34), calls=%async_computation.1 | async-start | bytes 655360 | tf_op jit(solution)/shard_map/all_to_all | solution.py:89
  177.6 32.8 %copy-start.16 = (bf16[2,256,512]{2,1,0:T(8,128)(2,1)S(1)}, bf16[2,256,512]{2,1,0:T(8,128)(2,1)}, u32[]{:S(2)}) copy-start(bf16[2,256,512]{2,1,0:T(8,128)(2,1)} %param.7) | copy-start | bytes 1572868
  180.2 30.2 %collective-permute-start.7 = (bf16[1024,256]{1,0:T(8,128)(2,1)}, bf16[1024,256]{1,0:T(8,128)(2,1)S(1)}, u32[]{:S(2)}, u32[]{:S(2)}) collective-permute-start(bf16[1024,256]{1,0:T(8,128)(2,1)} %convolution_convert_fusion), channel_id=1, source_target_pairs={{1,0},{2,1},{3,2},{4,3},{5,4},{6,5},{7,6},{8,7},{9,8},{10,9},{11,1... | collective-permute-start | bytes 1572872 | tf_op jit(solution)/shard_map/ppermute | solution.py:31
  199.3 24.5 %all-to-all-start.2 = ((f32[16,1,1280]{2,1,0:T(1,128)}), f32[16,1,1280]{2,1,0:T(1,128)S(1)}, u32[]{:S(2)}, u32[]{:S(2)}) async-start(f32[16,1,1280]{2,1,0:T(1,128)} %broadcast_in_dim.2), calls=%async_computation.2 | async-start | bytes 163840 | tf_op jit(solution)/shard_map/all_to_all | solution.py:91

commit v12 on v7

--- a/solution.py
+++ b/solution.py
@@ -168,7 +168,7 @@
         ).astype(jnp.bfloat16)
         arrived = return_past(sent_back, layer_at)
         operands = (earlier, current, gated_out, grad_preact, upstream)
-        near_list[layer_at] = near_sum(layer_term(operands, grad_scale), layer_at == 0)
+        near_list[layer_at] = near_sum(layer_term(operands, grad_scale), True)
         if layer_at > 0:
             near_list, arrived = lax.optimization_barrier((near_list, arrived))
         local_grad = upstream.astype(jnp.float32) + jnp.dot(

time: 220 us -> 222 us (level)
  starting transfers between devices: 93.9 us -> 87.2 us
  waiting for transfers between devices: 81.5 us -> 85.3 us
  matrix products: 17.5 us -> 20.7 us
    ppermute x3 -> x0, starting transfers between devices: 10.6 us -> none  [scatter_sum(): lax.ppermute(piece.astype(jnp.bfloat16), axes, [(i, (i + shift) % size) f...]
    all_to_all x0 -> x1, waiting for transfers between devices: none -> 4.26 us  [near_sum(): lax.all_to_all(pieces, 'x', 0, 0, tiled=True).astype(jnp.float32).sum(0)]
    all_to_all x0 -> x1, starting transfers between devices: none -> 4.13 us  [near_sum(): lax.all_to_all(pieces, 'x', 0, 0, tiled=True).astype(jnp.float32).sum(0)]
    dot_general x2, matrix products: 2.99 us -> 5.41 us  [local(): jnp.dot(grad_preact, conv_now[layer_at].T, preferred_element_type=jnp.flo...]
  transfers between devices with their start and end apart: 11 -> 9, of which waited for: 6 -> 6; matrix products, arithmetic and copies ran while one was open for 6% -> 7% of each run, Pallas kernels for 0% -> 0%
where the time goes in v12:
time: 222 us; the launch traced here: 221 us
  starting transfers between devices  87.2 us (39%)
  waiting for transfers between devices  85.3 us (38%)
  matrix products  20.7 us (9%)
  blocking collectives  10.7 us (5%)
  local copies, waits for them, and re-layouts  9.49 us (4%)
  other arithmetic  6.6 us (3%)
    ppermute x4, waiting for transfers between devices, from_behind(): return lax.ppermute(array, axes, pairs)  69.6 us
    all_to_all x1, starting transfers between devices, far_sum(): lax.all_to_all(rows.astype(jnp.bfloat16), ('y', 'z_hi', 'z_lo'), 0, 0, ti...  41.2 us
    ppermute x4, starting transfers between devices, from_behind(): return lax.ppermute(array, axes, pairs)  28.2 us
    all_to_all x1, waiting for transfers between devices, far_sum(): gathered = lax.all_to_all(spread, ('y', 'z_hi', 'core'), 0, 0, tiled=True)  10.9 us
    all_to_all x1, blocking collectives, near_sum(): lax.all_to_all(pieces, 'x', 0, 0, tiled=True).astype(jnp.float32).sum(0)  10.7 us
    all_to_all x1, starting transfers between devices, far_sum(): gathered = lax.all_to_all(spread, ('y', 'z_hi', 'core'), 0, 0, tiled=True)  8.7 us
    dot_general x2, matrix products, local(): jnp.dot(grad_preact, conv_now[layer_at].T, preferred_element_type=jnp.flo...  5.41 us
    ppermute x2, starting transfers between devices, near_sum(): moved = lax.ppermute(given.astype(jnp.bfloat16), 'core', [(0, 1), (1, 0)])  4.99 us
  transfers between devices with their start and end apart: 9, of which 6 were waited for; matrix products, arithmetic and copies ran while one was open for 7% of the time, Pallas kernels for 0%

profile of v12, /device:TPU:1, one launch (start us, length us, event | category | flops | bytes accessed | tf_op | source)
XLA Modules:
  0.0 221.2 jit_solution(379256652190839102)
XLA Ops:
  0.6 4.5 %collective-permute-start = (bf16[1024,256]{1,0:T(8,128)(2,1)}, bf16[1024,256]{1,0:T(8,128)(2,1)S(1)}, u32[]{:S(2)}, u32[]{:S(2)}) collective-permute-start(bf16[1024,256]{1,0:T(8,128)(2,1)} %param.5), channel_id=1, source_target_pairs={{0,1},{1,2},{2,3},{3,4},{4,5},{5,6},{6,7},{7,8},{8,9},{9,10},{10,1... | collective-permute-start | bytes 1572872 | tf_op jit(solution)/shard_map/ppermute | solution.py:31
  5.2 1.6 fusion.18
  6.8 20.6 %collective-permute-done = bf16[1024,256]{1,0:T(8,128)(2,1)S(1)} collective-permute-done((bf16[1024,256]{1,0:T(8,128)(2,1)}, bf16[1024,256]{1,0:T(8,128)(2,1)S(1)}, u32[]{:S(2)}, u32[]{:S(2)}) %collective-permute-start) | collective-permute-done | bytes 524320 | tf_op jit(solution)/shard_map/ppermute | solution.py:31
  27.3 0.5 convolution_add_fusion.1
  27.8 0.3 copy-done.11
  28.1 0.4 multiply_convert_fusion.5
  28.6 0.8 copy-done
  29.4 0.4 fusion
  29.7 10.2 %collective-permute-start.1 = (bf16[1024,256]{1,0:T(8,128)(2,1)S(1)}, bf16[1024,256]{1,0:T(8,128)(2,1)}, u32[]{:S(2)}, u32[]{:S(2)}) collective-permute-start(bf16[1024,256]{1,0:T(8,128)(2,1)S(1)} %fusion), channel_id=1, source_target_pairs={{0,64},{32,96},{64,128},{96,160},{128,192},{160,224},{192,256},{22... | collective-permute-start | bytes 1572872 | tf_op jit(solution)/shard_map/ppermute | solution.py:31
  39.9 1.4 fusion.13
  41.3 0.0 copy-start.13
  41.4 37.4 %collective-permute-done.1 = bf16[1024,256]{1,0:T(8,128)(2,1)} collective-permute-done((bf16[1024,256]{1,0:T(8,128)(2,1)S(1)}, bf16[1024,256]{1,0:T(8,128)(2,1)}, u32[]{:S(2)}, u32[]{:S(2)}) %collective-permute-start.1) | collective-permute-done | bytes 524320 | tf_op jit(solution)/shard_map/ppermute | solution.py:31
  78.8 1.5 convolution_add_fusion
  80.3 0.8 multiply_convert_fusion.3
  81.1 0.3 fusion.42
  81.4 0.5 fusion.40
  81.9 0.1 copy-done.19
  82.1 1.5 fusion.41
  83.6 1.2 maximum_multiply_fusion
  84.8 2.0 mul.65
  86.8 0.0 copy-start.9
  86.8 0.6 constant_dynamic-slice_fusion.2
  87.5 2.1 collective-permute-start.2
  89.6 1.3 convolution_convert_fusion.1
  90.9 1.3 collective-permute-start.3
  92.2 0.6 constant_dynamic-slice_fusion.3
  92.8 0.8 fusion.9
  93.6 4.1 %all-to-all-start = ((bf16[4,64,640]{2,1,0:T(8,128)(2,1)}), bf16[4,64,640]{2,1,0:T(8,128)(2,1)S(1)}, u32[]{:S(2)}, u32[]{:S(2)}) async-start(bf16[4,64,640]{2,1,0:T(8,128)(2,1)} %bitcast.7), calls=%async_computation | async-start | bytes 655360 | tf_op jit(solution)/shard_map/all_to_all | solution.py:80
  97.7 2.9 %convolution_add_fusion.5 = f32[1024,256]{1,0:T(8,128)} fusion(bf16[1024,256]{1,0:T(8,128)(2,1)} %param.9, bf16[2,256,512]{2,1,0:T(8,128)(2,1)} %param.7, bf16[1024,256]{0,1:T(8,128)(2,1)} %copy-done.19, bf16[1024,256]{0,1:T(8,128)(2,1)} %copy-done.17), kind=kOutput, calls=%fused_computation.5 | convolution fusion | flops 271056896 | bytes 2883584 | tf_op jit(solution)/shard_map/dot_general | solution.py:174
  100.6 4.3 %all-to-all-done = bf16[4,64,640]{2,1,0:T(8,128)(2,1)S(1)} async-done(((bf16[4,64,640]{2,1,0:T(8,128)(2,1)}), bf16[4,64,640]{2,1,0:T(8,128)(2,1)S(1)}, u32[]{:S(2)}, u32[]{:S(2)}) %all-to-all-start) | async-done | bytes 327712 | tf_op jit(solution)/shard_map/all_to_all | solution.py:80
  104.9 11.7 %collective-permute-done.3 = bf16[1024,256]{1,0:T(8,128)(2,1)} collective-permute-done((bf16[1024,256]{1,0:T(8,128)(2,1)}, bf16[1024,256]{1,0:T(8,128)(2,1)}, u32[]{:S(2)}, u32[]{:S(2)}) %collective-permute-start.3) | collective-permute-done | bytes 524320 | tf_op jit(solution)/shard_map/ppermute | solution.py:31
  116.6 1.5 add_convert_fusion.1
  118.1 0.7 multiply_convert_fusion.1
  118.8 0.3 copy-done.1
  119.1 0.3 fusion.43
  119.4 0.5 convolution_bitcast_fusion
  119.9 0.2 copy-done.22
  120.1 0.5 copy-done.12
  120.6 0.5 convolution_bitcast_fusion.1
  121.0 0.1 maximum_multiply_fusion.1
  121.2 0.7 mul.73
  121.9 0.6 constant_dynamic-slice_fusion
  122.5 2.9 %collective-permute-start.5 = (bf16[256,640]{1,0:T(8,128)(2,1)S(1)}, bf16[256,640]{1,0:T(8,128)(2,1)S(1)}, u32[]{:S(2)}, u32[]{:S(2)}) collective-permute-start(bf16[256,640]{1,0:T(8,128)(2,1)S(1)} %bitcast.98), channel_id=1, source_target_pairs={{0,32},{32,0},{1,33},{33,1},{2,34},{34,2},{3,35},{35,3},{4,36},{36... | collective-permute-start | bytes 983048 | tf_op jit(solution)/shard_map/ppermute | solution.py:74
  125.4 0.6 constant_dynamic-slice_fusion.1
  126.0 0.5 collective-permute-done.5
  126.5 0.1 fusion.8
  126.5 10.7 %all_to_all.20 = bf16[4,64,640]{2,1,0:T(8,128)(2,1)S(1)} all-to-all(bf16[4,64,640]{2,1,0:T(8,128)(2,1)S(1)} %bitcast.95), channel_id=1, replica_groups=mesh['y'=4,'z_hi'=2,'core'=2,'x'=4,'z_lo'=8] {'x'}, dimensions={0} | all-to-all | bytes 655360 | tf_op jit(solution)/shard_map/all_to_all | solution.py:80
  137.4 0.5 broadcast.36
  137.9 0.7 reduce.3
  138.6 0.7 reshape.58
  139.3 41.2 %all-to-all-start.2 = ((bf16[64,2,640]{2,1,0:T(2,128)(2,1)}), bf16[64,2,640]{2,1,0:T(2,128)(2,1)S(1)}, u32[]{:S(2)}, u32[]{:S(2)}) async-start(bf16[64,2,640]{2,1,0:T(2,128)(2,1)} %reshape.58), calls=%async_computation.2 | async-start | bytes 327680 | tf_op jit(solution)/shard_map/all_to_all | solution.py:89
  180.6 2.5 %convolution_convert_fusion = bf16[1024,256]{1,0:T(8,128)(2,1)} fusion(bf16[2,256,512]{2,1,0:T(8,128)(2,1)S(1)} %copy-done.10, bf16[1024,256]{0,1:T(8,128)(2,1)} %copy-done.22, bf16[1024,256]{0,1:T(8,128)(2,1)} %copy-done.21), kind=kOutput, calls=%fused_computation.8 | convolution fusion | flops 270794752 | bytes 1835008 | tf_op jit(solution)/shard_map/dot_general | solution.py:166
  183.1 12.2 %collective-permute-start.4 = (bf16[1024,256]{1,0:T(8,128)(2,1)}, bf16[1024,256]{1,0:T(8,128)(2,1)S(1)}, u32[]{:S(2)}, u32[]{:S(2)}) collective-permute-start(bf16[1024,256]{1,0:T(8,128)(2,1)} %convolution_convert_fusion), channel_id=1, source_target_pairs={{1,0},{2,1},{3,2},{4,3},{5,4},{6,5},{7,6},{8,7},{9,8},{10,9},{11,1... | collective-permute-start | bytes 1572872 | tf_op jit(solution)/shard_map/ppermute | solution.py:31
  195.3 0.1 reshape.59
  195.4 0.3 convert_reduce_fusion.1
  195.7 0.7 broadcast_in_dim.2
  196.4 8.7 %all-to-all-start.3 = ((f32[16,1,1280]{2,1,0:T(1,128)}), f32[16,1,1280]{2,1,0:T(1,128)S(1)}, u32[]{:S(2)}, u32[]{:S(2)}) async-start(f32[16,1,1280]{2,1,0:T(1,128)} %broadcast_in_dim.2), calls=%async_computation.3 | async-start | bytes 163840 | tf_op jit(solution)/shard_map/all_to_all | solution.py:92
  205.1 1.1 fusion.1
  206.3 2.5 %add_convert_fusion = bf16[1024,256]{1,0:T(8,128)(2,1)} fusion(bf16[1024,256]{1,0:T(8,128)(2,1)S(1)} %collective-permute-done.4, bf16[1024,256]{1,0:T(8,128)(2,1)S(1)} %add_convert_fusion.1, bf16[2,256,512]{2,1,0:T(8,128)(2,1)S(1)} %copy-done.14, bf16[1024,256]{0,1:T(8,128)(2,1)} %copy-done.22, bf16[1024,256]{0,1:T(8,128)(2,1)} %copy-done.21), kind=kOutput, calls=%fused_computation.26 | convolution fusion | flops 271843328 | bytes 2883584 | tf_op jit(solution)/shard_map/dot_general | solution.py:174
  208.7 10.9 %all-to-all-done.3 = f32[16,1,1280]{2,1,0:T(1,128)S(1)} async-done(((f32[16,1,1280]{2,1,0:T(1,128)}), f32[16,1,1280]{2,1,0:T(1,128)S(1)}, u32[]{:S(2)}, u32[]{:S(2)}) %all-to-all-start.3) | async-done | bytes 81952 | tf_op jit(solution)/shard_map/all_to_all | solution.py:92
  219.7 0.2 reduce.2
  219.9 0.1 reshape.54
  220.0 0.6 pad_maximum_fusion.4
  220.6 0.6 pad_maximum_fusion.2
  (53 shorter events, 0.4 us)
Async XLA Ops:
  0.6 26.7 %copy-start.8 = (bf16[2,256,512]{2,1,0:T(8,128)(2,1)S(1)}, bf16[2,256,512]{2,1,0:T(8,128)(2,1)}, u32[]{:S(2)}) copy-start(bf16[2,256,512]{2,1,0:T(8,128)(2,1)} %param.6) | copy-start | bytes 1572868
  0.6 26.7 %collective-permute-start = (bf16[1024,256]{1,0:T(8,128)(2,1)}, bf16[1024,256]{1,0:T(8,128)(2,1)S(1)}, u32[]{:S(2)}, u32[]{:S(2)}) collective-permute-start(bf16[1024,256]{1,0:T(8,128)(2,1)} %param.5), channel_id=1, source_target_pairs={{0,1},{1,2},{2,3},{3,4},{4,5},{5,6},{6,7},{7,8},{8,9},{9,10},{10,1... | collective-permute-start | bytes 1572872 | tf_op jit(solution)/shard_map/ppermute | solution.py:31
  27.3 0.8 copy-start.11
  28.1 1.2 copy-start.6
  28.1 1.2 copy-start.15
  28.6 0.8 copy-start
  29.7 51.7 %copy-start.2 = (bf16[1024,256]{1,0:T(8,128)(2,1)}, bf16[1024,256]{1,0:T(8,128)(2,1)S(1)}, u32[]{:S(2)}) copy-start(bf16[1024,256]{1,0:T(8,128)(2,1)S(1)} %fusion) | copy-start | bytes 1572868
  29.7 49.0 %collective-permute-start.1 = (bf16[1024,256]{1,0:T(8,128)(2,1)S(1)}, bf16[1024,256]{1,0:T(8,128)(2,1)}, u32[]{:S(2)}, u32[]{:S(2)}) collective-permute-start(bf16[1024,256]{1,0:T(8,128)(2,1)S(1)} %fusion), channel_id=1, source_target_pairs={{0,64},{32,96},{64,128},{96,160},{128,192},{160,224},{192,256},{22... | collective-permute-start | bytes 1572872 | tf_op jit(solution)/shard_map/ppermute | solution.py:31
  41.3 39.0 %copy-start.13 = (bf16[1024,256]{1,0:T(8,128)(2,1)S(1)}, bf16[1024,256]{1,0:T(8,128)(2,1)}, u32[]{:S(2)}) copy-start(bf16[1024,256]{1,0:T(8,128)(2,1)} %param.9) | copy-start | bytes 1572868
  81.1 0.8 copy-start.4
  81.1 1.0 copy-start.19
  81.1 2.5 %copy-start.17 = (bf16[1024,256]{0,1:T(8,128)(2,1)}, bf16[1024,256]{0,1:T(8,128)(2,1)S(1)}, u32[]{:S(2)}) copy-start(bf16[1024,256]{0,1:T(8,128)(2,1)S(1)} %get-tuple-element.11) | copy-start | bytes 1572868
  86.8 2.8 %copy-start.9 = (bf16[2,256,512]{2,1,0:T(8,128)(2,1)S(1)}, bf16[2,256,512]{2,1,0:T(8,128)(2,1)}, u32[]{:S(2)}) copy-start(bf16[2,256,512]{2,1,0:T(8,128)(2,1)} %param.6) | copy-start | bytes 1572868
  86.8 2.8 %copy-start.18 = (bf16[1024,256]{0,1:T(8,128)(2,1)S(1)}, bf16[1024,256]{0,1:T(8,128)(2,1)}, u32[]{:S(2)}) copy-start(bf16[1024,256]{0,1:T(8,128)(2,1)} %copy-done.17) | copy-start | bytes 1572868
  86.8 2.8 %copy-start.20 = (bf16[1024,256]{0,1:T(8,128)(2,1)S(1)}, bf16[1024,256]{0,1:T(8,128)(2,1)}, u32[]{:S(2)}) copy-start(bf16[1024,256]{0,1:T(8,128)(2,1)} %copy-done.19) | copy-start | bytes 1572868
  87.5 5.3 %collective-permute-start.2 = (bf16[256,640]{1,0:T(8,128)(2,1)S(1)}, bf16[256,640]{1,0:T(8,128)(2,1)S(1)}, u32[]{:S(2)}, u32[]{:S(2)}) collective-permute-start(bf16[256,640]{1,0:T(8,128)(2,1)S(1)} %bitcast.97), channel_id=1, source_target_pairs={{0,32},{32,0},{1,33},{33,1},{2,34},{34,2},{3,35},{35,3},{4,36},{36... | collective-permute-start | bytes 983048 | tf_op jit(solution)/shard_map/ppermute | solution.py:74
  90.9 25.7 %collective-permute-start.3 = (bf16[1024,256]{1,0:T(8,128)(2,1)}, bf16[1024,256]{1,0:T(8,128)(2,1)}, u32[]{:S(2)}, u32[]{:S(2)}) collective-permute-start(bf16[1024,256]{1,0:T(8,128)(2,1)} %convolution_convert_fusion.1), channel_id=1, source_target_pairs={{64,0},{96,32},{128,64},{160,96},{192,128},{224,160},{256,192},{28... | collective-permute-start | bytes 1572872 | tf_op jit(solution)/shard_map/ppermute | solution.py:31
  93.6 11.3 %all-to-all-start = ((bf16[4,64,640]{2,1,0:T(8,128)(2,1)}), bf16[4,64,640]{2,1,0:T(8,128)(2,1)S(1)}, u32[]{:S(2)}, u32[]{:S(2)}) async-start(bf16[4,64,640]{2,1,0:T(8,128)(2,1)} %bitcast.7), calls=%async_computation | async-start | bytes 655360 | tf_op jit(solution)/shard_map/all_to_all | solution.py:80
  97.7 20.4 %copy-start.16 = (bf16[2,256,256]{2,1,0:T(8,128)(2,1)S(1)}, bf16[2,256,256]{2,1,0:T(8,128)(2,1)}, u32[]{:S(2)}) copy-start(bf16[2,256,256]{2,1,0:T(8,128)(2,1)} %param.8) | copy-start | bytes 786436
  118.1 1.0 copy-start.1
  118.1 1.3 copy-start.7
  119.1 0.8 copy-start.21
  119.1 1.0 copy-start.22
  119.1 1.4 copy-start.12
  122.5 3.9 %collective-permute-start.5 = (bf16[256,640]{1,0:T(8,128)(2,1)S(1)}, bf16[256,640]{1,0:T(8,128)(2,1)S(1)}, u32[]{:S(2)}, u32[]{:S(2)}) collective-permute-start(bf16[256,640]{1,0:T(8,128)(2,1)S(1)} %bitcast.98), channel_id=1, source_target_pairs={{0,32},{32,0},{1,33},{33,1},{2,34},{34,2},{3,35},{35,3},{4,36},{36... | collective-permute-start | bytes 983048 | tf_op jit(solution)/shard_map/ppermute | solution.py:74
  126.0 54.6 %copy-start.10 = (bf16[2,256,512]{2,1,0:T(8,128)(2,1)S(1)}, bf16[2,256,512]{2,1,0:T(8,128)(2,1)}, u32[]{:S(2)}) copy-start(bf16[2,256,512]{2,1,0:T(8,128)(2,1)} %param.6) | copy-start | bytes 1572868
  139.3 65.8 %copy-start.3 = (bf16[1024,256]{1,0:T(8,128)(2,1)S(1)}, bf16[1024,256]{1,0:T(8,128)(2,1)}, u32[]{:S(2)}) copy-start(bf16[1024,256]{1,0:T(8,128)(2,1)} %copy-done.2) | copy-start | bytes 1572868
  139.3 65.8 %copy-start.5 = (bf16[1024,256]{0,1:T(8,128)(2,1)S(1)}, bf16[1024,256]{0,1:T(8,128)(2,1)}, u32[]{:S(2)}) copy-start(bf16[1024,256]{0,1:T(8,128)(2,1)} %copy-done.4) | copy-start | bytes 1572868
  139.3 56.0 %all-to-all-start.2 = ((bf16[64,2,640]{2,1,0:T(2,128)(2,1)}), bf16[64,2,640]{2,1,0:T(2,128)(2,1)S(1)}, u32[]{:S(2)}, u32[]{:S(2)}) async-start(bf16[64,2,640]{2,1,0:T(2,128)(2,1)} %reshape.58), calls=%async_computation.2 | async-start | bytes 327680 | tf_op jit(solution)/shard_map/all_to_all | solution.py:89
  183.0 23.2 %copy-start.14 = (bf16[2,256,512]{2,1,0:T(8,128)(2,1)S(1)}, bf16[2,256,512]{2,1,0:T(8,128)(2,1)}, u32[]{:S(2)}) copy-start(bf16[2,256,512]{2,1,0:T(8,128)(2,1)} %param.7) | copy-start | bytes 1572868
  183.1 23.2 %collective-permute-start.4 = (bf16[1024,256]{1,0:T(8,128)(2,1)}, bf16[1024,256]{1,0:T(8,128)(2,1)S(1)}, u32[]{:S(2)}, u32[]{:S(2)}) collective-permute-start(bf16[1024,256]{1,0:T(8,128)(2,1)} %convolution_convert_fusion), channel_id=1, source_target_pairs={{1,0},{2,1},{3,2},{4,3},{5,4},{6,5},{7,6},{8,7},{9,8},{10,9},{11,1... | collective-permute-start | bytes 1572872 | tf_op jit(solution)/shard_map/ppermute | solution.py:31
  196.4 23.3 %all-to-all-start.3 = ((f32[16,1,1280]{2,1,0:T(1,128)}), f32[16,1,1280]{2,1,0:T(1,128)S(1)}, u32[]{:S(2)}, u32[]{:S(2)}) async-start(f32[16,1,1280]{2,1,0:T(1,128)} %broadcast_in_dim.2), calls=%async_computation.3 | async-start | bytes 163840 | tf_op jit(solution)/shard_map/all_to_all | solution.py:92

commit v13 on v7

--- a/solution.py
+++ b/solution.py
@@ -88,8 +88,7 @@
     rows = rows.reshape(hi_size * lo_size, 1, term.shape[1])
     row = lax.all_to_all(rows.astype(jnp.bfloat16), ("y", "z_hi", "z_lo"), 0, 0, tiled=True)
     row = row.astype(jnp.float32).sum(0)
-    spread = jnp.broadcast_to(row[None], (hi_size * core_size, *row.shape))
-    gathered = lax.all_to_all(spread, ("y", "z_hi", "core"), 0, 0, tiled=True)
+    gathered = lax.all_gather(row, ("y", "z_hi", "core"), axis=0, tiled=False)
     return gathered.reshape(hi_size, core_size, term.shape[1])
 
 

time: 220 us -> 239 us (1.086)
  blocking collectives: 10.7 us -> 40.6 us
  starting transfers between devices: 93.9 us -> 82.7 us
    all_gather x0 -> x1, blocking collectives: none -> 40.6 us  [far_sum(): gathered = lax.all_gather(row, ('y', 'z_hi', 'core'), axis=0, tiled=False)]
    all_to_all x1, waiting for transfers between devices: 10.9 us -> 0.01 us  [near_sum(): lax.all_to_all(pieces, 'x', 0, 0, tiled=True).astype(jnp.float32).sum(0)]
    all_to_all x1 -> x0, blocking collectives: 10.7 us -> none  [near_sum(): lax.all_to_all(pieces, 'x', 0, 0, tiled=True).astype(jnp.float32).sum(0)]
    all_to_all x1, waiting for transfers between devices: 0.01 us -> 10.7 us  [far_sum(): lax.all_to_all(rows.astype(jnp.bfloat16), ('y', 'z_hi', 'z_lo'), 0, 0, ti...]
    all_to_all x1, starting transfers between devices: 8.7 us -> 4.12 us  [near_sum(): lax.all_to_all(pieces, 'x', 0, 0, tiled=True).astype(jnp.float32).sum(0)]
    all_to_all x1, starting transfers between devices: 41.2 us -> 37.7 us  [far_sum(): lax.all_to_all(rows.astype(jnp.bfloat16), ('y', 'z_hi', 'z_lo'), 0, 0, ti...]
    ppermute x4, starting transfers between devices: 28.3 us -> 25.1 us  [from_behind(): return lax.ppermute(array, axes, pairs)]
where the time goes in v13:
time: 239 us; the launch traced here: 238 us
  starting transfers between devices  82.7 us (35%)
  waiting for transfers between devices  81.3 us (34%)
  blocking collectives  40.6 us (17%)
  matrix products  17.6 us (7%)
  local copies, waits for them, and re-layouts  8.9 us (4%)
  other arithmetic  5.26 us (2%)
    ppermute x4, waiting for transfers between devices, from_behind(): return lax.ppermute(array, axes, pairs)  68.2 us
    all_gather x1, blocking collectives, far_sum(): gathered = lax.all_gather(row, ('y', 'z_hi', 'core'), axis=0, tiled=False)  40.6 us
    all_to_all x1, starting transfers between devices, far_sum(): lax.all_to_all(rows.astype(jnp.bfloat16), ('y', 'z_hi', 'z_lo'), 0, 0, ti...  37.7 us
    ppermute x4, starting transfers between devices, from_behind(): return lax.ppermute(array, axes, pairs)  25.1 us
    all_to_all x1, waiting for transfers between devices, far_sum(): lax.all_to_all(rows.astype(jnp.bfloat16), ('y', 'z_hi', 'z_lo'), 0, 0, ti...  10.7 us
    ppermute x3, starting transfers between devices, scatter_sum(): lax.ppermute(piece.astype(jnp.bfloat16), axes, [(i, (i + shift) % size) f...  10.6 us
    ppermute x2, starting transfers between devices, near_sum(): moved = lax.ppermute(given.astype(jnp.bfloat16), 'core', [(0, 1), (1, 0)])  5.12 us
  transfers between devices with their start and end apart: 11, of which 6 were waited for; matrix products, arithmetic and copies ran while one was open for 6% of the time, Pallas kernels for 0%

profile of v13, /device:TPU:1, one launch (start us, length us, event | category | flops | bytes accessed | tf_op | source)
XLA Modules:
  0.0 237.6 jit_solution(13078978698089393025)
XLA Ops:
  0.6 4.5 %collective-permute-start = (bf16[1024,256]{1,0:T(8,128)(2,1)}, bf16[1024,256]{1,0:T(8,128)(2,1)S(1)}, u32[]{:S(2)}, u32[]{:S(2)}) collective-permute-start(bf16[1024,256]{1,0:T(8,128)(2,1)} %param.5), channel_id=1, source_target_pairs={{0,1},{1,2},{2,3},{3,4},{4,5},{5,6},{6,7},{7,8},{8,9},{9,10},{10,1... | collective-permute-start | bytes 1572872 | tf_op jit(solution)/shard_map/ppermute | solution.py:31
  5.2 1.6 fusion.17
  6.8 20.6 %collective-permute-done = bf16[1024,256]{1,0:T(8,128)(2,1)S(1)} collective-permute-done((bf16[1024,256]{1,0:T(8,128)(2,1)}, bf16[1024,256]{1,0:T(8,128)(2,1)S(1)}, u32[]{:S(2)}, u32[]{:S(2)}) %collective-permute-start) | collective-permute-done | bytes 524320 | tf_op jit(solution)/shard_map/ppermute | solution.py:31
  27.3 0.5 convolution_add_fusion.1
  27.8 0.3 copy-done.11
  28.1 0.4 multiply_convert_fusion.5
  28.6 0.8 copy-done
  29.4 0.4 fusion
  29.7 10.2 %collective-permute-start.1 = (bf16[1024,256]{1,0:T(8,128)(2,1)S(1)}, bf16[1024,256]{1,0:T(8,128)(2,1)}, u32[]{:S(2)}, u32[]{:S(2)}) collective-permute-start(bf16[1024,256]{1,0:T(8,128)(2,1)S(1)} %fusion), channel_id=1, source_target_pairs={{0,64},{32,96},{64,128},{96,160},{128,192},{160,224},{192,256},{22... | collective-permute-start | bytes 1572872 | tf_op jit(solution)/shard_map/ppermute | solution.py:31
  39.9 1.4 fusion.12
  41.4 37.4 %collective-permute-done.1 = bf16[1024,256]{1,0:T(8,128)(2,1)} collective-permute-done((bf16[1024,256]{1,0:T(8,128)(2,1)S(1)}, bf16[1024,256]{1,0:T(8,128)(2,1)}, u32[]{:S(2)}, u32[]{:S(2)}) %collective-permute-start.1) | collective-permute-done | bytes 524320 | tf_op jit(solution)/shard_map/ppermute | solution.py:31
  78.8 1.5 convolution_add_fusion
  80.3 0.8 multiply_convert_fusion.3
  81.1 0.3 fusion.46
  81.4 0.5 fusion.44
  81.9 0.1 copy-done.21
  82.1 1.5 fusion.45
  83.6 1.2 maximum_multiply_fusion
  84.8 2.0 mul.65
  86.8 0.6 constant_dynamic-slice_fusion.2
  87.5 2.1 collective-permute-start.2
  89.6 0.5 convolution_convert_fusion.1
  90.1 1.4 collective-permute-start.6
  91.6 0.6 constant_dynamic-slice_fusion.3
  92.2 0.1 bitcast_add_fusion.1
  92.3 3.2 %collective-permute-start.3 = (bf16[64,640]{1,0:T(8,128)(2,1)S(1)}, bf16[64,640]{1,0:T(8,128)(2,1)S(1)}, u32[]{:S(2)}, u32[]{:S(2)}) collective-permute-start(bf16[64,640]{1,0:T(8,128)(2,1)S(1)} %get-tuple-element.14), channel_id=1, source_target_pairs={{0,8},{8,16},{16,24},{24,0},{1,9},{9,17},{17,25},{25,1},{2,10},{10... | collective-permute-start | bytes 245768 | tf_op jit(solution)/shard_map/ppermute | solution.py:41
  95.5 4.4 %collective-permute-start.4 = (bf16[64,640]{1,0:T(8,128)(2,1)S(1)}, bf16[64,640]{1,0:T(8,128)(2,1)S(1)}, u32[]{:S(2)}, u32[]{:S(2)}) collective-permute-start(bf16[64,640]{1,0:T(8,128)(2,1)S(1)} %get-tuple-element.16), channel_id=1, source_target_pairs={{0,16},{8,24},{16,0},{24,8},{1,17},{9,25},{17,1},{25,9},{2,18},{10... | collective-permute-start | bytes 245768 | tf_op jit(solution)/shard_map/ppermute | solution.py:41
  99.9 3.1 %collective-permute-start.5 = (bf16[64,640]{1,0:T(8,128)(2,1)S(1)}, bf16[64,640]{1,0:T(8,128)(2,1)S(1)}, u32[]{:S(2)}, u32[]{:S(2)}) collective-permute-start(bf16[64,640]{1,0:T(8,128)(2,1)S(1)} %get-tuple-element.15), channel_id=1, source_target_pairs={{0,24},{8,0},{16,8},{24,16},{1,25},{9,1},{17,9},{25,17},{2,26},{10... | collective-permute-start | bytes 245768 | tf_op jit(solution)/shard_map/ppermute | solution.py:41
  103.0 0.5 convolution_add_fusion.5
  103.5 1.9 collective-permute-done.5
  105.4 10.2 %collective-permute-done.6 = bf16[1024,256]{1,0:T(8,128)(2,1)S(1)} collective-permute-done((bf16[1024,256]{1,0:T(8,128)(2,1)S(1)}, bf16[1024,256]{1,0:T(8,128)(2,1)S(1)}, u32[]{:S(2)}, u32[]{:S(2)}) %collective-permute-start.6) | collective-permute-done | bytes 524320 | tf_op jit(solution)/shard_map/ppermute | solution.py:31
  115.6 0.1 add_convert_fusion.1
  115.8 0.7 multiply_convert_fusion.1
  116.5 0.3 copy-done.1
  116.8 0.3 fusion.47
  117.2 0.5 convolution_bitcast_fusion
  117.7 0.2 copy-done.24
  117.8 0.4 copy-done.12
  118.3 0.5 convolution_bitcast_fusion.1
  118.8 0.1 maximum_multiply_fusion.1
  118.9 0.7 mul.73
  119.6 0.6 constant_dynamic-slice_fusion
  120.3 3.0 %collective-permute-start.8 = (bf16[256,640]{1,0:T(8,128)(2,1)S(1)}, bf16[256,640]{1,0:T(8,128)(2,1)S(1)}, u32[]{:S(2)}, u32[]{:S(2)}) collective-permute-start(bf16[256,640]{1,0:T(8,128)(2,1)S(1)} %bitcast.109), channel_id=1, source_target_pairs={{0,32},{32,0},{1,33},{33,1},{2,34},{34,2},{3,35},{35,3},{4,36},{36... | collective-permute-start | bytes 983048 | tf_op jit(solution)/shard_map/ppermute | solution.py:74
  123.3 0.6 constant_dynamic-slice_fusion.1
  123.9 0.5 collective-permute-done.8
  124.3 0.8 fusion.8
  125.1 4.1 %all-to-all-start = ((bf16[4,64,640]{2,1,0:T(8,128)(2,1)}), bf16[4,64,640]{2,1,0:T(8,128)(2,1)S(1)}, u32[]{:S(2)}, u32[]{:S(2)}) async-start(bf16[4,64,640]{2,1,0:T(8,128)(2,1)} %bitcast.15), calls=%async_computation | async-start | bytes 655360 | tf_op jit(solution)/shard_map/all_to_all | solution.py:80
  129.3 2.6 %convolution_convert_fusion = bf16[1024,256]{1,0:T(8,128)(2,1)} fusion(bf16[2,256,512]{2,1,0:T(8,128)(2,1)S(1)} %copy-done.10, bf16[1024,256]{0,1:T(8,128)(2,1)} %copy-done.24, bf16[1024,256]{0,1:T(8,128)(2,1)} %copy-done.23), kind=kOutput, calls=%fused_computation.8 | convolution fusion | flops 270794752 | bytes 1835008 | tf_op jit(solution)/shard_map/dot_general | solution.py:165
  131.8 9.0 %collective-permute-start.7 = (bf16[1024,256]{1,0:T(8,128)(2,1)}, bf16[1024,256]{1,0:T(8,128)(2,1)S(1)}, u32[]{:S(2)}, u32[]{:S(2)}) collective-permute-start(bf16[1024,256]{1,0:T(8,128)(2,1)} %convolution_convert_fusion), channel_id=1, source_target_pairs={{1,0},{2,1},{3,2},{4,3},{5,4},{6,5},{7,6},{8,7},{9,8},{10,9},{11,1... | collective-permute-start | bytes 1572872 | tf_op jit(solution)/shard_map/ppermute | solution.py:31
  140.9 0.1 reduce.1
  141.0 0.5 broadcast.37
  141.5 0.7 reduce.3
  142.2 0.7 reshape.65
  142.9 37.7 %all-to-all-start.1 = ((bf16[64,2,640]{2,1,0:T(2,128)(2,1)}), bf16[64,2,640]{2,1,0:T(2,128)(2,1)S(1)}, u32[]{:S(2)}, u32[]{:S(2)}) async-start(bf16[64,2,640]{2,1,0:T(2,128)(2,1)} %reshape.65), calls=%async_computation.1 | async-start | bytes 327680 | tf_op jit(solution)/shard_map/all_to_all | solution.py:89
  180.7 1.2 fusion.1
  181.8 2.5 %add_convert_fusion = bf16[1024,256]{1,0:T(8,128)(2,1)} fusion(bf16[1024,256]{1,0:T(8,128)(2,1)S(1)} %collective-permute-done.7, bf16[1024,256]{1,0:T(8,128)(2,1)S(1)} %add_convert_fusion.1, bf16[2,256,512]{2,1,0:T(8,128)(2,1)S(1)} %copy-done.16, bf16[1024,256]{0,1:T(8,128)(2,1)} %copy-done.24, bf16[1024,256]{0,1:T(8,128)(2,1)} %copy-done.23), kind=kOutput, calls=%fused_computation.26 | convolution fusion | flops 271843328 | bytes 2883584 | tf_op jit(solution)/shard_map/dot_general | solution.py:173
  184.3 10.7 %all-to-all-done.1 = bf16[64,2,640]{2,1,0:T(2,128)(2,1)S(1)} async-done(((bf16[64,2,640]{2,1,0:T(2,128)(2,1)}), bf16[64,2,640]{2,1,0:T(2,128)(2,1)S(1)}, u32[]{:S(2)}, u32[]{:S(2)}) %all-to-all-start.1) | async-done | bytes 163872 | tf_op jit(solution)/shard_map/all_to_all | solution.py:89
  195.0 0.1 reshape.66
  195.1 0.3 convert_reduce_fusion
  195.5 40.6 %all-gather.1 = f32[16,1,1280]{2,1,0:T(1,128)S(1)} all-gather(f32[1,1,1280]{2,1,0:T(1,128)S(1)} %reshape.61), channel_id=2, replica_groups=mesh['y'=4,'z_hi'=2,'core'=2,'x'=4,'z_lo'=8] {'y','z_hi','core'}, dimensions={0}, use_global_device_ids=true | all-gather | bytes 87040 | tf_op jit(solution)/shard_map/all_gather | solution.py:91
  236.1 0.2 reduce.2
  236.3 0.1 reshape.56
  236.4 0.6 pad_maximum_fusion.4
  237.0 0.6 pad_maximum_fusion.2
  (62 shorter events, 0.4 us)
Async XLA Ops:
  0.6 26.7 %copy-start.8 = (bf16[2,256,512]{2,1,0:T(8,128)(2,1)S(1)}, bf16[2,256,512]{2,1,0:T(8,128)(2,1)}, u32[]{:S(2)}) copy-start(bf16[2,256,512]{2,1,0:T(8,128)(2,1)} %param.6) | copy-start | bytes 1572868
  0.6 26.7 %collective-permute-start = (bf16[1024,256]{1,0:T(8,128)(2,1)}, bf16[1024,256]{1,0:T(8,128)(2,1)S(1)}, u32[]{:S(2)}, u32[]{:S(2)}) collective-permute-start(bf16[1024,256]{1,0:T(8,128)(2,1)} %param.5), channel_id=1, source_target_pairs={{0,1},{1,2},{2,3},{3,4},{4,5},{5,6},{6,7},{7,8},{8,9},{9,10},{10,1... | collective-permute-start | bytes 1572872 | tf_op jit(solution)/shard_map/ppermute | solution.py:31
  27.3 0.8 copy-start.11
  28.1 1.2 copy-start.6
  28.1 1.2 copy-start.17
  28.6 0.8 copy-start
  29.7 51.7 %copy-start.2 = (bf16[1024,256]{1,0:T(8,128)(2,1)}, bf16[1024,256]{1,0:T(8,128)(2,1)S(1)}, u32[]{:S(2)}) copy-start(bf16[1024,256]{1,0:T(8,128)(2,1)S(1)} %fusion) | copy-start | bytes 1572868
  29.7 49.0 %collective-permute-start.1 = (bf16[1024,256]{1,0:T(8,128)(2,1)S(1)}, bf16[1024,256]{1,0:T(8,128)(2,1)}, u32[]{:S(2)}, u32[]{:S(2)}) collective-permute-start(bf16[1024,256]{1,0:T(8,128)(2,1)S(1)} %fusion), channel_id=1, source_target_pairs={{0,64},{32,96},{64,128},{96,160},{128,192},{160,224},{192,256},{22... | collective-permute-start | bytes 1572872 | tf_op jit(solution)/shard_map/ppermute | solution.py:31
  41.3 39.0 %copy-start.13 = (bf16[1024,256]{1,0:T(8,128)(2,1)S(1)}, bf16[1024,256]{1,0:T(8,128)(2,1)}, u32[]{:S(2)}) copy-start(bf16[1024,256]{1,0:T(8,128)(2,1)} %param.9) | copy-start | bytes 1572868
  81.1 0.8 copy-start.4
  81.1 1.0 copy-start.21
  81.1 2.5 %copy-start.19 = (bf16[1024,256]{0,1:T(8,128)(2,1)}, bf16[1024,256]{0,1:T(8,128)(2,1)S(1)}, u32[]{:S(2)}) copy-start(bf16[1024,256]{0,1:T(8,128)(2,1)S(1)} %get-tuple-element.11) | copy-start | bytes 1572868
  86.8 2.8 %copy-start.9 = (bf16[2,256,512]{2,1,0:T(8,128)(2,1)S(1)}, bf16[2,256,512]{2,1,0:T(8,128)(2,1)}, u32[]{:S(2)}) copy-start(bf16[2,256,512]{2,1,0:T(8,128)(2,1)} %param.6) | copy-start | bytes 1572868
  86.8 2.8 %copy-start.20 = (bf16[1024,256]{0,1:T(8,128)(2,1)S(1)}, bf16[1024,256]{0,1:T(8,128)(2,1)}, u32[]{:S(2)}) copy-start(bf16[1024,256]{0,1:T(8,128)(2,1)} %copy-done.19) | copy-start | bytes 1572868
  86.8 2.8 %copy-start.22 = (bf16[1024,256]{0,1:T(8,128)(2,1)S(1)}, bf16[1024,256]{0,1:T(8,128)(2,1)}, u32[]{:S(2)}) copy-start(bf16[1024,256]{0,1:T(8,128)(2,1)} %copy-done.21) | copy-start | bytes 1572868
  87.5 4.7 %collective-permute-start.2 = (bf16[256,640]{1,0:T(8,128)(2,1)S(1)}, bf16[256,640]{1,0:T(8,128)(2,1)S(1)}, u32[]{:S(2)}, u32[]{:S(2)}) collective-permute-start(bf16[256,640]{1,0:T(8,128)(2,1)S(1)} %bitcast.108), channel_id=1, source_target_pairs={{0,32},{32,0},{1,33},{33,1},{2,34},{34,2},{3,35},{35,3},{4,36},{36... | collective-permute-start | bytes 983048 | tf_op jit(solution)/shard_map/ppermute | solution.py:74
  90.1 12.8 %copy-start.14 = (bf16[1024,256]{1,0:T(8,128)(2,1)S(1)}, bf16[1024,256]{1,0:T(8,128)(2,1)}, u32[]{:S(2)}) copy-start(bf16[1024,256]{1,0:T(8,128)(2,1)} %param.9) | copy-start | bytes 1572868
  90.1 12.8 %copy-start.15 = (bf16[2,256,512]{2,1,0:T(8,128)(2,1)S(1)}, bf16[2,256,512]{2,1,0:T(8,128)(2,1)}, u32[]{:S(2)}) copy-start(bf16[2,256,512]{2,1,0:T(8,128)(2,1)} %param.7) | copy-start | bytes 1572868
  90.1 25.5 %collective-permute-start.6 = (bf16[1024,256]{1,0:T(8,128)(2,1)S(1)}, bf16[1024,256]{1,0:T(8,128)(2,1)S(1)}, u32[]{:S(2)}, u32[]{:S(2)}) collective-permute-start(bf16[1024,256]{1,0:T(8,128)(2,1)S(1)} %convolution_convert_fusion.1), channel_id=1, source_target_pairs={{64,0},{96,32},{128,64},{160,96},{192,128},{224,160},{256,192},{28... | collective-permute-start | bytes 1572872 | tf_op jit(solution)/shard_map/ppermute | solution.py:31
  92.3 11.2 %collective-permute-start.3 = (bf16[64,640]{1,0:T(8,128)(2,1)S(1)}, bf16[64,640]{1,0:T(8,128)(2,1)S(1)}, u32[]{:S(2)}, u32[]{:S(2)}) collective-permute-start(bf16[64,640]{1,0:T(8,128)(2,1)S(1)} %get-tuple-element.14), channel_id=1, source_target_pairs={{0,8},{8,16},{16,24},{24,0},{1,9},{9,17},{17,25},{25,1},{2,10},{10... | collective-permute-start | bytes 245768 | tf_op jit(solution)/shard_map/ppermute | solution.py:41
  95.5 8.0 %collective-permute-start.4 = (bf16[64,640]{1,0:T(8,128)(2,1)S(1)}, bf16[64,640]{1,0:T(8,128)(2,1)S(1)}, u32[]{:S(2)}, u32[]{:S(2)}) collective-permute-start(bf16[64,640]{1,0:T(8,128)(2,1)S(1)} %get-tuple-element.16), channel_id=1, source_target_pairs={{0,16},{8,24},{16,0},{24,8},{1,17},{9,25},{17,1},{25,9},{2,18},{10... | collective-permute-start | bytes 245768 | tf_op jit(solution)/shard_map/ppermute | solution.py:41
  99.9 5.5 %collective-permute-start.5 = (bf16[64,640]{1,0:T(8,128)(2,1)S(1)}, bf16[64,640]{1,0:T(8,128)(2,1)S(1)}, u32[]{:S(2)}, u32[]{:S(2)}) collective-permute-start(bf16[64,640]{1,0:T(8,128)(2,1)S(1)} %get-tuple-element.15), channel_id=1, source_target_pairs={{0,24},{8,0},{16,8},{24,16},{1,25},{9,1},{17,9},{25,17},{2,26},{10... | collective-permute-start | bytes 245768 | tf_op jit(solution)/shard_map/ppermute | solution.py:41
  103.5 12.3 %copy-start.18 = (bf16[2,256,256]{2,1,0:T(8,128)(2,1)S(1)}, bf16[2,256,256]{2,1,0:T(8,128)(2,1)}, u32[]{:S(2)}) copy-start(bf16[2,256,256]{2,1,0:T(8,128)(2,1)} %param.8) | copy-start | bytes 786436
  115.8 1.0 copy-start.1
  115.8 1.3 copy-start.7
  116.8 0.8 copy-start.23
  116.8 1.0 copy-start.24
  116.8 1.4 copy-start.12
  120.2 9.1 %copy-start.10 = (bf16[2,256,512]{2,1,0:T(8,128)(2,1)S(1)}, bf16[2,256,512]{2,1,0:T(8,128)(2,1)}, u32[]{:S(2)}) copy-start(bf16[2,256,512]{2,1,0:T(8,128)(2,1)} %param.6) | copy-start | bytes 1572868
  120.3 4.1 %collective-permute-start.8 = (bf16[256,640]{1,0:T(8,128)(2,1)S(1)}, bf16[256,640]{1,0:T(8,128)(2,1)S(1)}, u32[]{:S(2)}, u32[]{:S(2)}) collective-permute-start(bf16[256,640]{1,0:T(8,128)(2,1)S(1)} %bitcast.109), channel_id=1, source_target_pairs={{0,32},{32,0},{1,33},{33,1},{2,34},{34,2},{3,35},{35,3},{4,36},{36... | collective-permute-start | bytes 983048 | tf_op jit(solution)/shard_map/ppermute | solution.py:74
  125.1 15.7 %all-to-all-start = ((bf16[4,64,640]{2,1,0:T(8,128)(2,1)}), bf16[4,64,640]{2,1,0:T(8,128)(2,1)S(1)}, u32[]{:S(2)}, u32[]{:S(2)}) async-start(bf16[4,64,640]{2,1,0:T(8,128)(2,1)} %bitcast.15), calls=%async_computation | async-start | bytes 655360 | tf_op jit(solution)/shard_map/all_to_all | solution.py:80
  129.3 51.4 %copy-start.3 = (bf16[1024,256]{1,0:T(8,128)(2,1)S(1)}, bf16[1024,256]{1,0:T(8,128)(2,1)}, u32[]{:S(2)}) copy-start(bf16[1024,256]{1,0:T(8,128)(2,1)} %copy-done.2) | copy-start | bytes 1572868
  129.3 51.4 %copy-start.5 = (bf16[1024,256]{0,1:T(8,128)(2,1)S(1)}, bf16[1024,256]{0,1:T(8,128)(2,1)}, u32[]{:S(2)}) copy-start(bf16[1024,256]{0,1:T(8,128)(2,1)} %copy-done.4) | copy-start | bytes 1572868
  131.8 50.0 %copy-start.16 = (bf16[2,256,512]{2,1,0:T(8,128)(2,1)S(1)}, bf16[2,256,512]{2,1,0:T(8,128)(2,1)}, u32[]{:S(2)}) copy-start(bf16[2,256,512]{2,1,0:T(8,128)(2,1)} %param.7) | copy-start | bytes 1572868
  131.8 50.0 %collective-permute-start.7 = (bf16[1024,256]{1,0:T(8,128)(2,1)}, bf16[1024,256]{1,0:T(8,128)(2,1)S(1)}, u32[]{:S(2)}, u32[]{:S(2)}) collective-permute-start(bf16[1024,256]{1,0:T(8,128)(2,1)} %convolution_convert_fusion), channel_id=1, source_target_pairs={{1,0},{2,1},{3,2},{4,3},{5,4},{6,5},{7,6},{8,7},{9,8},{10,9},{11,1... | collective-permute-start | bytes 1572872 | tf_op jit(solution)/shard_map/ppermute | solution.py:31
  142.9 52.1 %all-to-all-start.1 = ((bf16[64,2,640]{2,1,0:T(2,128)(2,1)}), bf16[64,2,640]{2,1,0:T(2,128)(2,1)S(1)}, u32[]{:S(2)}, u32[]{:S(2)}) async-start(bf16[64,2,640]{2,1,0:T(2,128)(2,1)} %reshape.65), calls=%async_computation.1 | async-start | bytes 327680 | tf_op jit(solution)/shard_map/all_to_all | solution.py:89

commit v14 on v7

--- a/solution.py
+++ b/solution.py
@@ -169,8 +169,6 @@
         arrived = return_past(sent_back, layer_at)
         operands = (earlier, current, gated_out, grad_preact, upstream)
         near_list[layer_at] = near_sum(layer_term(operands, grad_scale), layer_at == 0)
-        if layer_at > 0:
-            near_list, arrived = lax.optimization_barrier((near_list, arrived))
         local_grad = upstream.astype(jnp.float32) + jnp.dot(
             grad_preact, conv_now[layer_at].T, preferred_element_type=jnp.float32
         )

time: 220 us -> 223 us (1.014)
  waiting for transfers between devices: 81.5 us -> 96.1 us
  blocking collectives: 10.7 us -> 0 us
    ppermute x4, waiting for transfers between devices: 68.2 us -> 79.3 us  [from_behind(): return lax.ppermute(array, axes, pairs)]
    all_to_all x1 -> x0, blocking collectives: 10.7 us -> none  [near_sum(): lax.all_to_all(pieces, 'x', 0, 0, tiled=True).astype(jnp.float32).sum(0)]
    all_to_all x0 -> x1, waiting for transfers between devices: none -> 5.78 us  [near_sum(): lax.all_to_all(pieces, 'x', 0, 0, tiled=True).astype(jnp.float32).sum(0)]
    all_to_all x0 -> x1, starting transfers between devices: none -> 3.45 us  [near_sum(): lax.all_to_all(pieces, 'x', 0, 0, tiled=True).astype(jnp.float32).sum(0)]
    all_to_all x1, starting transfers between devices: 41.2 us -> 38 us  [far_sum(): lax.all_to_all(rows.astype(jnp.bfloat16), ('y', 'z_hi', 'z_lo'), 0, 0, ti...]
    mul x2 -> x0, local copies, waits for them, and re-layouts: 2.68 us -> none  [layer_term(): jnp.concatenate([contract(earlier, grad_preact), contract(current, grad_p...]
  transfers between devices with their start and end apart: 11 -> 12, of which waited for: 6 -> 5; matrix products, arithmetic and copies ran while one was open for 6% -> 8% of each run, Pallas kernels for 0% -> 0%
where the time goes in v14:
time: 223 us; the launch traced here: 222 us
  waiting for transfers between devices  96.1 us (43%)
  starting transfers between devices  94 us (42%)
  matrix products  17.6 us (8%)
  local copies, waits for them, and re-layouts  7.46 us (3%)
  other arithmetic  5.61 us (3%)
    ppermute x4, waiting for transfers between devices, from_behind(): return lax.ppermute(array, axes, pairs)  79.3 us
    all_to_all x1, starting transfers between devices, far_sum(): lax.all_to_all(rows.astype(jnp.bfloat16), ('y', 'z_hi', 'z_lo'), 0, 0, ti...  38 us
    ppermute x4, starting transfers between devices, from_behind(): return lax.ppermute(array, axes, pairs)  29.1 us
    all_to_all x1, waiting for transfers between devices, far_sum(): gathered = lax.all_to_all(spread, ('y', 'z_hi', 'core'), 0, 0, tiled=True)  11 us
    ppermute x3, starting transfers between devices, scatter_sum(): lax.ppermute(piece.astype(jnp.bfloat16), axes, [(i, (i + shift) % size) f...  10.7 us
    all_to_all x1, starting transfers between devices, far_sum(): gathered = lax.all_to_all(spread, ('y', 'z_hi', 'core'), 0, 0, tiled=True)  7.59 us
    all_to_all x1, waiting for transfers between devices, near_sum(): lax.all_to_all(pieces, 'x', 0, 0, tiled=True).astype(jnp.float32).sum(0)  5.78 us
    ppermute x2, starting transfers between devices, near_sum(): moved = lax.ppermute(given.astype(jnp.bfloat16), 'core', [(0, 1), (1, 0)])  5.11 us
  transfers between devices with their start and end apart: 12, of which 5 were waited for; matrix products, arithmetic and copies ran while one was open for 8% of the time, Pallas kernels for 0%

profile of v14, /device:TPU:1, one launch (start us, length us, event | category | flops | bytes accessed | tf_op | source)
XLA Modules:
  0.0 222.0 jit_solution(9168716381835125187)
XLA Ops:
  0.6 4.5 %collective-permute-start = (bf16[1024,256]{1,0:T(8,128)(2,1)}, bf16[1024,256]{1,0:T(8,128)(2,1)S(1)}, u32[]{:S(2)}, u32[]{:S(2)}) collective-permute-start(bf16[1024,256]{1,0:T(8,128)(2,1)} %param.5), channel_id=1, source_target_pairs={{0,1},{1,2},{2,3},{3,4},{4,5},{5,6},{6,7},{7,8},{8,9},{9,10},{10,1... | collective-permute-start | bytes 1572872 | tf_op jit(solution)/shard_map/ppermute | solution.py:31
  5.2 1.6 fusion.16
  6.8 20.6 %collective-permute-done = bf16[1024,256]{1,0:T(8,128)(2,1)S(1)} collective-permute-done((bf16[1024,256]{1,0:T(8,128)(2,1)}, bf16[1024,256]{1,0:T(8,128)(2,1)S(1)}, u32[]{:S(2)}, u32[]{:S(2)}) %collective-permute-start) | collective-permute-done | bytes 524320 | tf_op jit(solution)/shard_map/ppermute | solution.py:31
  27.3 0.5 convolution_add_fusion.1
  27.8 0.3 copy-done.8
  28.1 0.4 multiply_convert_fusion.5
  28.5 0.6 copy-done.3
  29.2 0.1 copy-done.15
  29.2 0.4 fusion
  29.6 10.2 %collective-permute-start.1 = (bf16[1024,256]{1,0:T(8,128)(2,1)S(1)}, bf16[1024,256]{1,0:T(8,128)(2,1)}, u32[]{:S(2)}, u32[]{:S(2)}) collective-permute-start(bf16[1024,256]{1,0:T(8,128)(2,1)S(1)} %fusion), channel_id=1, source_target_pairs={{0,64},{32,96},{64,128},{96,160},{128,192},{160,224},{192,256},{22... | collective-permute-start | bytes 1572872 | tf_op jit(solution)/shard_map/ppermute | solution.py:31
  39.8 1.5 fusion.10
  41.3 37.5 %collective-permute-done.1 = bf16[1024,256]{1,0:T(8,128)(2,1)} collective-permute-done((bf16[1024,256]{1,0:T(8,128)(2,1)S(1)}, bf16[1024,256]{1,0:T(8,128)(2,1)}, u32[]{:S(2)}, u32[]{:S(2)}) %collective-permute-start.1) | collective-permute-done | bytes 524320 | tf_op jit(solution)/shard_map/ppermute | solution.py:31
  78.8 1.5 convolution_add_fusion
  80.4 0.8 multiply_convert_fusion.3
  81.1 0.5 convolution_convert_fusion.1
  81.6 0.5 fusion.47
  82.1 1.3 collective-permute-start.2
  83.4 0.4 fusion.49
  83.8 1.6 fusion.46
  85.4 0.1 maximum_multiply_fusion.1
  85.5 21.2 %collective-permute-done.2 = bf16[1024,256]{1,0:T(8,128)(2,1)S(1)} collective-permute-done((bf16[1024,256]{1,0:T(8,128)(2,1)S(1)}, bf16[1024,256]{1,0:T(8,128)(2,1)S(1)}, u32[]{:S(2)}, u32[]{:S(2)}) %collective-permute-start.2) | collective-permute-done | bytes 524320 | tf_op jit(solution)/shard_map/ppermute | solution.py:31
  106.7 0.5 add_convert_fusion.1
  107.2 0.7 multiply_convert_fusion.1
  107.9 0.1 copy-done.11
  108.0 0.4 fusion.48
  108.4 0.1 copy-done.4
  108.5 0.4 convolution_bitcast_fusion
  108.9 0.1 copy-done.18
  109.0 0.5 copy-done.9
  109.5 0.4 convolution_bitcast_fusion.1
  109.9 0.1 maximum_multiply_fusion
  110.0 0.1 constant_dynamic-slice_fusion
  110.1 0.9 copy.33
  111.0 3.2 %collective-permute-start.5 = (bf16[256,640]{1,0:T(8,128)(2,1)}, bf16[256,640]{1,0:T(8,128)(2,1)}, u32[]{:S(2)}, u32[]{:S(2)}) collective-permute-start(bf16[256,640]{1,0:T(8,128)(2,1)} %bitcast.88), channel_id=1, source_target_pairs={{0,32},{32,0},{1,33},{33,1},{2,34},{34,2},{3,35},{35,3},{4,36},{36... | collective-permute-start | bytes 983048 | tf_op jit(solution)/shard_map/ppermute | solution.py:74
  114.3 1.1 constant_dynamic-slice_fusion.1
  115.4 0.2 copy.25
  115.7 0.9 copy.32
  116.6 1.9 collective-permute-start.4
  118.5 0.1 constant_dynamic-slice_fusion.3
  118.5 0.2 copy.21
  118.8 1.0 bitcast_add_fusion
  119.9 3.1 %collective-permute-start.6 = (bf16[64,640]{1,0:T(8,128)(2,1)S(1)}, bf16[64,640]{1,0:T(8,128)(2,1)S(1)}, u32[]{:S(2)}, u32[]{:S(2)}) collective-permute-start(bf16[64,640]{1,0:T(8,128)(2,1)S(1)} %get-tuple-element.10), channel_id=1, source_target_pairs={{0,8},{8,16},{16,24},{24,0},{1,9},{9,17},{17,25},{25,1},{2,10},{10... | collective-permute-start | bytes 245768 | tf_op jit(solution)/shard_map/ppermute | solution.py:41
  123.0 4.4 %collective-permute-start.7 = (bf16[64,640]{1,0:T(8,128)(2,1)S(1)}, bf16[64,640]{1,0:T(8,128)(2,1)S(1)}, u32[]{:S(2)}, u32[]{:S(2)}) collective-permute-start(bf16[64,640]{1,0:T(8,128)(2,1)S(1)} %get-tuple-element.12), channel_id=1, source_target_pairs={{0,16},{8,24},{16,0},{24,8},{1,17},{9,25},{17,1},{25,9},{2,18},{10... | collective-permute-start | bytes 245768 | tf_op jit(solution)/shard_map/ppermute | solution.py:41
  127.4 3.2 %collective-permute-start.8 = (bf16[64,640]{1,0:T(8,128)(2,1)S(1)}, bf16[64,640]{1,0:T(8,128)(2,1)S(1)}, u32[]{:S(2)}, u32[]{:S(2)}) collective-permute-start(bf16[64,640]{1,0:T(8,128)(2,1)S(1)} %get-tuple-element.11), channel_id=1, source_target_pairs={{0,24},{8,0},{16,8},{24,16},{1,25},{9,1},{17,9},{25,17},{2,26},{10... | collective-permute-start | bytes 245768 | tf_op jit(solution)/shard_map/ppermute | solution.py:41
  130.6 0.8 fusion.8
  131.4 3.5 %all-to-all-start = ((bf16[4,64,640]{2,1,0:T(8,128)(2,1)}), bf16[4,64,640]{2,1,0:T(8,128)(2,1)S(1)}, u32[]{:S(2)}, u32[]{:S(2)}) async-start(bf16[4,64,640]{2,1,0:T(8,128)(2,1)} %bitcast.11), calls=%async_computation | async-start | bytes 655360 | tf_op jit(solution)/shard_map/all_to_all | solution.py:80
  134.9 5.8 %all-to-all-done = bf16[4,64,640]{2,1,0:T(8,128)(2,1)S(1)} async-done(((bf16[4,64,640]{2,1,0:T(8,128)(2,1)}), bf16[4,64,640]{2,1,0:T(8,128)(2,1)S(1)}, u32[]{:S(2)}, u32[]{:S(2)}) %all-to-all-start) | async-done | bytes 327712 | tf_op jit(solution)/shard_map/all_to_all | solution.py:80
  140.8 0.5 broadcast.39
  141.3 0.7 reduce.3
  142.0 0.7 reshape.63
  142.7 38.0 %all-to-all-start.1 = ((bf16[64,2,640]{2,1,0:T(2,128)(2,1)}), bf16[64,2,640]{2,1,0:T(2,128)(2,1)S(1)}, u32[]{:S(2)}, u32[]{:S(2)}) async-start(bf16[64,2,640]{2,1,0:T(2,128)(2,1)} %reshape.63), calls=%async_computation.1 | async-start | bytes 327680 | tf_op jit(solution)/shard_map/all_to_all | solution.py:89
  180.8 2.5 %convolution_convert_fusion = bf16[1024,256]{1,0:T(8,128)(2,1)} fusion(bf16[2,256,512]{2,1,0:T(8,128)(2,1)S(1)} %copy-done.7, bf16[1024,256]{0,1:T(8,128)(2,1)} %copy-done.18, bf16[1024,256]{0,1:T(8,128)(2,1)} %copy-done.17), kind=kOutput, calls=%fused_computation.7 | convolution fusion | flops 270794752 | bytes 1835008 | tf_op jit(solution)/shard_map/dot_general | solution.py:166
  183.3 13.1 %collective-permute-start.3 = (bf16[1024,256]{1,0:T(8,128)(2,1)}, bf16[1024,256]{1,0:T(8,128)(2,1)S(1)}, u32[]{:S(2)}, u32[]{:S(2)}) collective-permute-start(bf16[1024,256]{1,0:T(8,128)(2,1)} %convolution_convert_fusion), channel_id=1, source_target_pairs={{1,0},{2,1},{3,2},{4,3},{5,4},{6,5},{7,6},{8,7},{9,8},{10,9},{11,1... | collective-permute-start | bytes 1572872 | tf_op jit(solution)/shard_map/ppermute | solution.py:31
  196.4 0.1 reshape.64
  196.6 0.3 convert_reduce_fusion
  196.9 0.7 broadcast_in_dim.2
  197.5 7.6 %all-to-all-start.2 = ((f32[16,1,1280]{2,1,0:T(1,128)}), f32[16,1,1280]{2,1,0:T(1,128)S(1)}, u32[]{:S(2)}, u32[]{:S(2)}) async-start(f32[16,1,1280]{2,1,0:T(1,128)} %broadcast_in_dim.2), calls=%async_computation.2 | async-start | bytes 163840 | tf_op jit(solution)/shard_map/all_to_all | solution.py:92
  205.1 1.1 fusion.1
  206.3 2.5 %add_convert_fusion = bf16[1024,256]{1,0:T(8,128)(2,1)} fusion(bf16[1024,256]{1,0:T(8,128)(2,1)S(1)} %collective-permute-done.3, bf16[1024,256]{1,0:T(8,128)(2,1)S(1)} %copy-done.12, bf16[2,256,512]{2,1,0:T(8,128)(2,1)S(1)} %copy-done.14, bf16[1024,256]{0,1:T(8,128)(2,1)} %copy-done.18, bf16[1024,256]{0,1:T(8,128)(2,1)} %copy-done.17), kind=kOutput, calls=%fused_computation.25 | convolution fusion | flops 271843328 | bytes 2883584 | tf_op jit(solution)/shard_map/dot_general | solution.py:172
  208.8 11.0 %all-to-all-done.2 = f32[16,1,1280]{2,1,0:T(1,128)S(1)} async-done(((f32[16,1,1280]{2,1,0:T(1,128)}), f32[16,1,1280]{2,1,0:T(1,128)S(1)}, u32[]{:S(2)}, u32[]{:S(2)}) %all-to-all-start.2) | async-done | bytes 81952 | tf_op jit(solution)/shard_map/all_to_all | solution.py:92
  219.8 0.2 reduce.2
  220.2 0.6 pad_maximum_fusion.4
  220.8 0.6 pad_maximum_fusion.3
  221.4 0.6 pad_maximum_fusion.2
  (51 shorter events, 0.4 us)
Async XLA Ops:
  0.6 26.7 %copy-start.5 = (bf16[2,256,512]{2,1,0:T(8,128)(2,1)S(1)}, bf16[2,256,512]{2,1,0:T(8,128)(2,1)}, u32[]{:S(2)}) copy-start(bf16[2,256,512]{2,1,0:T(8,128)(2,1)} %param.6) | copy-start | bytes 1572868
  0.6 26.7 %collective-permute-start = (bf16[1024,256]{1,0:T(8,128)(2,1)}, bf16[1024,256]{1,0:T(8,128)(2,1)S(1)}, u32[]{:S(2)}, u32[]{:S(2)}) collective-permute-start(bf16[1024,256]{1,0:T(8,128)(2,1)} %param.5), channel_id=1, source_target_pairs={{0,1},{1,2},{2,3},{3,4},{4,5},{5,6},{6,7},{7,8},{8,9},{9,10},{10,1... | collective-permute-start | bytes 1572872 | tf_op jit(solution)/shard_map/ppermute | solution.py:31
  27.3 0.8 copy-start.8
  28.1 1.0 copy-start.3
  28.1 1.1 copy-start.15
  29.6 49.2 %collective-permute-start.1 = (bf16[1024,256]{1,0:T(8,128)(2,1)S(1)}, bf16[1024,256]{1,0:T(8,128)(2,1)}, u32[]{:S(2)}, u32[]{:S(2)}) collective-permute-start(bf16[1024,256]{1,0:T(8,128)(2,1)S(1)} %fusion), channel_id=1, source_target_pairs={{0,64},{32,96},{64,128},{96,160},{128,192},{160,224},{192,256},{22... | collective-permute-start | bytes 1572872 | tf_op jit(solution)/shard_map/ppermute | solution.py:31
  39.8 39.0 %copy-start.6 = (bf16[2,256,512]{2,1,0:T(8,128)(2,1)S(1)}, bf16[2,256,512]{2,1,0:T(8,128)(2,1)}, u32[]{:S(2)}) copy-start(bf16[2,256,512]{2,1,0:T(8,128)(2,1)} %param.6) | copy-start | bytes 1572868
  41.3 39.1 %copy-start.10 = (bf16[1024,256]{1,0:T(8,128)(2,1)S(1)}, bf16[1024,256]{1,0:T(8,128)(2,1)}, u32[]{:S(2)}) copy-start(bf16[1024,256]{1,0:T(8,128)(2,1)} %param.9) | copy-start | bytes 1572868
  81.1 2.3 %copy-start.1 = (bf16[1024,256]{0,1:T(8,128)(2,1)}, bf16[1024,256]{0,1:T(8,128)(2,1)S(1)}, u32[]{:S(2)}) copy-start(bf16[1024,256]{0,1:T(8,128)(2,1)S(1)} %get-tuple-element.9) | copy-start | bytes 1572868
  82.1 24.6 %collective-permute-start.2 = (bf16[1024,256]{1,0:T(8,128)(2,1)S(1)}, bf16[1024,256]{1,0:T(8,128)(2,1)S(1)}, u32[]{:S(2)}, u32[]{:S(2)}) collective-permute-start(bf16[1024,256]{1,0:T(8,128)(2,1)S(1)} %convolution_convert_fusion.1), channel_id=1, source_target_pairs={{64,0},{96,32},{128,64},{160,96},{192,128},{224,160},{256,192},{28... | collective-permute-start | bytes 1572872 | tf_op jit(solution)/shard_map/ppermute | solution.py:31
  83.8 22.9 %copy-start.13 = (bf16[2,256,512]{2,1,0:T(8,128)(2,1)S(1)}, bf16[2,256,512]{2,1,0:T(8,128)(2,1)}, u32[]{:S(2)}) copy-start(bf16[2,256,512]{2,1,0:T(8,128)(2,1)} %param.7) | copy-start | bytes 1572868
  85.5 24.6 %copy-start = (f32[256,1280]{0,1:T(8,128)}, f32[256,1280]{0,1:T(8,128)S(1)}, u32[]{:S(2)}) copy-start(f32[256,1280]{0,1:T(8,128)S(1)} %maximum_multiply_fusion.1) | copy-start | bytes 3932164
  107.2 0.8 copy-start.11
  107.2 1.2 copy-start.4
  108.0 0.9 copy-start.17
  108.0 1.0 copy-start.18
  108.0 1.4 copy-start.9
  111.0 7.7 %collective-permute-start.5 = (bf16[256,640]{1,0:T(8,128)(2,1)}, bf16[256,640]{1,0:T(8,128)(2,1)}, u32[]{:S(2)}, u32[]{:S(2)}) collective-permute-start(bf16[256,640]{1,0:T(8,128)(2,1)} %bitcast.88), channel_id=1, source_target_pairs={{0,32},{32,0},{1,33},{33,1},{2,34},{34,2},{3,35},{35,3},{4,36},{36... | collective-permute-start | bytes 983048 | tf_op jit(solution)/shard_map/ppermute | solution.py:74
  116.6 14.0 %collective-permute-start.4 = (bf16[256,640]{1,0:T(8,128)(2,1)}, bf16[256,640]{1,0:T(8,128)(2,1)S(1)}, u32[]{:S(2)}, u32[]{:S(2)}) collective-permute-start(bf16[256,640]{1,0:T(8,128)(2,1)} %bitcast.89), channel_id=1, source_target_pairs={{0,32},{32,0},{1,33},{33,1},{2,34},{34,2},{3,35},{35,3},{4,36},{36... | collective-permute-start | bytes 983048 | tf_op jit(solution)/shard_map/ppermute | solution.py:74
  119.9 15.0 %collective-permute-start.6 = (bf16[64,640]{1,0:T(8,128)(2,1)S(1)}, bf16[64,640]{1,0:T(8,128)(2,1)S(1)}, u32[]{:S(2)}, u32[]{:S(2)}) collective-permute-start(bf16[64,640]{1,0:T(8,128)(2,1)S(1)} %get-tuple-element.10), channel_id=1, source_target_pairs={{0,8},{8,16},{16,24},{24,0},{1,9},{9,17},{17,25},{25,1},{2,10},{10... | collective-permute-start | bytes 245768 | tf_op jit(solution)/shard_map/ppermute | solution.py:41
  123.0 11.9 %collective-permute-start.7 = (bf16[64,640]{1,0:T(8,128)(2,1)S(1)}, bf16[64,640]{1,0:T(8,128)(2,1)S(1)}, u32[]{:S(2)}, u32[]{:S(2)}) collective-permute-start(bf16[64,640]{1,0:T(8,128)(2,1)S(1)} %get-tuple-element.12), channel_id=1, source_target_pairs={{0,16},{8,24},{16,0},{24,8},{1,17},{9,25},{17,1},{25,9},{2,18},{10... | collective-permute-start | bytes 245768 | tf_op jit(solution)/shard_map/ppermute | solution.py:41
  127.4 53.4 %copy-start.7 = (bf16[2,256,512]{2,1,0:T(8,128)(2,1)S(1)}, bf16[2,256,512]{2,1,0:T(8,128)(2,1)}, u32[]{:S(2)}) copy-start(bf16[2,256,512]{2,1,0:T(8,128)(2,1)} %param.6) | copy-start | bytes 1572868
  127.4 7.5 %collective-permute-start.8 = (bf16[64,640]{1,0:T(8,128)(2,1)S(1)}, bf16[64,640]{1,0:T(8,128)(2,1)S(1)}, u32[]{:S(2)}, u32[]{:S(2)}) collective-permute-start(bf16[64,640]{1,0:T(8,128)(2,1)S(1)} %get-tuple-element.11), channel_id=1, source_target_pairs={{0,24},{8,0},{16,8},{24,16},{1,25},{9,1},{17,9},{25,17},{2,26},{10... | collective-permute-start | bytes 245768 | tf_op jit(solution)/shard_map/ppermute | solution.py:41
  131.4 9.3 %all-to-all-start = ((bf16[4,64,640]{2,1,0:T(8,128)(2,1)}), bf16[4,64,640]{2,1,0:T(8,128)(2,1)S(1)}, u32[]{:S(2)}, u32[]{:S(2)}) async-start(bf16[4,64,640]{2,1,0:T(8,128)(2,1)} %bitcast.11), calls=%async_computation | async-start | bytes 655360 | tf_op jit(solution)/shard_map/all_to_all | solution.py:80
  142.7 62.4 %copy-start.2 = (bf16[1024,256]{0,1:T(8,128)(2,1)S(1)}, bf16[1024,256]{0,1:T(8,128)(2,1)}, u32[]{:S(2)}) copy-start(bf16[1024,256]{0,1:T(8,128)(2,1)} %copy-done.1) | copy-start | bytes 1572868
  142.7 62.4 %copy-start.16 = (bf16[2,256,256]{2,1,0:T(8,128)(2,1)S(1)}, bf16[2,256,256]{2,1,0:T(8,128)(2,1)}, u32[]{:S(2)}) copy-start(bf16[2,256,256]{2,1,0:T(8,128)(2,1)} %param.8) | copy-start | bytes 786436
  142.7 53.7 %all-to-all-start.1 = ((bf16[64,2,640]{2,1,0:T(2,128)(2,1)}), bf16[64,2,640]{2,1,0:T(2,128)(2,1)S(1)}, u32[]{:S(2)}, u32[]{:S(2)}) async-start(bf16[64,2,640]{2,1,0:T(2,128)(2,1)} %reshape.63), calls=%async_computation.1 | async-start | bytes 327680 | tf_op jit(solution)/shard_map/all_to_all | solution.py:89
  183.3 23.0 %copy-start.12 = (bf16[1024,256]{1,0:T(8,128)(2,1)S(1)}, bf16[1024,256]{1,0:T(8,128)(2,1)}, u32[]{:S(2)}) copy-start(bf16[1024,256]{1,0:T(8,128)(2,1)} %copy-done.11) | copy-start | bytes 1572868
  183.3 23.0 %copy-start.14 = (bf16[2,256,512]{2,1,0:T(8,128)(2,1)S(1)}, bf16[2,256,512]{2,1,0:T(8,128)(2,1)}, u32[]{:S(2)}) copy-start(bf16[2,256,512]{2,1,0:T(8,128)(2,1)} %param.7) | copy-start | bytes 1572868
  183.3 23.0 %collective-permute-start.3 = (bf16[1024,256]{1,0:T(8,128)(2,1)}, bf16[1024,256]{1,0:T(8,128)(2,1)S(1)}, u32[]{:S(2)}, u32[]{:S(2)}) collective-permute-start(bf16[1024,256]{1,0:T(8,128)(2,1)} %convolution_convert_fusion), channel_id=1, source_target_pairs={{1,0},{2,1},{3,2},{4,3},{5,4},{6,5},{7,6},{8,7},{9,8},{10,9},{11,1... | collective-permute-start | bytes 1572872 | tf_op jit(solution)/shard_map/ppermute | solution.py:31
  197.5 22.3 %all-to-all-start.2 = ((f32[16,1,1280]{2,1,0:T(1,128)}), f32[16,1,1280]{2,1,0:T(1,128)S(1)}, u32[]{:S(2)}, u32[]{:S(2)}) async-start(f32[16,1,1280]{2,1,0:T(1,128)} %broadcast_in_dim.2), calls=%async_computation.2 | async-start | bytes 163840 | tf_op jit(solution)/shard_map/all_to_all | solution.py:92

commit v15 on v14

--- a/solution.py
+++ b/solution.py
@@ -169,6 +169,7 @@
         arrived = return_past(sent_back, layer_at)
         operands = (earlier, current, gated_out, grad_preact, upstream)
         near_list[layer_at] = near_sum(layer_term(operands, grad_scale), layer_at == 0)
+        near_list, arrived = lax.optimization_barrier((near_list, arrived))
         local_grad = upstream.astype(jnp.float32) + jnp.dot(
             grad_preact, conv_now[layer_at].T, preferred_element_type=jnp.float32
         )

time: 223 us -> 231 us (1.036)
  blocking collectives: 0 us -> 56.6 us
  starting transfers between devices: 94 us -> 46.5 us
    all_to_all x0 -> x2, blocking collectives: none -> 56.6 us  [the longest x1 45.5 us: far_sum(): lax.all_to_all(rows.astype(jnp.bfloat16), ('y', 'z_hi', 'z_lo'), 0, 0, ti...]
    all_to_all x2 -> x0, starting transfers between devices: 41.4 us -> none  [the longest x1 38 us: far_sum(): lax.all_to_all(rows.astype(jnp.bfloat16), ('y', 'z_hi', 'z_lo'), 0, 0, ti...]
    ppermute x4, starting transfers between devices: 29.1 us -> 22 us  [from_behind(): return lax.ppermute(array, axes, pairs)]
    all_to_all x2 -> x0, waiting for transfers between devices: 5.79 us -> none  [the longest x1 5.78 us: near_sum(): lax.all_to_all(pieces, 'x', 0, 0, tiled=True).astype(jnp.float32).sum(0)]
    ppermute x4, waiting for transfers between devices: 79.3 us -> 83.2 us  [from_behind(): return lax.ppermute(array, axes, pairs)]
    mul x0 -> x2, local copies, waits for them, and re-layouts: none -> 2.68 us  [layer_term(): jnp.concatenate([contract(earlier, grad_preact), contract(current, grad_p...]
  transfers between devices with their start and end apart: 12 -> 10, of which waited for: 5 -> 6; matrix products, arithmetic and copies ran while one was open for 8% -> 4% of each run, Pallas kernels for 0% -> 0%
where the time goes in v15:
time: 231 us; the launch traced here: 230 us
  waiting for transfers between devices  96 us (42%)
  blocking collectives  56.6 us (25%)
  starting transfers between devices  46.5 us (20%)
  matrix products  15.5 us (7%)
  local copies, waits for them, and re-layouts  9.62 us (4%)
  other arithmetic  4.51 us (2%)
    ppermute x4, waiting for transfers between devices, from_behind(): return lax.ppermute(array, axes, pairs)  83.2 us
    all_to_all x1, blocking collectives, far_sum(): lax.all_to_all(rows.astype(jnp.bfloat16), ('y', 'z_hi', 'z_lo'), 0, 0, ti...  45.5 us
    ppermute x4, starting transfers between devices, from_behind(): return lax.ppermute(array, axes, pairs)  22 us
    all_to_all x1, blocking collectives, near_sum(): lax.all_to_all(pieces, 'x', 0, 0, tiled=True).astype(jnp.float32).sum(0)  11 us
    all_to_all x1, waiting for transfers between devices, far_sum(): gathered = lax.all_to_all(spread, ('y', 'z_hi', 'core'), 0, 0, tiled=True)  11 us
    ppermute x3, starting transfers between devices, scatter_sum(): lax.ppermute(piece.astype(jnp.bfloat16), axes, [(i, (i + shift) % size) f...  10.7 us
    all_to_all x1, starting transfers between devices, far_sum(): gathered = lax.all_to_all(spread, ('y', 'z_hi', 'core'), 0, 0, tiled=True)  8.84 us
    ppermute x2, starting transfers between devices, near_sum(): moved = lax.ppermute(given.astype(jnp.bfloat16), 'core', [(0, 1), (1, 0)])  4.98 us
  transfers between devices with their start and end apart: 10, of which 6 were waited for; matrix products, arithmetic and copies ran while one was open for 4% of the time, Pallas kernels for 0%

profile of v15, /device:TPU:1, one launch (start us, length us, event | category | flops | bytes accessed | tf_op | source)
XLA Modules:
  0.0 230.1 jit_solution(13396037951549949682)
XLA Ops:
  0.6 4.5 %collective-permute-start = (bf16[1024,256]{1,0:T(8,128)(2,1)}, bf16[1024,256]{1,0:T(8,128)(2,1)S(1)}, u32[]{:S(2)}, u32[]{:S(2)}) collective-permute-start(bf16[1024,256]{1,0:T(8,128)(2,1)} %param.5), channel_id=1, source_target_pairs={{0,1},{1,2},{2,3},{3,4},{4,5},{5,6},{6,7},{7,8},{8,9},{9,10},{10,1... | collective-permute-start | bytes 1572872 | tf_op jit(solution)/shard_map/ppermute | solution.py:31
  5.2 1.6 fusion.17
  6.8 20.6 %collective-permute-done = bf16[1024,256]{1,0:T(8,128)(2,1)S(1)} collective-permute-done((bf16[1024,256]{1,0:T(8,128)(2,1)}, bf16[1024,256]{1,0:T(8,128)(2,1)S(1)}, u32[]{:S(2)}, u32[]{:S(2)}) %collective-permute-start) | collective-permute-done | bytes 524320 | tf_op jit(solution)/shard_map/ppermute | solution.py:31
  27.3 0.5 convolution_add_fusion.1
  27.8 0.3 copy-done.11
  28.1 0.4 multiply_convert_fusion.5
  28.6 0.8 copy-done
  29.4 0.4 fusion
  29.7 10.2 %collective-permute-start.1 = (bf16[1024,256]{1,0:T(8,128)(2,1)S(1)}, bf16[1024,256]{1,0:T(8,128)(2,1)}, u32[]{:S(2)}, u32[]{:S(2)}) collective-permute-start(bf16[1024,256]{1,0:T(8,128)(2,1)S(1)} %fusion), channel_id=1, source_target_pairs={{0,64},{32,96},{64,128},{96,160},{128,192},{160,224},{192,256},{22... | collective-permute-start | bytes 1572872 | tf_op jit(solution)/shard_map/ppermute | solution.py:31
  39.9 1.4 fusion.12
  41.4 37.4 %collective-permute-done.1 = bf16[1024,256]{1,0:T(8,128)(2,1)} collective-permute-done((bf16[1024,256]{1,0:T(8,128)(2,1)S(1)}, bf16[1024,256]{1,0:T(8,128)(2,1)}, u32[]{:S(2)}, u32[]{:S(2)}) %collective-permute-start.1) | collective-permute-done | bytes 524320 | tf_op jit(solution)/shard_map/ppermute | solution.py:31
  78.8 1.5 convolution_add_fusion
  80.3 0.8 multiply_convert_fusion.3
  81.1 0.3 fusion.48
  81.4 0.5 fusion.46
  81.9 0.1 copy-done.23
  82.1 1.5 fusion.47
  83.6 1.2 maximum_multiply_fusion
  84.8 2.0 mul.65
  86.8 0.6 constant_dynamic-slice_fusion.2
  87.5 2.1 collective-permute-start.2
  89.6 0.5 convolution_convert_fusion.1
  90.1 1.4 collective-permute-start.6
  91.6 0.6 constant_dynamic-slice_fusion.3
  92.2 0.1 bitcast_add_fusion.1
  92.3 3.2 %collective-permute-start.3 = (bf16[64,640]{1,0:T(8,128)(2,1)S(1)}, bf16[64,640]{1,0:T(8,128)(2,1)S(1)}, u32[]{:S(2)}, u32[]{:S(2)}) collective-permute-start(bf16[64,640]{1,0:T(8,128)(2,1)S(1)} %get-tuple-element.20), channel_id=1, source_target_pairs={{0,8},{8,16},{16,24},{24,0},{1,9},{9,17},{17,25},{25,1},{2,10},{10... | collective-permute-start | bytes 245768 | tf_op jit(solution)/shard_map/ppermute | solution.py:41
  95.5 4.3 %collective-permute-start.4 = (bf16[64,640]{1,0:T(8,128)(2,1)S(1)}, bf16[64,640]{1,0:T(8,128)(2,1)S(1)}, u32[]{:S(2)}, u32[]{:S(2)}) collective-permute-start(bf16[64,640]{1,0:T(8,128)(2,1)S(1)} %get-tuple-element.22), channel_id=1, source_target_pairs={{0,16},{8,24},{16,0},{24,8},{1,17},{9,25},{17,1},{25,9},{2,18},{10... | collective-permute-start | bytes 245768 | tf_op jit(solution)/shard_map/ppermute | solution.py:41
  99.9 3.1 %collective-permute-start.5 = (bf16[64,640]{1,0:T(8,128)(2,1)S(1)}, bf16[64,640]{1,0:T(8,128)(2,1)S(1)}, u32[]{:S(2)}, u32[]{:S(2)}) collective-permute-start(bf16[64,640]{1,0:T(8,128)(2,1)S(1)} %get-tuple-element.21), channel_id=1, source_target_pairs={{0,24},{8,0},{16,8},{24,16},{1,25},{9,1},{17,9},{25,17},{2,26},{10... | collective-permute-start | bytes 245768 | tf_op jit(solution)/shard_map/ppermute | solution.py:41
  103.0 0.5 convolution_add_fusion.5
  103.5 1.8 collective-permute-done.5
  105.4 10.3 %collective-permute-done.6 = bf16[1024,256]{1,0:T(8,128)(2,1)S(1)} collective-permute-done((bf16[1024,256]{1,0:T(8,128)(2,1)S(1)}, bf16[1024,256]{1,0:T(8,128)(2,1)S(1)}, u32[]{:S(2)}, u32[]{:S(2)}) %collective-permute-start.6) | collective-permute-done | bytes 524320 | tf_op jit(solution)/shard_map/ppermute | solution.py:31
  115.6 0.1 add_convert_fusion.1
  115.8 0.7 multiply_convert_fusion.1
  116.5 0.3 copy-done.1
  116.8 0.3 fusion.49
  117.1 0.5 convolution_bitcast_fusion
  117.6 0.2 copy-done.27
  117.8 0.4 copy-done.12
  118.3 0.5 convolution_bitcast_fusion.1
  118.7 0.1 maximum_multiply_fusion.1
  118.9 0.7 mul.73
  119.6 0.6 constant_dynamic-slice_fusion
  120.3 2.9 %collective-permute-start.7 = (bf16[256,640]{1,0:T(8,128)(2,1)S(1)}, bf16[256,640]{1,0:T(8,128)(2,1)S(1)}, u32[]{:S(2)}, u32[]{:S(2)}) collective-permute-start(bf16[256,640]{1,0:T(8,128)(2,1)S(1)} %bitcast.111), channel_id=1, source_target_pairs={{0,32},{32,0},{1,33},{33,1},{2,34},{34,2},{3,35},{35,3},{4,36},{36... | collective-permute-start | bytes 983048 | tf_op jit(solution)/shard_map/ppermute | solution.py:74
  123.2 0.5 convolution_convert_fusion
  123.7 5.9 %collective-permute-start.8 = (bf16[1024,256]{1,0:T(8,128)(2,1)S(1)}, bf16[1024,256]{1,0:T(8,128)(2,1)S(1)}, u32[]{:S(2)}, u32[]{:S(2)}) collective-permute-start(bf16[1024,256]{1,0:T(8,128)(2,1)S(1)} %convolution_convert_fusion), channel_id=1, source_target_pairs={{1,0},{2,1},{3,2},{4,3},{5,4},{6,5},{7,6},{8,7},{9,8},{10,9},{11,1... | collective-permute-start | bytes 1572872 | tf_op jit(solution)/shard_map/ppermute | solution.py:31
  129.6 0.6 constant_dynamic-slice_fusion.1
  130.2 0.1 fusion.8
  130.3 11.0 %all_to_all.15 = bf16[4,64,640]{2,1,0:T(8,128)(2,1)S(1)} all-to-all(bf16[4,64,640]{2,1,0:T(8,128)(2,1)S(1)} %bitcast.109), channel_id=1, replica_groups=mesh['y'=4,'z_hi'=2,'core'=2,'x'=4,'z_lo'=8] {'x'}, dimensions={0} | all-to-all | bytes 655360 | tf_op jit(solution)/shard_map/all_to_all | solution.py:80
  141.3 15.0 %collective-permute-done.8 = bf16[1024,256]{1,0:T(8,128)(2,1)S(1)} collective-permute-done((bf16[1024,256]{1,0:T(8,128)(2,1)S(1)}, bf16[1024,256]{1,0:T(8,128)(2,1)S(1)}, u32[]{:S(2)}, u32[]{:S(2)}) %collective-permute-start.8) | collective-permute-done | bytes 524320 | tf_op jit(solution)/shard_map/ppermute | solution.py:31
  156.4 0.7 copy-done.19
  157.1 0.5 broadcast.39
  157.6 0.7 reduce.2
  158.4 45.5 %all_to_all.16 = bf16[64,2,640]{2,1,0:T(2,128)(2,1)S(1)} all-to-all(bf16[64,2,640]{2,1,0:T(2,128)(2,1)S(1)} %reshape.63), channel_id=1, replica_groups=mesh['y'=4,'z_hi'=2,'core'=2,'x'=4,'z_lo'=8] {'y','z_hi','z_lo'}, dimensions={0} | all-to-all | bytes 327680 | tf_op jit(solution)/shard_map/all_to_all | solution.py:89
  203.9 0.1 reshape.64
  204.0 0.3 convert_reduce_fusion.1
  204.3 0.7 broadcast_in_dim.2
  205.0 8.8 %all-to-all-start.2 = ((f32[16,1,1280]{2,1,0:T(1,128)}), f32[16,1,1280]{2,1,0:T(1,128)S(1)}, u32[]{:S(2)}, u32[]{:S(2)}) async-start(f32[16,1,1280]{2,1,0:T(1,128)} %broadcast_in_dim.2), calls=%async_computation.2 | async-start | bytes 163840 | tf_op jit(solution)/shard_map/all_to_all | solution.py:92
  213.9 1.2 fusion.1
  215.0 2.5 %add_convert_fusion = bf16[1024,256]{1,0:T(8,128)(2,1)} fusion(bf16[1024,256]{1,0:T(8,128)(2,1)S(1)} %copy-done.20, bf16[1024,256]{1,0:T(8,128)(2,1)S(1)} %add_convert_fusion.1, bf16[2,256,512]{2,1,0:T(8,128)(2,1)S(1)} %copy-done.16, bf16[1024,256]{0,1:T(8,128)(2,1)} %copy-done.27, bf16[1024,256]{0,1:T(8,128)(2,1)} %copy-done.25), kind=kOutput, calls=%fused_computation.26 | convolution fusion | flops 271843328 | bytes 2883584 | tf_op jit(solution)/shard_map/dot_general | solution.py:173
  217.5 11.0 %all-to-all-done.2 = f32[16,1,1280]{2,1,0:T(1,128)S(1)} async-done(((f32[16,1,1280]{2,1,0:T(1,128)}), f32[16,1,1280]{2,1,0:T(1,128)S(1)}, u32[]{:S(2)}, u32[]{:S(2)}) %all-to-all-start.2) | async-done | bytes 81952 | tf_op jit(solution)/shard_map/all_to_all | solution.py:92
  228.5 0.2 reduce.1
  228.7 0.1 reshape.59
  228.8 0.6 pad_maximum_fusion.4
  229.5 0.6 pad_maximum_fusion.2
  (69 shorter events, 0.5 us)
Async XLA Ops:
  0.6 26.7 %copy-start.8 = (bf16[2,256,512]{2,1,0:T(8,128)(2,1)S(1)}, bf16[2,256,512]{2,1,0:T(8,128)(2,1)}, u32[]{:S(2)}) copy-start(bf16[2,256,512]{2,1,0:T(8,128)(2,1)} %param.6) | copy-start | bytes 1572868
  0.6 26.7 %collective-permute-start = (bf16[1024,256]{1,0:T(8,128)(2,1)}, bf16[1024,256]{1,0:T(8,128)(2,1)S(1)}, u32[]{:S(2)}, u32[]{:S(2)}) collective-permute-start(bf16[1024,256]{1,0:T(8,128)(2,1)} %param.5), channel_id=1, source_target_pairs={{0,1},{1,2},{2,3},{3,4},{4,5},{5,6},{6,7},{7,8},{8,9},{9,10},{10,1... | collective-permute-start | bytes 1572872 | tf_op jit(solution)/shard_map/ppermute | solution.py:31
  27.3 0.8 copy-start.11
  28.1 1.2 copy-start.6
  28.1 1.2 copy-start.17
  28.6 0.8 copy-start
  29.7 51.7 %copy-start.2 = (bf16[1024,256]{1,0:T(8,128)(2,1)}, bf16[1024,256]{1,0:T(8,128)(2,1)S(1)}, u32[]{:S(2)}) copy-start(bf16[1024,256]{1,0:T(8,128)(2,1)S(1)} %fusion) | copy-start | bytes 1572868
  29.7 49.0 %collective-permute-start.1 = (bf16[1024,256]{1,0:T(8,128)(2,1)S(1)}, bf16[1024,256]{1,0:T(8,128)(2,1)}, u32[]{:S(2)}, u32[]{:S(2)}) collective-permute-start(bf16[1024,256]{1,0:T(8,128)(2,1)S(1)} %fusion), channel_id=1, source_target_pairs={{0,64},{32,96},{64,128},{96,160},{128,192},{160,224},{192,256},{22... | collective-permute-start | bytes 1572872 | tf_op jit(solution)/shard_map/ppermute | solution.py:31
  41.3 39.0 %copy-start.13 = (bf16[1024,256]{1,0:T(8,128)(2,1)S(1)}, bf16[1024,256]{1,0:T(8,128)(2,1)}, u32[]{:S(2)}) copy-start(bf16[1024,256]{1,0:T(8,128)(2,1)} %param.9) | copy-start | bytes 1572868
  81.1 0.8 copy-start.4
  81.1 1.0 copy-start.23
  81.1 2.5 %copy-start.21 = (bf16[1024,256]{0,1:T(8,128)(2,1)}, bf16[1024,256]{0,1:T(8,128)(2,1)S(1)}, u32[]{:S(2)}) copy-start(bf16[1024,256]{0,1:T(8,128)(2,1)S(1)} %get-tuple-element.17) | copy-start | bytes 1572868
  86.8 2.8 %copy-start.9 = (bf16[2,256,512]{2,1,0:T(8,128)(2,1)S(1)}, bf16[2,256,512]{2,1,0:T(8,128)(2,1)}, u32[]{:S(2)}) copy-start(bf16[2,256,512]{2,1,0:T(8,128)(2,1)} %param.6) | copy-start | bytes 1572868
  86.8 2.8 %copy-start.22 = (bf16[1024,256]{0,1:T(8,128)(2,1)S(1)}, bf16[1024,256]{0,1:T(8,128)(2,1)}, u32[]{:S(2)}) copy-start(bf16[1024,256]{0,1:T(8,128)(2,1)} %copy-done.21) | copy-start | bytes 1572868
  86.8 2.8 %copy-start.24 = (bf16[1024,256]{0,1:T(8,128)(2,1)S(1)}, bf16[1024,256]{0,1:T(8,128)(2,1)}, u32[]{:S(2)}) copy-start(bf16[1024,256]{0,1:T(8,128)(2,1)} %copy-done.23) | copy-start | bytes 1572868
  87.5 4.7 %collective-permute-start.2 = (bf16[256,640]{1,0:T(8,128)(2,1)S(1)}, bf16[256,640]{1,0:T(8,128)(2,1)S(1)}, u32[]{:S(2)}, u32[]{:S(2)}) collective-permute-start(bf16[256,640]{1,0:T(8,128)(2,1)S(1)} %bitcast.112), channel_id=1, source_target_pairs={{0,32},{32,0},{1,33},{33,1},{2,34},{34,2},{3,35},{35,3},{4,36},{36... | collective-permute-start | bytes 983048 | tf_op jit(solution)/shard_map/ppermute | solution.py:74
  90.1 12.8 %copy-start.14 = (bf16[1024,256]{1,0:T(8,128)(2,1)S(1)}, bf16[1024,256]{1,0:T(8,128)(2,1)}, u32[]{:S(2)}) copy-start(bf16[1024,256]{1,0:T(8,128)(2,1)} %param.9) | copy-start | bytes 1572868
  90.1 12.8 %copy-start.15 = (bf16[2,256,512]{2,1,0:T(8,128)(2,1)S(1)}, bf16[2,256,512]{2,1,0:T(8,128)(2,1)}, u32[]{:S(2)}) copy-start(bf16[2,256,512]{2,1,0:T(8,128)(2,1)} %param.7) | copy-start | bytes 1572868
  90.1 25.5 %collective-permute-start.6 = (bf16[1024,256]{1,0:T(8,128)(2,1)S(1)}, bf16[1024,256]{1,0:T(8,128)(2,1)S(1)}, u32[]{:S(2)}, u32[]{:S(2)}) collective-permute-start(bf16[1024,256]{1,0:T(8,128)(2,1)S(1)} %convolution_convert_fusion.1), channel_id=1, source_target_pairs={{64,0},{96,32},{128,64},{160,96},{192,128},{224,160},{256,192},{28... | collective-permute-start | bytes 1572872 | tf_op jit(solution)/shard_map/ppermute | solution.py:31
  92.3 11.2 %collective-permute-start.3 = (bf16[64,640]{1,0:T(8,128)(2,1)S(1)}, bf16[64,640]{1,0:T(8,128)(2,1)S(1)}, u32[]{:S(2)}, u32[]{:S(2)}) collective-permute-start(bf16[64,640]{1,0:T(8,128)(2,1)S(1)} %get-tuple-element.20), channel_id=1, source_target_pairs={{0,8},{8,16},{16,24},{24,0},{1,9},{9,17},{17,25},{25,1},{2,10},{10... | collective-permute-start | bytes 245768 | tf_op jit(solution)/shard_map/ppermute | solution.py:41
  95.5 8.0 %collective-permute-start.4 = (bf16[64,640]{1,0:T(8,128)(2,1)S(1)}, bf16[64,640]{1,0:T(8,128)(2,1)S(1)}, u32[]{:S(2)}, u32[]{:S(2)}) collective-permute-start(bf16[64,640]{1,0:T(8,128)(2,1)S(1)} %get-tuple-element.22), channel_id=1, source_target_pairs={{0,16},{8,24},{16,0},{24,8},{1,17},{9,25},{17,1},{25,9},{2,18},{10... | collective-permute-start | bytes 245768 | tf_op jit(solution)/shard_map/ppermute | solution.py:41
  99.9 5.5 %collective-permute-start.5 = (bf16[64,640]{1,0:T(8,128)(2,1)S(1)}, bf16[64,640]{1,0:T(8,128)(2,1)S(1)}, u32[]{:S(2)}, u32[]{:S(2)}) collective-permute-start(bf16[64,640]{1,0:T(8,128)(2,1)S(1)} %get-tuple-element.21), channel_id=1, source_target_pairs={{0,24},{8,0},{16,8},{24,16},{1,25},{9,1},{17,9},{25,17},{2,26},{10... | collective-permute-start | bytes 245768 | tf_op jit(solution)/shard_map/ppermute | solution.py:41
  103.5 12.3 %copy-start.18 = (bf16[2,256,256]{2,1,0:T(8,128)(2,1)S(1)}, bf16[2,256,256]{2,1,0:T(8,128)(2,1)}, u32[]{:S(2)}) copy-start(bf16[2,256,256]{2,1,0:T(8,128)(2,1)} %param.8) | copy-start | bytes 786436
  115.8 1.0 copy-start.1
  115.8 1.3 copy-start.7
  116.8 0.8 copy-start.25
  116.8 1.0 copy-start.27
  116.8 1.4 copy-start.12
  119.6 3.6 %copy-start.10 = (bf16[2,256,512]{2,1,0:T(8,128)(2,1)S(1)}, bf16[2,256,512]{2,1,0:T(8,128)(2,1)}, u32[]{:S(2)}) copy-start(bf16[2,256,512]{2,1,0:T(8,128)(2,1)} %param.6) | copy-start | bytes 1572868
  119.6 3.6 %copy-start.26 = (bf16[1024,256]{0,1:T(8,128)(2,1)S(1)}, bf16[1024,256]{0,1:T(8,128)(2,1)}, u32[]{:S(2)}) copy-start(bf16[1024,256]{0,1:T(8,128)(2,1)} %copy-done.25) | copy-start | bytes 1572868
  119.6 3.6 %copy-start.28 = (bf16[1024,256]{0,1:T(8,128)(2,1)S(1)}, bf16[1024,256]{0,1:T(8,128)(2,1)}, u32[]{:S(2)}) copy-start(bf16[1024,256]{0,1:T(8,128)(2,1)} %copy-done.27) | copy-start | bytes 1572868
  120.3 9.9 %collective-permute-start.7 = (bf16[256,640]{1,0:T(8,128)(2,1)S(1)}, bf16[256,640]{1,0:T(8,128)(2,1)S(1)}, u32[]{:S(2)}, u32[]{:S(2)}) collective-permute-start(bf16[256,640]{1,0:T(8,128)(2,1)S(1)} %bitcast.111), channel_id=1, source_target_pairs={{0,32},{32,0},{1,33},{33,1},{2,34},{34,2},{3,35},{35,3},{4,36},{36... | collective-permute-start | bytes 983048 | tf_op jit(solution)/shard_map/ppermute | solution.py:74
  123.7 32.6 %collective-permute-start.8 = (bf16[1024,256]{1,0:T(8,128)(2,1)S(1)}, bf16[1024,256]{1,0:T(8,128)(2,1)S(1)}, u32[]{:S(2)}, u32[]{:S(2)}) collective-permute-start(bf16[1024,256]{1,0:T(8,128)(2,1)S(1)} %convolution_convert_fusion), channel_id=1, source_target_pairs={{1,0},{2,1},{3,2},{4,3},{5,4},{6,5},{7,6},{8,7},{9,8},{10,9},{11,1... | collective-permute-start | bytes 1572872 | tf_op jit(solution)/shard_map/ppermute | solution.py:31
  130.2 83.6 %copy-start.3 = (bf16[1024,256]{1,0:T(8,128)(2,1)S(1)}, bf16[1024,256]{1,0:T(8,128)(2,1)}, u32[]{:S(2)}) copy-start(bf16[1024,256]{1,0:T(8,128)(2,1)} %copy-done.2) | copy-start | bytes 1572868
  130.3 83.6 %copy-start.5 = (bf16[1024,256]{0,1:T(8,128)(2,1)S(1)}, bf16[1024,256]{0,1:T(8,128)(2,1)}, u32[]{:S(2)}) copy-start(bf16[1024,256]{0,1:T(8,128)(2,1)} %copy-done.4) | copy-start | bytes 1572868
  156.3 0.8 copy-start.19
  156.3 58.7 %copy-start.16 = (bf16[2,256,512]{2,1,0:T(8,128)(2,1)S(1)}, bf16[2,256,512]{2,1,0:T(8,128)(2,1)}, u32[]{:S(2)}) copy-start(bf16[2,256,512]{2,1,0:T(8,128)(2,1)} %param.7) | copy-start | bytes 1572868
  157.1 57.9 %copy-start.20 = (bf16[1024,256]{1,0:T(8,128)(2,1)S(1)}, bf16[1024,256]{1,0:T(8,128)(2,1)}, u32[]{:S(2)}) copy-start(bf16[1024,256]{1,0:T(8,128)(2,1)} %copy-done.19) | copy-start | bytes 1572868
  205.0 23.5 %all-to-all-start.2 = ((f32[16,1,1280]{2,1,0:T(1,128)}), f32[16,1,1280]{2,1,0:T(1,128)S(1)}, u32[]{:S(2)}, u32[]{:S(2)}) async-start(f32[16,1,1280]{2,1,0:T(1,128)} %broadcast_in_dim.2), calls=%async_computation.2 | async-start | bytes 163840 | tf_op jit(solution)/shard_map/all_to_all | solution.py:92

commit v16 on v10

--- a/solution.py
+++ b/solution.py
@@ -170,7 +170,7 @@
         ).astype(jnp.bfloat16)
         arrived = return_past(sent_back, layer_at)
         operands = (earlier, current, gated_out, grad_preact, upstream)
-        near_list[layer_at] = near_sum(layer_term(operands, grad_scale), layer_at == 0)
+        near_list[layer_at] = near_sum(layer_term(operands, grad_scale), True)
         if layer_at > 0:
             near_list, arrived = lax.optimization_barrier((near_list, arrived))
         local_grad = upstream.astype(jnp.float32) + jnp.dot(

time: 220 us -> 226 us (1.027)
  waiting for transfers between devices: 82.7 us -> 95.1 us
  starting transfers between devices: 89.3 us -> 80.1 us
    ppermute x4 -> x0, starting transfers between devices: 12.8 us -> none  [the longest x3 10.6 us: scatter_sum(): lax.ppermute(piece.astype(jnp.bfloat16), axes, [(i, (i + shift) % size) f...]
    ppermute x4, waiting for transfers between devices: 68.2 us -> 75.9 us  [from_behind(): return lax.ppermute(array, axes, pairs)]
    all_to_all x0 -> x1, waiting for transfers between devices: none -> 5.32 us  [near_sum(): lax.all_to_all(pieces.astype(jnp.bfloat16), ('core', 'x'), 0, 0, tiled=True)]
    all_to_all x0 -> x1, starting transfers between devices: none -> 4.6 us  [near_sum(): lax.all_to_all(pieces.astype(jnp.bfloat16), ('core', 'x'), 0, 0, tiled=True)]
    convert_element_type x2 -> x4, local copies, waits for them, and re-layouts: 0.23 us -> 4.8 us  [near_sum(): pieces.astype(jnp.bfloat16)]
  transfers between devices with their start and end apart: 10 -> 7, of which waited for: 6 -> 6; matrix products, arithmetic and copies ran while one was open for 5% -> 6% of each run, Pallas kernels for 0% -> 0%
where the time goes in v16:
time: 226 us; the launch traced here: 225 us
  waiting for transfers between devices  95.1 us (42%)
  starting transfers between devices  80.1 us (35%)
  matrix products  16.5 us (7%)
  blocking collectives  15.9 us (7%)
  local copies, waits for them, and re-layouts  9.5 us (4%)
  other arithmetic  6.68 us (3%)
    ppermute x4, waiting for transfers between devices, from_behind(): return lax.ppermute(array, axes, pairs)  75.9 us
    all_to_all x1, starting transfers between devices, far_sum(): lax.all_to_all(rows.astype(jnp.bfloat16), ('y', 'z_hi', 'z_lo'), 0, 0, ti...  41.2 us
    ppermute x4, starting transfers between devices, from_behind(): return lax.ppermute(array, axes, pairs)  26.8 us
    all_to_all x1, blocking collectives, near_sum(): lax.all_to_all(pieces.astype(jnp.bfloat16), ('core', 'x'), 0, 0, tiled=True)  15.9 us
    all_to_all x1, waiting for transfers between devices, far_sum(): gathered = lax.all_to_all(spread, ('y', 'z_hi', 'core'), 0, 0, tiled=True)  11 us
    all_to_all x1, starting transfers between devices, far_sum(): gathered = lax.all_to_all(spread, ('y', 'z_hi', 'core'), 0, 0, tiled=True)  7.5 us
    all_to_all x1, waiting for transfers between devices, near_sum(): lax.all_to_all(pieces.astype(jnp.bfloat16), ('core', 'x'), 0, 0, tiled=True)  5.32 us
    convert_element_type x4, local copies, waits for them, and re-layouts, near_sum(): pieces.astype(jnp.bfloat16)  4.8 us
  transfers between devices with their start and end apart: 7, of which 6 were waited for; matrix products, arithmetic and copies ran while one was open for 6% of the time, Pallas kernels for 0%

profile of v16, /device:TPU:1, one launch (start us, length us, event | category | flops | bytes accessed | tf_op | source)
XLA Modules:
  0.0 224.9 jit_solution(12999065324033518687)
XLA Ops:
  0.6 4.5 %collective-permute-start = (bf16[1024,256]{1,0:T(8,128)(2,1)}, bf16[1024,256]{1,0:T(8,128)(2,1)S(1)}, u32[]{:S(2)}, u32[]{:S(2)}) collective-permute-start(bf16[1024,256]{1,0:T(8,128)(2,1)} %param.5), channel_id=1, source_target_pairs={{0,1},{1,2},{2,3},{3,4},{4,5},{5,6},{6,7},{7,8},{8,9},{9,10},{10,1... | collective-permute-start | bytes 1572872 | tf_op jit(solution)/shard_map/ppermute | solution.py:31
  5.2 1.6 fusion.16
  6.8 20.6 %collective-permute-done = bf16[1024,256]{1,0:T(8,128)(2,1)S(1)} collective-permute-done((bf16[1024,256]{1,0:T(8,128)(2,1)}, bf16[1024,256]{1,0:T(8,128)(2,1)S(1)}, u32[]{:S(2)}, u32[]{:S(2)}) %collective-permute-start) | collective-permute-done | bytes 524320 | tf_op jit(solution)/shard_map/ppermute | solution.py:31
  27.3 0.5 convolution_add_fusion.1
  27.8 0.3 copy-done.8
  28.1 0.4 multiply_convert_fusion.5
  28.5 0.6 copy-done.2
  29.2 0.1 copy-done.15
  29.2 0.4 fusion.2
  29.6 9.4 %collective-permute-start.1 = (bf16[1024,256]{1,0:T(8,128)(2,1)S(1)}, bf16[1024,256]{1,0:T(8,128)(2,1)S(1)}, u32[]{:S(2)}, u32[]{:S(2)}) collective-permute-start(bf16[1024,256]{1,0:T(8,128)(2,1)S(1)} %fusion.2), channel_id=1, source_target_pairs={{0,64},{32,96},{64,128},{96,160},{128,192},{160,224},{192,256},{22... | collective-permute-start | bytes 1572872 | tf_op jit(solution)/shard_map/ppermute | solution.py:31
  39.0 0.5 fusion.11
  39.5 0.0 copy-start.10
  39.5 39.1 %collective-permute-done.1 = bf16[1024,256]{1,0:T(8,128)(2,1)S(1)} collective-permute-done((bf16[1024,256]{1,0:T(8,128)(2,1)S(1)}, bf16[1024,256]{1,0:T(8,128)(2,1)S(1)}, u32[]{:S(2)}, u32[]{:S(2)}) %collective-permute-start.1) | collective-permute-done | bytes 524320 | tf_op jit(solution)/shard_map/ppermute | solution.py:31
  78.6 0.5 convolution_add_fusion
  79.1 0.8 multiply_convert_fusion.3
  79.9 0.0 copy-start
  79.9 0.0 copy-start.18
  79.9 0.8 copy-done
  80.7 0.3 fusion.40
  81.0 0.5 fusion.38
  81.5 0.5 fusion.39
  82.0 1.0 fusion
  83.0 2.6 %convert_element_type.103 = bf16[4,64,2,640]{3,2,1,0:T(2,128)(2,1)} reshape(bf16[256,1280]{1,0:T(8,128)(2,1)} %fusion) | data formatting | bytes 1310720 | tf_op jit(solution)/shard_map/convert_element_type | solution.py:75
  85.5 2.0 copy.28
  87.6 4.6 %all-to-all-start = ((bf16[8,64,640]{2,1,0:T(8,128)(2,1)}), bf16[8,64,640]{2,1,0:T(8,128)(2,1)}, u32[]{:S(2)}, u32[]{:S(2)}) async-start(bf16[8,64,640]{2,1,0:T(8,128)(2,1)} %bitcast.85), calls=%async_computation | async-start | bytes 1310720 | tf_op jit(solution)/shard_map/all_to_all | solution.py:75
  92.2 2.7 %convolution_convert_fusion.1 = bf16[1024,256]{1,0:T(8,128)(2,1)} fusion(bf16[2,256,512]{2,1,0:T(8,128)(2,1)} %param.6, bf16[1024,256]{0,1:T(8,128)(2,1)} %copy-done.18, bf16[1024,256]{0,1:T(8,128)(2,1)} %copy-done.16), kind=kOutput, calls=%fused_computation.12 | convolution fusion | flops 270794752 | bytes 1835008 | tf_op jit(solution)/shard_map/dot_general | solution.py:168
  94.9 1.3 collective-permute-start.2
  96.2 1.5 convolution_add_fusion.5
  97.7 5.3 %all-to-all-done = bf16[8,64,640]{2,1,0:T(8,128)(2,1)} async-done(((bf16[8,64,640]{2,1,0:T(8,128)(2,1)}), bf16[8,64,640]{2,1,0:T(8,128)(2,1)}, u32[]{:S(2)}, u32[]{:S(2)}) %all-to-all-start) | async-done | bytes 655392 | tf_op jit(solution)/shard_map/all_to_all | solution.py:75
  103.0 1.2 convert_reduce_fusion
  104.2 16.2 %collective-permute-done.2 = bf16[1024,256]{1,0:T(8,128)(2,1)} collective-permute-done((bf16[1024,256]{1,0:T(8,128)(2,1)}, bf16[1024,256]{1,0:T(8,128)(2,1)}, u32[]{:S(2)}, u32[]{:S(2)}) %collective-permute-start.2) | collective-permute-done | bytes 524320 | tf_op jit(solution)/shard_map/ppermute | solution.py:31
  120.5 1.5 add_convert_fusion.1
  122.0 0.7 multiply_convert_fusion.1
  122.7 0.1 copy-done.4
  122.8 0.3 fusion.41
  123.1 0.1 copy-done.3
  123.2 0.5 convolution_bitcast_fusion
  123.7 0.1 copy-done.22
  123.8 0.4 copy-done.9
  124.2 0.5 convolution_bitcast_fusion.1
  124.7 0.1 fusion.1
  124.8 0.1 convert_element_type.115
  124.9 0.1 copy.32
  125.0 0.0 copy-start.7
  125.1 15.9 %all_to_all.20 = bf16[8,64,640]{2,1,0:T(8,128)(2,1)S(1)} all-to-all(bf16[8,64,640]{2,1,0:T(8,128)(2,1)S(1)} %bitcast.86), channel_id=1, replica_groups=mesh['y'=4,'z_hi'=2,'core'=2,'x'=4,'z_lo'=8] {'core','x'}, dimensions={0} | all-to-all | bytes 1310720 | tf_op jit(solution)/shard_map/all_to_all | solution.py:75
  141.0 0.1 reduce.1
  141.2 0.5 broadcast.36
  141.7 0.7 reduce.3
  142.4 0.7 reshape.58
  143.1 41.2 %all-to-all-start.2 = ((bf16[64,2,640]{2,1,0:T(2,128)(2,1)}), bf16[64,2,640]{2,1,0:T(2,128)(2,1)S(1)}, u32[]{:S(2)}, u32[]{:S(2)}) async-start(bf16[64,2,640]{2,1,0:T(2,128)(2,1)} %reshape.58), calls=%async_computation.2 | async-start | bytes 327680 | tf_op jit(solution)/shard_map/all_to_all | solution.py:91
  184.3 1.3 convolution_convert_fusion
  185.6 11.7 %collective-permute-start.3 = (bf16[1024,256]{1,0:T(8,128)(2,1)}, bf16[1024,256]{1,0:T(8,128)(2,1)S(1)}, u32[]{:S(2)}, u32[]{:S(2)}) collective-permute-start(bf16[1024,256]{1,0:T(8,128)(2,1)} %convolution_convert_fusion), channel_id=1, source_target_pairs={{1,0},{2,1},{3,2},{4,3},{5,4},{6,5},{7,6},{8,7},{9,8},{10,9},{11,1... | collective-permute-start | bytes 1572872 | tf_op jit(solution)/shard_map/ppermute | solution.py:31
  197.3 2.8 %all-to-all-done.2 = bf16[64,2,640]{2,1,0:T(2,128)(2,1)S(1)} async-done(((bf16[64,2,640]{2,1,0:T(2,128)(2,1)}), bf16[64,2,640]{2,1,0:T(2,128)(2,1)S(1)}, u32[]{:S(2)}, u32[]{:S(2)}) %all-to-all-start.2) | async-done | bytes 163872 | tf_op jit(solution)/shard_map/all_to_all | solution.py:91
  200.1 0.1 reshape.59
  200.2 0.3 convert_reduce_fusion.1
  200.5 0.7 broadcast_in_dim.2
  201.2 7.5 %all-to-all-start.3 = ((f32[16,1,1280]{2,1,0:T(1,128)}), f32[16,1,1280]{2,1,0:T(1,128)S(1)}, u32[]{:S(2)}, u32[]{:S(2)}) async-start(f32[16,1,1280]{2,1,0:T(1,128)} %broadcast_in_dim.2), calls=%async_computation.3 | async-start | bytes 163840 | tf_op jit(solution)/shard_map/all_to_all | solution.py:94
  208.7 1.1 fusion.3
  209.9 2.5 %add_convert_fusion = bf16[1024,256]{1,0:T(8,128)(2,1)} fusion(bf16[1024,256]{1,0:T(8,128)(2,1)S(1)} %collective-permute-done.3, bf16[1024,256]{1,0:T(8,128)(2,1)S(1)} %copy-done.5, bf16[2,256,512]{2,1,0:T(8,128)(2,1)S(1)} %copy-done.14, bf16[1024,256]{0,1:T(8,128)(2,1)} %copy-done.22, bf16[1024,256]{0,1:T(8,128)(2,1)} %copy-done.20), kind=kOutput, calls=%fused_computation.29 | convolution fusion | flops 271843328 | bytes 2883584 | tf_op jit(solution)/shard_map/dot_general | solution.py:176
  212.4 11.0 %all-to-all-done.3 = f32[16,1,1280]{2,1,0:T(1,128)S(1)} async-done(((f32[16,1,1280]{2,1,0:T(1,128)}), f32[16,1,1280]{2,1,0:T(1,128)S(1)}, u32[]{:S(2)}, u32[]{:S(2)}) %all-to-all-start.3) | async-done | bytes 81952 | tf_op jit(solution)/shard_map/all_to_all | solution.py:94
  223.4 0.2 reduce.2
  223.6 0.1 reshape.54
  223.7 0.6 pad_maximum_fusion.4
  224.3 0.6 pad_maximum_fusion.2
  (45 shorter events, 0.2 us)
Async XLA Ops:
  0.6 26.7 %copy-start.6 = (bf16[2,256,512]{2,1,0:T(8,128)(2,1)S(1)}, bf16[2,256,512]{2,1,0:T(8,128)(2,1)}, u32[]{:S(2)}) copy-start(bf16[2,256,512]{2,1,0:T(8,128)(2,1)} %param.6) | copy-start | bytes 1572868
  0.6 26.7 %collective-permute-start = (bf16[1024,256]{1,0:T(8,128)(2,1)}, bf16[1024,256]{1,0:T(8,128)(2,1)S(1)}, u32[]{:S(2)}, u32[]{:S(2)}) collective-permute-start(bf16[1024,256]{1,0:T(8,128)(2,1)} %param.5), channel_id=1, source_target_pairs={{0,1},{1,2},{2,3},{3,4},{4,5},{5,6},{6,7},{7,8},{8,9},{9,10},{10,1... | collective-permute-start | bytes 1572872 | tf_op jit(solution)/shard_map/ppermute | solution.py:31
  27.3 0.8 copy-start.8
  28.1 1.0 copy-start.2
  28.1 1.1 copy-start.15
  28.1 10.9 %copy-start.12 = (bf16[2,256,512]{2,1,0:T(8,128)(2,1)S(1)}, bf16[2,256,512]{2,1,0:T(8,128)(2,1)}, u32[]{:S(2)}) copy-start(bf16[2,256,512]{2,1,0:T(8,128)(2,1)} %param.7) | copy-start | bytes 1572868
  29.6 49.0 %collective-permute-start.1 = (bf16[1024,256]{1,0:T(8,128)(2,1)S(1)}, bf16[1024,256]{1,0:T(8,128)(2,1)S(1)}, u32[]{:S(2)}, u32[]{:S(2)}) collective-permute-start(bf16[1024,256]{1,0:T(8,128)(2,1)S(1)} %fusion.2), channel_id=1, source_target_pairs={{0,64},{32,96},{64,128},{96,160},{128,192},{160,224},{192,256},{22... | collective-permute-start | bytes 1572872 | tf_op jit(solution)/shard_map/ppermute | solution.py:31
  39.5 39.6 %copy-start.10 = (bf16[1024,256]{1,0:T(8,128)(2,1)S(1)}, bf16[1024,256]{1,0:T(8,128)(2,1)}, u32[]{:S(2)}) copy-start(bf16[1024,256]{1,0:T(8,128)(2,1)} %param.9) | copy-start | bytes 1572868
  79.9 0.8 copy-start
  79.9 1.6 copy-start.18
  79.9 2.1 copy-start.16
  87.6 15.5 %all-to-all-start = ((bf16[8,64,640]{2,1,0:T(8,128)(2,1)}), bf16[8,64,640]{2,1,0:T(8,128)(2,1)}, u32[]{:S(2)}, u32[]{:S(2)}) async-start(bf16[8,64,640]{2,1,0:T(8,128)(2,1)} %bitcast.85), calls=%async_computation | async-start | bytes 1310720 | tf_op jit(solution)/shard_map/all_to_all | solution.py:75
  92.2 4.0 %copy-start.11 = (bf16[1024,256]{1,0:T(8,128)(2,1)S(1)}, bf16[1024,256]{1,0:T(8,128)(2,1)}, u32[]{:S(2)}) copy-start(bf16[1024,256]{1,0:T(8,128)(2,1)} %param.9) | copy-start | bytes 1572868
  92.2 4.0 %copy-start.13 = (bf16[2,256,512]{2,1,0:T(8,128)(2,1)S(1)}, bf16[2,256,512]{2,1,0:T(8,128)(2,1)}, u32[]{:S(2)}) copy-start(bf16[2,256,512]{2,1,0:T(8,128)(2,1)} %param.7) | copy-start | bytes 1572868
  92.2 4.0 %copy-start.17 = (bf16[1024,256]{0,1:T(8,128)(2,1)S(1)}, bf16[1024,256]{0,1:T(8,128)(2,1)}, u32[]{:S(2)}) copy-start(bf16[1024,256]{0,1:T(8,128)(2,1)} %copy-done.16) | copy-start | bytes 1572868
  92.2 4.0 %copy-start.19 = (bf16[1024,256]{0,1:T(8,128)(2,1)S(1)}, bf16[1024,256]{0,1:T(8,128)(2,1)}, u32[]{:S(2)}) copy-start(bf16[1024,256]{0,1:T(8,128)(2,1)} %copy-done.18) | copy-start | bytes 1572868
  94.9 25.6 %collective-permute-start.2 = (bf16[1024,256]{1,0:T(8,128)(2,1)}, bf16[1024,256]{1,0:T(8,128)(2,1)}, u32[]{:S(2)}, u32[]{:S(2)}) collective-permute-start(bf16[1024,256]{1,0:T(8,128)(2,1)} %convolution_convert_fusion.1), channel_id=1, source_target_pairs={{64,0},{96,32},{128,64},{160,96},{192,128},{224,160},{256,192},{28... | collective-permute-start | bytes 1572872 | tf_op jit(solution)/shard_map/ppermute | solution.py:31
  121.9 0.8 copy-start.4
  121.9 1.2 copy-start.3
  122.8 0.9 copy-start.20
  122.8 1.0 copy-start.22
  122.8 1.4 copy-start.9
  125.0 59.3 %copy-start.7 = (bf16[2,256,512]{2,1,0:T(8,128)(2,1)S(1)}, bf16[2,256,512]{2,1,0:T(8,128)(2,1)}, u32[]{:S(2)}) copy-start(bf16[2,256,512]{2,1,0:T(8,128)(2,1)} %param.6) | copy-start | bytes 1572868
  125.0 59.3 %copy-start.21 = (bf16[1024,256]{0,1:T(8,128)(2,1)S(1)}, bf16[1024,256]{0,1:T(8,128)(2,1)}, u32[]{:S(2)}) copy-start(bf16[1024,256]{0,1:T(8,128)(2,1)} %copy-done.20) | copy-start | bytes 1572868
  125.1 59.3 %copy-start.23 = (bf16[1024,256]{0,1:T(8,128)(2,1)S(1)}, bf16[1024,256]{0,1:T(8,128)(2,1)}, u32[]{:S(2)}) copy-start(bf16[1024,256]{0,1:T(8,128)(2,1)} %copy-done.22) | copy-start | bytes 1572868
  143.1 65.6 %copy-start.1 = (bf16[1024,256]{0,1:T(8,128)(2,1)S(1)}, bf16[1024,256]{0,1:T(8,128)(2,1)}, u32[]{:S(2)}) copy-start(bf16[1024,256]{0,1:T(8,128)(2,1)} %copy-done) | copy-start | bytes 1572868
  143.1 57.0 %all-to-all-start.2 = ((bf16[64,2,640]{2,1,0:T(2,128)(2,1)}), bf16[64,2,640]{2,1,0:T(2,128)(2,1)S(1)}, u32[]{:S(2)}, u32[]{:S(2)}) async-start(bf16[64,2,640]{2,1,0:T(2,128)(2,1)} %reshape.58), calls=%async_computation.2 | async-start | bytes 327680 | tf_op jit(solution)/shard_map/all_to_all | solution.py:91
  185.6 24.3 %copy-start.5 = (bf16[1024,256]{1,0:T(8,128)(2,1)S(1)}, bf16[1024,256]{1,0:T(8,128)(2,1)}, u32[]{:S(2)}) copy-start(bf16[1024,256]{1,0:T(8,128)(2,1)} %copy-done.4) | copy-start | bytes 1572868
  185.6 24.3 %copy-start.14 = (bf16[2,256,512]{2,1,0:T(8,128)(2,1)S(1)}, bf16[2,256,512]{2,1,0:T(8,128)(2,1)}, u32[]{:S(2)}) copy-start(bf16[2,256,512]{2,1,0:T(8,128)(2,1)} %param.7) | copy-start | bytes 1572868
  185.6 24.3 %collective-permute-start.3 = (bf16[1024,256]{1,0:T(8,128)(2,1)}, bf16[1024,256]{1,0:T(8,128)(2,1)S(1)}, u32[]{:S(2)}, u32[]{:S(2)}) collective-permute-start(bf16[1024,256]{1,0:T(8,128)(2,1)} %convolution_convert_fusion), channel_id=1, source_target_pairs={{1,0},{2,1},{3,2},{4,3},{5,4},{6,5},{7,6},{8,7},{9,8},{10,9},{11,1... | collective-permute-start | bytes 1572872 | tf_op jit(solution)/shard_map/ppermute | solution.py:31
  201.2 22.2 %all-to-all-start.3 = ((f32[16,1,1280]{2,1,0:T(1,128)}), f32[16,1,1280]{2,1,0:T(1,128)S(1)}, u32[]{:S(2)}, u32[]{:S(2)}) async-start(f32[16,1,1280]{2,1,0:T(1,128)} %broadcast_in_dim.2), calls=%async_computation.3 | async-start | bytes 163840 | tf_op jit(solution)/shard_map/all_to_all | solution.py:94
